TPU v7x, 32 devices: a whole 2x2x4 slice. The times are simulated.
32 devices in a mesh: groups: 2 (over y), tm: 4 (over z), height: 2 (over x), chan: 2 (over core).
Axes of the slice: x: 2, y: 2, z: 4, core: 2. Of those that a mesh axis runs over, the one named last changes fastest.
Arguments:
- video: bfloat16 [16, 72, 320, 128], P(('groups', 'tm'), 'height', 'chan'), parts along dimension 0, may hold values from -52 to 52
- norm1_gain: float32 [320], P('chan'), may hold values from 0.25 to 1.75
- norm1_bias: float32 [320], P('chan'), may hold values from -3 to 3
- spatial_weight: bfloat16 [3, 3, 320, 320], P(None, None, 'tm', 'chan'), may hold values from -0.3125 to 0.3125
- spatial_bias: float32 [320], P('chan'), may hold values from -3 to 3
- norm2_gain: float32 [320], P('chan'), may hold values from 0.25 to 1.75
- norm2_bias: float32 [320], P('chan'), may hold values from -3 to 3
- temporal_weight: bfloat16 [3, 320, 320], P(None, 'tm', 'chan'), may hold values from -0.3125 to 0.3125
- temporal_bias: float32 [320], P('chan'), may hold values from -3 to 3
Outputs:
- clip_out: bfloat16 [16, 72, 320, 128], P(('groups', 'tm'), 'height', 'chan'), parts along dimension 0
There are 2 independent parts, one for each index of `groups`. A program takes and returns all parts, laid end to end along the dimension named above; an argument that names none is the same for every part. Nothing has to cross between parts.
All inputs are finite; a program needn't handle non-finite values.
Results may differ from a plain program's by a relative error of at most 0.0052.
Values may be sent and summed in bfloat16 or wider, within the bound.
No kernel may reach another device: no remote copies, remote signals or barrier semaphores. Data moves between devices by JAX's collectives and lax.ppermute only.
A program may use at most 128 MiB of HBM per device.

v0:
```python
import jax
import jax.numpy as jnp
from jax import lax
from jax.sharding import PartitionSpec as P

C = 320
GROUPS = 32


EPSILON = 1e-06


def with_halo(block, sides, width):
    for axis, dim in sides:
        count = lax.axis_size(axis)
        forward = [(i, i + 1) for i in range(count - 1)]
        backward = [(target, source) for source, target in forward]
        low = lax.ppermute(
            lax.slice_in_dim(block, block.shape[dim] - width, None, axis=dim), axis, forward
        )
        high = lax.ppermute(lax.slice_in_dim(block, 0, width, axis=dim), axis, backward)
        block = jnp.concatenate([low, block, high], axis=dim)
    return block


def spatial_taps(running, channel_slab, weight_piece, rows, width):
    for row_tap in range(3):
        for col_tap in range(3):
            window = channel_slab[:, row_tap : row_tap + rows, :, col_tap : col_tap + width]
            running = running + jnp.einsum(
                "frcw,co->frow",
                window,
                weight_piece[row_tap, col_tap],
                preferred_element_type=jnp.float32,
            )
    return running


def temporal_taps(running, channel_slab, weight_piece, frames):
    for frame_tap in range(3):
        window = channel_slab[frame_tap : frame_tap + frames]
        running = running + jnp.einsum(
            "frcw,co->frow", window, weight_piece[frame_tap], preferred_element_type=jnp.float32
        )
    return running


def body(
    video,
    norm1_gain,
    norm1_bias,
    spatial_weight,
    spatial_bias,
    norm2_gain,
    norm2_bias,
    temporal_weight,
    temporal_bias,
):
    frames, rows, local_chan, width = video.shape
    group_size = C // GROUPS
    local_groups = local_chan // group_size
    values = video.astype(jnp.float32)
    grouped = values.reshape(frames, rows, local_groups, group_size, width)
    entries = rows * lax.axis_size("height") * width * group_size
    totals = lax.psum(jnp.sum(grouped, axis=(1, 3, 4)), "height")
    average = (totals / entries).reshape(frames, 1, local_groups, 1, 1)
    centred = grouped - average
    squares = lax.psum(jnp.sum(centred * centred, axis=(1, 3, 4)), "height")
    variance = (squares / entries).reshape(frames, 1, local_groups, 1, 1)
    scaled = (centred * lax.rsqrt(variance + EPSILON)).reshape(frames, rows, local_chan, width)
    act_one = jax.nn.silu(scaled * norm1_gain[:, None] + norm1_bias[:, None]).astype(jnp.bfloat16)
    with_rows = with_halo(act_one, (("height", 1),), 1)
    all_inputs = lax.all_gather(with_rows, "chan", axis=2, tiled=True)
    padded = jnp.pad(all_inputs, ((0, 0), (0, 0), (0, 0), (1, 1)))
    empty = jnp.zeros((frames, rows, local_chan, width), jnp.float32)
    full_spatial = lax.all_gather(spatial_weight, "tm", axis=2, tiled=True)
    spatial_sum = spatial_taps(empty, padded, full_spatial, rows, width)
    hidden = (values + spatial_sum + spatial_bias[:, None]).astype(jnp.bfloat16)
    grouped_two = hidden.astype(jnp.float32).reshape(frames, rows, local_groups, group_size, width)
    entries_two = frames * lax.axis_size("tm") * entries
    totals_two = lax.psum(jnp.sum(grouped_two, axis=(0, 1, 3, 4)), ("tm", "height"))
    average_two = (totals_two / entries_two).reshape(1, 1, local_groups, 1, 1)
    centred_two = grouped_two - average_two
    squares_two = lax.psum(jnp.sum(centred_two * centred_two, axis=(0, 1, 3, 4)), ("tm", "height"))
    variance_two = (squares_two / entries_two).reshape(1, 1, local_groups, 1, 1)
    scaled_two = (centred_two * lax.rsqrt(variance_two + EPSILON)).reshape(
        frames, rows, local_chan, width
    )
    act_two = jax.nn.silu(scaled_two * norm2_gain[:, None] + norm2_bias[:, None]).astype(
        jnp.bfloat16
    )
    wide_two = lax.all_gather(act_two, "chan", axis=2, tiled=True)
    with_frames = with_halo(wide_two, (("tm", 0),), 1)
    full_temporal = lax.all_gather(temporal_weight, "tm", axis=1, tiled=True)
    temporal_sum = temporal_taps(empty, with_frames, full_temporal, frames)
    return (hidden.astype(jnp.float32) + temporal_sum + temporal_bias[:, None]).astype(jnp.bfloat16)


def solution(mesh):
    return jax.shard_map(
        body,
        mesh=mesh,
        in_specs=(
            P(("groups", "tm"), "height", "chan", None),
            P("chan"),
            P("chan"),
            P(None, None, "tm", "chan"),
            P("chan"),
            P("chan"),
            P("chan"),
            P(None, "tm", "chan"),
            P("chan"),
        ),
        out_specs=P(("groups", "tm"), "height", "chan", None),
        check_vma=False,
    )
```

profile of v0, /device:TPU:0, one launch (start us, length us, event | category | flops | bytes accessed | tf_op | source)
XLA Modules:
  0.0 309.7 jit_solution(8180734178120804956)
XLA Ops:
  6.5 2.5 convert_reduce_fusion.1
  9.0 0.1 reduce_sum.47
  9.1 0.1 reduce_sum.51
  9.2 5.8 %psum.28 = f32[2,16]{1,0:T(2,128)S(1)} all-reduce(f32[2,16]{1,0:T(2,128)S(1)} %reduce_sum.51), channel_id=1, replica_groups=mesh['groups'=2,'tm'=4,'height'=2,'chan'=2] {'height'}, use_global_device_ids=true, to_apply=%region_2.0 | all-reduce | flops 32 | bytes 256 | tf_op jit(solution)/shard_map/psum | solution.py:65
  15.0 0.1 sub.28
  15.1 0.1 sub.29
  15.2 2.7 fusion.13
  17.9 0.1 reduce_sum.53
  18.0 0.1 reduce_sum.54
  18.1 4.9 %psum.29 = f32[2,16]{1,0:T(2,128)S(1)} all-reduce(f32[2,16]{1,0:T(2,128)S(1)} %reduce_sum.54), channel_id=1, replica_groups=mesh['groups'=2,'tm'=4,'height'=2,'chan'=2] {'height'}, use_global_device_ids=true, to_apply=%region_5.6 | all-reduce | flops 32 | bytes 256 | tf_op jit(solution)/shard_map/psum | solution.py:68
  23.0 0.1 mul.58
  23.1 0.1 mul.59
  23.2 2.3 fusion.21
  25.6 4.1 %collective-permute-start = (bf16[2,1,160,128]{3,2,1,0:T(8,128)(2,1)S(1)}, bf16[2,1,160,128]{3,2,1,0:T(8,128)(2,1)S(1)}, u32[]{:S(2)}, u32[]{:S(2)}) collective-permute-start(bf16[2,1,160,128]{3,2,1,0:T(8,128)(2,1)S(1)} %get-tuple-element.7), channel_id=1, source_target_pairs={{0,2},{1,3},{4,6},{5,7},{8,10},{9,11},{12,14},{13,15},{16,18},{17,... | collective-permute-start | bytes 245768 | tf_op jit(solution)/shard_map/ppermute | solution.py:18
  29.7 1.3 collective-permute-start.1
  31.0 0.7 collective-permute-done
  31.7 4.3 %collective-permute-done.1 = bf16[2,1,160,128]{3,2,1,0:T(8,128)(2,1)S(1)} collective-permute-done((bf16[2,1,160,128]{3,2,1,0:T(8,128)(2,1)S(1)}, bf16[2,1,160,128]{3,2,1,0:T(8,128)(2,1)S(1)}, u32[]{:S(2)}, u32[]{:S(2)}) %collective-permute-start.1) | collective-permute-done | bytes 81952 | tf_op jit(solution)/shard_map/ppermute | solution.py:21
  36.0 2.1 pad_maximum_fusion.4
  38.2 0.3 copy.28
  38.5 33.1 %all_gather.13 = bf16[3,3,320,160]{3,1,0,2:T(4,128)(2,1)S(1)} all-gather(bf16[3,3,80,160]{3,1,0,2:T(4,128)(2,1)S(1)} %copy.28), channel_id=1, replica_groups=mesh['groups'=2,'tm'=4,'height'=2,'chan'=2] {'tm'}, dimensions={2}, use_global_device_ids=true | all-gather | bytes 1152000 | tf_op jit(solution)/shard_map/all_gather | solution.py:76
  71.5 2.6 fusion.67
  74.2 0.2 copy.54
  74.4 0.2 copy.56
  74.6 0.2 copy.57
  74.8 0.2 copy.59
  74.9 0.2 copy.60
  75.1 0.8 copy.61
  76.0 0.8 copy.58
  76.8 0.8 copy.55
  77.6 0.2 copy.62
  77.8 4.6 %fusion.26 = f32[2,36,128,160]{2,3,1,0:T(8,128)S(1)} fusion(bf16[2,38,320,128]{3,2,1,0:T(8,128)(2,1)} %all-gather.3.cloned.1.call-done, bf16[1,1,320,160]{2,3,1,0:T(8,128)(2,1)S(1)} %copy.54), kind=kOutput, calls=%fused_computation.38 | convolution fusion | flops 943718400 | bytes 12226560 | tf_op jit(solution)/shard_map/frcw,co->frow/dot_general | solution.py:30
  82.5 4.3 %fusion.27 = f32[2,36,128,160]{2,3,1,0:T(8,128)} fusion(bf16[2,38,320,128]{3,2,1,0:T(8,128)(2,1)S(1)} %copy-done, bf16[1,1,320,160]{2,3,1,0:T(8,128)(2,1)S(1)} %copy.56), kind=kOutput, calls=%fused_computation.39 | convolution fusion | flops 943718400 | bytes 12226560 | tf_op jit(solution)/shard_map/frcw,co->frow/dot_general | solution.py:30
  86.8 4.4 %fusion.28 = f32[2,36,128,160]{2,3,1,0:T(8,128)} fusion(bf16[2,38,320,128]{3,2,1,0:T(8,128)(2,1)S(1)} %copy-done, bf16[1,1,320,160]{2,3,1,0:T(8,128)(2,1)S(1)} %copy.57), kind=kOutput, calls=%fused_computation.40 | convolution fusion | flops 943718400 | bytes 12226560 | tf_op jit(solution)/shard_map/frcw,co->frow/dot_general | solution.py:30
  91.2 4.3 %fusion.29 = f32[2,36,128,160]{2,3,1,0:T(8,128)} fusion(bf16[2,38,320,128]{3,2,1,0:T(8,128)(2,1)S(1)} %copy-done, bf16[1,1,320,160]{2,3,1,0:T(8,128)(2,1)S(1)} %copy.59), kind=kOutput, calls=%fused_computation.41 | convolution fusion | flops 943718400 | bytes 12226560 | tf_op jit(solution)/shard_map/frcw,co->frow/dot_general | solution.py:30
  95.5 4.4 %fusion.30 = f32[2,36,128,160]{2,3,1,0:T(8,128)} fusion(bf16[2,38,320,128]{3,2,1,0:T(8,128)(2,1)S(1)} %copy-done, bf16[1,1,320,160]{2,3,1,0:T(8,128)(2,1)S(1)} %copy.60), kind=kOutput, calls=%fused_computation.42 | convolution fusion | flops 943718400 | bytes 12226560 | tf_op jit(solution)/shard_map/frcw,co->frow/dot_general | solution.py:30
  100.0 4.2 %fusion.36 = f32[2,36,128,160]{2,3,1,0:T(8,128)} fusion(bf16[2,38,320,128]{3,2,1,0:T(8,128)(2,1)S(1)} %copy-done, bf16[1,1,320,160]{2,3,1,0:T(8,128)(2,1)S(1)} %copy-done.3), kind=kOutput, calls=%fused_computation.50 | convolution fusion | flops 943718400 | bytes 11919360 | tf_op jit(solution)/shard_map/frcw,co->frow/dot_general | solution.py:30
  104.2 4.4 %fusion.38 = f32[2,36,128,160]{2,3,1,0:T(8,128)} fusion(bf16[2,38,320,128]{3,2,1,0:T(8,128)(2,1)S(1)} %copy-done, bf16[1,1,320,160]{2,3,1,0:T(8,128)(2,1)S(1)} %copy-done.4), kind=kOutput, calls=%fused_computation.52 | convolution fusion | flops 943718400 | bytes 11919360 | tf_op jit(solution)/shard_map/frcw,co->frow/dot_general | solution.py:30
  108.6 4.2 %fusion.40 = f32[2,36,128,160]{2,3,1,0:T(8,128)} fusion(bf16[2,38,320,128]{3,2,1,0:T(8,128)(2,1)S(1)} %copy-done, bf16[1,1,320,160]{2,3,1,0:T(8,128)(2,1)S(1)} %copy-done.5), kind=kOutput, calls=%fused_computation.54 | convolution fusion | flops 943718400 | bytes 11919360 | tf_op jit(solution)/shard_map/frcw,co->frow/dot_general | solution.py:30
  112.8 17.5 %convert_reduce_fusion = (f32[160]{0:T(256)S(1)}, bf16[2,36,160,128]{3,2,1,0:T(8,128)(2,1)}) fusion(f32[160]{0:T(256)S(1)} %copy-done.8, bf16[2,38,320,128]{3,2,1,0:T(8,128)(2,1)S(1)} %copy-done, bf16[1,1,320,160]{2,3,1,0:T(8,128)(2,1)S(1)} %copy.62, f32[2,36,128,160]{2,3,1,0:T(8,128)} %fusion.36, f32[2,36,128,160]{2,3,1,0:T(8,128)} %fusion.30, ...), kind=kOutput, calls=%fused_computation.8 | convolution fusion | flops 964362112 | bytes 59413760 | tf_op jit(solution)/shard_map/frcw,co->frow/dot_general | solution.py:30
  130.3 0.1 reduce_sum.59
  130.4 0.1 reduce_sum.72
  130.5 19.8 %psum.30 = f32[16]{0:T(128)S(1)} all-reduce(f32[16]{0:T(128)S(1)} %reduce_sum.72), channel_id=1, replica_groups=mesh['groups'=2,'tm'=4,'height'=2,'chan'=2] {'tm','height'}, use_global_device_ids=true, to_apply=%region_8.9 | all-reduce | flops 16 | bytes 128 | tf_op jit(solution)/shard_map/psum | solution.py:81
  150.3 0.1 sub.32
  150.4 0.1 sub.33
  150.5 2.8 fusion.4
  153.2 0.1 reduce_sum.74
  153.3 0.1 reduce_sum.75
  153.4 17.1 %psum.31 = f32[16]{0:T(128)S(1)} all-reduce(f32[16]{0:T(128)S(1)} %reduce_sum.75), channel_id=1, replica_groups=mesh['groups'=2,'tm'=4,'height'=2,'chan'=2] {'tm','height'}, use_global_device_ids=true, to_apply=%region_11.12 | all-reduce | flops 16 | bytes 128 | tf_op jit(solution)/shard_map/psum | solution.py:84
  170.6 0.1 mul.66
  170.7 0.1 mul.67
  170.8 5.1 %fusion.12 = bf16[2,36,160,128]{3,2,1,0:T(8,128)(2,1)} fusion(bf16[2,36,160,128]{3,2,1,0:T(8,128)(2,1)} %get-tuple-element.22, f32[160]{0:T(256)S(1)} %copy-done.12, f32[160]{0:T(256)S(1)} %copy-done.13, f32[160]{0:T(256)S(1)} %mul.67, f32[160]{0:T(256)S(1)} %sub.33), kind=kLoop, calls=%fused_computation.24 | loop fusion | flops 14745600 | bytes 5900800 | tf_op jit(solution)/shard_map/convert_element_type | solution.py:89
  175.9 15.1 %all-gather.5.cloned.1.call-done = bf16[2,36,320,128]{3,2,1,0:T(8,128)(2,1)} async-done(((bf16[2,36,160,128]{3,2,1,0:T(8,128)(2,1)}), bf16[2,36,320,128]{3,2,1,0:T(8,128)(2,1)}) %all-gather.5.cloned.1.call-update) | async-done | bytes 5898256 | tf_op jit(solution)/shard_map/all_gather | solution.py:92
  190.9 5.6 %fusion.65 = (bf16[1,36,320,128]{3,2,1,0:T(8,128)(2,1)}, bf16[1,36,320,128]{3,2,1,0:T(8,128)(2,1)}) fusion(bf16[2,36,320,128]{3,2,1,0:T(8,128)(2,1)} %all-gather.5.cloned.1.call-done), kind=kLoop, calls=%fused_computation.82 | loop fusion | bytes 11796480 | tf_op jit(solution)/shard_map/slice | solution.py:21
  196.5 5.3 %collective-permute-start.2 = (bf16[1,36,320,128]{3,2,1,0:T(8,128)(2,1)}, bf16[1,36,320,128]{3,2,1,0:T(8,128)(2,1)}, u32[]{:S(2)}, u32[]{:S(2)}) collective-permute-start(bf16[1,36,320,128]{3,2,1,0:T(8,128)(2,1)} %get-tuple-element.6), channel_id=1, source_target_pairs={{0,4},{4,8},{8,12},{1,5},{5,9},{9,13},{2,6},{6,10},{10,14},{3,7},{... | collective-permute-start | bytes 8847368 | tf_op jit(solution)/shard_map/ppermute | solution.py:18
  201.9 1.3 collective-permute-start.3
  203.2 0.1 copy.38
  203.2 79.8 %all_gather.15 = bf16[3,320,160]{2,0,1:T(4,128)(2,1)S(1)} all-gather(bf16[3,80,160]{2,0,1:T(4,128)(2,1)S(1)} %copy.38), channel_id=1, replica_groups=mesh['groups'=2,'tm'=4,'height'=2,'chan'=2] {'tm'}, dimensions={1}, use_global_device_ids=true | all-gather | bytes 384000 | tf_op jit(solution)/shard_map/all_gather | solution.py:94
  283.0 0.7 fusion.68
  283.7 0.2 copy.63
  283.9 0.2 copy.64
  284.1 0.2 copy.65
  284.3 4.5 %fusion.45 = f32[2,36,128,160]{2,3,1,0:T(8,128)S(1)} fusion(bf16[2,36,320,128]{3,2,1,0:T(8,128)(2,1)} %all-gather.5.cloned.1.call-done, bf16[1,320,160]{1,2,0:T(8,128)(2,1)S(1)} %copy.64), kind=kOutput, calls=%fused_computation.58 | convolution fusion | flops 943718400 | bytes 11898880 | tf_op jit(solution)/shard_map/frcw,co->frow/dot_general | solution.py:42
  288.9 6.2 %fusion.34 = f32[2,36,128,160]{2,3,1,0:T(8,128)} fusion(bf16[2,36,320,128]{3,2,1,0:T(8,128)(2,1)S(1)} %bitcast.94, bf16[1,36,320,128]{3,2,1,0:T(8,128)(2,1)} %collective-permute-done.2, bf16[1,320,160]{1,2,0:T(8,128)(2,1)S(1)} %copy.63), kind=kOutput, calls=%fused_computation.48 | convolution fusion | flops 955514880 | bytes 14848000 | tf_op jit(solution)/shard_map/frcw,co->frow/dot_general | solution.py:42
  295.1 7.7 %fusion.25 = bf16[2,36,160,128]{3,2,1,0:T(8,128)(2,1)} fusion(bf16[2,36,160,128]{3,2,1,0:T(8,128)(2,1)S(1)} %copy-done.1, f32[2,36,128,160]{2,3,1,0:T(8,128)} %fusion.34, f32[2,36,128,160]{2,3,1,0:T(8,128)S(1)} %fusion.45, f32[160]{0:T(256)S(1)} %copy-done.9, bf16[1,36,320,128]{3,2,1,0:T(8,128)(2,1)} %collective-permute-done.3, ...), kind=kOutput, calls=%fused_computation.37 | convolution fusion | flops 964362240 | bytes 26645120 | tf_op jit(solution)/shard_map/frcw,co->frow/dot_general | solution.py:42
  (45 shorter events, 0.2 us)
Async XLA Ops:
  6.5 16.7 %copy-start.2 = (bf16[2,36,160,128]{3,2,1,0:T(8,128)(2,1)S(1)}, bf16[2,36,160,128]{3,2,1,0:T(8,128)(2,1)}, u32[]{:S(2)}) copy-start(bf16[2,36,160,128]{3,2,1,0:T(8,128)(2,1)} %param.9) | copy-start | bytes 8847364
  6.5 16.7 %copy-start.11 = (f32[160]{0:T(256)S(1)}, f32[160]{0:T(256)}, u32[]{:S(2)}) copy-start(f32[160]{0:T(256)} %param.10) | copy-start | bytes 1924
  6.5 16.7 %copy-start.10 = (f32[160]{0:T(256)S(1)}, f32[160]{0:T(256)}, u32[]{:S(2)}) copy-start(f32[160]{0:T(256)} %param.11) | copy-start | bytes 1924
  6.5 71.3 %all-gather.3.cloned.1.call-start = ((), (), s32[]{:S(2)}) async-start(), calls=%async_computation | async-start | bytes 9338880 | tf_op jit(solution)/shard_map/all_gather | solution.py:73
  25.6 12.6 %copy-start.6 = (bf16[3,3,80,160]{3,2,1,0:T(8,128)(2,1)S(1)}, bf16[3,3,80,160]{3,2,1,0:T(8,128)(2,1)}, u32[]{:S(2)}) copy-start(bf16[3,3,80,160]{3,2,1,0:T(8,128)(2,1)} %param.12) | copy-start | bytes 691204
  25.6 6.1 %collective-permute-start = (bf16[2,1,160,128]{3,2,1,0:T(8,128)(2,1)S(1)}, bf16[2,1,160,128]{3,2,1,0:T(8,128)(2,1)S(1)}, u32[]{:S(2)}, u32[]{:S(2)}) collective-permute-start(bf16[2,1,160,128]{3,2,1,0:T(8,128)(2,1)S(1)} %get-tuple-element.7), channel_id=1, source_target_pairs={{0,2},{1,3},{4,6},{5,7},{8,10},{9,11},{12,14},{13,15},{16,18},{17,... | collective-permute-start | bytes 245768 | tf_op jit(solution)/shard_map/ppermute | solution.py:18
  29.7 6.3 %collective-permute-start.1 = (bf16[2,1,160,128]{3,2,1,0:T(8,128)(2,1)S(1)}, bf16[2,1,160,128]{3,2,1,0:T(8,128)(2,1)S(1)}, u32[]{:S(2)}, u32[]{:S(2)}) collective-permute-start(bf16[2,1,160,128]{3,2,1,0:T(8,128)(2,1)S(1)} %get-tuple-element.8), channel_id=1, source_target_pairs={{2,0},{3,1},{6,4},{7,5},{10,8},{11,9},{14,12},{15,13},{18,16},{19,... | collective-permute-start | bytes 245768 | tf_op jit(solution)/shard_map/ppermute | solution.py:21
  38.1 152.8 %all-gather.5.cloned.1.call-start = ((), (), s32[]{:S(2)}) async-start(), calls=%async_computation.1 | async-start | bytes 8847360 | tf_op jit(solution)/shard_map/all_gather | solution.py:92
  77.8 4.7 %copy-start = (bf16[2,38,320,128]{3,2,1,0:T(8,128)(2,1)S(1)}, bf16[2,38,320,128]{3,2,1,0:T(8,128)(2,1)}, u32[]{:S(2)}) copy-start(bf16[2,38,320,128]{3,2,1,0:T(8,128)(2,1)} %all-gather.3.cloned.1.call-done) | copy-start | bytes 18677764
  95.5 4.4 %copy-start.3 = (bf16[1,1,320,160]{2,3,1,0:T(8,128)(2,1)S(1)}, bf16[1,1,320,160]{2,3,1,0:T(8,128)(2,1)}, u32[]{:S(2)}) copy-start(bf16[1,1,320,160]{2,3,1,0:T(8,128)(2,1)} %copy.61) | copy-start | bytes 307204
  100.0 4.2 %copy-start.4 = (bf16[1,1,320,160]{2,3,1,0:T(8,128)(2,1)S(1)}, bf16[1,1,320,160]{2,3,1,0:T(8,128)(2,1)}, u32[]{:S(2)}) copy-start(bf16[1,1,320,160]{2,3,1,0:T(8,128)(2,1)} %copy.58) | copy-start | bytes 307204
  104.2 4.4 %copy-start.5 = (bf16[1,1,320,160]{2,3,1,0:T(8,128)(2,1)S(1)}, bf16[1,1,320,160]{2,3,1,0:T(8,128)(2,1)}, u32[]{:S(2)}) copy-start(bf16[1,1,320,160]{2,3,1,0:T(8,128)(2,1)} %copy.55) | copy-start | bytes 307204
  108.6 4.2 %copy-start.8 = (f32[160]{0:T(256)S(1)}, f32[160]{0:T(256)}, u32[]{:S(2)}) copy-start(f32[160]{0:T(256)} %param.13) | copy-start | bytes 1924
  112.8 57.9 %copy-start.12 = (f32[160]{0:T(256)S(1)}, f32[160]{0:T(256)}, u32[]{:S(2)}) copy-start(f32[160]{0:T(256)} %param.15) | copy-start | bytes 1924
  112.8 58.0 %copy-start.13 = (f32[160]{0:T(256)S(1)}, f32[160]{0:T(256)}, u32[]{:S(2)}) copy-start(f32[160]{0:T(256)} %param.14) | copy-start | bytes 1924
  175.9 27.3 %copy-start.7 = (bf16[3,80,160]{2,1,0:T(8,128)(2,1)S(1)}, bf16[3,80,160]{2,1,0:T(8,128)(2,1)}, u32[]{:S(2)}) copy-start(bf16[3,80,160]{2,1,0:T(8,128)(2,1)} %param.16) | copy-start | bytes 230404
  196.5 92.3 %collective-permute-start.2 = (bf16[1,36,320,128]{3,2,1,0:T(8,128)(2,1)}, bf16[1,36,320,128]{3,2,1,0:T(8,128)(2,1)}, u32[]{:S(2)}, u32[]{:S(2)}) collective-permute-start(bf16[1,36,320,128]{3,2,1,0:T(8,128)(2,1)} %get-tuple-element.6), channel_id=1, source_target_pairs={{0,4},{4,8},{8,12},{1,5},{5,9},{9,13},{2,6},{6,10},{10,14},{3,7},{... | collective-permute-start | bytes 8847368 | tf_op jit(solution)/shard_map/ppermute | solution.py:18
  201.9 93.3 %collective-permute-start.3 = (bf16[1,36,320,128]{3,2,1,0:T(8,128)(2,1)}, bf16[1,36,320,128]{3,2,1,0:T(8,128)(2,1)}, u32[]{:S(2)}, u32[]{:S(2)}) collective-permute-start(bf16[1,36,320,128]{3,2,1,0:T(8,128)(2,1)} %get-tuple-element.5), channel_id=1, source_target_pairs={{4,0},{8,4},{12,8},{5,1},{9,5},{13,9},{6,2},{10,6},{14,10},{7,3},{... | collective-permute-start | bytes 8847368 | tf_op jit(solution)/shard_map/ppermute | solution.py:21
  284.1 4.8 %slice-start = ((s8[5898240]{0:T(1024)(128)(4,1)}), s8[1703936]{0:T(1024)(128)(4,1)S(1)}, s32[]{:S(2)}) async-start(s8[5898240]{0:T(1024)(128)(4,1)} %bitcast.93), calls=%async_computation.2 | async-start | bytes 3407872
  284.3 4.6 %slice-start.1 = ((s8[5898240]{0:T(1024)(128)(4,1)}), s8[4194304]{0:T(1024)(128)(4,1)S(1)}, s32[]{:S(2)}) async-start(s8[5898240]{0:T(1024)(128)(4,1)} %bitcast.93), calls=%async_computation.3 | async-start | bytes 8388608
  288.8 6.3 %copy-start.1 = (bf16[2,36,160,128]{3,2,1,0:T(8,128)(2,1)S(1)}, bf16[2,36,160,128]{3,2,1,0:T(8,128)(2,1)}, u32[]{:S(2)}) copy-start(bf16[2,36,160,128]{3,2,1,0:T(8,128)(2,1)} %get-tuple-element.22) | copy-start | bytes 8847364
  288.9 6.3 %copy-start.9 = (f32[160]{0:T(256)S(1)}, f32[160]{0:T(256)}, u32[]{:S(2)}) copy-start(f32[160]{0:T(256)} %param.17) | copy-start | bytes 1924
Sparse Core Ops, SparseCore 0:
  38.3 16.9 all-gather.2
  176.0 14.9 all-gather.4
where the time goes:
time: 310 us
  blocking collectives  161 us (52%)
  matrix products  70.9 us (23%)
  waiting for transfers between devices  20.2 us (7%)
  other arithmetic  17.9 us (6%)
  local copies, waits for them, and re-layouts  14.5 us (5%)
  between operations  13.7 us (4%)
  starting transfers between devices  12 us (4%)
    all_gather x1, blocking collectives, body(): full_temporal = lax.all_gather(temporal_weight, 'tm', axis=1, tiled=True)  79.8 us
    dot_general x9, matrix products, spatial_taps(): jnp.einsum('frcw,co->frow', window, weight_piece[row_tap, col_tap], prefe...  52.5 us
    all_gather x1, blocking collectives, body(): full_spatial = lax.all_gather(spatial_weight, 'tm', axis=2, tiled=True)  33.1 us
    psum x1, blocking collectives, body(): lax.psum(jnp.sum(grouped_two, axis=(0, 1, 3, 4)), ('tm', 'height'))  19.8 us
    dot_general x3, matrix products, temporal_taps(): jnp.einsum('frcw,co->frow', window, weight_piece[frame_tap], preferred_el...  18.4 us
    psum x1, blocking collectives, body(): lax.psum(jnp.sum(centred_two * centred_two, axis=(0, 1, 3, 4)), ('tm', 'h...  17.1 us
    all_gather x1, waiting for transfers between devices, body(): wide_two = lax.all_gather(act_two, 'chan', axis=2, tiled=True)  15.1 us
    ppermute x2, starting transfers between devices, with_halo(): lax.ppermute(lax.slice_in_dim(block, block.shape[dim] - width, None, axis...  9.4 us
  transfers between devices with their start and end apart: 6, of which 3 were waited for; matrix products, arithmetic and copies ran while one was open for 6% of the time, Pallas kernels for 0%

commit v1 on v0

v1 whole, which is shorter than its diff:
```python
import jax
import jax.numpy as jnp
from jax import lax
from jax.sharding import PartitionSpec as P

C = 320
GROUPS = 32


EPSILON = 1e-06


def swap_chan(block):
    return lax.ppermute(block, "chan", [(0, 1), (1, 0)])


def row_halo(block):
    count = lax.axis_size("height")
    forward = [(i, i + 1) for i in range(count - 1)]
    backward = [(target, source) for source, target in forward]
    low = lax.ppermute(block[:, -1:], "height", forward)
    high = lax.ppermute(block[:, :1], "height", backward)
    return jnp.concatenate([low, block, high], axis=1)


def spatial_conv(inputs, weight):
    return lax.conv_general_dilated(
        inputs,
        weight,
        window_strides=(1, 1),
        padding=((0, 0), (1, 1)),
        dimension_numbers=("NHCW", "HWIO", "NHCW"),
        preferred_element_type=jnp.float32,
    )


def temporal_conv(inputs, weight):
    return lax.conv_general_dilated(
        inputs,
        weight[:, None],
        window_strides=(1, 1),
        padding=((0, 0), (0, 0)),
        dimension_numbers=("HNCW", "HWIO", "HNCW"),
        preferred_element_type=jnp.float32,
    )


def group_act(values, average, variance, gain, bias):
    frames, rows, local_chan, width = values.shape
    local_groups = average.shape[-1]
    grouped = values.reshape(frames, rows, local_groups, local_chan // local_groups, width)
    centred = grouped - average.reshape(-1, 1, local_groups, 1, 1)
    scaled = (centred * lax.rsqrt(variance.reshape(-1, 1, local_groups, 1, 1) + EPSILON)).reshape(
        frames, rows, local_chan, width
    )
    return jax.nn.silu(scaled * gain[:, None] + bias[:, None]).astype(jnp.bfloat16)


def body(
    video,
    norm1_gain,
    norm1_bias,
    spatial_weight,
    spatial_bias,
    norm2_gain,
    norm2_bias,
    temporal_weight,
    temporal_bias,
):
    frames, rows, local_chan, width = video.shape
    group_size = C // GROUPS
    local_groups = local_chan // group_size
    chan_index = lax.axis_index("chan")
    tm_index = lax.axis_index("tm")
    tm_count = lax.axis_size("tm")

    piece = spatial_weight.shape[2]
    merged = jnp.concatenate(
        [spatial_weight.reshape(9, piece, local_chan), temporal_weight], axis=0
    )
    full_weight = lax.all_gather(merged, "tm", axis=1, tiled=True)
    own_start = chan_index * local_chan
    other_start = (1 - chan_index) * local_chan
    own_weight = lax.dynamic_slice_in_dim(full_weight, own_start, local_chan, axis=1)
    other_weight = lax.dynamic_slice_in_dim(full_weight, other_start, local_chan, axis=1)
    spatial_own = own_weight[:9].reshape(3, 3, local_chan, local_chan)
    spatial_other = other_weight[:9].reshape(3, 3, local_chan, local_chan)
    temporal_own = own_weight[9:]
    temporal_other = other_weight[9:]

    values = video.astype(jnp.float32)
    grouped = values.reshape(frames, rows, local_groups, group_size, width)
    entries = rows * lax.axis_size("height") * width * group_size
    totals = lax.psum(jnp.sum(grouped, axis=(1, 3, 4)), "height")
    average = totals / entries
    centred = grouped - average.reshape(frames, 1, local_groups, 1, 1)
    squares = lax.psum(jnp.sum(centred * centred, axis=(1, 3, 4)), "height")
    variance = squares / entries
    act_one = group_act(values, average, variance, norm1_gain, norm1_bias)

    with_rows = row_halo(act_one)
    other_rows = swap_chan(with_rows)
    spatial_sum = spatial_conv(with_rows, spatial_own) + spatial_conv(other_rows, spatial_other)
    hidden = (values + spatial_sum + spatial_bias[:, None]).astype(jnp.bfloat16)

    forward = [(i, i + 1) for i in range(tm_count - 1)]
    backward = [(target, source) for source, target in forward]
    before = lax.ppermute(hidden[-1:], "tm", forward)
    after = lax.ppermute(hidden[:1], "tm", backward)

    hidden_values = hidden.astype(jnp.float32)
    grouped_two = hidden_values.reshape(frames, rows, local_groups, group_size, width)
    entries_two = frames * tm_count * entries
    totals_two = lax.psum(lax.psum(jnp.sum(grouped_two, axis=(0, 1, 3, 4)), "height"), "tm")
    average_two = totals_two / entries_two
    centred_two = grouped_two - average_two.reshape(1, 1, local_groups, 1, 1)
    squares_two = lax.psum(
        lax.psum(jnp.sum(centred_two * centred_two, axis=(0, 1, 3, 4)), "height"), "tm"
    )
    variance_two = squares_two / entries_two

    extended = jnp.concatenate([before, hidden, after], axis=0).astype(jnp.float32)
    act_two = group_act(extended, average_two, variance_two, norm2_gain, norm2_bias)
    frame_ids = jnp.arange(frames + 2)
    inside = (frame_ids > 0) | (tm_index > 0)
    inside = inside & ((frame_ids < frames + 1) | (tm_index < tm_count - 1))
    act_two = jnp.where(inside[:, None, None, None], act_two, jnp.zeros_like(act_two))

    other_two = swap_chan(act_two)
    temporal_sum = temporal_conv(act_two, temporal_own) + temporal_conv(other_two, temporal_other)
    return (hidden_values + temporal_sum + temporal_bias[:, None]).astype(jnp.bfloat16)


def solution(mesh):
    return jax.shard_map(
        body,
        mesh=mesh,
        in_specs=(
            P(("groups", "tm"), "height", "chan", None),
            P("chan"),
            P("chan"),
            P(None, None, "tm", "chan"),
            P("chan"),
            P("chan"),
            P("chan"),
            P(None, "tm", "chan"),
            P("chan"),
        ),
        out_specs=P(("groups", "tm"), "height", "chan", None),
        check_vma=False,
    )
```

time: 310 us -> 360 us (1.16); the launches traced: 310 us -> 353 us
  blocking collectives: 161 us -> 60.5 us
  local copies, waits for them, and re-layouts: 14.5 us -> 107 us
  other arithmetic: 17.9 us -> 55.5 us
  waiting for transfers between devices: 20.2 us -> 50.1 us
  matrix products: 70.9 us -> 53.9 us
    all_gather x2 -> x0, blocking collectives: 113 us -> none  [the longest x1 79.8 us: body(): full_temporal = lax.all_gather(temporal_weight, 'tm', axis=1, tiled=True)]
    dot_general x12 -> x0, matrix products: 70.9 us -> none  [the longest x9 52.5 us: spatial_taps(): jnp.einsum('frcw,co->frow', window, weight_piece[row_tap, col_tap], prefe...]
    conv_general_dilated x0 -> x4, matrix products: none -> 53.9 us  [the longest x2 29.3 us: spatial_conv(): lax.conv_general_dilated(inputs, weight, window_strides=(1, 1), padding=(...]
    ppermute x0 -> x4, local copies, waits for them, and re-layouts: none -> 26.4 us  [the longest x2 18.3 us: swap_chan(): return lax.ppermute(block, 'chan', [(0, 1), (1, 0)])]
    all_gather x2 -> x1, waiting for transfers between devices: 15.1 us -> 33.4 us  [body(): full_weight = lax.all_gather(merged, 'tm', axis=1, tiled=True)]
    select_n x0 -> x1, local copies, waits for them, and re-layouts: none -> 15.3 us  [body(): jnp.where(inside[:, None, None, None], act_two, jnp.zeros_like(act_two))]
    unnamed x46 -> x34, local copies, waits for them, and re-layouts: 4.6 us -> 19 us
    psum x2 -> x4, blocking collectives: 36.9 us -> 49.7 us  [the longest x1 31.3 us: body(): lax.psum(lax.psum(jnp.sum(grouped_two, axis=(0, 1, 3, 4)), 'height'), 'tm')]
  transfers between devices with their start and end apart: 6 -> 7, of which waited for: 3 -> 4; matrix products, arithmetic and copies ran while one was open for 6% -> 7% of each run, Pallas kernels for 0% -> 0%
where the time goes in v1:
time: 360 us; the launch traced here: 353 us
  local copies, waits for them, and re-layouts  107 us (30%)
  blocking collectives  60.5 us (17%)
  other arithmetic  55.5 us (15%)
  matrix products  53.9 us (15%)
  waiting for transfers between devices  50.1 us (14%)
  between operations  13.9 us (4%)
  starting transfers between devices  12.5 us (3%)
    all_gather x1, waiting for transfers between devices, body(): full_weight = lax.all_gather(merged, 'tm', axis=1, tiled=True)  33.4 us
    psum x1, blocking collectives, body(): lax.psum(lax.psum(jnp.sum(grouped_two, axis=(0, 1, 3, 4)), 'height'), 'tm')  31.3 us
    conv_general_dilated x2, matrix products, spatial_conv(): lax.conv_general_dilated(inputs, weight, window_strides=(1, 1), padding=(...  29.3 us
    conv_general_dilated x2, matrix products, temporal_conv(): lax.conv_general_dilated(inputs, weight[:, None], window_strides=(1, 1),...  24.6 us
    unnamed x34, local copies, waits for them, and re-layouts  19 us
    ppermute x2, local copies, waits for them, and re-layouts, swap_chan(): return lax.ppermute(block, 'chan', [(0, 1), (1, 0)])  18.3 us
    select_n x1, local copies, waits for them, and re-layouts, body(): jnp.where(inside[:, None, None, None], act_two, jnp.zeros_like(act_two))  15.3 us
    select_n x1, other arithmetic, body(): jnp.where(inside[:, None, None, None], act_two, jnp.zeros_like(act_two))  12.4 us
  transfers between devices with their start and end apart: 7, of which 4 were waited for; matrix products, arithmetic and copies ran while one was open for 7% of the time, Pallas kernels for 0%

profile of v1, /device:TPU:0, one launch (start us, length us, event | category | flops | bytes accessed | tf_op | source)
XLA Modules:
  0.0 353.1 jit_solution(10455121120181476812)
XLA Ops:
  6.5 8.0 %copy.55 = bf16[2,36,160,128]{2,1,3,0:T(8,128)(2,1)} copy(bf16[2,36,160,128]{3,2,1,0:T(8,128)(2,1)} %param.9) | data formatting | bytes 5898240 | tf_op args[0]
  14.5 3.4 convert_reduce_fusion.1
  17.9 0.1 reduce_sum.47
  18.0 0.1 reduce_sum.51
  18.1 5.8 %psum.42 = f32[2,16]{1,0:T(2,128)S(1)} all-reduce(f32[2,16]{1,0:T(2,128)S(1)} %reduce_sum.51), channel_id=1, replica_groups=mesh['groups'=2,'tm'=4,'height'=2,'chan'=2] {'height'}, use_global_device_ids=true, to_apply=%region_2.0 | all-reduce | flops 32 | bytes 256 | tf_op jit(solution)/shard_map/psum | solution.py:94
  24.0 0.1 sub.43
  24.0 0.1 sub.44
  24.1 4.1 %fusion.4 = f32[2,160]{1,0:T(2,128)S(1)} fusion(bf16[2,36,160,128]{2,1,3,0:T(8,128)(2,1)} %copy.55, f32[2,160]{1,0:T(2,128)S(1)} %sub.44), kind=kLoop, calls=%fused_computation.13 | loop fusion | flops 5897920 | bytes 2951680 | tf_op jit(solution)/shard_map/reduce_sum | solution.py:97
  28.2 0.1 reduce_sum.53
  28.3 0.1 reduce_sum.54
  28.4 4.9 %psum.43 = f32[2,16]{1,0:T(2,128)S(1)} all-reduce(f32[2,16]{1,0:T(2,128)S(1)} %reduce_sum.54), channel_id=1, replica_groups=mesh['groups'=2,'tm'=4,'height'=2,'chan'=2] {'height'}, use_global_device_ids=true, to_apply=%region_5.6 | all-reduce | flops 32 | bytes 256 | tf_op jit(solution)/shard_map/psum | solution.py:97
  33.3 0.1 mul.65
  33.4 0.1 mul.66
  33.5 5.4 %fusion.12 = bf16[2,36,160,128]{2,1,3,0:T(8,128)(2,1)S(1)} fusion(bf16[2,36,160,128]{2,1,3,0:T(8,128)(2,1)} %copy.55, f32[160]{0:T(256)S(1)} %copy-done.10, f32[160]{0:T(256)S(1)} %copy-done.11, f32[2,160]{1,0:T(2,128)S(1)} %mul.66, f32[2,160]{1,0:T(2,128)S(1)} %sub.44), kind=kLoop, calls=%fused_computation.21 | loop fusion | flops 14745600 | bytes 5902080 | tf_op jit(solution)/shard_map/convert_element_type | solution.py:56
  39.0 0.4 fusion.43
  39.4 4.0 %collective-permute-start = (bf16[2,1,160,128]{2,1,3,0:T(2,128)(2,1)S(1)}, bf16[2,1,160,128]{2,1,3,0:T(2,128)(2,1)S(1)}, u32[]{:S(2)}, u32[]{:S(2)}) collective-permute-start(bf16[2,1,160,128]{2,1,3,0:T(2,128)(2,1)S(1)} %get-tuple-element.9), channel_id=1, source_target_pairs={{0,2},{1,3},{4,6},{5,7},{8,10},{9,11},{12,14},{13,15},{16,18},{17,... | collective-permute-start | bytes 245768 | tf_op jit(solution)/shard_map/ppermute | solution.py:21
  43.3 1.5 collective-permute-start.1
  44.9 2.3 collective-permute-done
  47.2 4.4 %collective-permute-done.1 = bf16[2,1,160,128]{2,1,3,0:T(2,128)(2,1)S(1)} collective-permute-done((bf16[2,1,160,128]{2,1,3,0:T(2,128)(2,1)S(1)}, bf16[2,1,160,128]{2,1,3,0:T(2,128)(2,1)S(1)}, u32[]{:S(2)}, u32[]{:S(2)}) %collective-permute-start.1) | collective-permute-done | bytes 81952 | tf_op jit(solution)/shard_map/ppermute | solution.py:22
  51.6 0.7 copy-done.2
  52.3 4.8 %pad_maximum_fusion = bf16[2,38,160,128]{2,1,3,0:T(8,128)(2,1)} fusion(bf16[2,1,160,128]{2,1,3,0:T(2,128)(2,1)S(1)} %collective-permute-done.1, bf16[2,36,160,128]{2,1,3,0:T(8,128)(2,1)S(1)} %fusion.12, bf16[2,1,160,128]{2,1,3,0:T(2,128)(2,1)S(1)} %collective-permute-done), kind=kLoop, calls=%fused_computation.41 | loop fusion | flops 9338880 | bytes 6225920 | tf_op jit(solution)/shard_map/concatenate | solution.py:23
  57.1 8.6 %copy.58 = bf16[2,38,160,128]{3,2,1,0:T(8,128)(2,1)S(1)} copy(bf16[2,38,160,128]{2,1,3,0:T(8,128)(2,1)} %pad_maximum_fusion) | data formatting | bytes 6225920 | tf_op jit(solution)/shard_map/concatenate | solution.py:23
  65.8 1.9 pad_maximum_fusion.1
  67.7 5.4 %fusion.48 = bf16[38,160,2,128]{1,0,3,2:T(8,128)(2,1)S(1)} fusion(bf16[2,1,160,128]{2,1,3,0:T(2,128)(2,1)} %copy-done.2, bf16[2,36,160,128]{2,1,3,0:T(8,128)(2,1)} %copy-done, bf16[2,1,160,128]{2,1,3,0:T(2,128)(2,1)S(1)} %collective-permute-done), kind=kLoop, calls=%fused_computation.62 | loop fusion | flops 9338880 | bytes 6225920 | tf_op jit(solution)/shard_map/concatenate | solution.py:23
  73.1 1.0 pad
  74.1 1.1 copy.57
  75.2 2.3 copy-done.1
  77.4 1.0 slice.37
  78.5 33.4 %all-gather.2.cloned.1.call-done = bf16[12,320,160]{2,1,0:T(8,128)(2,1)} async-done(((bf16[12,80,160]{2,1,0:T(8,128)(2,1)}), bf16[12,320,160]{2,1,0:T(8,128)(2,1)}) %all-gather.2.cloned.1.call-update) | async-done | bytes 1228816 | tf_op jit(solution)/shard_map/all_gather | solution.py:81
  111.9 2.6 constant_dynamic-slice_fusion.1
  114.5 8.0 %copy.70 = bf16[38,160,2,128]{1,0,3,2:T(8,128)(2,1)} copy(bf16[38,160,2,128]{3,1,0,2:T(8,128)(2,1)} %bitcast.5) | data formatting | bytes 6225920
  122.5 3.5 pad.2.clone
  126.0 3.7 %fusion.20 = bf16[38,160,2,8,19]{1,0,4,3,2:T(8,128)(2,1)} fusion(bf16[38,160,2,7,2]{1,0,4,3,2:T(8,128)(2,1)S(1)} %slice.38, bf16[38,160,2,8,17]{1,0,4,3,2:T(8,128)(2,1)S(1)} %bitcast.40), kind=kLoop, calls=%fused_computation.31 | loop fusion | flops 11089920 | bytes 7344640 | tf_op jit(solution)/shard_map/conv_general_dilated | solution.py:27
  129.8 14.9 %fusion.28 = f32[36,16,17,160]{3,1,2,0:T(8,128)} fusion(bf16[3,3,160,160]{3,2,1,0:T(8,128)(2,1)S(1)} %bitcast.43, bf16[38,160,2,8,19]{1,0,4,3,2:T(8,128)(2,1)} %fusion.20), kind=kOutput, calls=%fused_computation.38 | convolution fusion | flops 4512153600 | bytes 10424320 | tf_op jit(solution)/shard_map/conv_general_dilated | solution.py:27
  144.7 14.4 %select_add_fusion = f32[36,16,17,160]{3,1,2,0:T(8,128)S(1)} fusion(f32[36,16,17,160]{3,1,2,0:T(8,128)} %fusion.28, pred[16,17]{0,1:T(8,128)(4,1)S(1)} %copy-done.13, bf16[3,3,160,160]{3,2,1,0:T(8,128)(2,1)S(1)} %bitcast.42, bf16[38,160,2,7,2]{1,3,2,4,0:T(8,128)(2,1)S(1)} %copy-done.5, bf16[38,160,2,8,17]{1,3,2,4,0:T(8,128)(2,1)} %copy-done.1), kind=kOutput, calls=%fused_computation.30 | convolution fusion | flops 4527943680 | bytes 16642832 | tf_op jit(solution)/shard_map/conv_general_dilated | solution.py:27
  159.1 10.1 %copy.61 = f32[36,16,17,160]{3,0,2,1:T(8,128)} copy(f32[36,16,17,160]{3,1,2,0:T(8,128)S(1)} %select_add_fusion) | data formatting | bytes 12533760 | tf_op jit(solution)/shard_map/add | solution.py:103
  169.2 9.8 %convert_reduce_fusion = (f32[160]{0:T(256)S(1)}, bf16[2,36,160,128]{2,1,3,0:T(8,128)(2,1)}) fusion(f32[160]{0:T(256)S(1)} %copy-done.7, f32[36,2,136,160]{3,0,2,1:T(8,128)} %bitcast.38, bf16[2,36,160,128]{2,1,3,0:T(8,128)(2,1)} %copy.55), kind=kLoop, calls=%fused_computation.3 | loop fusion | flops 8847200 | bytes 11797760 | tf_op jit(solution)/shard_map/reduce_sum | solution.py:114
  179.0 4.4 %fusion.42 = (bf16[1,36,160,128]{2,1,3,0:T(8,128)(2,1)S(1)}, bf16[1,36,160,128]{2,1,3,0:T(8,128)(2,1)}) fusion(bf16[2,36,160,128]{2,1,3,0:T(8,128)(2,1)} %get-tuple-element.6), kind=kLoop, calls=%fused_computation.60 | loop fusion | bytes 5898240 | tf_op jit(solution)/shard_map/slice | solution.py:108
  183.4 4.6 %copy.63 = bf16[1,36,160,128]{3,2,1,0:T(8,128)(2,1)} copy(bf16[1,36,160,128]{2,1,3,0:T(8,128)(2,1)} %get-tuple-element.8) | data formatting | bytes 2949120 | tf_op jit(solution)/shard_map/slice | solution.py:109
  188.0 1.3 collective-permute-start.4
  189.3 3.2 copy.62
  192.5 5.7 %collective-permute-start.3 = (bf16[1,36,160,128]{3,2,1,0:T(8,128)(2,1)}, bf16[1,36,160,128]{3,2,1,0:T(8,128)(2,1)}, u32[]{:S(2)}, u32[]{:S(2)}) collective-permute-start(bf16[1,36,160,128]{3,2,1,0:T(8,128)(2,1)} %copy.62), channel_id=1, source_target_pairs={{0,4},{4,8},{8,12},{1,5},{5,9},{9,13},{2,6},{6,10},{10,14},{3,7},{... | collective-permute-start | bytes 4423688 | tf_op jit(solution)/shard_map/ppermute | solution.py:108
  198.2 0.1 reduce_sum.59
  198.2 0.1 reduce_sum.72
  198.4 4.9 %psum.44 = f32[16]{0:T(128)S(1)} all-reduce(f32[16]{0:T(128)S(1)} %reduce_sum.72), channel_id=1, replica_groups=mesh['groups'=2,'tm'=4,'height'=2,'chan'=2] {'height'}, use_global_device_ids=true, to_apply=%region_8.9 | all-reduce | flops 16 | bytes 128 | tf_op jit(solution)/shard_map/psum | solution.py:114
  203.3 31.3 %psum.45 = f32[16]{0:T(128)S(1)} all-reduce(f32[16]{0:T(128)S(1)} %psum.44), channel_id=1, replica_groups=mesh['groups'=2,'tm'=4,'height'=2,'chan'=2] {'tm'}, use_global_device_ids=true, to_apply=%region_9.10 | all-reduce | flops 16 | bytes 128 | tf_op jit(solution)/shard_map/psum | solution.py:114
  234.6 0.1 sub.48
  234.7 0.1 sub.49
  234.8 4.1 %fusion.16 = f32[160]{0:T(256)S(1)} fusion(bf16[2,36,160,128]{2,1,3,0:T(8,128)(2,1)} %get-tuple-element.6, f32[160]{0:T(256)S(1)} %sub.49), kind=kLoop, calls=%fused_computation.25 | loop fusion | flops 5898080 | bytes 2950400 | tf_op jit(solution)/shard_map/reduce_sum | solution.py:118
  238.9 0.1 reduce_sum.74
  239.0 0.1 reduce_sum.75
  239.1 5.2 %psum.46 = f32[16]{0:T(128)S(1)} all-reduce(f32[16]{0:T(128)S(1)} %reduce_sum.75), channel_id=1, replica_groups=mesh['groups'=2,'tm'=4,'height'=2,'chan'=2] {'height'}, use_global_device_ids=true, to_apply=%region_12.13 | all-reduce | flops 16 | bytes 128 | tf_op jit(solution)/shard_map/psum | solution.py:118
  244.3 8.3 %psum.47 = f32[16]{0:T(128)S(1)} all-reduce(f32[16]{0:T(128)S(1)} %psum.46), channel_id=1, replica_groups=mesh['groups'=2,'tm'=4,'height'=2,'chan'=2] {'tm'}, use_global_device_ids=true, to_apply=%region_13.14 | all-reduce | flops 16 | bytes 128 | tf_op jit(solution)/shard_map/psum | solution.py:117
  252.6 0.1 mul.75
  252.7 0.1 mul.76
  252.8 3.6 %copy.65 = bf16[1,36,160,128]{2,1,3,0:T(8,128)(2,1)S(1)} copy(bf16[1,36,160,128]{3,2,1,0:T(8,128)(2,1)} %collective-permute-done.4) | data formatting | bytes 2949120 | tf_op jit(solution)/shard_map/ppermute | solution.py:109
  256.4 4.5 %copy.64 = bf16[1,36,160,128]{2,1,3,0:T(8,128)(2,1)} copy(bf16[1,36,160,128]{3,2,1,0:T(8,128)(2,1)} %collective-permute-done.3) | data formatting | bytes 2949120 | tf_op jit(solution)/shard_map/ppermute | solution.py:108
  260.9 12.4 %fusion.19 = bf16[4,36,160,128]{2,1,3,0:T(8,128)(2,1)} fusion(bf16[1,36,160,128]{2,1,3,0:T(8,128)(2,1)S(1)} %copy.65, bf16[2,36,160,128]{2,1,3,0:T(8,128)(2,1)} %get-tuple-element.6, bf16[1,36,160,128]{2,1,3,0:T(8,128)(2,1)} %copy.64, f32[160]{0:T(256)S(1)} %copy-done.8, f32[160]{0:T(256)S(1)} %copy-done.9, f32[160]{0:T(256)S(1)} %mul.76, f32[160]{0:T(256)S(1)} %sub.49, ...), kind=kLoop, calls=%fused_computation.28 | loop fusion | flops 38338560 | bytes 11799044 | tf_op jit(solution)/shard_map/jit(_where)/select_n | solution.py:127
  273.3 15.3 %copy.66 = bf16[4,36,160,128]{3,2,1,0:T(8,128)(2,1)} copy(bf16[4,36,160,128]{2,1,3,0:T(8,128)(2,1)} %fusion.19) | data formatting | bytes 11796480 | tf_op jit(solution)/shard_map/jit(_where)/select_n | solution.py:127
  288.6 9.9 %collective-permute-done.5 = bf16[4,36,160,128]{3,2,1,0:T(8,128)(2,1)} collective-permute-done((bf16[4,36,160,128]{3,2,1,0:T(8,128)(2,1)}, bf16[4,36,160,128]{3,2,1,0:T(8,128)(2,1)}, u32[]{:S(2)}, u32[]{:S(2)}) %collective-permute-start.5) | collective-permute-done | bytes 5898272 | tf_op jit(solution)/shard_map/ppermute | solution.py:14
  298.5 14.8 %copy.67 = bf16[4,36,160,128]{2,1,3,0:T(8,128)(2,1)} copy(bf16[4,36,160,128]{3,2,1,0:T(8,128)(2,1)} %collective-permute-done.5) | data formatting | bytes 11796480 | tf_op jit(solution)/shard_map/ppermute | solution.py:14
  313.3 11.0 %fusion.34 = f32[2,36,160,128]{2,1,3,0:T(8,128)} fusion(bf16[4,36,160,128]{2,1,3,0:T(8,128)(2,1)} %copy.67, bf16[12,320,160]{2,1,0:T(8,128)(2,1)} %all-gather.2.cloned.1.call-done, s32[]{:T(128)S(6)} %add.100, s32[]{:T(128)S(6)} %select_n.11), kind=kOutput, calls=%fused_computation.45 | convolution fusion | flops 1415577600 | bytes 16629768 | tf_op jit(solution)/shard_map/conv_general_dilated | solution.py:38
  324.4 13.6 %fusion.18 = bf16[2,36,160,128]{2,1,3,0:T(8,128)(2,1)} fusion(bf16[2,36,160,128]{2,1,3,0:T(8,128)(2,1)S(1)} %bitcast.37, f32[2,36,160,128]{2,1,3,0:T(8,128)} %fusion.34, f32[160]{0:T(256)S(1)} %copy-done.12, bf16[4,36,160,128]{2,1,3,0:T(8,128)(2,1)} %fusion.19, bf16[12,320,160]{2,1,0:T(8,128)(2,1)} %all-gather.2.cloned.1.call-done, s32[]{:T(128)S(6)} %add.100, ...), kind=kOutput, calls=%fused_computation.27 | convolution fusion | flops 1422950400 | bytes 27116168 | tf_op jit(solution)/shard_map/conv_general_dilated | solution.py:38
  338.0 8.1 %copy.69 = bf16[2,36,160,128]{3,2,1,0:T(8,128)(2,1)} copy(bf16[2,36,160,128]{2,1,3,0:T(8,128)(2,1)} %fusion.18) | data formatting | bytes 5898240 | tf_op jit(solution)/shard_map/convert_element_type | solution.py:131
  (44 shorter events, 0.2 us)
Async XLA Ops:
  6.5 27.0 %copy-start.10 = (f32[160]{0:T(256)S(1)}, f32[160]{0:T(256)}, u32[]{:S(2)}) copy-start(f32[160]{0:T(256)} %param.11) | copy-start | bytes 1924
  6.5 27.0 %copy-start.11 = (f32[160]{0:T(256)S(1)}, f32[160]{0:T(256)}, u32[]{:S(2)}) copy-start(f32[160]{0:T(256)} %param.10) | copy-start | bytes 1924
  6.5 105.3 %all-gather.2.cloned.1.call-start = ((), (), s32[]{:S(2)}) async-start(), calls=%async_computation | async-start | bytes 2457600 | tf_op jit(solution)/shard_map/all_gather | solution.py:81
  38.9 12.7 %copy-start = (bf16[2,36,160,128]{2,1,3,0:T(8,128)(2,1)}, bf16[2,36,160,128]{2,1,3,0:T(8,128)(2,1)S(1)}, u32[]{:S(2)}) copy-start(bf16[2,36,160,128]{2,1,3,0:T(8,128)(2,1)S(1)} %fusion.12) | copy-start | bytes 8847364
  38.9 26.9 %copy-start.6 = (bf16[3,80,160]{2,1,0:T(8,128)(2,1)S(1)}, bf16[3,80,160]{2,1,0:T(8,128)(2,1)}, u32[]{:S(2)}) copy-start(bf16[3,80,160]{2,1,0:T(8,128)(2,1)} %param.16) | copy-start | bytes 230404
  39.4 7.8 %collective-permute-start = (bf16[2,1,160,128]{2,1,3,0:T(2,128)(2,1)S(1)}, bf16[2,1,160,128]{2,1,3,0:T(2,128)(2,1)S(1)}, u32[]{:S(2)}, u32[]{:S(2)}) collective-permute-start(bf16[2,1,160,128]{2,1,3,0:T(2,128)(2,1)S(1)} %get-tuple-element.9), channel_id=1, source_target_pairs={{0,2},{1,3},{4,6},{5,7},{8,10},{9,11},{12,14},{13,15},{16,18},{17,... | collective-permute-start | bytes 245768 | tf_op jit(solution)/shard_map/ppermute | solution.py:21
  43.3 8.3 %collective-permute-start.1 = (bf16[2,1,160,128]{2,1,3,0:T(2,128)(2,1)S(1)}, bf16[2,1,160,128]{2,1,3,0:T(2,128)(2,1)S(1)}, u32[]{:S(2)}, u32[]{:S(2)}) collective-permute-start(bf16[2,1,160,128]{2,1,3,0:T(2,128)(2,1)S(1)} %get-tuple-element.10), channel_id=1, source_target_pairs={{2,0},{3,1},{6,4},{7,5},{10,8},{11,9},{14,12},{15,13},{18,16},{19,... | collective-permute-start | bytes 245768 | tf_op jit(solution)/shard_map/ppermute | solution.py:22
  51.6 0.7 copy-start.2
  65.8 48.7 %collective-permute-start.2 = (bf16[2,38,160,128]{3,2,1,0:T(8,128)(2,1)S(1)}, bf16[2,38,160,128]{3,2,1,0:T(8,128)(2,1)}, u32[]{:S(2)}, u32[]{:S(2)}) collective-permute-start(bf16[2,38,160,128]{3,2,1,0:T(8,128)(2,1)S(1)} %copy.58), channel_id=1, source_target_pairs={{0,1},{1,0},{2,3},{3,2},{4,5},{5,4},{6,7},{7,6},{8,9},{9,8},{10,11... | collective-permute-start | bytes 9338888 | tf_op jit(solution)/shard_map/ppermute | solution.py:14
  75.2 2.3 copy-start.1
  122.5 7.3 %copy-start.4 = (bf16[9,160,160]{2,1,0:T(8,128)(2,1)S(1)}, bf16[9,160,160]{2,1,0:T(8,128)(2,1)}, u32[]{:S(2)}) copy-start(bf16[9,160,160]{2,1,0:T(8,128)(2,1)} %get-tuple-element.12) | copy-start | bytes 1382404
  129.7 14.9 %copy-start.3 = (bf16[9,160,160]{2,1,0:T(8,128)(2,1)S(1)}, bf16[9,160,160]{2,1,0:T(8,128)(2,1)}, u32[]{:S(2)}) copy-start(bf16[9,160,160]{2,1,0:T(8,128)(2,1)} %get-tuple-element.11) | copy-start | bytes 1382404
  129.8 14.9 %copy-start.5 = (bf16[38,160,2,7,2]{1,3,2,4,0:T(8,128)(2,1)S(1)}, bf16[38,160,2,7,2]{1,3,2,4,0:T(8,128)(2,1)}, u32[]{:S(2)}) copy-start(bf16[38,160,2,7,2]{1,3,2,4,0:T(8,128)(2,1)} %slice.37) | copy-start | bytes 1021444
  129.8 14.9 %copy-start.13 = (pred[16,17]{0,1:T(8,128)(4,1)S(1)}, pred[16,17]{0,1:T(8,128)(4,1)}, u32[]{:S(2)}) copy-start(pred[16,17]{0,1:T(8,128)(4,1)} %constant.50) | copy-start | bytes 820
  159.1 10.1 %copy-start.7 = (f32[160]{0:T(256)S(1)}, f32[160]{0:T(256)}, u32[]{:S(2)}) copy-start(f32[160]{0:T(256)} %param.13) | copy-start | bytes 1924
  183.4 77.5 %copy-start.8 = (f32[160]{0:T(256)S(1)}, f32[160]{0:T(256)}, u32[]{:S(2)}) copy-start(f32[160]{0:T(256)} %param.15) | copy-start | bytes 1924
  183.4 77.5 %copy-start.9 = (f32[160]{0:T(256)S(1)}, f32[160]{0:T(256)}, u32[]{:S(2)}) copy-start(f32[160]{0:T(256)} %param.14) | copy-start | bytes 1924
  188.0 64.8 %collective-permute-start.4 = (bf16[1,36,160,128]{3,2,1,0:T(8,128)(2,1)}, bf16[1,36,160,128]{3,2,1,0:T(8,128)(2,1)}, u32[]{:S(2)}, u32[]{:S(2)}) collective-permute-start(bf16[1,36,160,128]{3,2,1,0:T(8,128)(2,1)} %copy.63), channel_id=1, source_target_pairs={{4,0},{8,4},{12,8},{5,1},{9,5},{13,9},{6,2},{10,6},{14,10},{7,3},{... | collective-permute-start | bytes 4423688 | tf_op jit(solution)/shard_map/ppermute | solution.py:109
  192.5 64.0 %collective-permute-start.3 = (bf16[1,36,160,128]{3,2,1,0:T(8,128)(2,1)}, bf16[1,36,160,128]{3,2,1,0:T(8,128)(2,1)}, u32[]{:S(2)}, u32[]{:S(2)}) collective-permute-start(bf16[1,36,160,128]{3,2,1,0:T(8,128)(2,1)} %copy.62), channel_id=1, source_target_pairs={{0,4},{4,8},{8,12},{1,5},{5,9},{9,13},{2,6},{6,10},{10,14},{3,7},{... | collective-permute-start | bytes 4423688 | tf_op jit(solution)/shard_map/ppermute | solution.py:108
  288.6 9.9 %collective-permute-start.5 = (bf16[4,36,160,128]{3,2,1,0:T(8,128)(2,1)}, bf16[4,36,160,128]{3,2,1,0:T(8,128)(2,1)}, u32[]{:S(2)}, u32[]{:S(2)}) collective-permute-start(bf16[4,36,160,128]{3,2,1,0:T(8,128)(2,1)} %copy.66), channel_id=1, source_target_pairs={{0,1},{1,0},{2,3},{3,2},{4,5},{5,4},{6,7},{7,6},{8,9},{9,8},{10,11... | collective-permute-start | bytes 17694728 | tf_op jit(solution)/shard_map/ppermute | solution.py:14
  298.5 25.9 %slice-start = ((s8[5242880]{0:T(1024)(128)(4,1)}), s8[1048576]{0:T(1024)(128)(4,1)S(1)}, s32[]{:S(2)}) async-start(s8[5242880]{0:T(1024)(128)(4,1)} %bitcast.36), calls=%async_computation.1 | async-start | bytes 2097152
  313.3 11.0 %slice-start.1 = ((s8[5242880]{0:T(1024)(128)(4,1)}), s8[4194304]{0:T(1024)(128)(4,1)S(1)}, s32[]{:S(2)}) async-start(s8[5242880]{0:T(1024)(128)(4,1)} %bitcast.36), calls=%async_computation.2 | async-start | bytes 8388608
  313.3 11.0 %copy-start.12 = (f32[160]{0:T(256)S(1)}, f32[160]{0:T(256)}, u32[]{:S(2)}) copy-start(f32[160]{0:T(256)} %param.17) | copy-start | bytes 1924
Sparse Core Ops, SparseCore 0:
  67.8 44.0 all-gather.1

commit v2 on v1

v2 whole, which is shorter than its diff:
```python
import jax
import jax.numpy as jnp
from jax import lax
from jax.sharding import PartitionSpec as P

C = 320
GROUPS = 32


EPSILON = 1e-06


def swap_chan(block):
    return lax.ppermute(block, "chan", [(0, 1), (1, 0)])


def row_halo(block):
    count = lax.axis_size("height")
    forward = [(i, i + 1) for i in range(count - 1)]
    backward = [(target, source) for source, target in forward]
    low = lax.ppermute(block[:, -1:], "height", forward)
    high = lax.ppermute(block[:, :1], "height", backward)
    return jnp.concatenate([low, block, high], axis=1)


def gather_tm(piece):
    count = lax.axis_size("tm")
    index = lax.axis_index("tm")
    pieces = [piece]
    for shift in range(1, count):
        pairs = [(i, (i - shift) % count) for i in range(count)]
        pieces.append(lax.ppermute(piece, "tm", pairs))
    stacked = jnp.roll(jnp.stack(pieces), index, axis=0)
    return stacked


def group_stats(grouped, axes, slot_axes):
    count = 1
    for axis in axes:
        count *= grouped.shape[axis]
    local_mean = jnp.sum(grouped, axis=axes) / count
    centred = grouped - jnp.expand_dims(local_mean, axes)
    local_m2 = jnp.sum(centred * centred, axis=axes)
    slots = 1
    for name in slot_axes:
        slots *= lax.axis_size(name)
    slot = 0
    for name in slot_axes:
        slot = slot * lax.axis_size(name) + lax.axis_index(name)
    mine = jnp.stack([local_mean, local_m2])
    table = jnp.zeros((slots,) + mine.shape, jnp.float32)
    table = lax.dynamic_update_index_in_dim(table, mine, slot, 0)
    for name in reversed(slot_axes):
        table = lax.psum(table, name)
    means = table[:, 0]
    average = jnp.sum(means, axis=0) / slots
    spread = means - average
    m2 = jnp.sum(table[:, 1], axis=0) + count * jnp.sum(spread * spread, axis=0)
    variance = m2 / (count * slots)
    return average, variance


def group_act(values, average, variance, gain, bias):
    frames, rows, local_chan, width = values.shape
    local_groups = average.shape[-1]
    grouped = values.reshape(frames, rows, local_groups, local_chan // local_groups, width)
    centred = grouped - average.reshape(-1, 1, local_groups, 1, 1)
    scaled = (centred * lax.rsqrt(variance.reshape(-1, 1, local_groups, 1, 1) + EPSILON)).reshape(
        frames, rows, local_chan, width
    )
    return jax.nn.silu(scaled * gain[:, None] + bias[:, None]).astype(jnp.bfloat16)


def both_halves(own, other, chan_index):
    first = jnp.where(chan_index == 0, own, other)
    second = jnp.where(chan_index == 0, other, own)
    return jnp.concatenate([first, second], axis=2)


def spatial_taps(running, channel_slab, weight, rows, width):
    for row_tap in range(3):
        for col_tap in range(3):
            window = channel_slab[:, row_tap : row_tap + rows, :, col_tap : col_tap + width]
            running = running + jnp.einsum(
                "frcw,co->frow", window, weight[row_tap, col_tap], preferred_element_type=jnp.float32
            )
    return running


def temporal_taps(running, channel_slab, weight, frames):
    for frame_tap in range(3):
        window = channel_slab[frame_tap : frame_tap + frames]
        running = running + jnp.einsum(
            "frcw,co->frow", window, weight[frame_tap], preferred_element_type=jnp.float32
        )
    return running


def body(
    video,
    norm1_gain,
    norm1_bias,
    spatial_weight,
    spatial_bias,
    norm2_gain,
    norm2_bias,
    temporal_weight,
    temporal_bias,
):
    frames, rows, local_chan, width = video.shape
    group_size = C // GROUPS
    local_groups = local_chan // group_size
    chan_index = lax.axis_index("chan")
    tm_index = lax.axis_index("tm")
    tm_count = lax.axis_size("tm")

    piece = spatial_weight.shape[2]
    merged = jnp.concatenate([spatial_weight.reshape(9, piece, local_chan), temporal_weight], axis=0)
    gathered = gather_tm(merged)
    full_weight = jnp.moveaxis(gathered, 0, 1).reshape(12, tm_count * piece, local_chan)
    spatial_full = full_weight[:9].reshape(3, 3, C, local_chan)
    temporal_full = full_weight[9:]

    values = video.astype(jnp.float32)
    grouped = values.reshape(frames, rows, local_groups, group_size, width)
    average, variance = group_stats(grouped, (1, 3, 4), ("height",))
    act_one = group_act(values, average, variance, norm1_gain, norm1_bias)

    with_rows = row_halo(act_one)
    all_rows = both_halves(with_rows, swap_chan(with_rows), chan_index)
    padded = jnp.pad(all_rows, ((0, 0), (0, 0), (0, 0), (1, 1)))
    empty = jnp.zeros((frames, rows, local_chan, width), jnp.float32)
    spatial_sum = spatial_taps(empty, padded, spatial_full, rows, width)
    hidden = (values + spatial_sum + spatial_bias[:, None]).astype(jnp.bfloat16)

    forward = [(i, i + 1) for i in range(tm_count - 1)]
    backward = [(target, source) for source, target in forward]
    before = lax.ppermute(hidden[-1:], "tm", forward)
    after = lax.ppermute(hidden[:1], "tm", backward)

    hidden_values = hidden.astype(jnp.float32)
    grouped_two = hidden_values.reshape(frames, rows, local_groups, group_size, width)
    average_two, variance_two = group_stats(grouped_two, (0, 1, 3, 4), ("tm", "height"))

    extended = jnp.concatenate([before, hidden, after], axis=0).astype(jnp.float32)
    act_two = group_act(extended, average_two, variance_two, norm2_gain, norm2_bias)
    frame_ids = jnp.arange(frames + 2)
    inside = (frame_ids > 0) | (tm_index > 0)
    inside = inside & ((frame_ids < frames + 1) | (tm_index < tm_count - 1))
    act_two = jnp.where(inside[:, None, None, None], act_two, jnp.zeros_like(act_two))

    all_two = both_halves(act_two, swap_chan(act_two), chan_index)
    temporal_sum = temporal_taps(empty, all_two, temporal_full, frames)
    return (hidden_values + temporal_sum + temporal_bias[:, None]).astype(jnp.bfloat16)


def solution(mesh):
    return jax.shard_map(
        body,
        mesh=mesh,
        in_specs=(
            P(("groups", "tm"), "height", "chan", None),
            P("chan"),
            P("chan"),
            P(None, None, "tm", "chan"),
            P("chan"),
            P("chan"),
            P("chan"),
            P(None, "tm", "chan"),
            P("chan"),
        ),
        out_specs=P(("groups", "tm"), "height", "chan", None),
        check_vma=False,
    )
```

time: 360 us -> 227 us (0.63); the launches traced: 353 us -> 227 us
  local copies, waits for them, and re-layouts: 107 us -> 20.9 us
  other arithmetic: 55.5 us -> 31.8 us
  blocking collectives: 60.5 us -> 40.6 us
  between operations: 13.9 us -> 0.37 us
  matrix products: 53.9 us -> 65.3 us
    dot_general x0 -> x12, matrix products: none -> 65.3 us  [the longest x9 51.4 us: spatial_taps(): jnp.einsum('frcw,co->frow', window, weight[row_tap, col_tap], preferred_e...]
    conv_general_dilated x4 -> x0, matrix products: 53.9 us -> none  [the longest x2 29.3 us: spatial_conv(): lax.conv_general_dilated(inputs, weight, window_strides=(1, 1), padding=(...]
    ppermute x0 -> x3, waiting for transfers between devices: none -> 39.9 us  [gather_tm(): pieces.append(lax.ppermute(piece, 'tm', pairs))]
    all_gather x1 -> x0, waiting for transfers between devices: 33.4 us -> none  [body(): full_weight = lax.all_gather(merged, 'tm', axis=1, tiled=True)]
    ppermute x4 -> x0, local copies, waits for them, and re-layouts: 26.4 us -> none  [the longest x2 18.3 us: swap_chan(): return lax.ppermute(block, 'chan', [(0, 1), (1, 0)])]
    psum x6 -> x3, blocking collectives: 60.5 us -> 40.6 us  [group_stats(): table = lax.psum(table, name)]
    reduce_sum x8 -> x11, other arithmetic: 21.9 us -> 6.62 us  [the longest x4 3.88 us: group_stats(): local_m2 = jnp.sum(centred * centred, axis=axes)]
    select_n x1 -> x0, local copies, waits for them, and re-layouts: 15.3 us -> none  [body(): jnp.where(inside[:, None, None, None], act_two, jnp.zeros_like(act_two))]
  transfers between devices with their start and end apart: 7 -> 9, of which waited for: 4 -> 5; matrix products, arithmetic and copies ran while one was open for 7% -> 9% of each run, Pallas kernels for 0% -> 0%
where the time goes in v2:
time: 227 us
  matrix products  65.3 us (29%)
  waiting for transfers between devices  53.5 us (24%)
  blocking collectives  40.6 us (18%)
  other arithmetic  31.8 us (14%)
  local copies, waits for them, and re-layouts  20.9 us (9%)
  starting transfers between devices  14.6 us (6%)
    dot_general x9, matrix products, spatial_taps(): jnp.einsum('frcw,co->frow', window, weight[row_tap, col_tap], preferred_e...  51.4 us
    psum x3, blocking collectives, group_stats(): table = lax.psum(table, name)  40.6 us
    ppermute x3, waiting for transfers between devices, gather_tm(): pieces.append(lax.ppermute(piece, 'tm', pairs))  39.9 us
    dot_general x3, matrix products, temporal_taps(): jnp.einsum('frcw,co->frow', window, weight[frame_tap], preferred_element_...  13.9 us
    select_n x2, other arithmetic, both_halves(): second = jnp.where(chan_index == 0, other, own)  9.9 us
    ppermute x2, waiting for transfers between devices, swap_chan(): return lax.ppermute(block, 'chan', [(0, 1), (1, 0)])  8.47 us
    select_n x1, other arithmetic, body(): jnp.where(inside[:, None, None, None], act_two, jnp.zeros_like(act_two))  6.12 us
    unnamed x39, local copies, waits for them, and re-layouts  5.44 us
  transfers between devices with their start and end apart: 9, of which 5 were waited for; matrix products, arithmetic and copies ran while one was open for 9% of the time, Pallas kernels for 0%

profile of v2, /device:TPU:0, one launch (start us, length us, event | category | flops | bytes accessed | tf_op | source)
XLA Modules:
  0.0 226.9 jit_solution(17469428537658887844)
XLA Ops:
  0.0 2.5 %convert_reduce_fusion = f32[2,160]{1,0:T(2,128)S(1)} fusion(bf16[2,36,160,128]{3,2,1,0:T(8,128)(2,1)} %param.9), kind=kLoop, calls=%fused_computation.14 | loop fusion | flops 2948800 | bytes 2950400 | tf_op jit(solution)/shard_map/reduce_sum | solution.py:41
  2.5 0.1 reduce_sum.101
  2.5 0.1 reduce_sum.120
  2.7 0.1 sub.74
  2.8 2.7 %fusion.14 = f32[2,160]{1,0:T(2,128)S(1)} fusion(bf16[2,36,160,128]{3,2,1,0:T(8,128)(2,1)} %param.9, f32[2,160]{1,0:T(2,128)S(1)} %sub.74), kind=kLoop, calls=%fused_computation.36 | loop fusion | flops 5897920 | bytes 2951680 | tf_op jit(solution)/shard_map/reduce_sum | solution.py:43
  5.6 0.1 reduce_sum.122
  5.7 0.1 reduce_sum.123
  5.8 5.9 %psum.21 = f32[2,2,2,16]{3,2,0,1:T(2,128)S(1)} all-reduce(f32[2,2,2,16]{3,2,0,1:T(2,128)S(1)} %fusion.43), channel_id=1, replica_groups=mesh['groups'=2,'tm'=4,'height'=2,'chan'=2] {'height'}, use_global_device_ids=true, to_apply=%region_4.5 | all-reduce | flops 128 | bytes 1024 | tf_op jit(solution)/shard_map/psum | solution.py:54
  11.7 0.1 mul.85
  11.9 0.1 sub.78
  12.1 2.3 %fusion.23 = bf16[2,36,160,128]{3,2,1,0:T(8,128)(2,1)S(1)} fusion(bf16[2,36,160,128]{3,2,1,0:T(8,128)(2,1)S(1)} %copy-done, f32[160]{0:T(256)S(1)} %copy-done.15, f32[160]{0:T(256)S(1)} %copy-done.16, f32[2,160]{1,0:T(2,128)S(1)} %mul.85, f32[2,160]{1,0:T(2,128)S(1)} %sub.78), kind=kLoop, calls=%fused_computation.45 | loop fusion | flops 14745600 | bytes 5902080 | tf_op jit(solution)/shard_map/convert_element_type | solution.py:71
  14.4 4.0 %collective-permute-start.3 = (bf16[2,1,160,128]{3,2,1,0:T(8,128)(2,1)S(1)}, bf16[2,1,160,128]{3,2,1,0:T(8,128)(2,1)S(1)}, u32[]{:S(2)}, u32[]{:S(2)}) collective-permute-start(bf16[2,1,160,128]{3,2,1,0:T(8,128)(2,1)S(1)} %get-tuple-element.15), channel_id=1, source_target_pairs={{0,2},{1,3},{4,6},{5,7},{8,10},{9,11},{12,14},{13,15},{16,18},{17,... | collective-permute-start | bytes 245768 | tf_op jit(solution)/shard_map/ppermute | solution.py:21
  18.4 1.3 collective-permute-start.4
  19.7 0.7 collective-permute-done.3
  20.4 4.3 %collective-permute-done.4 = bf16[2,1,160,128]{3,2,1,0:T(8,128)(2,1)S(1)} collective-permute-done((bf16[2,1,160,128]{3,2,1,0:T(8,128)(2,1)S(1)}, bf16[2,1,160,128]{3,2,1,0:T(8,128)(2,1)S(1)}, u32[]{:S(2)}, u32[]{:S(2)}) %collective-permute-start.4) | collective-permute-done | bytes 81952 | tf_op jit(solution)/shard_map/ppermute | solution.py:22
  24.7 2.1 pad_maximum_fusion.3
  26.8 0.1 pad_maximum_fusion.4
  26.9 3.7 %collective-permute-start = (bf16[12,80,160]{2,1,0:T(8,128)(2,1)S(1)}, bf16[12,80,160]{2,1,0:T(8,128)(2,1)S(1)}, u32[]{:S(2)}, u32[]{:S(2)}) collective-permute-start(bf16[12,80,160]{2,1,0:T(8,128)(2,1)S(1)} %pad_maximum_fusion.4), channel_id=1, source_target_pairs={{0,12},{4,0},{8,4},{12,8},{1,13},{5,1},{9,5},{13,9},{2,14},{6,2},{... | collective-permute-start | bytes 921608 | tf_op jit(solution)/shard_map/ppermute | solution.py:32
  30.6 1.0 collective-permute-start.2
  31.6 0.9 bitcast_dynamic-update-slice_fusion.6
  32.4 9.8 %collective-permute-done = bf16[12,80,160]{2,1,0:T(8,128)(2,1)S(1)} collective-permute-done((bf16[12,80,160]{2,1,0:T(8,128)(2,1)S(1)}, bf16[12,80,160]{2,1,0:T(8,128)(2,1)S(1)}, u32[]{:S(2)}, u32[]{:S(2)}) %collective-permute-start) | collective-permute-done | bytes 307232 | tf_op jit(solution)/shard_map/ppermute | solution.py:32
  42.2 0.8 bitcast_dynamic-update-slice_fusion.4
  43.0 30.2 %collective-permute-done.1 = bf16[12,80,160]{2,1,0:T(8,128)(2,1)S(1)} collective-permute-done((bf16[12,80,160]{2,1,0:T(8,128)(2,1)S(1)}, bf16[12,80,160]{2,1,0:T(8,128)(2,1)S(1)}, u32[]{:S(2)}, u32[]{:S(2)}) %collective-permute-start.1) | collective-permute-done | bytes 307232 | tf_op jit(solution)/shard_map/ppermute | solution.py:32
  73.2 0.8 bitcast_dynamic-update-slice_fusion.2
  74.0 0.8 bitcast_dynamic-update-slice_fusion
  74.8 0.9 bitcast_dynamic-update-slice_fusion.7
  75.7 0.8 bitcast_dynamic-update-slice_fusion.5
  76.5 0.8 bitcast_dynamic-update-slice_fusion.3
  77.4 0.8 bitcast_dynamic-update-slice_fusion.1
  78.2 1.8 dynamic-slice_bitcast_fusion
  80.0 1.3 copy-done.5
  81.3 1.2 slice.144
  82.5 3.7 %copy.26 = bf16[9,4,80,160]{2,1,3,0:T(4,128)(2,1)} copy(bf16[9,4,80,160]{3,2,0,1:T(8,128)(2,1)} %slice.144) | data formatting | bytes 1843200 | tf_op jit(solution)/shard_map/slice | solution.py:121
  86.2 3.6 %reshape.119 = bf16[3,3,320,160]{2,3,1,0:T(8,128)(2,1)} reshape(bf16[9,4,80,160]{2,1,3,0:T(4,128)(2,1)} %copy.26) | data formatting | bytes 1843200 | tf_op jit(solution)/shard_map/reshape | solution.py:121
  89.8 2.2 broadcast_select_fusion.2
  92.0 4.6 %fusion.7 = f32[160,2,36,128]{3,0,2,1:T(8,128)} fusion(bf16[2,38,160,128]{3,2,1,0:T(8,128)(2,1)S(1)} %get-tuple-element.12, bf16[2,38,160,128]{3,2,1,0:T(8,128)(2,1)S(1)} %get-tuple-element.11, bf16[3,3,320,160]{2,3,1,0:T(8,128)(2,1)} %reshape.119), kind=kOutput, calls=%fused_computation.30 | convolution fusion | flops 955514880 | bytes 12247040 | tf_op jit(solution)/shard_map/frcw,co->frow/dot_general | solution.py:84
  96.6 4.4 %fusion.4 = f32[160,2,36,128]{3,0,2,1:T(8,128)} fusion(bf16[2,38,160,128]{3,2,1,0:T(8,128)(2,1)S(1)} %get-tuple-element.12, bf16[2,38,160,128]{3,2,1,0:T(8,128)(2,1)S(1)} %get-tuple-element.11, bf16[3,3,320,160]{2,3,1,0:T(8,128)(2,1)} %reshape.119), kind=kOutput, calls=%fused_computation.28 | convolution fusion | flops 955514880 | bytes 12247040 | tf_op jit(solution)/shard_map/frcw,co->frow/dot_general | solution.py:84
  101.0 4.4 %fusion.1 = f32[160,2,36,128]{3,0,2,1:T(8,128)} fusion(bf16[2,38,160,128]{3,2,1,0:T(8,128)(2,1)S(1)} %get-tuple-element.12, bf16[2,38,160,128]{3,2,1,0:T(8,128)(2,1)S(1)} %get-tuple-element.11, bf16[3,3,320,160]{2,3,1,0:T(8,128)(2,1)} %reshape.119), kind=kOutput, calls=%fused_computation.26 | convolution fusion | flops 955514880 | bytes 12247040 | tf_op jit(solution)/shard_map/frcw,co->frow/dot_general | solution.py:84
  105.4 2.9 %pad_maximum_fusion = bf16[2,38,320,128]{3,2,1,0:T(8,128)(2,1)S(1)} fusion(bf16[2,38,160,128]{3,2,1,0:T(8,128)(2,1)S(1)} %get-tuple-element.11, bf16[2,38,160,128]{3,2,1,0:T(8,128)(2,1)} %copy-done.4), kind=kLoop, calls=%fused_computation.21 | loop fusion | flops 12451840 | bytes 12451840 | tf_op jit(solution)/shard_map/concatenate | solution.py:77
  108.3 4.3 %fusion.34 = f32[160,2,36,128]{3,0,2,1:T(8,128)} fusion(bf16[2,38,320,128]{3,2,1,0:T(8,128)(2,1)S(1)} %pad_maximum_fusion, bf16[3,3,320,160]{2,3,1,0:T(8,128)(2,1)S(1)} %copy-done.7), kind=kOutput, calls=%fused_computation.54 | convolution fusion | flops 943718400 | bytes 12247040 | tf_op jit(solution)/shard_map/frcw,co->frow/dot_general | solution.py:84
  112.6 4.3 %fusion.35 = f32[160,2,36,128]{3,0,2,1:T(8,128)} fusion(bf16[2,38,320,128]{3,2,1,0:T(8,128)(2,1)S(1)} %pad_maximum_fusion, bf16[3,3,320,160]{2,3,1,0:T(8,128)(2,1)S(1)} %copy-done.7), kind=kOutput, calls=%fused_computation.55 | convolution fusion | flops 943718400 | bytes 12247040 | tf_op jit(solution)/shard_map/frcw,co->frow/dot_general | solution.py:84
  116.9 4.3 %fusion.36 = f32[160,2,36,128]{3,0,2,1:T(8,128)} fusion(bf16[2,38,320,128]{3,2,1,0:T(8,128)(2,1)S(1)} %pad_maximum_fusion, bf16[3,3,320,160]{2,3,1,0:T(8,128)(2,1)S(1)} %copy-done.7), kind=kOutput, calls=%fused_computation.56 | convolution fusion | flops 943718400 | bytes 12247040 | tf_op jit(solution)/shard_map/frcw,co->frow/dot_general | solution.py:84
  121.2 4.3 %fusion.37 = f32[160,2,36,128]{3,0,2,1:T(8,128)} fusion(bf16[2,38,320,128]{3,2,1,0:T(8,128)(2,1)S(1)} %pad_maximum_fusion, bf16[3,3,320,160]{2,3,1,0:T(8,128)(2,1)S(1)} %copy-done.7), kind=kOutput, calls=%fused_computation.57 | convolution fusion | flops 943718400 | bytes 12247040 | tf_op jit(solution)/shard_map/frcw,co->frow/dot_general | solution.py:84
  125.5 4.4 %fusion.33 = f32[160,2,36,128]{3,0,2,1:T(8,128)} fusion(bf16[2,38,320,128]{3,2,1,0:T(8,128)(2,1)S(1)} %pad_maximum_fusion, bf16[3,3,320,160]{2,3,1,0:T(8,128)(2,1)S(1)} %copy-done.7), kind=kOutput, calls=%fused_computation.53 | convolution fusion | flops 943718400 | bytes 12247040 | tf_op jit(solution)/shard_map/frcw,co->frow/dot_general | solution.py:84
  129.8 16.4 %convert_reduce_fusion.1 = (f32[160]{0:T(256)S(1)}, bf16[2,36,160,128]{3,2,1,0:T(8,128)(2,1)S(1)}) fusion(f32[160]{0:T(256)S(1)} %copy-done.11, bf16[2,38,320,128]{3,2,1,0:T(8,128)(2,1)S(1)} %pad_maximum_fusion, bf16[3,3,320,160]{2,3,1,0:T(8,128)(2,1)} %reshape.119, f32[160,2,36,128]{3,0,2,1:T(8,128)} %fusion.7, f32[160,2,36,128]{3,0,2,1:T(8,128)} %fusion.37, ...), kind=kOutput, calls=%fused_computation.17 | convolution fusion | flops 964362112 | bytes 59434240 | tf_op jit(solution)/shard_map/frcw,co->frow/dot_general | solution.py:84
  146.3 1.8 fusion.60
  148.1 3.1 %collective-permute-start.6 = (bf16[1,36,160,128]{3,2,1,0:T(8,128)(2,1)}, bf16[1,36,160,128]{3,2,1,0:T(8,128)(2,1)}, u32[]{:S(2)}, u32[]{:S(2)}) collective-permute-start(bf16[1,36,160,128]{3,2,1,0:T(8,128)(2,1)} %get-tuple-element.13), channel_id=1, source_target_pairs={{0,4},{4,8},{8,12},{1,5},{5,9},{9,13},{2,6},{6,10},{10,14},{3,7},{... | collective-permute-start | bytes 4423688 | tf_op jit(solution)/shard_map/ppermute | solution.py:138
  151.2 1.5 collective-permute-start.7
  152.8 0.1 reduce_sum.129
  153.0 0.1 sub.84
  153.1 0.9 fusion.10
  154.0 0.1 reduce_sum.131
  154.1 0.1 reduce_sum.132
  154.3 5.0 %psum.22 = f32[8,2,16]{2,0,1:T(8,128)S(1)} all-reduce(f32[8,2,16]{2,0,1:T(8,128)S(1)} %dynamic_update_slice.9), channel_id=1, replica_groups=mesh['groups'=2,'tm'=4,'height'=2,'chan'=2] {'height'}, use_global_device_ids=true, to_apply=%region_12.13 | all-reduce | flops 256 | bytes 2048 | tf_op jit(solution)/shard_map/psum | solution.py:54
  159.3 29.7 %psum.23 = f32[8,2,16]{2,0,1:T(8,128)S(1)} all-reduce(f32[8,2,16]{2,0,1:T(8,128)S(1)} %psum.22), channel_id=1, replica_groups=mesh['groups'=2,'tm'=4,'height'=2,'chan'=2] {'tm'}, use_global_device_ids=true, to_apply=%region_13.14 | all-reduce | flops 256 | bytes 2048 | tf_op jit(solution)/shard_map/psum | solution.py:54
  189.1 0.1 mul.96
  189.3 0.1 sub.88
  189.4 6.1 %fusion.26 = bf16[4,36,160,128]{3,2,1,0:T(8,128)(2,1)S(1)} fusion(bf16[1,36,160,128]{3,2,1,0:T(8,128)(2,1)} %collective-permute-done.7, bf16[2,36,160,128]{3,2,1,0:T(8,128)(2,1)S(1)} %get-tuple-element.25, bf16[1,36,160,128]{3,2,1,0:T(8,128)(2,1)} %collective-permute-done.6, f32[160]{0:T(256)S(1)} %copy-done.12, f32[160]{0:T(256)S(1)} %copy-done.13, ...), kind=kLoop, calls=%fused_computation.48 | loop fusion | flops 38338560 | bytes 11799044 | tf_op jit(solution)/shard_map/jit(_where)/select_n | solution.py:150
  195.7 1.1 fusion.62
  196.8 8.5 %collective-permute-done.8 = bf16[4,36,160,128]{3,2,1,0:T(8,128)(2,1)S(1)} collective-permute-done((bf16[4,36,160,128]{3,2,1,0:T(8,128)(2,1)S(1)}, bf16[4,36,160,128]{3,2,1,0:T(8,128)(2,1)S(1)}, u32[]{:S(2)}, u32[]{:S(2)}) %collective-permute-start.8) | collective-permute-done | bytes 5898272 | tf_op jit(solution)/shard_map/ppermute | solution.py:14
  205.2 7.7 %broadcast_select_fusion = (bf16[4,36,160,128]{3,2,1,0:T(8,128)(2,1)S(1)}, bf16[4,36,160,128]{3,2,1,0:T(8,128)(2,1)S(1)}) fusion(bf16[4,36,160,128]{3,2,1,0:T(8,128)(2,1)S(1)} %collective-permute-done.8, pred[]{:T(512)S(6)} %eq.5, f32[160]{0:T(256)S(1)} %copy-done.12, f32[160]{0:T(256)S(1)} %copy-done.13, f32[160]{0:T(256)S(1)} %mul.96, f32[160]{0:T(256)S(1)} %sub.88, ...), kind=kLoop, calls=%fused_computation.62 | loop fusion | flops 44236800 | bytes 23595524 | tf_op jit(solution)/shard_map/jit(_where)/select_n | solution.py:76
  213.0 3.6 %fusion.31 = f32[160,2,36,128]{3,0,2,1:T(8,128)} fusion(bf16[320,160,1,1]{1,0,3,2:T(8,128)(2,1)S(1)} %bitcast.132, bf16[4,36,160,128]{3,2,1,0:T(8,128)(2,1)S(1)} %get-tuple-element.10, bf16[4,36,160,128]{3,2,1,0:T(8,128)(2,1)S(1)} %get-tuple-element.9), kind=kOutput, calls=%fused_computation.52 | convolution fusion | flops 955514880 | bytes 17797120 | tf_op jit(solution)/shard_map/frcw,co->frow/dot_general | solution.py:93
  216.5 3.6 %fusion.28 = f32[160,2,36,128]{3,0,2,1:T(8,128)} fusion(bf16[320,160,1,1]{1,0,3,2:T(8,128)(2,1)S(1)} %bitcast.131, bf16[4,36,160,128]{3,2,1,0:T(8,128)(2,1)S(1)} %get-tuple-element.10, bf16[4,36,160,128]{3,2,1,0:T(8,128)(2,1)S(1)} %get-tuple-element.9), kind=kOutput, calls=%fused_computation.50 | convolution fusion | flops 955514880 | bytes 17797120 | tf_op jit(solution)/shard_map/frcw,co->frow/dot_general | solution.py:93
  220.1 6.8 %fusion.12 = bf16[2,36,160,128]{3,2,1,0:T(8,128)(2,1)} fusion(bf16[2,36,160,128]{3,2,1,0:T(8,128)(2,1)S(1)} %get-tuple-element.25, f32[160,2,36,128]{3,0,2,1:T(8,128)} %fusion.31, f32[160,2,36,128]{3,0,2,1:T(8,128)} %fusion.28, f32[160]{0:T(256)S(1)} %copy-done.14, bf16[320,160,1,1]{1,0,3,2:T(8,128)(2,1)S(1)} %bitcast.130, ...), kind=kOutput, calls=%fused_computation.34 | convolution fusion | flops 964362240 | bytes 29594240 | tf_op jit(solution)/shard_map/frcw,co->frow/dot_general | solution.py:93
  (64 shorter events, 0.9 us)
Async XLA Ops:
  0.0 12.0 %copy-start = (bf16[2,36,160,128]{3,2,1,0:T(8,128)(2,1)S(1)}, bf16[2,36,160,128]{3,2,1,0:T(8,128)(2,1)}, u32[]{:S(2)}) copy-start(bf16[2,36,160,128]{3,2,1,0:T(8,128)(2,1)} %param.9) | copy-start | bytes 8847364
  0.0 12.0 %copy-start.15 = (f32[160]{0:T(256)S(1)}, f32[160]{0:T(256)}, u32[]{:S(2)}) copy-start(f32[160]{0:T(256)} %param.11) | copy-start | bytes 1924
  0.0 12.0 %copy-start.16 = (f32[160]{0:T(256)S(1)}, f32[160]{0:T(256)}, u32[]{:S(2)}) copy-start(f32[160]{0:T(256)} %param.10) | copy-start | bytes 1924
  12.0 14.8 %copy-start.6 = (bf16[3,3,80,160]{3,2,1,0:T(8,128)(2,1)S(1)}, bf16[3,3,80,160]{3,2,1,0:T(8,128)(2,1)}, u32[]{:S(2)}) copy-start(bf16[3,3,80,160]{3,2,1,0:T(8,128)(2,1)} %param.12) | copy-start | bytes 691204
  12.1 14.8 %copy-start.8 = (bf16[3,80,160]{2,1,0:T(8,128)(2,1)S(1)}, bf16[3,80,160]{2,1,0:T(8,128)(2,1)}, u32[]{:S(2)}) copy-start(bf16[3,80,160]{2,1,0:T(8,128)(2,1)} %param.16) | copy-start | bytes 230404
  14.4 10.3 %copy-start.2 = (bf16[2,36,160,128]{3,2,1,0:T(8,128)(2,1)}, bf16[2,36,160,128]{3,2,1,0:T(8,128)(2,1)S(1)}, u32[]{:S(2)}) copy-start(bf16[2,36,160,128]{3,2,1,0:T(8,128)(2,1)S(1)} %fusion.23) | copy-start | bytes 8847364
  14.4 6.0 %collective-permute-start.3 = (bf16[2,1,160,128]{3,2,1,0:T(8,128)(2,1)S(1)}, bf16[2,1,160,128]{3,2,1,0:T(8,128)(2,1)S(1)}, u32[]{:S(2)}, u32[]{:S(2)}) collective-permute-start(bf16[2,1,160,128]{3,2,1,0:T(8,128)(2,1)S(1)} %get-tuple-element.15), channel_id=1, source_target_pairs={{0,2},{1,3},{4,6},{5,7},{8,10},{9,11},{12,14},{13,15},{16,18},{17,... | collective-permute-start | bytes 245768 | tf_op jit(solution)/shard_map/ppermute | solution.py:21
  18.4 6.3 %collective-permute-start.4 = (bf16[2,1,160,128]{3,2,1,0:T(8,128)(2,1)S(1)}, bf16[2,1,160,128]{3,2,1,0:T(8,128)(2,1)S(1)}, u32[]{:S(2)}, u32[]{:S(2)}) collective-permute-start(bf16[2,1,160,128]{3,2,1,0:T(8,128)(2,1)S(1)} %get-tuple-element.16), channel_id=1, source_target_pairs={{2,0},{3,1},{6,4},{7,5},{10,8},{11,9},{14,12},{15,13},{18,16},{19,... | collective-permute-start | bytes 245768 | tf_op jit(solution)/shard_map/ppermute | solution.py:22
  24.7 6.8 %copy-start.9 = (bf16[2,1,160,128]{3,2,1,0:T(8,128)(2,1)}, bf16[2,1,160,128]{3,2,1,0:T(8,128)(2,1)S(1)}, u32[]{:S(2)}) copy-start(bf16[2,1,160,128]{3,2,1,0:T(8,128)(2,1)S(1)} %collective-permute-done.4) | copy-start | bytes 245764
  26.8 63.0 %collective-permute-start.5 = (bf16[2,38,160,128]{3,2,1,0:T(8,128)(2,1)}, bf16[2,38,160,128]{3,2,1,0:T(8,128)(2,1)}, u32[]{:S(2)}, u32[]{:S(2)}) collective-permute-start(bf16[2,38,160,128]{3,2,1,0:T(8,128)(2,1)} %pad_maximum_fusion.3), channel_id=1, source_target_pairs={{0,1},{1,0},{2,3},{3,2},{4,5},{5,4},{6,7},{7,6},{8,9},{9,8},{10,11... | collective-permute-start | bytes 9338888 | tf_op jit(solution)/shard_map/ppermute | solution.py:14
  26.9 15.3 %collective-permute-start = (bf16[12,80,160]{2,1,0:T(8,128)(2,1)S(1)}, bf16[12,80,160]{2,1,0:T(8,128)(2,1)S(1)}, u32[]{:S(2)}, u32[]{:S(2)}) collective-permute-start(bf16[12,80,160]{2,1,0:T(8,128)(2,1)S(1)} %pad_maximum_fusion.4), channel_id=1, source_target_pairs={{0,12},{4,0},{8,4},{12,8},{1,13},{5,1},{9,5},{13,9},{2,14},{6,2},{... | collective-permute-start | bytes 921608 | tf_op jit(solution)/shard_map/ppermute | solution.py:32
  30.6 42.6 %collective-permute-start.1 = (bf16[12,80,160]{2,1,0:T(8,128)(2,1)S(1)}, bf16[12,80,160]{2,1,0:T(8,128)(2,1)S(1)}, u32[]{:S(2)}, u32[]{:S(2)}) collective-permute-start(bf16[12,80,160]{2,1,0:T(8,128)(2,1)S(1)} %pad_maximum_fusion.4), channel_id=1, source_target_pairs={{0,8},{4,12},{8,0},{12,4},{1,9},{5,13},{9,1},{13,5},{2,10},{6,14},... | collective-permute-start | bytes 921608 | tf_op jit(solution)/shard_map/ppermute | solution.py:32
  30.6 43.5 %collective-permute-start.2 = (bf16[12,80,160]{2,1,0:T(8,128)(2,1)S(1)}, bf16[12,80,160]{2,1,0:T(8,128)(2,1)S(1)}, u32[]{:S(2)}, u32[]{:S(2)}) collective-permute-start(bf16[12,80,160]{2,1,0:T(8,128)(2,1)S(1)} %pad_maximum_fusion.4), channel_id=1, source_target_pairs={{0,4},{4,8},{8,12},{12,0},{1,5},{5,9},{9,13},{13,1},{2,6},{6,10},{... | collective-permute-start | bytes 921608 | tf_op jit(solution)/shard_map/ppermute | solution.py:32
  78.2 11.6 %copy-start.3 = (bf16[2,36,160,128]{3,2,1,0:T(8,128)(2,1)S(1)}, bf16[2,36,160,128]{3,2,1,0:T(8,128)(2,1)}, u32[]{:S(2)}) copy-start(bf16[2,36,160,128]{3,2,1,0:T(8,128)(2,1)} %copy-done.2) | copy-start | bytes 8847364
  78.2 11.6 %copy-start.10 = (bf16[2,1,160,128]{3,2,1,0:T(8,128)(2,1)S(1)}, bf16[2,1,160,128]{3,2,1,0:T(8,128)(2,1)}, u32[]{:S(2)}) copy-start(bf16[2,1,160,128]{3,2,1,0:T(8,128)(2,1)} %copy-done.9) | copy-start | bytes 245764
  80.0 1.3 copy-start.5
  92.0 9.0 %copy-start.4 = (bf16[2,38,160,128]{3,2,1,0:T(8,128)(2,1)}, bf16[2,38,160,128]{3,2,1,0:T(8,128)(2,1)S(1)}, u32[]{:S(2)}) copy-start(bf16[2,38,160,128]{3,2,1,0:T(8,128)(2,1)S(1)} %get-tuple-element.12) | copy-start | bytes 9338884
  105.4 2.9 %copy-start.7 = (bf16[3,3,320,160]{2,3,1,0:T(8,128)(2,1)S(1)}, bf16[3,3,320,160]{2,3,1,0:T(8,128)(2,1)}, u32[]{:S(2)}) copy-start(bf16[3,3,320,160]{2,3,1,0:T(8,128)(2,1)} %reshape.119) | copy-start | bytes 2764804
  125.5 4.4 %copy-start.1 = (bf16[2,36,160,128]{3,2,1,0:T(8,128)(2,1)S(1)}, bf16[2,36,160,128]{3,2,1,0:T(8,128)(2,1)}, u32[]{:S(2)}) copy-start(bf16[2,36,160,128]{3,2,1,0:T(8,128)(2,1)} %param.9) | copy-start | bytes 8847364
  125.5 4.4 %copy-start.11 = (f32[160]{0:T(256)S(1)}, f32[160]{0:T(256)}, u32[]{:S(2)}) copy-start(f32[160]{0:T(256)} %param.13) | copy-start | bytes 1924
  146.3 43.1 %copy-start.12 = (f32[160]{0:T(256)S(1)}, f32[160]{0:T(256)}, u32[]{:S(2)}) copy-start(f32[160]{0:T(256)} %param.15) | copy-start | bytes 1924
  146.3 43.1 %copy-start.13 = (f32[160]{0:T(256)S(1)}, f32[160]{0:T(256)}, u32[]{:S(2)}) copy-start(f32[160]{0:T(256)} %param.14) | copy-start | bytes 1924
  148.1 41.3 %collective-permute-start.6 = (bf16[1,36,160,128]{3,2,1,0:T(8,128)(2,1)}, bf16[1,36,160,128]{3,2,1,0:T(8,128)(2,1)}, u32[]{:S(2)}, u32[]{:S(2)}) collective-permute-start(bf16[1,36,160,128]{3,2,1,0:T(8,128)(2,1)} %get-tuple-element.13), channel_id=1, source_target_pairs={{0,4},{4,8},{8,12},{1,5},{5,9},{9,13},{2,6},{6,10},{10,14},{3,7},{... | collective-permute-start | bytes 4423688 | tf_op jit(solution)/shard_map/ppermute | solution.py:138
  151.2 38.2 %collective-permute-start.7 = (bf16[1,36,160,128]{3,2,1,0:T(8,128)(2,1)}, bf16[1,36,160,128]{3,2,1,0:T(8,128)(2,1)}, u32[]{:S(2)}, u32[]{:S(2)}) collective-permute-start(bf16[1,36,160,128]{3,2,1,0:T(8,128)(2,1)} %get-tuple-element.14), channel_id=1, source_target_pairs={{4,0},{8,4},{12,8},{5,1},{9,5},{13,9},{6,2},{10,6},{14,10},{7,3},{... | collective-permute-start | bytes 4423688 | tf_op jit(solution)/shard_map/ppermute | solution.py:139
  195.6 9.7 %collective-permute-start.8 = (bf16[4,36,160,128]{3,2,1,0:T(8,128)(2,1)S(1)}, bf16[4,36,160,128]{3,2,1,0:T(8,128)(2,1)S(1)}, u32[]{:S(2)}, u32[]{:S(2)}) collective-permute-start(bf16[4,36,160,128]{3,2,1,0:T(8,128)(2,1)S(1)} %fusion.26), channel_id=1, source_target_pairs={{0,1},{1,0},{2,3},{3,2},{4,5},{5,4},{6,7},{7,6},{8,9},{9,8},{10,11... | collective-permute-start | bytes 17694728 | tf_op jit(solution)/shard_map/ppermute | solution.py:14
  216.5 3.6 %copy-start.14 = (f32[160]{0:T(256)S(1)}, f32[160]{0:T(256)}, u32[]{:S(2)}) copy-start(f32[160]{0:T(256)} %param.17) | copy-start | bytes 1924

commit v3 on v2

--- a/solution.py
+++ b/solution.py
@@ -71,10 +71,10 @@
     return jax.nn.silu(scaled * gain[:, None] + bias[:, None]).astype(jnp.bfloat16)
 
 
-def both_halves(own, other, chan_index):
-    first = jnp.where(chan_index == 0, own, other)
-    second = jnp.where(chan_index == 0, other, own)
-    return jnp.concatenate([first, second], axis=2)
+def own_first(weight, own_start, other_start, size):
+    own = lax.dynamic_slice_in_dim(weight, own_start, size, axis=1)
+    other = lax.dynamic_slice_in_dim(weight, other_start, size, axis=1)
+    return jnp.concatenate([own, other], axis=1)
 
 
 def spatial_taps(running, channel_slab, weight, rows, width):
@@ -114,12 +114,15 @@
     tm_index = lax.axis_index("tm")
     tm_count = lax.axis_size("tm")
 
-    piece = spatial_weight.shape[2]
-    merged = jnp.concatenate([spatial_weight.reshape(9, piece, local_chan), temporal_weight], axis=0)
-    gathered = gather_tm(merged)
-    full_weight = jnp.moveaxis(gathered, 0, 1).reshape(12, tm_count * piece, local_chan)
-    spatial_full = full_weight[:9].reshape(3, 3, C, local_chan)
-    temporal_full = full_weight[9:]
+    spatial_full = lax.all_gather(spatial_weight, "tm", axis=2, tiled=True).reshape(9, C, local_chan)
+    temporal_pieces = gather_tm(temporal_weight)
+    temporal_full = jnp.moveaxis(temporal_pieces, 0, 1).reshape(3, C, local_chan)
+    own_start = chan_index * local_chan
+    other_start = (1 - chan_index) * local_chan
+    spatial_full = own_first(spatial_full, own_start, other_start, local_chan).reshape(
+        3, 3, C, local_chan
+    )
+    temporal_full = own_first(temporal_full, own_start, other_start, local_chan)
 
     values = video.astype(jnp.float32)
     grouped = values.reshape(frames, rows, local_groups, group_size, width)
@@ -127,7 +130,7 @@
     act_one = group_act(values, average, variance, norm1_gain, norm1_bias)
 
     with_rows = row_halo(act_one)
-    all_rows = both_halves(with_rows, swap_chan(with_rows), chan_index)
+    all_rows = jnp.concatenate([with_rows, swap_chan(with_rows)], axis=2)
     padded = jnp.pad(all_rows, ((0, 0), (0, 0), (0, 0), (1, 1)))
     empty = jnp.zeros((frames, rows, local_chan, width), jnp.float32)
     spatial_sum = spatial_taps(empty, padded, spatial_full, rows, width)
@@ -149,7 +152,7 @@
     inside = inside & ((frame_ids < frames + 1) | (tm_index < tm_count - 1))
     act_two = jnp.where(inside[:, None, None, None], act_two, jnp.zeros_like(act_two))
 
-    all_two = both_halves(act_two, swap_chan(act_two), chan_index)
+    all_two = jnp.concatenate([act_two, swap_chan(act_two)], axis=2)
     temporal_sum = temporal_taps(empty, all_two, temporal_full, frames)
     return (hidden_values + temporal_sum + temporal_bias[:, None]).astype(jnp.bfloat16)
 

time: 227 us -> 210 us (0.925)
  waiting for transfers between devices: 53.5 us -> 15.3 us
  blocking collectives: 40.6 us -> 70 us
  other arithmetic: 31.8 us -> 24.6 us
  local copies, waits for them, and re-layouts: 20.9 us -> 18.3 us
    ppermute x3, waiting for transfers between devices: 39.9 us -> 10.2 us  [gather_tm(): pieces.append(lax.ppermute(piece, 'tm', pairs))]
    all_gather x0 -> x1, blocking collectives: none -> 29 us  [body(): lax.all_gather(spatial_weight, 'tm', axis=2, tiled=True)]
    select_n x2 -> x0, other arithmetic: 9.9 us -> none  [both_halves(): second = jnp.where(chan_index == 0, other, own)]
    ppermute x2, waiting for transfers between devices: 8.47 us -> 0.01 us  [swap_chan(): return lax.ppermute(block, 'chan', [(0, 1), (1, 0)])]
    slice x3 -> x0, local copies, waits for them, and re-layouts: 5.99 us -> none  [the longest x2 4.87 us: body(): spatial_full = full_weight[:9].reshape(3, 3, C, local_chan)]
    unnamed x39 -> x35, local copies, waits for them, and re-layouts: 5.44 us -> 9.4 us
    concatenate x2, other arithmetic: 2.97 us -> 5.88 us  [the longest x1 4.12 us: body(): all_rows = jnp.concatenate([with_rows, swap_chan(with_rows)], axis=2)]
  transfers between devices with their start and end apart: 9 -> 9, of which waited for: 5 -> 4; matrix products, arithmetic and copies ran while one was open for 9% -> 9% of each run, Pallas kernels for 0% -> 0%
where the time goes in v3:
time: 210 us; the launch traced here: 209 us
  blocking collectives  70 us (33%)
  matrix products  65.5 us (31%)
  other arithmetic  24.6 us (12%)
  local copies, waits for them, and re-layouts  18.3 us (9%)
  waiting for transfers between devices  15.3 us (7%)
  starting transfers between devices  15 us (7%)
    dot_general x9, matrix products, spatial_taps(): jnp.einsum('frcw,co->frow', window, weight[row_tap, col_tap], preferred_e...  50.9 us
    psum x3, blocking collectives, group_stats(): table = lax.psum(table, name)  41.1 us
    all_gather x1, blocking collectives, body(): lax.all_gather(spatial_weight, 'tm', axis=2, tiled=True)  29 us
    dot_general x3, matrix products, temporal_taps(): jnp.einsum('frcw,co->frow', window, weight[frame_tap], preferred_element_...  14.5 us
    ppermute x3, waiting for transfers between devices, gather_tm(): pieces.append(lax.ppermute(piece, 'tm', pairs))  10.2 us
    unnamed x35, local copies, waits for them, and re-layouts  9.4 us
    select_n x1, other arithmetic, body(): jnp.where(inside[:, None, None, None], act_two, jnp.zeros_like(act_two))  7.66 us
    ppermute x1, starting transfers between devices, body(): before = lax.ppermute(hidden[-1:], 'tm', forward)  4.68 us
  transfers between devices with their start and end apart: 9, of which 4 were waited for; matrix products, arithmetic and copies ran while one was open for 9% of the time, Pallas kernels for 0%

profile of v3, /device:TPU:0, one launch (start us, length us, event | category | flops | bytes accessed | tf_op | source)
XLA Modules:
  0.0 209.1 jit_solution(13403399214884537902)
XLA Ops:
  0.0 2.5 %convert_reduce_fusion = f32[2,160]{1,0:T(2,128)S(1)} fusion(bf16[2,36,160,128]{3,2,1,0:T(8,128)(2,1)} %param.9), kind=kLoop, calls=%fused_computation.14 | loop fusion | flops 2948800 | bytes 2950400 | tf_op jit(solution)/shard_map/reduce_sum | solution.py:41
  2.5 0.1 reduce_sum.101
  2.5 0.1 reduce_sum.120
  2.7 0.1 sub.77
  2.8 2.7 %fusion.5 = f32[2,160]{1,0:T(2,128)S(1)} fusion(bf16[2,36,160,128]{3,2,1,0:T(8,128)(2,1)} %param.9, f32[2,160]{1,0:T(2,128)S(1)} %sub.77), kind=kLoop, calls=%fused_computation.24 | loop fusion | flops 5897920 | bytes 2951680 | tf_op jit(solution)/shard_map/reduce_sum | solution.py:43
  5.6 0.1 reduce_sum.122
  5.7 0.1 reduce_sum.123
  5.8 5.9 %psum.21 = f32[2,2,2,16]{3,2,0,1:T(2,128)S(1)} all-reduce(f32[2,2,2,16]{3,2,0,1:T(2,128)S(1)} %fusion.51), channel_id=1, replica_groups=mesh['groups'=2,'tm'=4,'height'=2,'chan'=2] {'height'}, use_global_device_ids=true, to_apply=%region_4.5 | all-reduce | flops 128 | bytes 1024 | tf_op jit(solution)/shard_map/psum | solution.py:54
  11.7 0.1 mul.93
  11.9 0.1 sub.81
  12.1 2.3 %fusion.14 = bf16[2,36,160,128]{3,2,1,0:T(8,128)(2,1)S(1)} fusion(bf16[2,36,160,128]{3,2,1,0:T(8,128)(2,1)S(1)} %copy-done, f32[160]{0:T(256)S(1)} %copy-done.9, f32[160]{0:T(256)S(1)} %copy-done.10, f32[2,160]{1,0:T(2,128)S(1)} %mul.93, f32[2,160]{1,0:T(2,128)S(1)} %sub.81), kind=kLoop, calls=%fused_computation.33 | loop fusion | flops 14745600 | bytes 5902080 | tf_op jit(solution)/shard_map/convert_element_type | solution.py:71
  14.4 4.0 %collective-permute-start = (bf16[2,1,160,128]{3,2,1,0:T(8,128)(2,1)S(1)}, bf16[2,1,160,128]{3,2,1,0:T(8,128)(2,1)S(1)}, u32[]{:S(2)}, u32[]{:S(2)}) collective-permute-start(bf16[2,1,160,128]{3,2,1,0:T(8,128)(2,1)S(1)} %get-tuple-element.11), channel_id=1, source_target_pairs={{0,2},{1,3},{4,6},{5,7},{8,10},{9,11},{12,14},{13,15},{16,18},{17,... | collective-permute-start | bytes 245768 | tf_op jit(solution)/shard_map/ppermute | solution.py:21
  18.4 1.3 collective-permute-start.1
  19.7 0.7 collective-permute-done
  20.4 4.3 %collective-permute-done.1 = bf16[2,1,160,128]{3,2,1,0:T(8,128)(2,1)S(1)} collective-permute-done((bf16[2,1,160,128]{3,2,1,0:T(8,128)(2,1)S(1)}, bf16[2,1,160,128]{3,2,1,0:T(8,128)(2,1)S(1)}, u32[]{:S(2)}, u32[]{:S(2)}) %collective-permute-start.1) | collective-permute-done | bytes 81952 | tf_op jit(solution)/shard_map/ppermute | solution.py:22
  24.7 2.1 pad_maximum_fusion.3
  26.8 29.0 %all_gather.3 = bf16[3,3,320,160]{3,2,1,0:T(8,128)(2,1)S(1)} all-gather(bf16[3,3,80,160]{3,2,1,0:T(8,128)(2,1)S(1)} %copy-done.6), channel_id=1, replica_groups=mesh['groups'=2,'tm'=4,'height'=2,'chan'=2] {'tm'}, dimensions={2}, use_global_device_ids=true | all-gather | bytes 1152000 | tf_op jit(solution)/shard_map/all_gather | solution.py:117
  55.8 1.3 constant_dynamic-slice_fusion.3
  57.0 2.4 %copy.37 = bf16[9,160,160]{1,2,0:T(8,128)(2,1)} copy(bf16[9,160,160]{2,1,0:T(8,128)(2,1)} %get-tuple-element.13) | data formatting | bytes 921600
  59.4 2.4 %copy.38 = bf16[9,160,160]{1,2,0:T(8,128)(2,1)} copy(bf16[9,160,160]{2,1,0:T(8,128)(2,1)} %get-tuple-element.14) | data formatting | bytes 921600
  61.8 1.8 pad_maximum_fusion.4
  63.5 4.1 %pad_maximum_fusion = bf16[2,38,320,128]{3,2,1,0:T(8,128)(2,1)S(1)} fusion(bf16[2,38,160,128]{3,2,1,0:T(8,128)(2,1)} %collective-permute-done.2, bf16[2,1,160,128]{3,2,1,0:T(8,128)(2,1)S(1)} %collective-permute-done.1, bf16[2,36,160,128]{3,2,1,0:T(8,128)(2,1)S(1)} %copy-done.3, bf16[2,1,160,128]{3,2,1,0:T(8,128)(2,1)S(1)} %collective-permute-done), kind=kLoop, calls=%fused_computation.18 | loop fusion | flops 24903680 | bytes 12451840 | tf_op jit(solution)/shard_map/concatenate | solution.py:133
  67.7 4.3 %fusion.24 = f32[160,2,36,128]{3,0,2,1:T(8,128)} fusion(bf16[2,38,320,128]{3,2,1,0:T(8,128)(2,1)S(1)} %pad_maximum_fusion, bf16[3,3,320,160]{2,3,1,0:T(8,128)(2,1)S(1)} %bitcast.140), kind=kOutput, calls=%fused_computation.41 | convolution fusion | flops 943718400 | bytes 12247040 | tf_op jit(solution)/shard_map/frcw,co->frow/dot_general | solution.py:84
  72.0 4.3 %fusion.25 = f32[160,2,36,128]{3,0,2,1:T(8,128)} fusion(bf16[2,38,320,128]{3,2,1,0:T(8,128)(2,1)S(1)} %pad_maximum_fusion, bf16[3,3,320,160]{2,3,1,0:T(8,128)(2,1)S(1)} %bitcast.141), kind=kOutput, calls=%fused_computation.42 | convolution fusion | flops 943718400 | bytes 12247040 | tf_op jit(solution)/shard_map/frcw,co->frow/dot_general | solution.py:84
  76.3 4.3 %fusion.26 = f32[160,2,36,128]{3,0,2,1:T(8,128)} fusion(bf16[2,38,320,128]{3,2,1,0:T(8,128)(2,1)S(1)} %pad_maximum_fusion, bf16[3,3,320,160]{2,3,1,0:T(8,128)(2,1)S(1)} %bitcast.142), kind=kOutput, calls=%fused_computation.43 | convolution fusion | flops 943718400 | bytes 12247040 | tf_op jit(solution)/shard_map/frcw,co->frow/dot_general | solution.py:84
  80.6 4.3 %fusion.27 = f32[160,2,36,128]{3,0,2,1:T(8,128)} fusion(bf16[2,38,320,128]{3,2,1,0:T(8,128)(2,1)S(1)} %pad_maximum_fusion, bf16[3,3,320,160]{2,3,1,0:T(8,128)(2,1)S(1)} %bitcast.143), kind=kOutput, calls=%fused_computation.44 | convolution fusion | flops 943718400 | bytes 12247040 | tf_op jit(solution)/shard_map/frcw,co->frow/dot_general | solution.py:84
  84.9 4.4 %fusion.28 = f32[160,2,36,128]{3,0,2,1:T(8,128)} fusion(bf16[2,38,320,128]{3,2,1,0:T(8,128)(2,1)S(1)} %pad_maximum_fusion, bf16[3,3,320,160]{2,3,1,0:T(8,128)(2,1)S(1)} %bitcast.144), kind=kOutput, calls=%fused_computation.45 | convolution fusion | flops 943718400 | bytes 12247040 | tf_op jit(solution)/shard_map/frcw,co->frow/dot_general | solution.py:84
  89.3 4.2 %fusion.34 = f32[160,2,36,128]{3,0,2,1:T(8,128)} fusion(bf16[2,38,320,128]{3,2,1,0:T(8,128)(2,1)S(1)} %pad_maximum_fusion, bf16[3,3,320,160]{2,3,1,0:T(8,128)(2,1)S(1)} %bitcast.145), kind=kOutput, calls=%fused_computation.52 | convolution fusion | flops 943718400 | bytes 11919360 | tf_op jit(solution)/shard_map/frcw,co->frow/dot_general | solution.py:84
  93.5 4.2 %fusion.36 = f32[160,2,36,128]{3,0,2,1:T(8,128)} fusion(bf16[2,38,320,128]{3,2,1,0:T(8,128)(2,1)S(1)} %pad_maximum_fusion, bf16[3,3,320,160]{2,3,1,0:T(8,128)(2,1)S(1)} %bitcast.146), kind=kOutput, calls=%fused_computation.54 | convolution fusion | flops 943718400 | bytes 11919360 | tf_op jit(solution)/shard_map/frcw,co->frow/dot_general | solution.py:84
  97.7 4.4 %fusion.32 = f32[160,2,36,128]{3,0,2,1:T(8,128)} fusion(bf16[2,38,320,128]{3,2,1,0:T(8,128)(2,1)S(1)} %pad_maximum_fusion, bf16[3,3,320,160]{2,3,1,0:T(8,128)(2,1)S(1)} %bitcast.147), kind=kOutput, calls=%fused_computation.50 | convolution fusion | flops 943718400 | bytes 11919360 | tf_op jit(solution)/shard_map/frcw,co->frow/dot_general | solution.py:84
  102.2 16.5 %convert_reduce_fusion.1 = (f32[160]{0:T(256)S(1)}, bf16[2,36,160,128]{3,2,1,0:T(8,128)(2,1)S(1)}) fusion(f32[160]{0:T(256)S(1)} %copy-done.7, bf16[2,38,320,128]{3,2,1,0:T(8,128)(2,1)S(1)} %pad_maximum_fusion, bf16[3,3,320,160]{2,3,1,0:T(8,128)(2,1)} %bitcast.148, f32[160,2,36,128]{3,0,2,1:T(8,128)} %fusion.32, f32[160,2,36,128]{3,0,2,1:T(8,128)} %fusion.28, ...), kind=kOutput, calls=%fused_computation.17 | convolution fusion | flops 964362112 | bytes 59434240 | tf_op jit(solution)/shard_map/frcw,co->frow/dot_general | solution.py:84
  118.7 1.8 fusion.65
  120.5 4.7 %collective-permute-start.6 = (bf16[1,36,160,128]{3,2,1,0:T(8,128)(2,1)}, bf16[1,36,160,128]{3,2,1,0:T(8,128)(2,1)}, u32[]{:S(2)}, u32[]{:S(2)}) collective-permute-start(bf16[1,36,160,128]{3,2,1,0:T(8,128)(2,1)} %get-tuple-element.9), channel_id=1, source_target_pairs={{0,4},{4,8},{8,12},{1,5},{5,9},{9,13},{2,6},{6,10},{10,14},{3,7},{... | collective-permute-start | bytes 4423688 | tf_op jit(solution)/shard_map/ppermute | solution.py:141
  125.1 1.3 collective-permute-start.7
  126.5 0.1 reduce_sum.128
  126.5 0.1 reduce_sum.129
  126.7 0.1 sub.88
  126.8 0.9 fusion.1
  127.8 0.1 reduce_sum.131
  127.9 0.1 reduce_sum.132
  128.1 5.0 %psum.22 = f32[8,2,16]{2,0,1:T(8,128)S(1)} all-reduce(f32[8,2,16]{2,0,1:T(8,128)S(1)} %dynamic_update_slice.9), channel_id=1, replica_groups=mesh['groups'=2,'tm'=4,'height'=2,'chan'=2] {'height'}, use_global_device_ids=true, to_apply=%region_12.13 | all-reduce | flops 256 | bytes 2048 | tf_op jit(solution)/shard_map/psum | solution.py:54
  133.1 30.2 %psum.23 = f32[8,2,16]{2,0,1:T(8,128)S(1)} all-reduce(f32[8,2,16]{2,0,1:T(8,128)S(1)} %psum.22), channel_id=1, replica_groups=mesh['groups'=2,'tm'=4,'height'=2,'chan'=2] {'tm'}, use_global_device_ids=true, to_apply=%region_13.14 | all-reduce | flops 256 | bytes 2048 | tf_op jit(solution)/shard_map/psum | solution.py:54
  163.4 0.1 mul.104
  163.6 0.1 sub.92
  163.7 7.7 %fusion.17 = bf16[4,36,160,128]{3,2,1,0:T(8,128)(2,1)} fusion(bf16[1,36,160,128]{3,2,1,0:T(8,128)(2,1)} %collective-permute-done.7, bf16[2,36,160,128]{3,2,1,0:T(8,128)(2,1)S(1)} %get-tuple-element.22, bf16[1,36,160,128]{3,2,1,0:T(8,128)(2,1)} %collective-permute-done.6, f32[160]{0:T(256)S(1)} %copy-done.11, f32[160]{0:T(256)S(1)} %copy-done.12, ...), kind=kLoop, calls=%fused_computation.36 | loop fusion | flops 38338560 | bytes 11799044 | tf_op jit(solution)/shard_map/jit(_where)/select_n | solution.py:153
  171.4 2.4 %collective-permute-start.3 = (bf16[3,80,160]{2,1,0:T(8,128)(2,1)S(1)}, bf16[3,80,160]{2,1,0:T(8,128)(2,1)S(1)}, u32[]{:S(2)}, u32[]{:S(2)}) collective-permute-start(bf16[3,80,160]{2,1,0:T(8,128)(2,1)S(1)} %copy-done.5), channel_id=1, source_target_pairs={{0,12},{4,0},{8,4},{12,8},{1,13},{5,1},{9,5},{13,9},{2,14},{6,2},{... | collective-permute-start | bytes 230408 | tf_op jit(solution)/shard_map/ppermute | solution.py:32
  173.8 1.4 collective-permute-start.4
  175.2 0.7 bitcast_dynamic-update-slice_fusion.6
  175.9 1.8 collective-permute-done.3
  177.7 0.7 bitcast_dynamic-update-slice_fusion.4
  178.3 8.4 %collective-permute-done.4 = bf16[3,80,160]{2,1,0:T(8,128)(2,1)S(1)} collective-permute-done((bf16[3,80,160]{2,1,0:T(8,128)(2,1)S(1)}, bf16[3,80,160]{2,1,0:T(8,128)(2,1)S(1)}, u32[]{:S(2)}, u32[]{:S(2)}) %collective-permute-start.4) | collective-permute-done | bytes 76832 | tf_op jit(solution)/shard_map/ppermute | solution.py:32
  186.8 0.7 bitcast_dynamic-update-slice_fusion.2
  187.4 0.7 bitcast_dynamic-update-slice_fusion
  188.1 0.7 bitcast_dynamic-update-slice_fusion.7
  188.7 0.7 bitcast_dynamic-update-slice_fusion.5
  189.4 0.7 bitcast_dynamic-update-slice_fusion.3
  190.0 0.7 bitcast_dynamic-update-slice_fusion.1
  190.7 1.1 dynamic-slice_bitcast_fusion
  191.8 1.1 copy.23
  192.8 1.4 reshape.113
  194.2 0.2 constant_dynamic-slice_fusion
  194.5 3.8 %fusion.19 = f32[160,2,36,128]{3,0,2,1:T(8,128)S(1)} fusion(bf16[4,36,160,128]{3,2,1,0:T(8,128)(2,1)} %fusion.17, bf16[4,36,160,128]{3,2,1,0:T(8,128)(2,1)} %collective-permute-done.8, bf16[3,160,160]{1,2,0:T(8,128)(2,1)S(1)} %get-tuple-element.16, bf16[3,160,160]{1,2,0:T(8,128)(2,1)S(1)} %get-tuple-element.15), kind=kOutput, calls=%fused_computation.38 | convolution fusion | flops 955719680 | bytes 18001920 | tf_op jit(solution)/shard_map/frcw,co->frow/dot_general | solution.py:93
  198.3 3.8 %fusion.22 = f32[160,2,36,128]{3,0,2,1:T(8,128)S(1)} fusion(bf16[4,36,160,128]{3,2,1,0:T(8,128)(2,1)} %fusion.17, bf16[4,36,160,128]{3,2,1,0:T(8,128)(2,1)} %collective-permute-done.8, bf16[3,160,160]{1,2,0:T(8,128)(2,1)S(1)} %get-tuple-element.16, bf16[3,160,160]{1,2,0:T(8,128)(2,1)S(1)} %get-tuple-element.15), kind=kOutput, calls=%fused_computation.40 | convolution fusion | flops 955719680 | bytes 18001920 | tf_op jit(solution)/shard_map/frcw,co->frow/dot_general | solution.py:93
  202.2 6.9 %fusion.3 = bf16[2,36,160,128]{3,2,1,0:T(8,128)(2,1)} fusion(bf16[2,36,160,128]{3,2,1,0:T(8,128)(2,1)S(1)} %get-tuple-element.22, f32[160,2,36,128]{3,0,2,1:T(8,128)S(1)} %fusion.22, f32[160,2,36,128]{3,0,2,1:T(8,128)S(1)} %fusion.19, f32[160]{0:T(256)S(1)} %copy-done.8, bf16[4,36,160,128]{3,2,1,0:T(8,128)(2,1)} %collective-permute-done.8, ...), kind=kOutput, calls=%fused_computation.22 | convolution fusion | flops 964567040 | bytes 29799040 | tf_op jit(solution)/shard_map/frcw,co->frow/dot_general | solution.py:93
  (57 shorter events, 0.7 us)
Async XLA Ops:
  0.0 12.0 %copy-start = (bf16[2,36,160,128]{3,2,1,0:T(8,128)(2,1)S(1)}, bf16[2,36,160,128]{3,2,1,0:T(8,128)(2,1)}, u32[]{:S(2)}) copy-start(bf16[2,36,160,128]{3,2,1,0:T(8,128)(2,1)} %param.9) | copy-start | bytes 8847364
  0.0 12.0 %copy-start.10 = (f32[160]{0:T(256)S(1)}, f32[160]{0:T(256)}, u32[]{:S(2)}) copy-start(f32[160]{0:T(256)} %param.10) | copy-start | bytes 1924
  0.0 12.0 %copy-start.9 = (f32[160]{0:T(256)S(1)}, f32[160]{0:T(256)}, u32[]{:S(2)}) copy-start(f32[160]{0:T(256)} %param.11) | copy-start | bytes 1924
  12.0 14.7 %copy-start.6 = (bf16[3,3,80,160]{3,2,1,0:T(8,128)(2,1)S(1)}, bf16[3,3,80,160]{3,2,1,0:T(8,128)(2,1)}, u32[]{:S(2)}) copy-start(bf16[3,3,80,160]{3,2,1,0:T(8,128)(2,1)} %param.12) | copy-start | bytes 691204
  14.4 10.3 %copy-start.2 = (bf16[2,36,160,128]{3,2,1,0:T(8,128)(2,1)}, bf16[2,36,160,128]{3,2,1,0:T(8,128)(2,1)S(1)}, u32[]{:S(2)}) copy-start(bf16[2,36,160,128]{3,2,1,0:T(8,128)(2,1)S(1)} %fusion.14) | copy-start | bytes 8847364
  14.4 6.0 %collective-permute-start = (bf16[2,1,160,128]{3,2,1,0:T(8,128)(2,1)S(1)}, bf16[2,1,160,128]{3,2,1,0:T(8,128)(2,1)S(1)}, u32[]{:S(2)}, u32[]{:S(2)}) collective-permute-start(bf16[2,1,160,128]{3,2,1,0:T(8,128)(2,1)S(1)} %get-tuple-element.11), channel_id=1, source_target_pairs={{0,2},{1,3},{4,6},{5,7},{8,10},{9,11},{12,14},{13,15},{16,18},{17,... | collective-permute-start | bytes 245768 | tf_op jit(solution)/shard_map/ppermute | solution.py:21
  18.4 6.3 %collective-permute-start.1 = (bf16[2,1,160,128]{3,2,1,0:T(8,128)(2,1)S(1)}, bf16[2,1,160,128]{3,2,1,0:T(8,128)(2,1)S(1)}, u32[]{:S(2)}, u32[]{:S(2)}) collective-permute-start(bf16[2,1,160,128]{3,2,1,0:T(8,128)(2,1)S(1)} %get-tuple-element.12), channel_id=1, source_target_pairs={{2,0},{3,1},{6,4},{7,5},{10,8},{11,9},{14,12},{15,13},{18,16},{19,... | collective-permute-start | bytes 245768 | tf_op jit(solution)/shard_map/ppermute | solution.py:22
  26.8 36.8 %copy-start.3 = (bf16[2,36,160,128]{3,2,1,0:T(8,128)(2,1)S(1)}, bf16[2,36,160,128]{3,2,1,0:T(8,128)(2,1)}, u32[]{:S(2)}) copy-start(bf16[2,36,160,128]{3,2,1,0:T(8,128)(2,1)} %copy-done.2) | copy-start | bytes 8847364
  26.8 36.8 %collective-permute-start.2 = (bf16[2,38,160,128]{3,2,1,0:T(8,128)(2,1)}, bf16[2,38,160,128]{3,2,1,0:T(8,128)(2,1)}, u32[]{:S(2)}, u32[]{:S(2)}) collective-permute-start(bf16[2,38,160,128]{3,2,1,0:T(8,128)(2,1)} %pad_maximum_fusion.3), channel_id=1, source_target_pairs={{0,1},{1,0},{2,3},{3,2},{4,5},{5,4},{6,7},{7,6},{8,9},{9,8},{10,11... | collective-permute-start | bytes 9338888 | tf_op jit(solution)/shard_map/ppermute | solution.py:14
  63.5 34.2 %copy-start.4 = (bf16[9,320,160]{1,2,0:T(8,128)(2,1)}, bf16[9,320,160]{1,2,0:T(8,128)(2,1)S(1)}, u32[]{:S(2)}) copy-start(bf16[9,320,160]{1,2,0:T(8,128)(2,1)S(1)} %pad_maximum_fusion.4) | copy-start | bytes 2764804
  97.7 4.5 %copy-start.1 = (bf16[2,36,160,128]{3,2,1,0:T(8,128)(2,1)S(1)}, bf16[2,36,160,128]{3,2,1,0:T(8,128)(2,1)}, u32[]{:S(2)}) copy-start(bf16[2,36,160,128]{3,2,1,0:T(8,128)(2,1)} %param.9) | copy-start | bytes 8847364
  97.7 4.5 %copy-start.7 = (f32[160]{0:T(256)S(1)}, f32[160]{0:T(256)}, u32[]{:S(2)}) copy-start(f32[160]{0:T(256)} %param.13) | copy-start | bytes 1924
  118.6 45.1 %copy-start.11 = (f32[160]{0:T(256)S(1)}, f32[160]{0:T(256)}, u32[]{:S(2)}) copy-start(f32[160]{0:T(256)} %param.15) | copy-start | bytes 1924
  118.6 45.1 %copy-start.12 = (f32[160]{0:T(256)S(1)}, f32[160]{0:T(256)}, u32[]{:S(2)}) copy-start(f32[160]{0:T(256)} %param.14) | copy-start | bytes 1924
  120.5 43.2 %collective-permute-start.6 = (bf16[1,36,160,128]{3,2,1,0:T(8,128)(2,1)}, bf16[1,36,160,128]{3,2,1,0:T(8,128)(2,1)}, u32[]{:S(2)}, u32[]{:S(2)}) collective-permute-start(bf16[1,36,160,128]{3,2,1,0:T(8,128)(2,1)} %get-tuple-element.9), channel_id=1, source_target_pairs={{0,4},{4,8},{8,12},{1,5},{5,9},{9,13},{2,6},{6,10},{10,14},{3,7},{... | collective-permute-start | bytes 4423688 | tf_op jit(solution)/shard_map/ppermute | solution.py:141
  125.1 38.5 %collective-permute-start.7 = (bf16[1,36,160,128]{3,2,1,0:T(8,128)(2,1)}, bf16[1,36,160,128]{3,2,1,0:T(8,128)(2,1)}, u32[]{:S(2)}, u32[]{:S(2)}) collective-permute-start(bf16[1,36,160,128]{3,2,1,0:T(8,128)(2,1)} %get-tuple-element.10), channel_id=1, source_target_pairs={{4,0},{8,4},{12,8},{5,1},{9,5},{13,9},{6,2},{10,6},{14,10},{7,3},{... | collective-permute-start | bytes 4423688 | tf_op jit(solution)/shard_map/ppermute | solution.py:142
  163.7 7.7 %copy-start.5 = (bf16[3,80,160]{2,1,0:T(8,128)(2,1)S(1)}, bf16[3,80,160]{2,1,0:T(8,128)(2,1)}, u32[]{:S(2)}) copy-start(bf16[3,80,160]{2,1,0:T(8,128)(2,1)} %param.16) | copy-start | bytes 230404
  171.4 23.1 %collective-permute-start.8 = (bf16[4,36,160,128]{3,2,1,0:T(8,128)(2,1)}, bf16[4,36,160,128]{3,2,1,0:T(8,128)(2,1)}, u32[]{:S(2)}, u32[]{:S(2)}) collective-permute-start(bf16[4,36,160,128]{3,2,1,0:T(8,128)(2,1)} %fusion.17), channel_id=1, source_target_pairs={{0,1},{1,0},{2,3},{3,2},{4,5},{5,4},{6,7},{7,6},{8,9},{9,8},{10,11... | collective-permute-start | bytes 17694728 | tf_op jit(solution)/shard_map/ppermute | solution.py:14
  171.4 6.3 %collective-permute-start.3 = (bf16[3,80,160]{2,1,0:T(8,128)(2,1)S(1)}, bf16[3,80,160]{2,1,0:T(8,128)(2,1)S(1)}, u32[]{:S(2)}, u32[]{:S(2)}) collective-permute-start(bf16[3,80,160]{2,1,0:T(8,128)(2,1)S(1)} %copy-done.5), channel_id=1, source_target_pairs={{0,12},{4,0},{8,4},{12,8},{1,13},{5,1},{9,5},{13,9},{2,14},{6,2},{... | collective-permute-start | bytes 230408 | tf_op jit(solution)/shard_map/ppermute | solution.py:32
  173.8 12.9 %collective-permute-start.4 = (bf16[3,80,160]{2,1,0:T(8,128)(2,1)S(1)}, bf16[3,80,160]{2,1,0:T(8,128)(2,1)S(1)}, u32[]{:S(2)}, u32[]{:S(2)}) collective-permute-start(bf16[3,80,160]{2,1,0:T(8,128)(2,1)S(1)} %copy-done.5), channel_id=1, source_target_pairs={{0,8},{4,12},{8,0},{12,4},{1,9},{5,13},{9,1},{13,5},{2,10},{6,14},... | collective-permute-start | bytes 230408 | tf_op jit(solution)/shard_map/ppermute | solution.py:32
  175.2 12.2 %collective-permute-start.5 = (bf16[3,80,160]{2,1,0:T(8,128)(2,1)S(1)}, bf16[3,80,160]{2,1,0:T(8,128)(2,1)S(1)}, u32[]{:S(2)}, u32[]{:S(2)}) collective-permute-start(bf16[3,80,160]{2,1,0:T(8,128)(2,1)S(1)} %copy-done.5), channel_id=1, source_target_pairs={{0,4},{4,8},{8,12},{12,0},{1,5},{5,9},{9,13},{13,1},{2,6},{6,10},{... | collective-permute-start | bytes 230408 | tf_op jit(solution)/shard_map/ppermute | solution.py:32
  198.3 3.8 %copy-start.8 = (f32[160]{0:T(256)S(1)}, f32[160]{0:T(256)}, u32[]{:S(2)}) copy-start(f32[160]{0:T(256)} %param.17) | copy-start | bytes 1924

commit v4 on v3

--- a/solution.py
+++ b/solution.py
@@ -1,6 +1,8 @@
 import jax
 import jax.numpy as jnp
 from jax import lax
+from jax.experimental import pallas as pl
+from jax.experimental.pallas import tpu as pltpu
 from jax.sharding import PartitionSpec as P
 
 C = 320
@@ -71,10 +73,97 @@
     return jax.nn.silu(scaled * gain[:, None] + bias[:, None]).astype(jnp.bfloat16)
 
 
-def own_first(weight, own_start, other_start, size):
-    own = lax.dynamic_slice_in_dim(weight, own_start, size, axis=1)
-    other = lax.dynamic_slice_in_dim(weight, other_start, size, axis=1)
-    return jnp.concatenate([own, other], axis=1)
+def in_order(own, other, chan_index):
+    size = own.shape[2]
+    joined = jnp.zeros(own.shape[:2] + (2 * size,) + own.shape[3:], own.dtype)
+    joined = lax.dynamic_update_slice_in_dim(joined, own, chan_index * size, axis=2)
+    return lax.dynamic_update_slice_in_dim(joined, other, (1 - chan_index) * size, axis=2)
+
+
+def spatial_kernel(x_ref, w_ref, res_ref, b_ref, o_ref):
+    rows, local_chan, width = o_ref.shape[1], o_ref.shape[2], o_ref.shape[3]
+    lane = lax.broadcasted_iota(jnp.int32, (local_chan, width), 1)
+    bias = b_ref[...]
+
+    def one_row(r, carry):
+        y = jnp.dot(w_ref[0], x_ref[0, r], preferred_element_type=jnp.float32)
+        y = y + jnp.dot(w_ref[1], x_ref[0, r + 1], preferred_element_type=jnp.float32)
+        y = y + jnp.dot(w_ref[2], x_ref[0, r + 2], preferred_element_type=jnp.float32)
+        left = pltpu.roll(y[:local_chan], 1, 1)
+        left = jnp.where(lane == 0, 0.0, left)
+        right = pltpu.roll(y[2 * local_chan :], width - 1, 1)
+        right = jnp.where(lane == width - 1, 0.0, right)
+        total = left + y[local_chan : 2 * local_chan] + right
+        o_ref[0, r] = (res_ref[0, r].astype(jnp.float32) + total + bias).astype(o_ref.dtype)
+        return carry
+
+    lax.fori_loop(0, rows, one_row, 0)
+
+
+def spatial_call(inputs, weight, residual, bias):
+    frames, rows, local_chan, width = residual.shape
+    chans = inputs.shape[2]
+    return pl.pallas_call(
+        spatial_kernel,
+        out_shape=jax.ShapeDtypeStruct(residual.shape, jnp.bfloat16),
+        grid=(frames,),
+        in_specs=[
+            pl.BlockSpec((1, rows + 2, chans, width), lambda f: (f, 0, 0, 0)),
+            pl.BlockSpec((3, 3 * local_chan, chans), lambda f: (0, 0, 0)),
+            pl.BlockSpec((1, rows, local_chan, width), lambda f: (f, 0, 0, 0)),
+            pl.BlockSpec((local_chan, 1), lambda f: (0, 0)),
+        ],
+        out_specs=pl.BlockSpec((1, rows, local_chan, width), lambda f: (f, 0, 0, 0)),
+        compiler_params=pltpu.CompilerParams(vmem_limit_bytes=48 * 1024 * 1024),
+        cost_estimate=pl.CostEstimate(
+            flops=2 * frames * rows * width * 9 * chans * local_chan,
+            transcendentals=0,
+            bytes_accessed=inputs.size * 2 + weight.size * 2 + 4 * residual.size,
+        ),
+    )(inputs, weight, residual, bias)
+
+
+def temporal_kernel(a_ref, b_ref, c_ref, w_ref, res_ref, bias_ref, o_ref):
+    rows = o_ref.shape[1]
+    bias = bias_ref[...]
+
+    def one_row(r, carry):
+        y = jnp.dot(w_ref[0], a_ref[0, r], preferred_element_type=jnp.float32)
+        y = y + jnp.dot(w_ref[1], b_ref[0, r], preferred_element_type=jnp.float32)
+        y = y + jnp.dot(w_ref[2], c_ref[0, r], preferred_element_type=jnp.float32)
+        o_ref[0, r] = (res_ref[0, r].astype(jnp.float32) + y + bias).astype(o_ref.dtype)
+        return carry
+
+    lax.fori_loop(0, rows, one_row, 0)
+
+
+def frame_spec(tap, rows, chans, width):
+    return pl.BlockSpec((1, rows, chans, width), lambda f: (f + tap, 0, 0, 0))
+
+
+def temporal_call(inputs, weight, residual, bias):
+    frames, rows, local_chan, width = residual.shape
+    chans = inputs.shape[2]
+    return pl.pallas_call(
+        temporal_kernel,
+        out_shape=jax.ShapeDtypeStruct(residual.shape, jnp.bfloat16),
+        grid=(frames,),
+        in_specs=[
+            frame_spec(0, rows, chans, width),
+            frame_spec(1, rows, chans, width),
+            frame_spec(2, rows, chans, width),
+            pl.BlockSpec((3, local_chan, chans), lambda f: (0, 0, 0)),
+            pl.BlockSpec((1, rows, local_chan, width), lambda f: (f, 0, 0, 0)),
+            pl.BlockSpec((local_chan, 1), lambda f: (0, 0)),
+        ],
+        out_specs=pl.BlockSpec((1, rows, local_chan, width), lambda f: (f, 0, 0, 0)),
+        compiler_params=pltpu.CompilerParams(vmem_limit_bytes=48 * 1024 * 1024),
+        cost_estimate=pl.CostEstimate(
+            flops=2 * frames * rows * width * 3 * chans * local_chan,
+            transcendentals=0,
+            bytes_accessed=3 * residual.size * 4 + weight.size * 2 + 4 * residual.size,
+        ),
+    )(inputs, inputs, inputs, weight, residual, bias)
 
 
 def spatial_taps(running, channel_slab, weight, rows, width):
@@ -117,12 +206,7 @@
     spatial_full = lax.all_gather(spatial_weight, "tm", axis=2, tiled=True).reshape(9, C, local_chan)
     temporal_pieces = gather_tm(temporal_weight)
     temporal_full = jnp.moveaxis(temporal_pieces, 0, 1).reshape(3, C, local_chan)
-    own_start = chan_index * local_chan
-    other_start = (1 - chan_index) * local_chan
-    spatial_full = own_first(spatial_full, own_start, other_start, local_chan).reshape(
-        3, 3, C, local_chan
-    )
-    temporal_full = own_first(temporal_full, own_start, other_start, local_chan)
+    spatial_full = spatial_full.reshape(3, 3, C, local_chan)
 
     values = video.astype(jnp.float32)
     grouped = values.reshape(frames, rows, local_groups, group_size, width)
@@ -130,11 +214,9 @@
     act_one = group_act(values, average, variance, norm1_gain, norm1_bias)
 
     with_rows = row_halo(act_one)
-    all_rows = jnp.concatenate([with_rows, swap_chan(with_rows)], axis=2)
-    padded = jnp.pad(all_rows, ((0, 0), (0, 0), (0, 0), (1, 1)))
-    empty = jnp.zeros((frames, rows, local_chan, width), jnp.float32)
-    spatial_sum = spatial_taps(empty, padded, spatial_full, rows, width)
-    hidden = (values + spatial_sum + spatial_bias[:, None]).astype(jnp.bfloat16)
+    all_rows = in_order(with_rows, swap_chan(with_rows), chan_index)
+    spatial_rows = jnp.transpose(spatial_full, (0, 1, 3, 2)).reshape(3, 3 * local_chan, C)
+    hidden = spatial_call(all_rows, spatial_rows, video, spatial_bias[:, None])
 
     forward = [(i, i + 1) for i in range(tm_count - 1)]
     backward = [(target, source) for source, target in forward]
@@ -152,9 +234,9 @@
     inside = inside & ((frame_ids < frames + 1) | (tm_index < tm_count - 1))
     act_two = jnp.where(inside[:, None, None, None], act_two, jnp.zeros_like(act_two))
 
-    all_two = jnp.concatenate([act_two, swap_chan(act_two)], axis=2)
-    temporal_sum = temporal_taps(empty, all_two, temporal_full, frames)
-    return (hidden_values + temporal_sum + temporal_bias[:, None]).astype(jnp.bfloat16)
+    all_two = in_order(act_two, swap_chan(act_two), chan_index)
+    temporal_rows = jnp.transpose(temporal_full, (0, 2, 1))
+    return temporal_call(all_two, temporal_rows, hidden, temporal_bias[:, None])
 
 
 def solution(mesh):

time: 210 us -> 223 us (1.062)
  matrix products: 65.5 us -> 0 us
  Pallas kernels: 0 us -> 63.4 us
  local copies, waits for them, and re-layouts: 18.3 us -> 38 us
  other arithmetic: 24.6 us -> 20 us
    dot_general x12 -> x0, matrix products: 65.5 us -> none  [the longest x9 50.9 us: spatial_taps(): jnp.einsum('frcw,co->frow', window, weight[row_tap, col_tap], preferred_e...]
    pallas_call x0 -> x2, Pallas kernels: none -> 63.4 us  [the longest x1 39.3 us: spatial_call(): pl.pallas_call(spatial_kernel, out_shape=jax.ShapeDtypeStruct(residual.sh...]
    dynamic_update_slice x0 -> x2, local copies, waits for them, and re-layouts: none -> 10.7 us  [in_order(): lax.dynamic_update_slice_in_dim(joined, other, (1 - chan_index) * size, a...]
    broadcast_in_dim x0 -> x4, local copies, waits for them, and re-layouts: none -> 9.07 us  [the longest x2 8.86 us: in_order(): joined = jnp.zeros(own.shape[:2] + (2 * size,) + own.shape[3:], own.dtype)]
    dynamic_update_slice x0 -> x1, other arithmetic: none -> 8.3 us  [in_order(): lax.dynamic_update_slice_in_dim(joined, own, chan_index * size, axis=2)]
    select_n x1 -> x0, other arithmetic: 7.66 us -> none  [body(): jnp.where(inside[:, None, None, None], act_two, jnp.zeros_like(act_two))]
    concatenate x2 -> x0, other arithmetic: 5.88 us -> none  [the longest x1 4.12 us: body(): all_rows = jnp.concatenate([with_rows, swap_chan(with_rows)], axis=2)]
    unnamed x35 -> x33, local copies, waits for them, and re-layouts: 9.4 us -> 8.87 us
  transfers between devices with their start and end apart: 9 -> 9, of which waited for: 4 -> 4; matrix products, arithmetic and copies ran while one was open for 9% -> 6% of each run, Pallas kernels for 0% -> 0%
where the time goes in v4:
time: 223 us; the launch traced here: 222 us
  blocking collectives  70.3 us (32%)
  Pallas kernels  63.4 us (28%)
  local copies, waits for them, and re-layouts  38 us (17%)
  other arithmetic  20 us (9%)
  starting transfers between devices  15.2 us (7%)
  waiting for transfers between devices  15.2 us (7%)
    psum x3, blocking collectives, group_stats(): table = lax.psum(table, name)  41.4 us
    pallas_call x1, Pallas kernels, spatial_call(): pl.pallas_call(spatial_kernel, out_shape=jax.ShapeDtypeStruct(residual.sh...  39.3 us
    all_gather x1, blocking collectives, body(): lax.all_gather(spatial_weight, 'tm', axis=2, tiled=True)  28.9 us
    pallas_call x1, Pallas kernels, temporal_call(): pl.pallas_call(temporal_kernel, out_shape=jax.ShapeDtypeStruct(residual.s...  24.1 us
    dynamic_update_slice x2, local copies, waits for them, and re-layouts, in_order(): lax.dynamic_update_slice_in_dim(joined, other, (1 - chan_index) * size, a...  10.7 us
    ppermute x3, waiting for transfers between devices, gather_tm(): pieces.append(lax.ppermute(piece, 'tm', pairs))  10.1 us
    unnamed x33, local copies, waits for them, and re-layouts  8.87 us
    broadcast_in_dim x2, local copies, waits for them, and re-layouts, in_order(): joined = jnp.zeros(own.shape[:2] + (2 * size,) + own.shape[3:], own.dtype)  8.86 us
  transfers between devices with their start and end apart: 9, of which 4 were waited for; matrix products, arithmetic and copies ran while one was open for 6% of the time, Pallas kernels for 0%

profile of v4, /device:TPU:0, one launch (start us, length us, event | category | flops | bytes accessed | tf_op | source)
XLA Modules:
  0.0 222.4 jit_solution(16592672814382029632)
XLA Ops:
  0.0 2.5 %convert_reduce_fusion = f32[2,160]{1,0:T(2,128)S(1)} fusion(bf16[2,36,160,128]{3,2,1,0:T(8,128)(2,1)} %res_ref.1), kind=kLoop, calls=%fused_computation.3 | loop fusion | flops 2948800 | bytes 2950400 | tf_op jit(solution)/shard_map/reduce_sum | solution.py:43
  2.5 0.1 reduce_sum.101
  2.5 0.1 reduce_sum.120
  2.6 0.1 sub.76
  2.7 0.1 sub.77
  2.8 2.7 %fusion.3 = f32[2,160]{1,0:T(2,128)S(1)} fusion(bf16[2,36,160,128]{3,2,1,0:T(8,128)(2,1)} %res_ref.1, f32[2,160]{1,0:T(2,128)S(1)} %sub.77), kind=kLoop, calls=%fused_computation.9 | loop fusion | flops 5897920 | bytes 2951680 | tf_op jit(solution)/shard_map/reduce_sum | solution.py:45
  5.6 0.1 reduce_sum.122
  5.7 0.1 reduce_sum.123
  5.8 5.9 %psum.21 = f32[2,2,2,16]{3,2,0,1:T(2,128)S(1)} all-reduce(f32[2,2,2,16]{3,2,0,1:T(2,128)S(1)} %fusion.16), channel_id=1, replica_groups=mesh['groups'=2,'tm'=4,'height'=2,'chan'=2] {'height'}, use_global_device_ids=true, to_apply=%region_4.5 | all-reduce | flops 128 | bytes 1024 | tf_op jit(solution)/shard_map/psum | solution.py:56
  11.7 0.1 mul.92
  11.7 0.1 mul.93
  11.8 0.1 sub.80
  11.9 0.1 sub.81
  12.0 2.3 %fusion.12 = bf16[2,36,160,128]{3,2,1,0:T(8,128)(2,1)S(1)} fusion(bf16[2,36,160,128]{3,2,1,0:T(8,128)(2,1)S(1)} %copy-done.1, f32[160]{0:T(256)S(1)} %copy-done.7, f32[160]{0:T(256)S(1)} %copy-done.8, f32[2,160]{1,0:T(2,128)S(1)} %mul.93, f32[2,160]{1,0:T(2,128)S(1)} %sub.81), kind=kLoop, calls=%fused_computation.18 | loop fusion | flops 14745600 | bytes 5902080 | tf_op jit(solution)/shard_map/convert_element_type | solution.py:73
  14.4 1.6 copy-done.2
  16.0 4.2 %collective-permute-start = (bf16[2,1,160,128]{3,2,1,0:T(8,128)(2,1)S(1)}, bf16[2,1,160,128]{3,2,1,0:T(8,128)(2,1)S(1)}, u32[]{:S(2)}, u32[]{:S(2)}) collective-permute-start(bf16[2,1,160,128]{3,2,1,0:T(8,128)(2,1)S(1)} %get-tuple-element.15), channel_id=1, source_target_pairs={{0,2},{1,3},{4,6},{5,7},{8,10},{9,11},{12,14},{13,15},{16,18},{17,... | collective-permute-start | bytes 245768 | tf_op jit(solution)/shard_map/ppermute | solution.py:23
  20.2 1.3 collective-permute-start.1
  21.5 0.7 collective-permute-done
  22.3 4.3 %collective-permute-done.1 = bf16[2,1,160,128]{3,2,1,0:T(8,128)(2,1)S(1)} collective-permute-done((bf16[2,1,160,128]{3,2,1,0:T(8,128)(2,1)S(1)}, bf16[2,1,160,128]{3,2,1,0:T(8,128)(2,1)S(1)}, u32[]{:S(2)}, u32[]{:S(2)}) %collective-permute-start.1) | collective-permute-done | bytes 81952 | tf_op jit(solution)/shard_map/ppermute | solution.py:24
  26.6 1.5 broadcast_in_dim.44
  28.1 2.2 pad_maximum_fusion
  30.3 2.6 %copy-done.4 = bf16[2,38,320,128]{3,2,1,0:T(8,128)(2,1)} copy-done((bf16[2,38,320,128]{3,2,1,0:T(8,128)(2,1)}, bf16[2,38,320,128]{3,2,1,0:T(8,128)(2,1)S(1)}, u32[]{:S(2)}) %copy-start.4) | copy-done | bytes 6225944
  32.9 28.9 %all_gather.3 = bf16[3,3,320,160]{3,2,1,0:T(8,128)(2,1)S(1)} all-gather(bf16[3,3,80,160]{3,2,1,0:T(8,128)(2,1)S(1)} %copy-done.6), channel_id=1, replica_groups=mesh['groups'=2,'tm'=4,'height'=2,'chan'=2] {'tm'}, dimensions={2}, use_global_device_ids=true | all-gather | bytes 1152000 | tf_op jit(solution)/shard_map/all_gather | solution.py:206
  61.8 2.0 copy.21
  63.7 0.1 copy.22.b_ref
  63.9 4.2 %constant_dynamic-update-slice_fusion.2.x_ref = bf16[2,38,320,128]{3,2,1,0:T(8,128)(2,1)} fusion(bf16[2,38,320,128]{3,2,1,0:T(8,128)(2,1)} %copy-done.4, bf16[2,38,160,128]{3,2,1,0:T(8,128)(2,1)} %collective-permute-done.2, s32[]{:T(128)S(6)} %select_n.35), kind=kLoop, calls=%fused_computation.45 | loop fusion | bytes 6225924 | tf_op jit(solution)/shard_map/dynamic_update_slice | solution.py:80
  68.1 39.3 %shard_map.91.res_ref = bf16[2,36,160,128]{3,2,1,0:T(8,128)(2,1)S(1)} custom-call(bf16[2,38,320,128]{3,2,1,0:T(8,128)(2,1)} %constant_dynamic-update-slice_fusion.2.x_ref, bf16[3,480,320]{2,1,0:T(8,128)(2,1)S(1)} %bitcast.49, bf16[2,36,160,128]{3,2,1,0:T(8,128)(2,1)} %res_ref.1, f32[160,1]{1,0:T(8,128)S(1)} %copy.22.b_ref), custom_call_target="tpu_custom_call" | custom-call | flops 8493465600 | bytes 13045760 | tf_op jit(solution)/shard_map/pallas_call | solution.py:106
  107.4 1.8 fusion.22
  109.2 4.6 %collective-permute-start.3 = (bf16[1,36,160,128]{3,2,1,0:T(8,128)(2,1)}, bf16[1,36,160,128]{3,2,1,0:T(8,128)(2,1)}, u32[]{:S(2)}, u32[]{:S(2)}) collective-permute-start(bf16[1,36,160,128]{3,2,1,0:T(8,128)(2,1)} %get-tuple-element.13), channel_id=1, source_target_pairs={{0,4},{4,8},{8,12},{1,5},{5,9},{9,13},{2,6},{6,10},{10,14},{3,7},{... | collective-permute-start | bytes 4423688 | tf_op jit(solution)/shard_map/ppermute | solution.py:223
  113.8 1.3 collective-permute-start.4
  115.1 0.5 convert_reduce_fusion.1
  115.6 0.1 reduce_sum.128
  115.7 0.1 reduce_sum.129
  115.8 0.1 sub.87
  115.9 0.1 sub.88
  116.0 0.9 fusion.1
  117.0 0.1 reduce_sum.131
  117.0 0.1 reduce_sum.132
  117.2 5.0 %psum.22 = f32[8,2,16]{2,0,1:T(8,128)S(1)} all-reduce(f32[8,2,16]{2,0,1:T(8,128)S(1)} %dynamic_update_slice.23), channel_id=1, replica_groups=mesh['groups'=2,'tm'=4,'height'=2,'chan'=2] {'height'}, use_global_device_ids=true, to_apply=%region_12.13 | all-reduce | flops 256 | bytes 2048 | tf_op jit(solution)/shard_map/psum | solution.py:56
  122.2 30.6 %psum.23 = f32[8,2,16]{2,0,1:T(8,128)S(1)} all-reduce(f32[8,2,16]{2,0,1:T(8,128)S(1)} %psum.22), channel_id=1, replica_groups=mesh['groups'=2,'tm'=4,'height'=2,'chan'=2] {'tm'}, use_global_device_ids=true, to_apply=%region_13.14 | all-reduce | flops 256 | bytes 2048 | tf_op jit(solution)/shard_map/psum | solution.py:56
  152.9 0.1 mul.105
  152.9 0.1 mul.106
  153.0 0.1 sub.91
  153.1 0.1 sub.92
  153.2 7.4 %broadcast_in_dim.42 = bf16[4,36,320,128]{3,2,1,0:T(8,128)(2,1)} broadcast(bf16[]{:T(256)} %constant.35.clone.1), dimensions={} | broadcast | bytes 11796482 | tf_op jit(solution)/shard_map/broadcast_in_dim | solution.py:78
  160.6 8.3 %constant_dynamic-update-slice_fusion.1 = (bf16[4,36,320,128]{3,2,1,0:T(8,128)(2,1)}, bf16[4,36,160,128]{3,2,1,0:T(8,128)(2,1)}) fusion(bf16[4,36,320,128]{3,2,1,0:T(8,128)(2,1)} %broadcast_in_dim.42, s32[]{:T(128)S(6)} %select_n.34, f32[160]{0:T(256)S(1)} %copy-done.9, f32[160]{0:T(256)S(1)} %copy-done.10, f32[160]{0:T(256)S(1)} %mul.106, f32[160]{0:T(256)S(1)} %sub.92, ...), kind=kLoop, calls=%fused_computation.44 | loop fusion | flops 47185920 | bytes 17697288 | tf_op jit(solution)/shard_map/dynamic_update_slice | solution.py:79
  168.9 2.4 %collective-permute-start.6 = (bf16[3,80,160]{2,1,0:T(8,128)(2,1)S(1)}, bf16[3,80,160]{2,1,0:T(8,128)(2,1)S(1)}, u32[]{:S(2)}, u32[]{:S(2)}) collective-permute-start(bf16[3,80,160]{2,1,0:T(8,128)(2,1)S(1)} %copy-done.5), channel_id=1, source_target_pairs={{0,12},{4,0},{8,4},{12,8},{1,13},{5,1},{9,5},{13,9},{2,14},{6,2},{... | collective-permute-start | bytes 230408 | tf_op jit(solution)/shard_map/ppermute | solution.py:34
  171.4 1.4 collective-permute-start.7
  172.7 0.7 bitcast_dynamic-update-slice_fusion.6
  173.4 0.1 copy.25.bias_ref
  173.5 1.7 collective-permute-done.6
  175.2 0.7 bitcast_dynamic-update-slice_fusion.4
  175.9 8.4 %collective-permute-done.7 = bf16[3,80,160]{2,1,0:T(8,128)(2,1)S(1)} collective-permute-done((bf16[3,80,160]{2,1,0:T(8,128)(2,1)S(1)}, bf16[3,80,160]{2,1,0:T(8,128)(2,1)S(1)}, u32[]{:S(2)}, u32[]{:S(2)}) %collective-permute-start.7) | collective-permute-done | bytes 76832 | tf_op jit(solution)/shard_map/ppermute | solution.py:34
  184.3 0.7 bitcast_dynamic-update-slice_fusion.2
  184.9 0.7 bitcast_dynamic-update-slice_fusion
  185.6 0.7 bitcast_dynamic-update-slice_fusion.7
  186.3 0.7 bitcast_dynamic-update-slice_fusion.5
  186.9 0.7 bitcast_dynamic-update-slice_fusion.3
  187.6 0.7 bitcast_dynamic-update-slice_fusion.1
  188.2 1.1 dynamic-slice_bitcast_fusion
  189.3 1.1 copy.24
  190.4 1.4 reshape.107
  191.8 6.6 %constant_dynamic-update-slice_fusion.a_ref.b_ref.c_ref = bf16[4,36,320,128]{3,2,1,0:T(8,128)(2,1)} fusion(bf16[4,36,320,128]{3,2,1,0:T(8,128)(2,1)} %get-tuple-element.9, bf16[4,36,160,128]{3,2,1,0:T(8,128)(2,1)} %collective-permute-done.5, s32[]{:T(128)S(6)} %select_n.35), kind=kLoop, calls=%fused_computation.43 | loop fusion | bytes 11796484 | tf_op jit(solution)/shard_map/dynamic_update_slice | solution.py:80
  198.3 24.1 %shard_map.92 = bf16[2,36,160,128]{3,2,1,0:T(8,128)(2,1)} custom-call(bf16[4,36,320,128]{3,2,1,0:T(8,128)(2,1)} %constant_dynamic-update-slice_fusion.a_ref.b_ref.c_ref, bf16[4,36,320,128]{3,2,1,0:T(8,128)(2,1)} %constant_dynamic-update-slice_fusion.a_ref.b_ref.c_ref, bf16[4,36,320,128]{3,2,1,0:T(8,128)(2,1)} %constant_dynamic-update-slice_fusion.a_ref.b_ref.c_ref, ...), custom_call_target="tpu_custom_call" | custom-call | flops 2831155200 | bytes 23900160 | tf_op jit(solution)/shard_map/pallas_call | solution.py:147
  (49 shorter events, 0.3 us)
Async XLA Ops:
  0.0 12.0 %copy-start.1 = (bf16[2,36,160,128]{3,2,1,0:T(8,128)(2,1)S(1)}, bf16[2,36,160,128]{3,2,1,0:T(8,128)(2,1)}, u32[]{:S(2)}) copy-start(bf16[2,36,160,128]{3,2,1,0:T(8,128)(2,1)} %res_ref.1) | copy-start | bytes 8847364
  0.0 12.0 %copy-start.8 = (f32[160]{0:T(256)S(1)}, f32[160]{0:T(256)}, u32[]{:S(2)}) copy-start(f32[160]{0:T(256)} %param.10) | copy-start | bytes 1924
  0.0 12.0 %copy-start.7 = (f32[160]{0:T(256)S(1)}, f32[160]{0:T(256)}, u32[]{:S(2)}) copy-start(f32[160]{0:T(256)} %param.11) | copy-start | bytes 1924
  14.4 1.6 copy-start.2
  16.0 12.1 %copy-start.3 = (bf16[2,36,160,128]{3,2,1,0:T(8,128)(2,1)S(1)}, bf16[2,36,160,128]{3,2,1,0:T(8,128)(2,1)}, u32[]{:S(2)}) copy-start(bf16[2,36,160,128]{3,2,1,0:T(8,128)(2,1)} %copy-done.2) | copy-start | bytes 8847364
  16.0 6.3 %collective-permute-start = (bf16[2,1,160,128]{3,2,1,0:T(8,128)(2,1)S(1)}, bf16[2,1,160,128]{3,2,1,0:T(8,128)(2,1)S(1)}, u32[]{:S(2)}, u32[]{:S(2)}) collective-permute-start(bf16[2,1,160,128]{3,2,1,0:T(8,128)(2,1)S(1)} %get-tuple-element.15), channel_id=1, source_target_pairs={{0,2},{1,3},{4,6},{5,7},{8,10},{9,11},{12,14},{13,15},{16,18},{17,... | collective-permute-start | bytes 245768 | tf_op jit(solution)/shard_map/ppermute | solution.py:23
  20.2 6.3 %collective-permute-start.1 = (bf16[2,1,160,128]{3,2,1,0:T(8,128)(2,1)S(1)}, bf16[2,1,160,128]{3,2,1,0:T(8,128)(2,1)S(1)}, u32[]{:S(2)}, u32[]{:S(2)}) collective-permute-start(bf16[2,1,160,128]{3,2,1,0:T(8,128)(2,1)S(1)} %get-tuple-element.16), channel_id=1, source_target_pairs={{2,0},{3,1},{6,4},{7,5},{10,8},{11,9},{14,12},{15,13},{18,16},{19,... | collective-permute-start | bytes 245768 | tf_op jit(solution)/shard_map/ppermute | solution.py:24
  28.1 4.8 %copy-start.6 = (bf16[3,3,80,160]{3,2,1,0:T(8,128)(2,1)S(1)}, bf16[3,3,80,160]{3,2,1,0:T(8,128)(2,1)}, u32[]{:S(2)}) copy-start(bf16[3,3,80,160]{3,2,1,0:T(8,128)(2,1)} %param.12) | copy-start | bytes 691204
  28.1 35.7 %copy-start.11 = (f32[160]{0:T(256)S(1)}, f32[160]{0:T(256)}, u32[]{:S(2)}) copy-start(f32[160]{0:T(256)} %param.13) | copy-start | bytes 1924
  30.3 2.6 %copy-start.4 = (bf16[2,38,320,128]{3,2,1,0:T(8,128)(2,1)}, bf16[2,38,320,128]{3,2,1,0:T(8,128)(2,1)S(1)}, u32[]{:S(2)}) copy-start(bf16[2,38,320,128]{3,2,1,0:T(8,128)(2,1)S(1)} %get-tuple-element.12) | copy-start | bytes 18677764
  32.9 31.0 %collective-permute-start.2 = (bf16[2,38,160,128]{3,2,1,0:T(8,128)(2,1)}, bf16[2,38,160,128]{3,2,1,0:T(8,128)(2,1)}, u32[]{:S(2)}, u32[]{:S(2)}) collective-permute-start(bf16[2,38,160,128]{3,2,1,0:T(8,128)(2,1)} %get-tuple-element.11), channel_id=1, source_target_pairs={{0,1},{1,0},{2,3},{3,2},{4,5},{5,4},{6,7},{7,6},{8,9},{9,8},{10,11... | collective-permute-start | bytes 9338888 | tf_op jit(solution)/shard_map/ppermute | solution.py:16
  63.9 4.2 %copy-start = (bf16[3,3,160,320]{3,2,1,0:T(8,128)(2,1)S(1)}, bf16[3,3,160,320]{3,2,1,0:T(8,128)(2,1)}, u32[]{:S(2)}) copy-start(bf16[3,3,160,320]{3,2,1,0:T(8,128)(2,1)} %copy.21) | copy-start | bytes 2764804
  109.2 44.0 %collective-permute-start.3 = (bf16[1,36,160,128]{3,2,1,0:T(8,128)(2,1)}, bf16[1,36,160,128]{3,2,1,0:T(8,128)(2,1)}, u32[]{:S(2)}, u32[]{:S(2)}) collective-permute-start(bf16[1,36,160,128]{3,2,1,0:T(8,128)(2,1)} %get-tuple-element.13), channel_id=1, source_target_pairs={{0,4},{4,8},{8,12},{1,5},{5,9},{9,13},{2,6},{6,10},{10,14},{3,7},{... | collective-permute-start | bytes 4423688 | tf_op jit(solution)/shard_map/ppermute | solution.py:223
  113.8 39.4 %collective-permute-start.4 = (bf16[1,36,160,128]{3,2,1,0:T(8,128)(2,1)}, bf16[1,36,160,128]{3,2,1,0:T(8,128)(2,1)}, u32[]{:S(2)}, u32[]{:S(2)}) collective-permute-start(bf16[1,36,160,128]{3,2,1,0:T(8,128)(2,1)} %get-tuple-element.14), channel_id=1, source_target_pairs={{4,0},{8,4},{12,8},{5,1},{9,5},{13,9},{6,2},{10,6},{14,10},{7,3},{... | collective-permute-start | bytes 4423688 | tf_op jit(solution)/shard_map/ppermute | solution.py:224
  153.2 7.4 %copy-start.9 = (f32[160]{0:T(256)S(1)}, f32[160]{0:T(256)}, u32[]{:S(2)}) copy-start(f32[160]{0:T(256)} %param.15) | copy-start | bytes 1924
  153.2 7.4 %copy-start.10 = (f32[160]{0:T(256)S(1)}, f32[160]{0:T(256)}, u32[]{:S(2)}) copy-start(f32[160]{0:T(256)} %param.14) | copy-start | bytes 1924
  160.6 8.3 %copy-start.5 = (bf16[3,80,160]{2,1,0:T(8,128)(2,1)S(1)}, bf16[3,80,160]{2,1,0:T(8,128)(2,1)}, u32[]{:S(2)}) copy-start(bf16[3,80,160]{2,1,0:T(8,128)(2,1)} %param.16) | copy-start | bytes 230404
  160.6 12.8 %copy-start.12 = (f32[160]{0:T(256)S(1)}, f32[160]{0:T(256)}, u32[]{:S(2)}) copy-start(f32[160]{0:T(256)} %param.17) | copy-start | bytes 1924
  168.9 22.9 %collective-permute-start.5 = (bf16[4,36,160,128]{3,2,1,0:T(8,128)(2,1)}, bf16[4,36,160,128]{3,2,1,0:T(8,128)(2,1)}, u32[]{:S(2)}, u32[]{:S(2)}) collective-permute-start(bf16[4,36,160,128]{3,2,1,0:T(8,128)(2,1)} %get-tuple-element.10), channel_id=1, source_target_pairs={{0,1},{1,0},{2,3},{3,2},{4,5},{5,4},{6,7},{7,6},{8,9},{9,8},{10,11... | collective-permute-start | bytes 17694728 | tf_op jit(solution)/shard_map/ppermute | solution.py:16
  168.9 6.3 %collective-permute-start.6 = (bf16[3,80,160]{2,1,0:T(8,128)(2,1)S(1)}, bf16[3,80,160]{2,1,0:T(8,128)(2,1)S(1)}, u32[]{:S(2)}, u32[]{:S(2)}) collective-permute-start(bf16[3,80,160]{2,1,0:T(8,128)(2,1)S(1)} %copy-done.5), channel_id=1, source_target_pairs={{0,12},{4,0},{8,4},{12,8},{1,13},{5,1},{9,5},{13,9},{2,14},{6,2},{... | collective-permute-start | bytes 230408 | tf_op jit(solution)/shard_map/ppermute | solution.py:34
  171.4 12.9 %collective-permute-start.7 = (bf16[3,80,160]{2,1,0:T(8,128)(2,1)S(1)}, bf16[3,80,160]{2,1,0:T(8,128)(2,1)S(1)}, u32[]{:S(2)}, u32[]{:S(2)}) collective-permute-start(bf16[3,80,160]{2,1,0:T(8,128)(2,1)S(1)} %copy-done.5), channel_id=1, source_target_pairs={{0,8},{4,12},{8,0},{12,4},{1,9},{5,13},{9,1},{13,5},{2,10},{6,14},... | collective-permute-start | bytes 230408 | tf_op jit(solution)/shard_map/ppermute | solution.py:34
  172.7 12.2 %collective-permute-start.8 = (bf16[3,80,160]{2,1,0:T(8,128)(2,1)S(1)}, bf16[3,80,160]{2,1,0:T(8,128)(2,1)S(1)}, u32[]{:S(2)}, u32[]{:S(2)}) collective-permute-start(bf16[3,80,160]{2,1,0:T(8,128)(2,1)S(1)} %copy-done.5), channel_id=1, source_target_pairs={{0,4},{4,8},{8,12},{12,0},{1,5},{5,9},{9,13},{13,1},{2,6},{6,10},{... | collective-permute-start | bytes 230408 | tf_op jit(solution)/shard_map/ppermute | solution.py:34

commit v5 on v4

--- a/solution.py
+++ b/solution.py
@@ -80,90 +80,114 @@
     return lax.dynamic_update_slice_in_dim(joined, other, (1 - chan_index) * size, axis=2)
 
 
-def spatial_kernel(x_ref, w_ref, res_ref, b_ref, o_ref):
+def pair(ref, first):
+    return jnp.concatenate([ref[0, first], ref[0, first + 1]], axis=1)
+
+
+def spatial_kernel(xo_ref, xt_ref, wo_ref, wt_ref, res_ref, b_ref, o_ref):
     rows, local_chan, width = o_ref.shape[1], o_ref.shape[2], o_ref.shape[3]
     lane = lax.broadcasted_iota(jnp.int32, (local_chan, width), 1)
     bias = b_ref[...]
 
-    def one_row(r, carry):
-        y = jnp.dot(w_ref[0], x_ref[0, r], preferred_element_type=jnp.float32)
-        y = y + jnp.dot(w_ref[1], x_ref[0, r + 1], preferred_element_type=jnp.float32)
-        y = y + jnp.dot(w_ref[2], x_ref[0, r + 2], preferred_element_type=jnp.float32)
-        left = pltpu.roll(y[:local_chan], 1, 1)
-        left = jnp.where(lane == 0, 0.0, left)
-        right = pltpu.roll(y[2 * local_chan :], width - 1, 1)
-        right = jnp.where(lane == width - 1, 0.0, right)
-        total = left + y[local_chan : 2 * local_chan] + right
-        o_ref[0, r] = (res_ref[0, r].astype(jnp.float32) + total + bias).astype(o_ref.dtype)
+    def two_rows(i, carry):
+        r = 2 * i
+        y = jnp.dot(wo_ref[0], pair(xo_ref, r), preferred_element_type=jnp.float32)
+        y = y + jnp.dot(wt_ref[0], pair(xt_ref, r), preferred_element_type=jnp.float32)
+        for tap in (1, 2):
+            y = y + jnp.dot(wo_ref[tap], pair(xo_ref, r + tap), preferred_element_type=jnp.float32)
+            y = y + jnp.dot(wt_ref[tap], pair(xt_ref, r + tap), preferred_element_type=jnp.float32)
+        for half in range(2):
+            part = y[:, half * width : (half + 1) * width]
+            left = pltpu.roll(part[:local_chan], 1, 1)
+            left = jnp.where(lane == 0, 0.0, left)
+            right = pltpu.roll(part[2 * local_chan :], width - 1, 1)
+            right = jnp.where(lane == width - 1, 0.0, right)
+            total = left + part[local_chan : 2 * local_chan] + right
+            o_ref[0, r + half] = (res_ref[0, r + half].astype(jnp.float32) + total + bias).astype(
+                o_ref.dtype
+            )
         return carry
 
-    lax.fori_loop(0, rows, one_row, 0)
-
-
-def spatial_call(inputs, weight, residual, bias):
+    lax.fori_loop(0, rows // 2, two_rows, 0)
+
+
+def spatial_call(own, other, weight_own, weight_other, residual, bias):
     frames, rows, local_chan, width = residual.shape
-    chans = inputs.shape[2]
+    act_spec = pl.BlockSpec((1, rows + 2, local_chan, width), lambda f: (f, 0, 0, 0))
+    weight_spec = pl.BlockSpec((3, 3 * local_chan, local_chan), lambda f: (0, 0, 0))
     return pl.pallas_call(
         spatial_kernel,
         out_shape=jax.ShapeDtypeStruct(residual.shape, jnp.bfloat16),
         grid=(frames,),
         in_specs=[
-            pl.BlockSpec((1, rows + 2, chans, width), lambda f: (f, 0, 0, 0)),
-            pl.BlockSpec((3, 3 * local_chan, chans), lambda f: (0, 0, 0)),
+            act_spec,
+            act_spec,
+            weight_spec,
+            weight_spec,
             pl.BlockSpec((1, rows, local_chan, width), lambda f: (f, 0, 0, 0)),
             pl.BlockSpec((local_chan, 1), lambda f: (0, 0)),
         ],
         out_specs=pl.BlockSpec((1, rows, local_chan, width), lambda f: (f, 0, 0, 0)),
         compiler_params=pltpu.CompilerParams(vmem_limit_bytes=48 * 1024 * 1024),
         cost_estimate=pl.CostEstimate(
-            flops=2 * frames * rows * width * 9 * chans * local_chan,
+            flops=2 * frames * rows * width * 18 * local_chan * local_chan,
             transcendentals=0,
-            bytes_accessed=inputs.size * 2 + weight.size * 2 + 4 * residual.size,
+            bytes_accessed=4 * own.size + 4 * weight_own.size + 4 * residual.size,
         ),
-    )(inputs, weight, residual, bias)
-
-
-def temporal_kernel(a_ref, b_ref, c_ref, w_ref, res_ref, bias_ref, o_ref):
-    rows = o_ref.shape[1]
+    )(own, other, weight_own, weight_other, residual, bias)
+
+
+def temporal_kernel(*refs):
+    own_refs, other_refs = refs[0:3], refs[3:6]
+    wo_ref, wt_ref, res_ref, bias_ref, o_ref = refs[6:]
+    rows, width = o_ref.shape[1], o_ref.shape[3]
     bias = bias_ref[...]
 
-    def one_row(r, carry):
-        y = jnp.dot(w_ref[0], a_ref[0, r], preferred_element_type=jnp.float32)
-        y = y + jnp.dot(w_ref[1], b_ref[0, r], preferred_element_type=jnp.float32)
-        y = y + jnp.dot(w_ref[2], c_ref[0, r], preferred_element_type=jnp.float32)
-        o_ref[0, r] = (res_ref[0, r].astype(jnp.float32) + y + bias).astype(o_ref.dtype)
+    def two_rows(i, carry):
+        r = 2 * i
+        y = jnp.dot(wo_ref[0], pair(own_refs[0], r), preferred_element_type=jnp.float32)
+        y = y + jnp.dot(wt_ref[0], pair(other_refs[0], r), preferred_element_type=jnp.float32)
+        for tap in (1, 2):
+            y = y + jnp.dot(wo_ref[tap], pair(own_refs[tap], r), preferred_element_type=jnp.float32)
+            y = y + jnp.dot(wt_ref[tap], pair(other_refs[tap], r), preferred_element_type=jnp.float32)
+        for half in range(2):
+            part = y[:, half * width : (half + 1) * width]
+            o_ref[0, r + half] = (res_ref[0, r + half].astype(jnp.float32) + part + bias).astype(
+                o_ref.dtype
+            )
         return carry
 
-    lax.fori_loop(0, rows, one_row, 0)
+    lax.fori_loop(0, rows // 2, two_rows, 0)
 
 
 def frame_spec(tap, rows, chans, width):
     return pl.BlockSpec((1, rows, chans, width), lambda f: (f + tap, 0, 0, 0))
 
 
-def temporal_call(inputs, weight, residual, bias):
+def temporal_call(own, other, weight_own, weight_other, residual, bias):
     frames, rows, local_chan, width = residual.shape
-    chans = inputs.shape[2]
+    taps = [frame_spec(tap, rows, local_chan, width) for tap in range(3)]
+    weight_spec = pl.BlockSpec((3, local_chan, local_chan), lambda f: (0, 0, 0))
     return pl.pallas_call(
         temporal_kernel,
         out_shape=jax.ShapeDtypeStruct(residual.shape, jnp.bfloat16),
         grid=(frames,),
-        in_specs=[
-            frame_spec(0, rows, chans, width),
-            frame_spec(1, rows, chans, width),
-            frame_spec(2, rows, chans, width),
-            pl.BlockSpec((3, local_chan, chans), lambda f: (0, 0, 0)),
+        in_specs=taps
+        + taps
+        + [
+            weight_spec,
+            weight_spec,
             pl.BlockSpec((1, rows, local_chan, width), lambda f: (f, 0, 0, 0)),
             pl.BlockSpec((local_chan, 1), lambda f: (0, 0)),
         ],
         out_specs=pl.BlockSpec((1, rows, local_chan, width), lambda f: (f, 0, 0, 0)),
         compiler_params=pltpu.CompilerParams(vmem_limit_bytes=48 * 1024 * 1024),
         cost_estimate=pl.CostEstimate(
-            flops=2 * frames * rows * width * 3 * chans * local_chan,
+            flops=2 * frames * rows * width * 6 * local_chan * local_chan,
             transcendentals=0,
-            bytes_accessed=3 * residual.size * 4 + weight.size * 2 + 4 * residual.size,
+            bytes_accessed=12 * residual.size + 4 * weight_own.size + 4 * residual.size,
         ),
-    )(inputs, inputs, inputs, weight, residual, bias)
+    )(own, own, own, other, other, other, weight_own, weight_other, residual, bias)
 
 
 def spatial_taps(running, channel_slab, weight, rows, width):
@@ -214,9 +238,17 @@
     act_one = group_act(values, average, variance, norm1_gain, norm1_bias)
 
     with_rows = row_halo(act_one)
-    all_rows = in_order(with_rows, swap_chan(with_rows), chan_index)
+    own_start = chan_index * local_chan
+    other_start = (1 - chan_index) * local_chan
     spatial_rows = jnp.transpose(spatial_full, (0, 1, 3, 2)).reshape(3, 3 * local_chan, C)
-    hidden = spatial_call(all_rows, spatial_rows, video, spatial_bias[:, None])
+    hidden = spatial_call(
+        with_rows,
+        swap_chan(with_rows),
+        lax.dynamic_slice_in_dim(spatial_rows, own_start, local_chan, axis=2),
+        lax.dynamic_slice_in_dim(spatial_rows, other_start, local_chan, axis=2),
+        video,
+        spatial_bias[:, None],
+    )
 
     forward = [(i, i + 1) for i in range(tm_count - 1)]
     backward = [(target, source) for source, target in forward]
@@ -234,9 +266,15 @@
     inside = inside & ((frame_ids < frames + 1) | (tm_index < tm_count - 1))
     act_two = jnp.where(inside[:, None, None, None], act_two, jnp.zeros_like(act_two))
 
-    all_two = in_order(act_two, swap_chan(act_two), chan_index)
     temporal_rows = jnp.transpose(temporal_full, (0, 2, 1))
-    return temporal_call(all_two, temporal_rows, hidden, temporal_bias[:, None])
+    return temporal_call(
+        act_two,
+        swap_chan(act_two),
+        lax.dynamic_slice_in_dim(temporal_rows, own_start, local_chan, axis=2),
+        lax.dynamic_slice_in_dim(temporal_rows, other_start, local_chan, axis=2),
+        hidden,
+        temporal_bias[:, None],
+    )
 
 
 def solution(mesh):

time: 223 us -> 175 us (0.78)
  local copies, waits for them, and re-layouts: 38 us -> 14.1 us
  Pallas kernels: 63.4 us -> 40.2 us
    pallas_call x1, Pallas kernels: 39.3 us -> 24.2 us  [spatial_call(): pl.pallas_call(spatial_kernel, out_shape=jax.ShapeDtypeStruct(residual.sh...]
    dynamic_update_slice x2 -> x0, local copies, waits for them, and re-layouts: 10.7 us -> none  [in_order(): lax.dynamic_update_slice_in_dim(joined, other, (1 - chan_index) * size, a...]
    broadcast_in_dim x4 -> x2, local copies, waits for them, and re-layouts: 9.07 us -> 0.21 us  [the longest x1 0.11 us: body(): spatial_bias[:, None]]
    dynamic_update_slice x1 -> x0, other arithmetic: 8.3 us -> none  [in_order(): lax.dynamic_update_slice_in_dim(joined, own, chan_index * size, axis=2)]
    pallas_call x1, Pallas kernels: 24.1 us -> 16 us  [temporal_call(): pl.pallas_call(temporal_kernel, out_shape=jax.ShapeDtypeStruct(residual.s...]
    select_n x0 -> x1, other arithmetic: none -> 7.66 us  [body(): jnp.where(inside[:, None, None, None], act_two, jnp.zeros_like(act_two))]
    unnamed x33 -> x25, local copies, waits for them, and re-layouts: 8.87 us -> 4.65 us
  transfers between devices with their start and end apart: 9 -> 9, of which waited for: 4 -> 4; matrix products, arithmetic and copies ran while one was open for 6% -> 8% of each run, Pallas kernels for 0% -> 0%
where the time goes in v5:
time: 175 us; the launch traced here: 174 us
  blocking collectives  70 us (40%)
  Pallas kernels  40.2 us (23%)
  other arithmetic  19.2 us (11%)
  waiting for transfers between devices  15.2 us (9%)
  starting transfers between devices  15 us (9%)
  local copies, waits for them, and re-layouts  14.1 us (8%)
    psum x3, blocking collectives, group_stats(): table = lax.psum(table, name)  41.2 us
    all_gather x1, blocking collectives, body(): lax.all_gather(spatial_weight, 'tm', axis=2, tiled=True)  28.9 us
    pallas_call x1, Pallas kernels, spatial_call(): pl.pallas_call(spatial_kernel, out_shape=jax.ShapeDtypeStruct(residual.sh...  24.2 us
    pallas_call x1, Pallas kernels, temporal_call(): pl.pallas_call(temporal_kernel, out_shape=jax.ShapeDtypeStruct(residual.s...  16 us
    ppermute x3, waiting for transfers between devices, gather_tm(): pieces.append(lax.ppermute(piece, 'tm', pairs))  10.1 us
    select_n x1, other arithmetic, body(): jnp.where(inside[:, None, None, None], act_two, jnp.zeros_like(act_two))  7.66 us
    ppermute x1, starting transfers between devices, body(): before = lax.ppermute(hidden[-1:], 'tm', forward)  4.69 us
    unnamed x25, local copies, waits for them, and re-layouts  4.65 us
  transfers between devices with their start and end apart: 9, of which 4 were waited for; matrix products, arithmetic and copies ran while one was open for 8% of the time, Pallas kernels for 0%

profile of v5, /device:TPU:0, one launch (start us, length us, event | category | flops | bytes accessed | tf_op | source)
XLA Modules:
  0.0 174.1 jit_solution(4953968928938790997)
XLA Ops:
  0.0 2.5 %convert_reduce_fusion = f32[2,160]{1,0:T(2,128)S(1)} fusion(bf16[2,36,160,128]{3,2,1,0:T(8,128)(2,1)} %res_ref.1), kind=kLoop, calls=%fused_computation.3 | loop fusion | flops 2948800 | bytes 2950400 | tf_op jit(solution)/shard_map/reduce_sum | solution.py:43
  2.5 0.1 reduce_sum.101
  2.5 0.1 reduce_sum.120
  2.6 0.1 sub.75
  2.7 0.1 sub.76
  2.8 2.7 %fusion.3 = f32[2,160]{1,0:T(2,128)S(1)} fusion(bf16[2,36,160,128]{3,2,1,0:T(8,128)(2,1)} %res_ref.1, f32[2,160]{1,0:T(2,128)S(1)} %sub.76), kind=kLoop, calls=%fused_computation.9 | loop fusion | flops 5897920 | bytes 2951680 | tf_op jit(solution)/shard_map/reduce_sum | solution.py:45
  5.6 0.1 reduce_sum.122
  5.7 0.1 reduce_sum.123
  5.8 5.9 %psum.21 = f32[2,2,2,16]{3,2,0,1:T(2,128)S(1)} all-reduce(f32[2,2,2,16]{3,2,0,1:T(2,128)S(1)} %fusion.16), channel_id=1, replica_groups=mesh['groups'=2,'tm'=4,'height'=2,'chan'=2] {'height'}, use_global_device_ids=true, to_apply=%region_4.5 | all-reduce | flops 128 | bytes 1024 | tf_op jit(solution)/shard_map/psum | solution.py:56
  11.7 0.1 mul.90
  11.7 0.1 mul.91
  11.8 0.1 sub.79
  11.9 0.1 sub.80
  12.0 0.0 copy-start.7
  12.1 0.0 copy-start.2
  12.1 2.3 %fusion.12 = bf16[2,36,160,128]{3,2,1,0:T(8,128)(2,1)S(1)} fusion(bf16[2,36,160,128]{3,2,1,0:T(8,128)(2,1)S(1)} %copy-done, f32[160]{0:T(256)S(1)} %copy-done.3, f32[160]{0:T(256)S(1)} %copy-done.4, f32[2,160]{1,0:T(2,128)S(1)} %mul.91, f32[2,160]{1,0:T(2,128)S(1)} %sub.80), kind=kLoop, calls=%fused_computation.18 | loop fusion | flops 14745600 | bytes 5902080 | tf_op jit(solution)/shard_map/convert_element_type | solution.py:73
  14.4 4.0 %collective-permute-start = (bf16[2,1,160,128]{3,2,1,0:T(8,128)(2,1)S(1)}, bf16[2,1,160,128]{3,2,1,0:T(8,128)(2,1)S(1)}, u32[]{:S(2)}, u32[]{:S(2)}) collective-permute-start(bf16[2,1,160,128]{3,2,1,0:T(8,128)(2,1)S(1)} %get-tuple-element.11), channel_id=1, source_target_pairs={{0,2},{1,3},{4,6},{5,7},{8,10},{9,11},{12,14},{13,15},{16,18},{17,... | collective-permute-start | bytes 245768 | tf_op jit(solution)/shard_map/ppermute | solution.py:23
  18.4 1.3 collective-permute-start.1
  19.7 0.7 collective-permute-done
  20.4 4.3 %collective-permute-done.1 = bf16[2,1,160,128]{3,2,1,0:T(8,128)(2,1)S(1)} collective-permute-done((bf16[2,1,160,128]{3,2,1,0:T(8,128)(2,1)S(1)}, bf16[2,1,160,128]{3,2,1,0:T(8,128)(2,1)S(1)}, u32[]{:S(2)}, u32[]{:S(2)}) %collective-permute-start.1) | collective-permute-done | bytes 81952 | tf_op jit(solution)/shard_map/ppermute | solution.py:24
  24.7 2.1 %pad_maximum_fusion.xo_ref = bf16[2,38,160,128]{3,2,1,0:T(8,128)(2,1)} fusion(bf16[2,1,160,128]{3,2,1,0:T(8,128)(2,1)S(1)} %collective-permute-done.1, bf16[2,36,160,128]{3,2,1,0:T(8,128)(2,1)S(1)} %fusion.12, bf16[2,1,160,128]{3,2,1,0:T(8,128)(2,1)S(1)} %collective-permute-done), kind=kLoop, calls=%fused_computation.20 | loop fusion | flops 3112960 | bytes 6225920 | tf_op jit(solution)/shard_map/concatenate | solution.py:25
  26.8 0.1 copy.22.b_ref
  26.9 28.9 %all_gather.3 = bf16[3,3,320,160]{3,2,1,0:T(8,128)(2,1)S(1)} all-gather(bf16[3,3,80,160]{3,2,1,0:T(8,128)(2,1)S(1)} %copy-done.2), channel_id=1, replica_groups=mesh['groups'=2,'tm'=4,'height'=2,'chan'=2] {'tm'}, dimensions={2}, use_global_device_ids=true | all-gather | bytes 1152000 | tf_op jit(solution)/shard_map/all_gather | solution.py:230
  55.8 0.9 copy.21
  56.7 0.7 constant_dynamic-slice_fusion
  57.4 24.2 %shard_map.91.refs_8_ = bf16[2,36,160,128]{3,2,1,0:T(8,128)(2,1)S(1)} custom-call(bf16[2,38,160,128]{3,2,1,0:T(8,128)(2,1)} %pad_maximum_fusion.xo_ref, bf16[2,38,160,128]{3,2,1,0:T(8,128)(2,1)} %collective-permute-done.2.xt_ref, bf16[3,480,160]{2,1,0:T(8,128)(2,1)S(1)} %get-tuple-element.14.wo_ref, bf16[3,480,160]{2,1,0:T(8,128)(2,1)S(1)} %get-tuple-element.13.wt_ref, ...), custom_call_target="tpu_custom_call" | custom-call | flops 8493465600 | bytes 13045760 | tf_op jit(solution)/shard_map/pallas_call | solution.py:118
  81.6 0.0 copy-start.5
  81.7 1.8 %fusion.21 = (bf16[1,36,160,128]{3,2,1,0:T(8,128)(2,1)}, bf16[1,36,160,128]{3,2,1,0:T(8,128)(2,1)}) fusion(bf16[2,36,160,128]{3,2,1,0:T(8,128)(2,1)S(1)} %shard_map.91.refs_8_), kind=kLoop, calls=%fused_computation.56 | loop fusion | bytes 5898240 | tf_op jit(solution)/shard_map/slice | solution.py:255
  83.5 4.7 %collective-permute-start.3 = (bf16[1,36,160,128]{3,2,1,0:T(8,128)(2,1)}, bf16[1,36,160,128]{3,2,1,0:T(8,128)(2,1)}, u32[]{:S(2)}, u32[]{:S(2)}) collective-permute-start(bf16[1,36,160,128]{3,2,1,0:T(8,128)(2,1)} %get-tuple-element.9), channel_id=1, source_target_pairs={{0,4},{4,8},{8,12},{1,5},{5,9},{9,13},{2,6},{6,10},{10,14},{3,7},{... | collective-permute-start | bytes 4423688 | tf_op jit(solution)/shard_map/ppermute | solution.py:255
  88.2 1.3 collective-permute-start.4
  89.4 0.5 convert_reduce_fusion.1
  89.9 0.1 reduce_sum.128
  90.0 0.1 reduce_sum.129
  90.2 0.1 sub.86
  90.2 0.1 sub.87
  90.3 0.9 fusion.1
  91.3 0.1 reduce_sum.131
  91.4 0.1 reduce_sum.132
  91.5 5.0 %psum.22 = f32[8,2,16]{2,0,1:T(8,128)S(1)} all-reduce(f32[8,2,16]{2,0,1:T(8,128)S(1)} %dynamic_update_slice.9), channel_id=1, replica_groups=mesh['groups'=2,'tm'=4,'height'=2,'chan'=2] {'height'}, use_global_device_ids=true, to_apply=%region_12.13 | all-reduce | flops 256 | bytes 2048 | tf_op jit(solution)/shard_map/psum | solution.py:56
  96.6 30.3 %psum.23 = f32[8,2,16]{2,0,1:T(8,128)S(1)} all-reduce(f32[8,2,16]{2,0,1:T(8,128)S(1)} %psum.22), channel_id=1, replica_groups=mesh['groups'=2,'tm'=4,'height'=2,'chan'=2] {'tm'}, use_global_device_ids=true, to_apply=%region_13.14 | all-reduce | flops 256 | bytes 2048 | tf_op jit(solution)/shard_map/psum | solution.py:56
  126.9 0.1 mul.103
  127.0 0.1 mul.104
  127.1 0.1 sub.90
  127.2 0.1 sub.91
  127.3 7.7 %fusion.13.refs_0_.refs_1_.refs_2_ = bf16[4,36,160,128]{3,2,1,0:T(8,128)(2,1)} fusion(bf16[1,36,160,128]{3,2,1,0:T(8,128)(2,1)} %collective-permute-done.4, bf16[2,36,160,128]{3,2,1,0:T(8,128)(2,1)S(1)} %shard_map.91.refs_8_, bf16[1,36,160,128]{3,2,1,0:T(8,128)(2,1)} %collective-permute-done.3, f32[160]{0:T(256)S(1)} %copy-done.5, f32[160]{0:T(256)S(1)} %copy-done.6, ...), kind=kLoop, calls=%fused_computation.19 | loop fusion | flops 38338560 | bytes 11799044 | tf_op jit(solution)/shard_map/jit(_where)/select_n | solution.py:267
  135.0 2.4 %collective-permute-start.6 = (bf16[3,80,160]{2,1,0:T(8,128)(2,1)S(1)}, bf16[3,80,160]{2,1,0:T(8,128)(2,1)S(1)}, u32[]{:S(2)}, u32[]{:S(2)}) collective-permute-start(bf16[3,80,160]{2,1,0:T(8,128)(2,1)S(1)} %copy-done.1), channel_id=1, source_target_pairs={{0,12},{4,0},{8,4},{12,8},{1,13},{5,1},{9,5},{13,9},{2,14},{6,2},{... | collective-permute-start | bytes 230408 | tf_op jit(solution)/shard_map/ppermute | solution.py:34
  137.4 0.0 collective-permute-start.8
  137.4 1.4 collective-permute-start.7
  138.8 0.7 bitcast_dynamic-update-slice_fusion.6
  139.5 0.1 copy.25.refs_9_
  139.6 1.7 collective-permute-done.6
  141.3 0.7 bitcast_dynamic-update-slice_fusion.4
  141.9 8.4 %collective-permute-done.7 = bf16[3,80,160]{2,1,0:T(8,128)(2,1)S(1)} collective-permute-done((bf16[3,80,160]{2,1,0:T(8,128)(2,1)S(1)}, bf16[3,80,160]{2,1,0:T(8,128)(2,1)S(1)}, u32[]{:S(2)}, u32[]{:S(2)}) %collective-permute-start.7) | collective-permute-done | bytes 76832 | tf_op jit(solution)/shard_map/ppermute | solution.py:34
  150.4 0.7 bitcast_dynamic-update-slice_fusion.2
  151.0 0.7 bitcast_dynamic-update-slice_fusion
  151.7 0.7 bitcast_dynamic-update-slice_fusion.7
  152.3 0.7 bitcast_dynamic-update-slice_fusion.5
  153.0 0.7 bitcast_dynamic-update-slice_fusion.3
  153.6 0.7 bitcast_dynamic-update-slice_fusion.1
  154.3 1.1 dynamic-slice_bitcast_fusion
  155.4 1.1 copy.24
  156.4 1.4 reshape.107
  157.8 0.2 dynamic-slice_bitcast_fusion.1
  158.1 16.0 %shard_map.92 = bf16[2,36,160,128]{3,2,1,0:T(8,128)(2,1)} custom-call(bf16[4,36,160,128]{3,2,1,0:T(8,128)(2,1)} %fusion.13.refs_0_.refs_1_.refs_2_, bf16[4,36,160,128]{3,2,1,0:T(8,128)(2,1)} %fusion.13.refs_0_.refs_1_.refs_2_, bf16[4,36,160,128]{3,2,1,0:T(8,128)(2,1)} %fusion.13.refs_0_.refs_1_.refs_2_, ...), custom_call_target="tpu_custom_call" | custom-call | flops 2831155200 | bytes 23900160 | tf_op jit(solution)/shard_map/pallas_call | solution.py:171
  (39 shorter events, 0.3 us)
Async XLA Ops:
  0.0 12.0 %copy-start = (bf16[2,36,160,128]{3,2,1,0:T(8,128)(2,1)S(1)}, bf16[2,36,160,128]{3,2,1,0:T(8,128)(2,1)}, u32[]{:S(2)}) copy-start(bf16[2,36,160,128]{3,2,1,0:T(8,128)(2,1)} %res_ref.1) | copy-start | bytes 8847364
  0.0 12.0 %copy-start.3 = (f32[160]{0:T(256)S(1)}, f32[160]{0:T(256)}, u32[]{:S(2)}) copy-start(f32[160]{0:T(256)} %param.11) | copy-start | bytes 1924
  0.0 12.0 %copy-start.4 = (f32[160]{0:T(256)S(1)}, f32[160]{0:T(256)}, u32[]{:S(2)}) copy-start(f32[160]{0:T(256)} %param.10) | copy-start | bytes 1924
  12.0 14.7 %copy-start.7 = (f32[160]{0:T(256)S(1)}, f32[160]{0:T(256)}, u32[]{:S(2)}) copy-start(f32[160]{0:T(256)} %param.13) | copy-start | bytes 1924
  12.1 14.8 %copy-start.2 = (bf16[3,3,80,160]{3,2,1,0:T(8,128)(2,1)S(1)}, bf16[3,3,80,160]{3,2,1,0:T(8,128)(2,1)}, u32[]{:S(2)}) copy-start(bf16[3,3,80,160]{3,2,1,0:T(8,128)(2,1)} %param.12) | copy-start | bytes 691204
  14.4 6.0 %collective-permute-start = (bf16[2,1,160,128]{3,2,1,0:T(8,128)(2,1)S(1)}, bf16[2,1,160,128]{3,2,1,0:T(8,128)(2,1)S(1)}, u32[]{:S(2)}, u32[]{:S(2)}) collective-permute-start(bf16[2,1,160,128]{3,2,1,0:T(8,128)(2,1)S(1)} %get-tuple-element.11), channel_id=1, source_target_pairs={{0,2},{1,3},{4,6},{5,7},{8,10},{9,11},{12,14},{13,15},{16,18},{17,... | collective-permute-start | bytes 245768 | tf_op jit(solution)/shard_map/ppermute | solution.py:23
  18.4 6.3 %collective-permute-start.1 = (bf16[2,1,160,128]{3,2,1,0:T(8,128)(2,1)S(1)}, bf16[2,1,160,128]{3,2,1,0:T(8,128)(2,1)S(1)}, u32[]{:S(2)}, u32[]{:S(2)}) collective-permute-start(bf16[2,1,160,128]{3,2,1,0:T(8,128)(2,1)S(1)} %get-tuple-element.12), channel_id=1, source_target_pairs={{2,0},{3,1},{6,4},{7,5},{10,8},{11,9},{14,12},{15,13},{18,16},{19,... | collective-permute-start | bytes 245768 | tf_op jit(solution)/shard_map/ppermute | solution.py:24
  26.8 30.6 %collective-permute-start.2 = (bf16[2,38,160,128]{3,2,1,0:T(8,128)(2,1)}, bf16[2,38,160,128]{3,2,1,0:T(8,128)(2,1)}, u32[]{:S(2)}, u32[]{:S(2)}) collective-permute-start(bf16[2,38,160,128]{3,2,1,0:T(8,128)(2,1)} %pad_maximum_fusion.xo_ref), channel_id=1, source_target_pairs={{0,1},{1,0},{2,3},{3,2},{4,5},{5,4},{6,7},{7,6},{8,9},{9,8},{10,11... | collective-permute-start | bytes 9338888 | tf_op jit(solution)/shard_map/ppermute | solution.py:16
  81.6 45.7 %copy-start.5 = (f32[160]{0:T(256)S(1)}, f32[160]{0:T(256)}, u32[]{:S(2)}) copy-start(f32[160]{0:T(256)} %param.15) | copy-start | bytes 1924
  81.6 45.7 %copy-start.6 = (f32[160]{0:T(256)S(1)}, f32[160]{0:T(256)}, u32[]{:S(2)}) copy-start(f32[160]{0:T(256)} %param.14) | copy-start | bytes 1924
  83.5 43.8 %collective-permute-start.3 = (bf16[1,36,160,128]{3,2,1,0:T(8,128)(2,1)}, bf16[1,36,160,128]{3,2,1,0:T(8,128)(2,1)}, u32[]{:S(2)}, u32[]{:S(2)}) collective-permute-start(bf16[1,36,160,128]{3,2,1,0:T(8,128)(2,1)} %get-tuple-element.9), channel_id=1, source_target_pairs={{0,4},{4,8},{8,12},{1,5},{5,9},{9,13},{2,6},{6,10},{10,14},{3,7},{... | collective-permute-start | bytes 4423688 | tf_op jit(solution)/shard_map/ppermute | solution.py:255
  88.2 39.1 %collective-permute-start.4 = (bf16[1,36,160,128]{3,2,1,0:T(8,128)(2,1)}, bf16[1,36,160,128]{3,2,1,0:T(8,128)(2,1)}, u32[]{:S(2)}, u32[]{:S(2)}) collective-permute-start(bf16[1,36,160,128]{3,2,1,0:T(8,128)(2,1)} %get-tuple-element.10), channel_id=1, source_target_pairs={{4,0},{8,4},{12,8},{5,1},{9,5},{13,9},{6,2},{10,6},{14,10},{7,3},{... | collective-permute-start | bytes 4423688 | tf_op jit(solution)/shard_map/ppermute | solution.py:256
  127.3 7.7 %copy-start.1 = (bf16[3,80,160]{2,1,0:T(8,128)(2,1)S(1)}, bf16[3,80,160]{2,1,0:T(8,128)(2,1)}, u32[]{:S(2)}) copy-start(bf16[3,80,160]{2,1,0:T(8,128)(2,1)} %param.16) | copy-start | bytes 230404
  127.3 12.2 %copy-start.8 = (f32[160]{0:T(256)S(1)}, f32[160]{0:T(256)}, u32[]{:S(2)}) copy-start(f32[160]{0:T(256)} %param.17) | copy-start | bytes 1924
  135.0 23.1 %collective-permute-start.5 = (bf16[4,36,160,128]{3,2,1,0:T(8,128)(2,1)}, bf16[4,36,160,128]{3,2,1,0:T(8,128)(2,1)}, u32[]{:S(2)}, u32[]{:S(2)}) collective-permute-start(bf16[4,36,160,128]{3,2,1,0:T(8,128)(2,1)} %fusion.13.refs_0_.refs_1_.refs_2_), channel_id=1, source_target_pairs={{0,1},{1,0},{2,3},{3,2},{4,5},{5,4},{6,7},{7,6},{8,9},{9,8},{10,11... | collective-permute-start | bytes 17694728 | tf_op jit(solution)/shard_map/ppermute | solution.py:16
  135.0 6.3 %collective-permute-start.6 = (bf16[3,80,160]{2,1,0:T(8,128)(2,1)S(1)}, bf16[3,80,160]{2,1,0:T(8,128)(2,1)S(1)}, u32[]{:S(2)}, u32[]{:S(2)}) collective-permute-start(bf16[3,80,160]{2,1,0:T(8,128)(2,1)S(1)} %copy-done.1), channel_id=1, source_target_pairs={{0,12},{4,0},{8,4},{12,8},{1,13},{5,1},{9,5},{13,9},{2,14},{6,2},{... | collective-permute-start | bytes 230408 | tf_op jit(solution)/shard_map/ppermute | solution.py:34
  137.4 13.6 %collective-permute-start.8 = (bf16[3,80,160]{2,1,0:T(8,128)(2,1)S(1)}, bf16[3,80,160]{2,1,0:T(8,128)(2,1)S(1)}, u32[]{:S(2)}, u32[]{:S(2)}) collective-permute-start(bf16[3,80,160]{2,1,0:T(8,128)(2,1)S(1)} %copy-done.1), channel_id=1, source_target_pairs={{0,4},{4,8},{8,12},{12,0},{1,5},{5,9},{9,13},{13,1},{2,6},{6,10},{... | collective-permute-start | bytes 230408 | tf_op jit(solution)/shard_map/ppermute | solution.py:34
  137.4 12.9 %collective-permute-start.7 = (bf16[3,80,160]{2,1,0:T(8,128)(2,1)S(1)}, bf16[3,80,160]{2,1,0:T(8,128)(2,1)S(1)}, u32[]{:S(2)}, u32[]{:S(2)}) collective-permute-start(bf16[3,80,160]{2,1,0:T(8,128)(2,1)S(1)} %copy-done.1), channel_id=1, source_target_pairs={{0,8},{4,12},{8,0},{12,4},{1,9},{5,13},{9,1},{13,5},{2,10},{6,14},... | collective-permute-start | bytes 230408 | tf_op jit(solution)/shard_map/ppermute | solution.py:34

commit v6 on v5

--- a/solution.py
+++ b/solution.py
@@ -227,9 +227,11 @@
     tm_index = lax.axis_index("tm")
     tm_count = lax.axis_size("tm")
 
-    spatial_full = lax.all_gather(spatial_weight, "tm", axis=2, tiled=True).reshape(9, C, local_chan)
-    temporal_pieces = gather_tm(temporal_weight)
-    temporal_full = jnp.moveaxis(temporal_pieces, 0, 1).reshape(3, C, local_chan)
+    piece = spatial_weight.shape[2]
+    merged = jnp.concatenate([spatial_weight.reshape(9, piece, local_chan), temporal_weight], axis=0)
+    full_weight = lax.all_gather(merged, "tm", axis=1, tiled=True)
+    spatial_full = full_weight[:9]
+    temporal_full = full_weight[9:]
     spatial_full = spatial_full.reshape(3, 3, C, local_chan)
 
     values = video.astype(jnp.float32)

time: 175 us -> 202 us (1.15)
  waiting for transfers between devices: 15.2 us -> 65.1 us
  blocking collectives: 70 us -> 40.4 us
  between operations: 0.35 us -> 13.7 us
  starting transfers between devices: 15 us -> 9.27 us
    all_gather x0 -> x1, waiting for transfers between devices: none -> 55.3 us  [body(): full_weight = lax.all_gather(merged, 'tm', axis=1, tiled=True)]
    all_gather x1 -> x0, blocking collectives: 28.9 us -> none  [body(): lax.all_gather(spatial_weight, 'tm', axis=2, tiled=True)]
    ppermute x3 -> x0, waiting for transfers between devices: 10.1 us -> none  [gather_tm(): pieces.append(lax.ppermute(piece, 'tm', pairs))]
    ppermute x2, waiting for transfers between devices: 0.01 us -> 4.72 us  [swap_chan(): return lax.ppermute(block, 'chan', [(0, 1), (1, 0)])]
    ppermute x3 -> x0, starting transfers between devices: 3.81 us -> none  [gather_tm(): pieces.append(lax.ppermute(piece, 'tm', pairs))]
    transpose x3 -> x0, local copies, waits for them, and re-layouts: 3.05 us -> none  [the longest x2 2.13 us: body(): jnp.moveaxis(temporal_pieces, 0, 1).reshape(3, C, local_chan)]
    unnamed x25 -> x21, local copies, waits for them, and re-layouts: 4.65 us -> 6.08 us
  transfers between devices with their start and end apart: 9 -> 7, of which waited for: 4 -> 4; matrix products, arithmetic and copies ran while one was open for 8% -> 7% of each run, Pallas kernels for 0% -> 0%
where the time goes in v6:
time: 202 us
  waiting for transfers between devices  65.1 us (32%)
  blocking collectives  40.4 us (20%)
  Pallas kernels  40.2 us (20%)
  other arithmetic  19.3 us (10%)
  local copies, waits for them, and re-layouts  13.9 us (7%)
  between operations  13.7 us (7%)
  starting transfers between devices  9.27 us (5%)
    all_gather x1, waiting for transfers between devices, body(): full_weight = lax.all_gather(merged, 'tm', axis=1, tiled=True)  55.3 us
    psum x3, blocking collectives, group_stats(): table = lax.psum(table, name)  40.4 us
    pallas_call x1, Pallas kernels, spatial_call(): pl.pallas_call(spatial_kernel, out_shape=jax.ShapeDtypeStruct(residual.sh...  24.2 us
    pallas_call x1, Pallas kernels, temporal_call(): pl.pallas_call(temporal_kernel, out_shape=jax.ShapeDtypeStruct(residual.s...  16 us
    select_n x1, other arithmetic, body(): jnp.where(inside[:, None, None, None], act_two, jnp.zeros_like(act_two))  7.66 us
    unnamed x21, local copies, waits for them, and re-layouts  6.08 us
    ppermute x2, waiting for transfers between devices, swap_chan(): return lax.ppermute(block, 'chan', [(0, 1), (1, 0)])  4.72 us
    ppermute x1, waiting for transfers between devices, row_halo(): high = lax.ppermute(block[:, :1], 'height', backward)  4.3 us
  transfers between devices with their start and end apart: 7, of which 4 were waited for; matrix products, arithmetic and copies ran while one was open for 7% of the time, Pallas kernels for 0%

profile of v6, /device:TPU:0, one launch (start us, length us, event | category | flops | bytes accessed | tf_op | source)
XLA Modules:
  0.0 201.9 jit_solution(17733671054067848961)
XLA Ops:
  6.5 2.5 %convert_reduce_fusion = f32[2,160]{1,0:T(2,128)S(1)} fusion(bf16[2,36,160,128]{3,2,1,0:T(8,128)(2,1)} %res_ref.1), kind=kLoop, calls=%fused_computation.3 | loop fusion | flops 2948800 | bytes 2950400 | tf_op jit(solution)/shard_map/reduce_sum | solution.py:43
  9.0 0.1 reduce_sum.101
  9.1 0.1 reduce_sum.120
  9.2 0.1 sub.71
  9.3 0.1 sub.72
  9.4 2.7 %fusion.3 = f32[2,160]{1,0:T(2,128)S(1)} fusion(bf16[2,36,160,128]{3,2,1,0:T(8,128)(2,1)} %res_ref.1, f32[2,160]{1,0:T(2,128)S(1)} %sub.72), kind=kLoop, calls=%fused_computation.9 | loop fusion | flops 5897920 | bytes 2951680 | tf_op jit(solution)/shard_map/reduce_sum | solution.py:45
  12.1 0.1 reduce_sum.122
  12.2 0.1 reduce_sum.123
  12.3 5.8 %psum.21 = f32[2,2,2,16]{3,2,0,1:T(2,128)S(1)} all-reduce(f32[2,2,2,16]{3,2,0,1:T(2,128)S(1)} %fusion.16), channel_id=1, replica_groups=mesh['groups'=2,'tm'=4,'height'=2,'chan'=2] {'height'}, use_global_device_ids=true, to_apply=%region_4.5 | all-reduce | flops 128 | bytes 1024 | tf_op jit(solution)/shard_map/psum | solution.py:56
  18.2 0.1 mul.90
  18.3 0.1 mul.91
  18.4 0.1 sub.75
  18.4 0.1 sub.76
  18.5 0.0 copy-done
  18.6 0.0 copy-start.1
  18.6 0.0 copy-start.2
  18.6 2.3 %fusion.12 = bf16[2,36,160,128]{3,2,1,0:T(8,128)(2,1)S(1)} fusion(bf16[2,36,160,128]{3,2,1,0:T(8,128)(2,1)S(1)} %copy-done, f32[160]{0:T(256)S(1)} %copy-done.3, f32[160]{0:T(256)S(1)} %copy-done.4, f32[2,160]{1,0:T(2,128)S(1)} %mul.91, f32[2,160]{1,0:T(2,128)S(1)} %sub.76), kind=kLoop, calls=%fused_computation.18 | loop fusion | flops 14745600 | bytes 5902080 | tf_op jit(solution)/shard_map/convert_element_type | solution.py:73
  20.9 0.0 copy-start.7
  20.9 4.0 %collective-permute-start = (bf16[2,1,160,128]{3,2,1,0:T(8,128)(2,1)S(1)}, bf16[2,1,160,128]{3,2,1,0:T(8,128)(2,1)S(1)}, u32[]{:S(2)}, u32[]{:S(2)}) collective-permute-start(bf16[2,1,160,128]{3,2,1,0:T(8,128)(2,1)S(1)} %get-tuple-element.11), channel_id=1, source_target_pairs={{0,2},{1,3},{4,6},{5,7},{8,10},{9,11},{12,14},{13,15},{16,18},{17,... | collective-permute-start | bytes 245768 | tf_op jit(solution)/shard_map/ppermute | solution.py:23
  24.9 1.3 collective-permute-start.1
  26.2 0.7 collective-permute-done
  26.9 4.3 %collective-permute-done.1 = bf16[2,1,160,128]{3,2,1,0:T(8,128)(2,1)S(1)} collective-permute-done((bf16[2,1,160,128]{3,2,1,0:T(8,128)(2,1)S(1)}, bf16[2,1,160,128]{3,2,1,0:T(8,128)(2,1)S(1)}, u32[]{:S(2)}, u32[]{:S(2)}) %collective-permute-start.1) | collective-permute-done | bytes 81952 | tf_op jit(solution)/shard_map/ppermute | solution.py:24
  31.2 2.1 %pad_maximum_fusion.xo_ref = bf16[2,38,160,128]{3,2,1,0:T(8,128)(2,1)} fusion(bf16[2,1,160,128]{3,2,1,0:T(8,128)(2,1)S(1)} %collective-permute-done.1, bf16[2,36,160,128]{3,2,1,0:T(8,128)(2,1)S(1)} %fusion.12, bf16[2,1,160,128]{3,2,1,0:T(8,128)(2,1)S(1)} %collective-permute-done), kind=kLoop, calls=%fused_computation.20 | loop fusion | flops 3112960 | bytes 6225920 | tf_op jit(solution)/shard_map/concatenate | solution.py:25
  33.3 0.0 collective-permute-start.2
  33.3 0.1 pad_maximum_fusion.1
  33.4 1.0 copy.36
  34.4 0.0 all-gather.2.cloned.1.call-update
  34.5 0.1 copy.38.b_ref
  34.6 55.3 %all-gather.2.cloned.1.call-done = bf16[12,320,160]{2,0,1:T(8,128)(2,1)} async-done(((bf16[12,80,160]{2,0,1:T(8,128)(2,1)}), bf16[12,320,160]{2,0,1:T(8,128)(2,1)}) %all-gather.2.cloned.1.call-update) | async-done | bytes 1228816 | tf_op jit(solution)/shard_map/all_gather | solution.py:232
  89.9 3.7 %copy.42 = bf16[9,320,160]{1,2,0:T(8,128)(2,1)S(1)} copy(bf16[9,320,160]{2,0,1:T(8,128)(2,1)} %bitcast.41) | data formatting | bytes 1843200
  93.6 0.7 constant_dynamic-slice_fusion.2
  94.2 0.0 collective-permute-done.2.xt_ref
  94.3 24.2 %shard_map.91.refs_8_ = bf16[2,36,160,128]{3,2,1,0:T(8,128)(2,1)S(1)} custom-call(bf16[2,38,160,128]{3,2,1,0:T(8,128)(2,1)} %pad_maximum_fusion.xo_ref, bf16[2,38,160,128]{3,2,1,0:T(8,128)(2,1)} %collective-permute-done.2.xt_ref, bf16[3,480,160]{2,1,0:T(8,128)(2,1)S(1)} %get-tuple-element.14.wo_ref, bf16[3,480,160]{2,1,0:T(8,128)(2,1)S(1)} %get-tuple-element.13.wt_ref, ...), custom_call_target="tpu_custom_call" | custom-call | flops 8493465600 | bytes 13045760 | tf_op jit(solution)/shard_map/pallas_call | solution.py:118
  118.5 0.0 copy-start.5
  118.5 0.0 copy-start.6
  118.5 1.9 fusion.21
  120.4 2.7 %collective-permute-start.3 = (bf16[1,36,160,128]{3,2,1,0:T(8,128)(2,1)}, bf16[1,36,160,128]{3,2,1,0:T(8,128)(2,1)}, u32[]{:S(2)}, u32[]{:S(2)}) collective-permute-start(bf16[1,36,160,128]{3,2,1,0:T(8,128)(2,1)} %get-tuple-element.9), channel_id=1, source_target_pairs={{0,4},{4,8},{8,12},{1,5},{5,9},{9,13},{2,6},{6,10},{10,14},{3,7},{... | collective-permute-start | bytes 4423688 | tf_op jit(solution)/shard_map/ppermute | solution.py:257
  123.1 1.3 collective-permute-start.4
  124.4 0.5 convert_reduce_fusion.1
  124.9 0.1 reduce_sum.128
  125.0 0.1 reduce_sum.129
  125.1 0.1 sub.82
  125.2 0.1 sub.83
  125.3 0.9 fusion.1
  126.2 0.1 reduce_sum.131
  126.3 0.1 reduce_sum.132
  126.5 5.0 %psum.22 = f32[8,2,16]{2,0,1:T(8,128)S(1)} all-reduce(f32[8,2,16]{2,0,1:T(8,128)S(1)} %dynamic_update_slice.9), channel_id=1, replica_groups=mesh['groups'=2,'tm'=4,'height'=2,'chan'=2] {'height'}, use_global_device_ids=true, to_apply=%region_12.13 | all-reduce | flops 256 | bytes 2048 | tf_op jit(solution)/shard_map/psum | solution.py:56
  131.5 29.5 %psum.23 = f32[8,2,16]{2,0,1:T(8,128)S(1)} all-reduce(f32[8,2,16]{2,0,1:T(8,128)S(1)} %psum.22), channel_id=1, replica_groups=mesh['groups'=2,'tm'=4,'height'=2,'chan'=2] {'tm'}, use_global_device_ids=true, to_apply=%region_13.14 | all-reduce | flops 256 | bytes 2048 | tf_op jit(solution)/shard_map/psum | solution.py:56
  161.1 0.1 mul.103
  161.2 0.1 mul.104
  161.3 0.1 sub.86
  161.3 0.1 sub.87
  161.4 0.0 copy-start.8
  161.5 0.0 collective-permute-done.3
  161.5 0.0 collective-permute-done.4
  161.5 7.7 %fusion.13.refs_0_.refs_1_.refs_2_ = bf16[4,36,160,128]{3,2,1,0:T(8,128)(2,1)} fusion(bf16[1,36,160,128]{3,2,1,0:T(8,128)(2,1)} %collective-permute-done.4, bf16[2,36,160,128]{3,2,1,0:T(8,128)(2,1)S(1)} %shard_map.91.refs_8_, bf16[1,36,160,128]{3,2,1,0:T(8,128)(2,1)} %collective-permute-done.3, f32[160]{0:T(256)S(1)} %copy-done.5, f32[160]{0:T(256)S(1)} %copy-done.6, ...), kind=kLoop, calls=%fused_computation.19 | loop fusion | flops 38338560 | bytes 11799044 | tf_op jit(solution)/shard_map/jit(_where)/select_n | solution.py:269
  169.2 0.0 collective-permute-start.5
  169.2 0.1 copy.41.refs_9_
  169.3 1.7 slice.49
  170.9 1.1 constant_dynamic-slice_fusion
  172.0 1.2 copy.45
  173.2 1.2 copy.44
  174.4 4.7 %collective-permute-done.5.refs_3_.refs_4_.refs_5_ = bf16[4,36,160,128]{3,2,1,0:T(8,128)(2,1)} collective-permute-done((bf16[4,36,160,128]{3,2,1,0:T(8,128)(2,1)}, bf16[4,36,160,128]{3,2,1,0:T(8,128)(2,1)}, u32[]{:S(2)}, u32[]{:S(2)}) %collective-permute-start.5) | collective-permute-done | bytes 5898272 | tf_op jit(solution)/shard_map/ppermute | solution.py:16
  179.1 16.0 %shard_map.92 = bf16[2,36,160,128]{3,2,1,0:T(8,128)(2,1)} custom-call(bf16[4,36,160,128]{3,2,1,0:T(8,128)(2,1)} %fusion.13.refs_0_.refs_1_.refs_2_, bf16[4,36,160,128]{3,2,1,0:T(8,128)(2,1)} %fusion.13.refs_0_.refs_1_.refs_2_, bf16[4,36,160,128]{3,2,1,0:T(8,128)(2,1)} %fusion.13.refs_0_.refs_1_.refs_2_, ...), custom_call_target="tpu_custom_call" | custom-call | flops 2831155200 | bytes 23900160 | tf_op jit(solution)/shard_map/pallas_call | solution.py:171
  (29 shorter events, 0.2 us)
Async XLA Ops:
  6.5 12.0 %copy-start = (bf16[2,36,160,128]{3,2,1,0:T(8,128)(2,1)S(1)}, bf16[2,36,160,128]{3,2,1,0:T(8,128)(2,1)}, u32[]{:S(2)}) copy-start(bf16[2,36,160,128]{3,2,1,0:T(8,128)(2,1)} %res_ref.1) | copy-start | bytes 8847364
  6.5 12.0 %copy-start.3 = (f32[160]{0:T(256)S(1)}, f32[160]{0:T(256)}, u32[]{:S(2)}) copy-start(f32[160]{0:T(256)} %param.11) | copy-start | bytes 1924
  6.5 12.0 %copy-start.4 = (f32[160]{0:T(256)S(1)}, f32[160]{0:T(256)}, u32[]{:S(2)}) copy-start(f32[160]{0:T(256)} %param.10) | copy-start | bytes 1924
  6.5 83.3 %all-gather.2.cloned.1.call-start = ((), (), s32[]{:S(2)}) async-start(), calls=%async_computation | async-start | bytes 3276800 | tf_op jit(solution)/shard_map/all_gather | solution.py:232
  18.6 14.8 %copy-start.1 = (bf16[3,3,80,160]{3,2,1,0:T(8,128)(2,1)S(1)}, bf16[3,3,80,160]{3,2,1,0:T(8,128)(2,1)}, u32[]{:S(2)}) copy-start(bf16[3,3,80,160]{3,2,1,0:T(8,128)(2,1)} %param.12) | copy-start | bytes 691204
  18.6 14.7 %copy-start.2 = (bf16[3,80,160]{2,1,0:T(8,128)(2,1)S(1)}, bf16[3,80,160]{2,1,0:T(8,128)(2,1)}, u32[]{:S(2)}) copy-start(bf16[3,80,160]{2,1,0:T(8,128)(2,1)} %param.16) | copy-start | bytes 230404
  20.9 13.5 %copy-start.7 = (f32[160]{0:T(256)S(1)}, f32[160]{0:T(256)}, u32[]{:S(2)}) copy-start(f32[160]{0:T(256)} %param.13) | copy-start | bytes 1924
  20.9 6.0 %collective-permute-start = (bf16[2,1,160,128]{3,2,1,0:T(8,128)(2,1)S(1)}, bf16[2,1,160,128]{3,2,1,0:T(8,128)(2,1)S(1)}, u32[]{:S(2)}, u32[]{:S(2)}) collective-permute-start(bf16[2,1,160,128]{3,2,1,0:T(8,128)(2,1)S(1)} %get-tuple-element.11), channel_id=1, source_target_pairs={{0,2},{1,3},{4,6},{5,7},{8,10},{9,11},{12,14},{13,15},{16,18},{17,... | collective-permute-start | bytes 245768 | tf_op jit(solution)/shard_map/ppermute | solution.py:23
  24.9 6.3 %collective-permute-start.1 = (bf16[2,1,160,128]{3,2,1,0:T(8,128)(2,1)S(1)}, bf16[2,1,160,128]{3,2,1,0:T(8,128)(2,1)S(1)}, u32[]{:S(2)}, u32[]{:S(2)}) collective-permute-start(bf16[2,1,160,128]{3,2,1,0:T(8,128)(2,1)S(1)} %get-tuple-element.12), channel_id=1, source_target_pairs={{2,0},{3,1},{6,4},{7,5},{10,8},{11,9},{14,12},{15,13},{18,16},{19,... | collective-permute-start | bytes 245768 | tf_op jit(solution)/shard_map/ppermute | solution.py:24
  33.3 60.9 %collective-permute-start.2 = (bf16[2,38,160,128]{3,2,1,0:T(8,128)(2,1)}, bf16[2,38,160,128]{3,2,1,0:T(8,128)(2,1)}, u32[]{:S(2)}, u32[]{:S(2)}) collective-permute-start(bf16[2,38,160,128]{3,2,1,0:T(8,128)(2,1)} %pad_maximum_fusion.xo_ref), channel_id=1, source_target_pairs={{0,1},{1,0},{2,3},{3,2},{4,5},{5,4},{6,7},{7,6},{8,9},{9,8},{10,11... | collective-permute-start | bytes 9338888 | tf_op jit(solution)/shard_map/ppermute | solution.py:16
  118.5 43.0 %copy-start.5 = (f32[160]{0:T(256)S(1)}, f32[160]{0:T(256)}, u32[]{:S(2)}) copy-start(f32[160]{0:T(256)} %param.15) | copy-start | bytes 1924
  118.5 43.0 %copy-start.6 = (f32[160]{0:T(256)S(1)}, f32[160]{0:T(256)}, u32[]{:S(2)}) copy-start(f32[160]{0:T(256)} %param.14) | copy-start | bytes 1924
  120.4 41.1 %collective-permute-start.3 = (bf16[1,36,160,128]{3,2,1,0:T(8,128)(2,1)}, bf16[1,36,160,128]{3,2,1,0:T(8,128)(2,1)}, u32[]{:S(2)}, u32[]{:S(2)}) collective-permute-start(bf16[1,36,160,128]{3,2,1,0:T(8,128)(2,1)} %get-tuple-element.9), channel_id=1, source_target_pairs={{0,4},{4,8},{8,12},{1,5},{5,9},{9,13},{2,6},{6,10},{10,14},{3,7},{... | collective-permute-start | bytes 4423688 | tf_op jit(solution)/shard_map/ppermute | solution.py:257
  123.1 38.4 %collective-permute-start.4 = (bf16[1,36,160,128]{3,2,1,0:T(8,128)(2,1)}, bf16[1,36,160,128]{3,2,1,0:T(8,128)(2,1)}, u32[]{:S(2)}, u32[]{:S(2)}) collective-permute-start(bf16[1,36,160,128]{3,2,1,0:T(8,128)(2,1)} %get-tuple-element.10), channel_id=1, source_target_pairs={{4,0},{8,4},{12,8},{5,1},{9,5},{13,9},{6,2},{10,6},{14,10},{7,3},{... | collective-permute-start | bytes 4423688 | tf_op jit(solution)/shard_map/ppermute | solution.py:258
  161.4 7.7 %copy-start.8 = (f32[160]{0:T(256)S(1)}, f32[160]{0:T(256)}, u32[]{:S(2)}) copy-start(f32[160]{0:T(256)} %param.17) | copy-start | bytes 1924
  169.2 9.9 %collective-permute-start.5 = (bf16[4,36,160,128]{3,2,1,0:T(8,128)(2,1)}, bf16[4,36,160,128]{3,2,1,0:T(8,128)(2,1)}, u32[]{:S(2)}, u32[]{:S(2)}) collective-permute-start(bf16[4,36,160,128]{3,2,1,0:T(8,128)(2,1)} %fusion.13.refs_0_.refs_1_.refs_2_), channel_id=1, source_target_pairs={{0,1},{1,0},{2,3},{3,2},{4,5},{5,4},{6,7},{7,6},{8,9},{9,8},{10,11... | collective-permute-start | bytes 17694728 | tf_op jit(solution)/shard_map/ppermute | solution.py:16
Sparse Core Ops, SparseCore 0:
  34.6 55.2 all-gather.1

commit v7 on v5

--- a/solution.py
+++ b/solution.py
@@ -84,7 +84,7 @@
     return jnp.concatenate([ref[0, first], ref[0, first + 1]], axis=1)
 
 
-def spatial_kernel(xo_ref, xt_ref, wo_ref, wt_ref, res_ref, b_ref, o_ref):
+def spatial_kernel(xo_ref, xt_ref, wo_ref, wt_ref, res_ref, b_ref, early_ref, o_ref):
     rows, local_chan, width = o_ref.shape[1], o_ref.shape[2], o_ref.shape[3]
     lane = lax.broadcasted_iota(jnp.int32, (local_chan, width), 1)
     bias = b_ref[...]
@@ -111,7 +111,7 @@
     lax.fori_loop(0, rows // 2, two_rows, 0)
 
 
-def spatial_call(own, other, weight_own, weight_other, residual, bias):
+def spatial_call(own, other, weight_own, weight_other, residual, bias, early):
     frames, rows, local_chan, width = residual.shape
     act_spec = pl.BlockSpec((1, rows + 2, local_chan, width), lambda f: (f, 0, 0, 0))
     weight_spec = pl.BlockSpec((3, 3 * local_chan, local_chan), lambda f: (0, 0, 0))
@@ -126,6 +126,7 @@
             weight_spec,
             pl.BlockSpec((1, rows, local_chan, width), lambda f: (f, 0, 0, 0)),
             pl.BlockSpec((local_chan, 1), lambda f: (0, 0)),
+            pl.BlockSpec(memory_space=pl.ANY),
         ],
         out_specs=pl.BlockSpec((1, rows, local_chan, width), lambda f: (f, 0, 0, 0)),
         compiler_params=pltpu.CompilerParams(vmem_limit_bytes=48 * 1024 * 1024),
@@ -134,7 +135,7 @@
             transcendentals=0,
             bytes_accessed=4 * own.size + 4 * weight_own.size + 4 * residual.size,
         ),
-    )(own, other, weight_own, weight_other, residual, bias)
+    )(own, other, weight_own, weight_other, residual, bias, early)
 
 
 def temporal_kernel(*refs):
@@ -248,6 +249,7 @@
         lax.dynamic_slice_in_dim(spatial_rows, other_start, local_chan, axis=2),
         video,
         spatial_bias[:, None],
+        temporal_pieces,
     )
 
     forward = [(i, i + 1) for i in range(tm_count - 1)]

time: 175 us -> 169 us (0.966)
  local copies, waits for them, and re-layouts: 14.1 us -> 8.96 us
  waiting for transfers between devices: 15.2 us -> 11.1 us
  blocking collectives: 70 us -> 72.2 us
    ppermute x3, waiting for transfers between devices: 10.1 us -> 0.01 us  [gather_tm(): pieces.append(lax.ppermute(piece, 'tm', pairs))]
    ppermute x2, waiting for transfers between devices: 0.01 us -> 6.04 us  [swap_chan(): return lax.ppermute(block, 'chan', [(0, 1), (1, 0)])]
    unnamed x25 -> x27, local copies, waits for them, and re-layouts: 4.65 us -> 0.13 us
    all_gather x1, blocking collectives: 28.9 us -> 32.5 us  [body(): lax.all_gather(spatial_weight, 'tm', axis=2, tiled=True)]
  transfers between devices with their start and end apart: 9 -> 9, of which waited for: 4 -> 3; matrix products, arithmetic and copies ran while one was open for 8% -> 5% of each run, Pallas kernels for 0% -> 0%
where the time goes in v7:
time: 169 us
  blocking collectives  72.2 us (43%)
  Pallas kernels  40.5 us (24%)
  other arithmetic  19.2 us (11%)
  starting transfers between devices  16.5 us (10%)
  waiting for transfers between devices  11.1 us (7%)
  local copies, waits for them, and re-layouts  8.96 us (5%)
    psum x3, blocking collectives, group_stats(): table = lax.psum(table, name)  39.7 us
    all_gather x1, blocking collectives, body(): lax.all_gather(spatial_weight, 'tm', axis=2, tiled=True)  32.5 us
    pallas_call x1, Pallas kernels, spatial_call(): pl.pallas_call(spatial_kernel, out_shape=jax.ShapeDtypeStruct(residual.sh...  24.5 us
    pallas_call x1, Pallas kernels, temporal_call(): pl.pallas_call(temporal_kernel, out_shape=jax.ShapeDtypeStruct(residual.s...  16 us
    select_n x1, other arithmetic, body(): jnp.where(inside[:, None, None, None], act_two, jnp.zeros_like(act_two))  7.66 us
    ppermute x2, waiting for transfers between devices, swap_chan(): return lax.ppermute(block, 'chan', [(0, 1), (1, 0)])  6.04 us
    ppermute x1, starting transfers between devices, body(): before = lax.ppermute(hidden[-1:], 'tm', forward)  5.39 us
    ppermute x3, starting transfers between devices, gather_tm(): pieces.append(lax.ppermute(piece, 'tm', pairs))  4.62 us
  transfers between devices with their start and end apart: 9, of which 3 were waited for; matrix products, arithmetic and copies ran while one was open for 5% of the time, Pallas kernels for 0%

profile of v7, /device:TPU:0, one launch (start us, length us, event | category | flops | bytes accessed | tf_op | source)
XLA Modules:
  0.0 169.0 jit_solution(2972722163601260682)
XLA Ops:
  0.0 2.5 %convert_reduce_fusion = f32[2,160]{1,0:T(2,128)S(1)} fusion(bf16[2,36,160,128]{3,2,1,0:T(8,128)(2,1)} %res_ref.1), kind=kLoop, calls=%fused_computation.3 | loop fusion | flops 2948800 | bytes 2950400 | tf_op jit(solution)/shard_map/reduce_sum | solution.py:43
  2.5 0.1 reduce_sum.101
  2.5 0.1 reduce_sum.120
  2.6 0.1 sub.75
  2.7 0.1 sub.76
  2.8 2.7 %fusion.3 = f32[2,160]{1,0:T(2,128)S(1)} fusion(bf16[2,36,160,128]{3,2,1,0:T(8,128)(2,1)} %res_ref.1, f32[2,160]{1,0:T(2,128)S(1)} %sub.76), kind=kLoop, calls=%fused_computation.9 | loop fusion | flops 5897920 | bytes 2951680 | tf_op jit(solution)/shard_map/reduce_sum | solution.py:45
  5.6 0.1 reduce_sum.122
  5.7 0.1 reduce_sum.123
  5.8 5.9 %psum.21 = f32[2,2,2,16]{3,2,0,1:T(2,128)S(1)} all-reduce(f32[2,2,2,16]{3,2,0,1:T(2,128)S(1)} %fusion.16), channel_id=1, replica_groups=mesh['groups'=2,'tm'=4,'height'=2,'chan'=2] {'height'}, use_global_device_ids=true, to_apply=%region_4.5 | all-reduce | flops 128 | bytes 1024 | tf_op jit(solution)/shard_map/psum | solution.py:56
  11.7 0.1 mul.90
  11.7 0.1 mul.91
  11.8 0.1 sub.79
  11.9 0.1 sub.80
  12.0 0.0 copy-start.2
  12.1 0.0 copy-start.8
  12.1 0.0 copy-start.3
  12.1 2.3 %fusion.12 = bf16[2,36,160,128]{3,2,1,0:T(8,128)(2,1)S(1)} fusion(bf16[2,36,160,128]{3,2,1,0:T(8,128)(2,1)S(1)} %copy-done, f32[160]{0:T(256)S(1)} %copy-done.4, f32[160]{0:T(256)S(1)} %copy-done.5, f32[2,160]{1,0:T(2,128)S(1)} %mul.91, f32[2,160]{1,0:T(2,128)S(1)} %sub.80), kind=kLoop, calls=%fused_computation.18 | loop fusion | flops 14745600 | bytes 5902080 | tf_op jit(solution)/shard_map/convert_element_type | solution.py:73
  14.4 4.0 %collective-permute-start = (bf16[2,1,160,128]{3,2,1,0:T(8,128)(2,1)S(1)}, bf16[2,1,160,128]{3,2,1,0:T(8,128)(2,1)S(1)}, u32[]{:S(2)}, u32[]{:S(2)}) collective-permute-start(bf16[2,1,160,128]{3,2,1,0:T(8,128)(2,1)S(1)} %get-tuple-element.11), channel_id=1, source_target_pairs={{0,2},{1,3},{4,6},{5,7},{8,10},{9,11},{12,14},{13,15},{16,18},{17,... | collective-permute-start | bytes 245768 | tf_op jit(solution)/shard_map/ppermute | solution.py:23
  18.4 1.3 collective-permute-start.1
  19.7 0.7 collective-permute-done
  20.4 4.3 %collective-permute-done.1 = bf16[2,1,160,128]{3,2,1,0:T(8,128)(2,1)S(1)} collective-permute-done((bf16[2,1,160,128]{3,2,1,0:T(8,128)(2,1)S(1)}, bf16[2,1,160,128]{3,2,1,0:T(8,128)(2,1)S(1)}, u32[]{:S(2)}, u32[]{:S(2)}) %collective-permute-start.1) | collective-permute-done | bytes 81952 | tf_op jit(solution)/shard_map/ppermute | solution.py:24
  24.7 2.1 %pad_maximum_fusion.xo_ref = bf16[2,38,160,128]{3,2,1,0:T(8,128)(2,1)} fusion(bf16[2,1,160,128]{3,2,1,0:T(8,128)(2,1)S(1)} %collective-permute-done.1, bf16[2,36,160,128]{3,2,1,0:T(8,128)(2,1)S(1)} %fusion.12, bf16[2,1,160,128]{3,2,1,0:T(8,128)(2,1)S(1)} %collective-permute-done), kind=kLoop, calls=%fused_computation.20 | loop fusion | flops 3112960 | bytes 6225920 | tf_op jit(solution)/shard_map/concatenate | solution.py:25
  26.8 0.0 collective-permute-start.2
  26.8 3.6 %collective-permute-start.3 = (bf16[3,80,160]{2,1,0:T(8,128)(2,1)S(1)}, bf16[3,80,160]{2,1,0:T(8,128)(2,1)S(1)}, u32[]{:S(2)}, u32[]{:S(2)}) collective-permute-start(bf16[3,80,160]{2,1,0:T(8,128)(2,1)S(1)} %copy-done.2), channel_id=1, source_target_pairs={{0,12},{4,0},{8,4},{12,8},{1,13},{5,1},{9,5},{13,9},{2,14},{6,2},{... | collective-permute-start | bytes 230408 | tf_op jit(solution)/shard_map/ppermute | solution.py:34
  30.4 0.0 collective-permute-start.5
  30.4 1.0 collective-permute-start.4
  31.4 0.1 copy.22.b_ref
  31.5 32.5 %all_gather.3 = bf16[3,3,320,160]{3,2,1,0:T(8,128)(2,1)S(1)} all-gather(bf16[3,3,80,160]{3,2,1,0:T(8,128)(2,1)S(1)} %copy-done.3), channel_id=1, replica_groups=mesh['groups'=2,'tm'=4,'height'=2,'chan'=2] {'tm'}, dimensions={2}, use_global_device_ids=true | all-gather | bytes 1152000 | tf_op jit(solution)/shard_map/all_gather | solution.py:231
  64.0 0.9 copy.21
  65.0 0.7 constant_dynamic-slice_fusion.1
  65.7 0.0 collective-permute-done.3
  65.7 0.0 collective-permute-done.4
  65.9 0.0 collective-permute-done.2.xt_ref
  65.9 24.5 %shard_map.91.refs_8_ = bf16[2,36,160,128]{3,2,1,0:T(8,128)(2,1)S(1)} custom-call(bf16[2,38,160,128]{3,2,1,0:T(8,128)(2,1)} %pad_maximum_fusion.xo_ref, bf16[2,38,160,128]{3,2,1,0:T(8,128)(2,1)} %collective-permute-done.2.xt_ref, bf16[3,480,160]{2,1,0:T(8,128)(2,1)S(1)} %get-tuple-element.14.wo_ref, bf16[3,480,160]{2,1,0:T(8,128)(2,1)S(1)} %get-tuple-element.13.wt_ref, ...), custom_call_target="tpu_custom_call" | custom-call | flops 8493465600 | bytes 13045760 | tf_op jit(solution)/shard_map/pallas_call | solution.py:118
  90.4 0.0 copy-start.6
  90.5 0.0 copy-start.7
  90.5 1.8 %fusion.21 = (bf16[1,36,160,128]{3,2,1,0:T(8,128)(2,1)}, bf16[1,36,160,128]{3,2,1,0:T(8,128)(2,1)}) fusion(bf16[2,36,160,128]{3,2,1,0:T(8,128)(2,1)S(1)} %shard_map.91.refs_8_), kind=kLoop, calls=%fused_computation.56 | loop fusion | bytes 5898240 | tf_op jit(solution)/shard_map/slice | solution.py:257
  92.3 5.4 %collective-permute-start.6 = (bf16[1,36,160,128]{3,2,1,0:T(8,128)(2,1)}, bf16[1,36,160,128]{3,2,1,0:T(8,128)(2,1)}, u32[]{:S(2)}, u32[]{:S(2)}) collective-permute-start(bf16[1,36,160,128]{3,2,1,0:T(8,128)(2,1)} %get-tuple-element.9), channel_id=1, source_target_pairs={{0,4},{4,8},{8,12},{1,5},{5,9},{9,13},{2,6},{6,10},{10,14},{3,7},{... | collective-permute-start | bytes 4423688 | tf_op jit(solution)/shard_map/ppermute | solution.py:257
  97.7 1.3 collective-permute-start.7
  99.0 0.5 convert_reduce_fusion.1
  99.5 0.1 reduce_sum.128
  99.5 0.1 reduce_sum.129
  99.7 0.1 sub.87
  99.8 0.1 sub.88
  99.9 0.9 fusion.1
  100.8 0.1 reduce_sum.131
  100.9 0.1 reduce_sum.132
  101.1 5.0 %psum.22 = f32[8,2,16]{2,0,1:T(8,128)S(1)} all-reduce(f32[8,2,16]{2,0,1:T(8,128)S(1)} %dynamic_update_slice.9), channel_id=1, replica_groups=mesh['groups'=2,'tm'=4,'height'=2,'chan'=2] {'height'}, use_global_device_ids=true, to_apply=%region_12.13 | all-reduce | flops 256 | bytes 2048 | tf_op jit(solution)/shard_map/psum | solution.py:56
  106.1 28.9 %psum.23 = f32[8,2,16]{2,0,1:T(8,128)S(1)} all-reduce(f32[8,2,16]{2,0,1:T(8,128)S(1)} %psum.22), channel_id=1, replica_groups=mesh['groups'=2,'tm'=4,'height'=2,'chan'=2] {'tm'}, use_global_device_ids=true, to_apply=%region_13.14 | all-reduce | flops 256 | bytes 2048 | tf_op jit(solution)/shard_map/psum | solution.py:56
  135.0 0.1 mul.103
  135.1 0.1 mul.104
  135.2 0.1 sub.91
  135.3 0.1 sub.92
  135.4 0.0 copy-start.9
  135.4 0.0 collective-permute-done.6
  135.4 0.0 collective-permute-done.7
  135.4 7.7 %fusion.13.refs_0_.refs_1_.refs_2_ = bf16[4,36,160,128]{3,2,1,0:T(8,128)(2,1)} fusion(bf16[1,36,160,128]{3,2,1,0:T(8,128)(2,1)} %collective-permute-done.7, bf16[2,36,160,128]{3,2,1,0:T(8,128)(2,1)S(1)} %shard_map.91.refs_8_, bf16[1,36,160,128]{3,2,1,0:T(8,128)(2,1)} %collective-permute-done.6, f32[160]{0:T(256)S(1)} %copy-done.6, f32[160]{0:T(256)S(1)} %copy-done.7, ...), kind=kLoop, calls=%fused_computation.19 | loop fusion | flops 38338560 | bytes 11799044 | tf_op jit(solution)/shard_map/jit(_where)/select_n | solution.py:269
  143.1 0.1 copy.25.refs_9_
  143.2 1.1 fusion.23
  144.3 1.1 copy.24
  145.3 1.4 reshape.107
  146.7 0.2 dynamic-slice_bitcast_fusion
  147.0 6.0 %collective-permute-done.8.refs_3_.refs_4_.refs_5_ = bf16[4,36,160,128]{3,2,1,0:T(8,128)(2,1)} collective-permute-done((bf16[4,36,160,128]{3,2,1,0:T(8,128)(2,1)}, bf16[4,36,160,128]{3,2,1,0:T(8,128)(2,1)}, u32[]{:S(2)}, u32[]{:S(2)}) %collective-permute-start.8) | collective-permute-done | bytes 5898272 | tf_op jit(solution)/shard_map/ppermute | solution.py:16
  153.0 16.0 %shard_map.92 = bf16[2,36,160,128]{3,2,1,0:T(8,128)(2,1)} custom-call(bf16[4,36,160,128]{3,2,1,0:T(8,128)(2,1)} %fusion.13.refs_0_.refs_1_.refs_2_, bf16[4,36,160,128]{3,2,1,0:T(8,128)(2,1)} %fusion.13.refs_0_.refs_1_.refs_2_, bf16[4,36,160,128]{3,2,1,0:T(8,128)(2,1)} %fusion.13.refs_0_.refs_1_.refs_2_, ...), custom_call_target="tpu_custom_call" | custom-call | flops 2831155200 | bytes 23900160 | tf_op jit(solution)/shard_map/pallas_call | solution.py:172
  (42 shorter events, 0.4 us)
Async XLA Ops:
  0.0 12.0 %copy-start = (bf16[2,36,160,128]{3,2,1,0:T(8,128)(2,1)S(1)}, bf16[2,36,160,128]{3,2,1,0:T(8,128)(2,1)}, u32[]{:S(2)}) copy-start(bf16[2,36,160,128]{3,2,1,0:T(8,128)(2,1)} %res_ref.1) | copy-start | bytes 8847364
  0.0 12.0 %copy-start.4 = (f32[160]{0:T(256)S(1)}, f32[160]{0:T(256)}, u32[]{:S(2)}) copy-start(f32[160]{0:T(256)} %param.11) | copy-start | bytes 1924
  0.0 12.0 %copy-start.5 = (f32[160]{0:T(256)S(1)}, f32[160]{0:T(256)}, u32[]{:S(2)}) copy-start(f32[160]{0:T(256)} %param.10) | copy-start | bytes 1924
  12.0 14.8 %copy-start.2 = (bf16[3,80,160]{2,1,0:T(8,128)(2,1)S(1)}, bf16[3,80,160]{2,1,0:T(8,128)(2,1)}, u32[]{:S(2)}) copy-start(bf16[3,80,160]{2,1,0:T(8,128)(2,1)} %param.16) | copy-start | bytes 230404
  12.1 19.4 %copy-start.8 = (f32[160]{0:T(256)S(1)}, f32[160]{0:T(256)}, u32[]{:S(2)}) copy-start(f32[160]{0:T(256)} %param.13) | copy-start | bytes 1924
  12.1 19.5 %copy-start.3 = (bf16[3,3,80,160]{3,2,1,0:T(8,128)(2,1)S(1)}, bf16[3,3,80,160]{3,2,1,0:T(8,128)(2,1)}, u32[]{:S(2)}) copy-start(bf16[3,3,80,160]{3,2,1,0:T(8,128)(2,1)} %param.12) | copy-start | bytes 691204
  14.4 6.0 %collective-permute-start = (bf16[2,1,160,128]{3,2,1,0:T(8,128)(2,1)S(1)}, bf16[2,1,160,128]{3,2,1,0:T(8,128)(2,1)S(1)}, u32[]{:S(2)}, u32[]{:S(2)}) collective-permute-start(bf16[2,1,160,128]{3,2,1,0:T(8,128)(2,1)S(1)} %get-tuple-element.11), channel_id=1, source_target_pairs={{0,2},{1,3},{4,6},{5,7},{8,10},{9,11},{12,14},{13,15},{16,18},{17,... | collective-permute-start | bytes 245768 | tf_op jit(solution)/shard_map/ppermute | solution.py:23
  18.4 6.3 %collective-permute-start.1 = (bf16[2,1,160,128]{3,2,1,0:T(8,128)(2,1)S(1)}, bf16[2,1,160,128]{3,2,1,0:T(8,128)(2,1)S(1)}, u32[]{:S(2)}, u32[]{:S(2)}) collective-permute-start(bf16[2,1,160,128]{3,2,1,0:T(8,128)(2,1)S(1)} %get-tuple-element.12), channel_id=1, source_target_pairs={{2,0},{3,1},{6,4},{7,5},{10,8},{11,9},{14,12},{15,13},{18,16},{19,... | collective-permute-start | bytes 245768 | tf_op jit(solution)/shard_map/ppermute | solution.py:24
  26.8 39.1 %collective-permute-start.2 = (bf16[2,38,160,128]{3,2,1,0:T(8,128)(2,1)}, bf16[2,38,160,128]{3,2,1,0:T(8,128)(2,1)}, u32[]{:S(2)}, u32[]{:S(2)}) collective-permute-start(bf16[2,38,160,128]{3,2,1,0:T(8,128)(2,1)} %pad_maximum_fusion.xo_ref), channel_id=1, source_target_pairs={{0,1},{1,0},{2,3},{3,2},{4,5},{5,4},{6,7},{7,6},{8,9},{9,8},{10,11... | collective-permute-start | bytes 9338888 | tf_op jit(solution)/shard_map/ppermute | solution.py:16
  26.8 38.9 %collective-permute-start.3 = (bf16[3,80,160]{2,1,0:T(8,128)(2,1)S(1)}, bf16[3,80,160]{2,1,0:T(8,128)(2,1)S(1)}, u32[]{:S(2)}, u32[]{:S(2)}) collective-permute-start(bf16[3,80,160]{2,1,0:T(8,128)(2,1)S(1)} %copy-done.2), channel_id=1, source_target_pairs={{0,12},{4,0},{8,4},{12,8},{1,13},{5,1},{9,5},{13,9},{2,14},{6,2},{... | collective-permute-start | bytes 230408 | tf_op jit(solution)/shard_map/ppermute | solution.py:34
  30.4 35.4 %collective-permute-start.5 = (bf16[3,80,160]{2,1,0:T(8,128)(2,1)S(1)}, bf16[3,80,160]{2,1,0:T(8,128)(2,1)S(1)}, u32[]{:S(2)}, u32[]{:S(2)}) collective-permute-start(bf16[3,80,160]{2,1,0:T(8,128)(2,1)S(1)} %copy-done.2), channel_id=1, source_target_pairs={{0,4},{4,8},{8,12},{12,0},{1,5},{5,9},{9,13},{13,1},{2,6},{6,10},{... | collective-permute-start | bytes 230408 | tf_op jit(solution)/shard_map/ppermute | solution.py:34
  30.4 35.3 %collective-permute-start.4 = (bf16[3,80,160]{2,1,0:T(8,128)(2,1)S(1)}, bf16[3,80,160]{2,1,0:T(8,128)(2,1)S(1)}, u32[]{:S(2)}, u32[]{:S(2)}) collective-permute-start(bf16[3,80,160]{2,1,0:T(8,128)(2,1)S(1)} %copy-done.2), channel_id=1, source_target_pairs={{0,8},{4,12},{8,0},{12,4},{1,9},{5,13},{9,1},{13,5},{2,10},{6,14},... | collective-permute-start | bytes 230408 | tf_op jit(solution)/shard_map/ppermute | solution.py:34
  65.9 24.6 %copy-start.1 = (bf16[8,3,80,160]{3,2,1,0:T(8,128)(2,1)}, bf16[8,3,80,160]{3,2,1,0:T(8,128)(2,1)S(1)}, u32[]{:S(2)}) copy-start(bf16[8,3,80,160]{3,2,1,0:T(8,128)(2,1)S(1)} %bitcast_dynamic-update-slice_fusion.1) | copy-start | bytes 1843204
  90.4 44.9 %copy-start.6 = (f32[160]{0:T(256)S(1)}, f32[160]{0:T(256)}, u32[]{:S(2)}) copy-start(f32[160]{0:T(256)} %param.15) | copy-start | bytes 1924
  90.5 44.9 %copy-start.7 = (f32[160]{0:T(256)S(1)}, f32[160]{0:T(256)}, u32[]{:S(2)}) copy-start(f32[160]{0:T(256)} %param.14) | copy-start | bytes 1924
  92.3 43.1 %collective-permute-start.6 = (bf16[1,36,160,128]{3,2,1,0:T(8,128)(2,1)}, bf16[1,36,160,128]{3,2,1,0:T(8,128)(2,1)}, u32[]{:S(2)}, u32[]{:S(2)}) collective-permute-start(bf16[1,36,160,128]{3,2,1,0:T(8,128)(2,1)} %get-tuple-element.9), channel_id=1, source_target_pairs={{0,4},{4,8},{8,12},{1,5},{5,9},{9,13},{2,6},{6,10},{10,14},{3,7},{... | collective-permute-start | bytes 4423688 | tf_op jit(solution)/shard_map/ppermute | solution.py:257
  97.7 37.7 %collective-permute-start.7 = (bf16[1,36,160,128]{3,2,1,0:T(8,128)(2,1)}, bf16[1,36,160,128]{3,2,1,0:T(8,128)(2,1)}, u32[]{:S(2)}, u32[]{:S(2)}) collective-permute-start(bf16[1,36,160,128]{3,2,1,0:T(8,128)(2,1)} %get-tuple-element.10), channel_id=1, source_target_pairs={{4,0},{8,4},{12,8},{5,1},{9,5},{13,9},{6,2},{10,6},{14,10},{7,3},{... | collective-permute-start | bytes 4423688 | tf_op jit(solution)/shard_map/ppermute | solution.py:258
  135.4 7.7 %copy-start.9 = (f32[160]{0:T(256)S(1)}, f32[160]{0:T(256)}, u32[]{:S(2)}) copy-start(f32[160]{0:T(256)} %param.17) | copy-start | bytes 1924
  143.1 9.9 %collective-permute-start.8 = (bf16[4,36,160,128]{3,2,1,0:T(8,128)(2,1)}, bf16[4,36,160,128]{3,2,1,0:T(8,128)(2,1)}, u32[]{:S(2)}, u32[]{:S(2)}) collective-permute-start(bf16[4,36,160,128]{3,2,1,0:T(8,128)(2,1)} %fusion.13.refs_0_.refs_1_.refs_2_), channel_id=1, source_target_pairs={{0,1},{1,0},{2,3},{3,2},{4,5},{5,4},{6,7},{7,6},{8,9},{9,8},{10,11... | collective-permute-start | bytes 17694728 | tf_op jit(solution)/shard_map/ppermute | solution.py:16

commit v8 on v7

--- a/solution.py
+++ b/solution.py
@@ -228,15 +228,16 @@
     tm_index = lax.axis_index("tm")
     tm_count = lax.axis_size("tm")
 
-    spatial_full = lax.all_gather(spatial_weight, "tm", axis=2, tiled=True).reshape(9, C, local_chan)
+    spatial_pieces = gather_tm(spatial_weight)
     temporal_pieces = gather_tm(temporal_weight)
     temporal_full = jnp.moveaxis(temporal_pieces, 0, 1).reshape(3, C, local_chan)
-    spatial_full = spatial_full.reshape(3, 3, C, local_chan)
 
     values = video.astype(jnp.float32)
     grouped = values.reshape(frames, rows, local_groups, group_size, width)
     average, variance = group_stats(grouped, (1, 3, 4), ("height",))
     act_one = group_act(values, average, variance, norm1_gain, norm1_bias)
+    act_one, spatial_pieces = lax.optimization_barrier((act_one, spatial_pieces))
+    spatial_full = jnp.moveaxis(spatial_pieces, 0, 2).reshape(3, 3, C, local_chan)
 
     with_rows = row_halo(act_one)
     own_start = chan_index * local_chan

time: 169 us -> 173 us (1.024)
  blocking collectives: 72.2 us -> 40.2 us
  waiting for transfers between devices: 11.1 us -> 37.4 us
  local copies, waits for them, and re-layouts: 8.96 us -> 20.7 us
  other arithmetic: 19.2 us -> 15.2 us
    all_gather x1 -> x0, blocking collectives: 32.5 us -> none  [body(): lax.all_gather(spatial_weight, 'tm', axis=2, tiled=True)]
    ppermute x3 -> x6, waiting for transfers between devices: 0.01 us -> 29 us  [gather_tm(): pieces.append(lax.ppermute(piece, 'tm', pairs))]
    unnamed x27 -> x36, local copies, waits for them, and re-layouts: 0.13 us -> 8.91 us
    ppermute x3 -> x6, starting transfers between devices: 4.62 us -> 9.38 us  [gather_tm(): pieces.append(lax.ppermute(piece, 'tm', pairs))]
    ppermute x1, starting transfers between devices: 5.39 us -> 2.63 us  [body(): before = lax.ppermute(hidden[-1:], 'tm', forward)]
    ppermute x1, waiting for transfers between devices: 4.3 us -> 1.69 us  [row_halo(): high = lax.ppermute(block[:, :1], 'height', backward)]
    concatenate x1 -> x0, other arithmetic: 2.06 us -> none  [row_halo(): return jnp.concatenate([low, block, high], axis=1)]
    reduce_sum x4, other arithmetic: 3.88 us -> 2.05 us  [group_stats(): local_m2 = jnp.sum(centred * centred, axis=axes)]
  transfers between devices with their start and end apart: 9 -> 12, of which waited for: 3 -> 6; matrix products, arithmetic and copies ran while one was open for 5% -> 12% of each run, Pallas kernels for 0% -> 0%
where the time goes in v8:
time: 173 us; the launch traced here: 172 us
  blocking collectives  40.2 us (23%)
  Pallas kernels  40.2 us (23%)
  waiting for transfers between devices  37.4 us (22%)
  local copies, waits for them, and re-layouts  20.7 us (12%)
  starting transfers between devices  18.1 us (10%)
  other arithmetic  15.2 us (9%)
    psum x3, blocking collectives, group_stats(): table = lax.psum(table, name)  40.2 us
    ppermute x6, waiting for transfers between devices, gather_tm(): pieces.append(lax.ppermute(piece, 'tm', pairs))  29 us
    pallas_call x1, Pallas kernels, spatial_call(): pl.pallas_call(spatial_kernel, out_shape=jax.ShapeDtypeStruct(residual.sh...  24.2 us
    pallas_call x1, Pallas kernels, temporal_call(): pl.pallas_call(temporal_kernel, out_shape=jax.ShapeDtypeStruct(residual.s...  16 us
    ppermute x6, starting transfers between devices, gather_tm(): pieces.append(lax.ppermute(piece, 'tm', pairs))  9.38 us
    unnamed x36, local copies, waits for them, and re-layouts  8.91 us
    select_n x1, other arithmetic, body(): jnp.where(inside[:, None, None, None], act_two, jnp.zeros_like(act_two))  7.66 us
    ppermute x2, waiting for transfers between devices, swap_chan(): return lax.ppermute(block, 'chan', [(0, 1), (1, 0)])  6.04 us
  transfers between devices with their start and end apart: 12, of which 6 were waited for; matrix products, arithmetic and copies ran while one was open for 12% of the time, Pallas kernels for 0%

profile of v8, /device:TPU:0, one launch (start us, length us, event | category | flops | bytes accessed | tf_op | source)
XLA Modules:
  0.0 172.2 jit_solution(11085456204856977703)
XLA Ops:
  0.0 5.1 %collective-permute-start = (bf16[3,3,80,160]{3,2,1,0:T(8,128)(2,1)}, bf16[3,3,80,160]{3,2,1,0:T(8,128)(2,1)}, u32[]{:S(2)}, u32[]{:S(2)}) collective-permute-start(bf16[3,3,80,160]{3,2,1,0:T(8,128)(2,1)} %param.12), channel_id=1, source_target_pairs={{0,12},{4,0},{8,4},{12,8},{1,13},{5,1},{9,5},{13,9},{2,14},{6,2},{... | collective-permute-start | bytes 691208 | tf_op jit(solution)/shard_map/ppermute | solution.py:34
  5.1 1.0 collective-permute-start.1
  6.1 2.3 %convert_reduce_fusion = f32[2,160]{1,0:T(2,128)S(1)} fusion(bf16[2,36,160,128]{3,2,1,0:T(8,128)(2,1)} %res_ref.1), kind=kLoop, calls=%fused_computation.3 | loop fusion | flops 2948800 | bytes 2950400 | tf_op jit(solution)/shard_map/reduce_sum | solution.py:43
  8.4 0.1 reduce_sum.101
  8.5 0.1 reduce_sum.120
  8.6 0.1 sub.77
  8.7 0.1 sub.78
  8.8 0.9 fusion.3
  9.7 0.1 reduce_sum.122
  9.8 0.1 reduce_sum.123
  9.9 4.9 %psum.21 = f32[2,2,2,16]{3,2,0,1:T(2,128)S(1)} all-reduce(f32[2,2,2,16]{3,2,0,1:T(2,128)S(1)} %fusion.16), channel_id=1, replica_groups=mesh['groups'=2,'tm'=4,'height'=2,'chan'=2] {'height'}, use_global_device_ids=true, to_apply=%region_4.5 | all-reduce | flops 128 | bytes 1024 | tf_op jit(solution)/shard_map/psum | solution.py:56
  14.9 0.1 mul.90
  15.0 0.1 mul.91
  15.1 0.1 sub.81
  15.1 0.1 sub.82
  15.3 2.3 %fusion.12 = bf16[2,36,160,128]{3,2,1,0:T(8,128)(2,1)S(1)} fusion(bf16[2,36,160,128]{3,2,1,0:T(8,128)(2,1)S(1)} %copy-done, f32[160]{0:T(256)S(1)} %copy-done.4, f32[160]{0:T(256)S(1)} %copy-done.5, f32[2,160]{1,0:T(2,128)S(1)} %mul.91, f32[2,160]{1,0:T(2,128)S(1)} %sub.82), kind=kLoop, calls=%fused_computation.18 | loop fusion | flops 14745600 | bytes 5902080 | tf_op jit(solution)/shard_map/convert_element_type | solution.py:73
  17.7 1.0 bitcast_dynamic-update-slice_fusion.4
  18.7 18.2 %collective-permute-done.1 = bf16[3,3,80,160]{3,2,1,0:T(8,128)(2,1)} collective-permute-done((bf16[3,3,80,160]{3,2,1,0:T(8,128)(2,1)}, bf16[3,3,80,160]{3,2,1,0:T(8,128)(2,1)}, u32[]{:S(2)}, u32[]{:S(2)}) %collective-permute-start.1) | collective-permute-done | bytes 230432 | tf_op jit(solution)/shard_map/ppermute | solution.py:34
  36.9 1.0 bitcast_dynamic-update-slice_fusion.2
  37.9 1.0 bitcast_dynamic-update-slice_fusion
  38.9 1.0 bitcast_dynamic-update-slice_fusion.5
  40.0 1.0 bitcast_dynamic-update-slice_fusion.3
  41.0 1.0 bitcast_dynamic-update-slice_fusion.1
  42.0 0.1 constant_dynamic-slice_fusion.3
  42.1 3.4 %collective-permute-start.3 = (bf16[2,1,160,128]{3,2,1,0:T(8,128)(2,1)S(1)}, bf16[2,1,160,128]{3,2,1,0:T(8,128)(2,1)S(1)}, u32[]{:S(2)}, u32[]{:S(2)}) collective-permute-start(bf16[2,1,160,128]{3,2,1,0:T(8,128)(2,1)S(1)} %get-tuple-element.16), channel_id=1, source_target_pairs={{0,2},{1,3},{4,6},{5,7},{8,10},{9,11},{12,14},{13,15},{16,18},{17,... | collective-permute-start | bytes 245768 | tf_op jit(solution)/shard_map/ppermute | solution.py:23
  45.6 1.4 collective-permute-start.4
  47.0 0.6 collective-permute-done.3
  47.6 0.6 constant_dynamic-update-slice_fusion.2
  48.2 2.1 %constant_dynamic-update-slice_fusion.1 = bf16[2,38,160,128]{3,2,1,0:T(8,128)(2,1)} fusion(bf16[2,38,160,128]{3,2,1,0:T(8,128)(2,1)} %constant_dynamic-update-slice_fusion.2, bf16[2,36,160,128]{3,2,1,0:T(8,128)(2,1)S(1)} %fusion.12), kind=kLoop, calls=%fused_computation.39 | loop fusion | bytes 5898240
  50.3 1.7 collective-permute-done.4
  52.0 0.6 constant_dynamic-update-slice_fusion.xo_ref
  52.7 2.6 %collective-permute-start.6 = (bf16[3,80,160]{2,1,0:T(8,128)(2,1)S(1)}, bf16[3,80,160]{2,1,0:T(8,128)(2,1)S(1)}, u32[]{:S(2)}, u32[]{:S(2)}) collective-permute-start(bf16[3,80,160]{2,1,0:T(8,128)(2,1)S(1)} %copy-done.3), channel_id=1, source_target_pairs={{0,12},{4,0},{8,4},{12,8},{1,13},{5,1},{9,5},{13,9},{2,14},{6,2},{... | collective-permute-start | bytes 230408 | tf_op jit(solution)/shard_map/ppermute | solution.py:34
  55.3 0.6 collective-permute-start.7
  55.9 0.1 copy.21.b_ref
  56.1 2.9 %collective-permute-done.6 = bf16[3,80,160]{2,1,0:T(8,128)(2,1)S(1)} collective-permute-done((bf16[3,80,160]{2,1,0:T(8,128)(2,1)S(1)}, bf16[3,80,160]{2,1,0:T(8,128)(2,1)S(1)}, u32[]{:S(2)}, u32[]{:S(2)}) %collective-permute-start.6) | collective-permute-done | bytes 76832 | tf_op jit(solution)/shard_map/ppermute | solution.py:34
  59.0 7.9 %collective-permute-done.7 = bf16[3,80,160]{2,1,0:T(8,128)(2,1)S(1)} collective-permute-done((bf16[3,80,160]{2,1,0:T(8,128)(2,1)S(1)}, bf16[3,80,160]{2,1,0:T(8,128)(2,1)S(1)}, u32[]{:S(2)}, u32[]{:S(2)}) %collective-permute-start.7) | collective-permute-done | bytes 76832 | tf_op jit(solution)/shard_map/ppermute | solution.py:34
  67.1 0.9 copy-done.2
  68.0 1.1 copy.20
  69.1 1.0 reshape.109
  70.1 0.7 constant_dynamic-slice_fusion.1
  70.8 24.2 %shard_map.91.refs_8_ = bf16[2,36,160,128]{3,2,1,0:T(8,128)(2,1)S(1)} custom-call(bf16[2,38,160,128]{3,2,1,0:T(8,128)(2,1)} %constant_dynamic-update-slice_fusion.xo_ref, bf16[2,38,160,128]{3,2,1,0:T(8,128)(2,1)} %collective-permute-done.5.xt_ref, bf16[3,480,160]{2,1,0:T(8,128)(2,1)S(1)} %get-tuple-element.18.wo_ref, ...), custom_call_target="tpu_custom_call" | custom-call | flops 8493465600 | bytes 13045760 | tf_op jit(solution)/shard_map/pallas_call | solution.py:118
  95.1 1.8 %fusion.21 = (bf16[1,36,160,128]{3,2,1,0:T(8,128)(2,1)}, bf16[1,36,160,128]{3,2,1,0:T(8,128)(2,1)}) fusion(bf16[2,36,160,128]{3,2,1,0:T(8,128)(2,1)S(1)} %shard_map.91.refs_8_), kind=kLoop, calls=%fused_computation.67 | loop fusion | bytes 5898240 | tf_op jit(solution)/shard_map/slice | solution.py:258
  96.9 2.6 %collective-permute-start.9 = (bf16[1,36,160,128]{3,2,1,0:T(8,128)(2,1)}, bf16[1,36,160,128]{3,2,1,0:T(8,128)(2,1)}, u32[]{:S(2)}, u32[]{:S(2)}) collective-permute-start(bf16[1,36,160,128]{3,2,1,0:T(8,128)(2,1)} %get-tuple-element.13), channel_id=1, source_target_pairs={{0,4},{4,8},{8,12},{1,5},{5,9},{9,13},{2,6},{6,10},{10,14},{3,7},{... | collective-permute-start | bytes 4423688 | tf_op jit(solution)/shard_map/ppermute | solution.py:258
  99.5 1.3 collective-permute-start.10
  100.8 0.5 convert_reduce_fusion.1
  101.3 0.1 reduce_sum.128
  101.4 0.1 reduce_sum.129
  101.6 0.1 sub.90
  101.7 0.9 fusion.1
  102.6 0.1 reduce_sum.131
  102.7 0.1 reduce_sum.132
  102.9 5.0 %psum.22 = f32[8,2,16]{2,0,1:T(8,128)S(1)} all-reduce(f32[8,2,16]{2,0,1:T(8,128)S(1)} %dynamic_update_slice.9), channel_id=1, replica_groups=mesh['groups'=2,'tm'=4,'height'=2,'chan'=2] {'height'}, use_global_device_ids=true, to_apply=%region_12.13 | all-reduce | flops 256 | bytes 2048 | tf_op jit(solution)/shard_map/psum | solution.py:56
  107.9 30.2 %psum.23 = f32[8,2,16]{2,0,1:T(8,128)S(1)} all-reduce(f32[8,2,16]{2,0,1:T(8,128)S(1)} %psum.22), channel_id=1, replica_groups=mesh['groups'=2,'tm'=4,'height'=2,'chan'=2] {'tm'}, use_global_device_ids=true, to_apply=%region_13.14 | all-reduce | flops 256 | bytes 2048 | tf_op jit(solution)/shard_map/psum | solution.py:56
  138.2 0.1 mul.103
  138.3 0.1 mul.104
  138.4 0.1 sub.94
  138.6 7.7 %fusion.13.refs_0_.refs_1_.refs_2_ = bf16[4,36,160,128]{3,2,1,0:T(8,128)(2,1)} fusion(bf16[1,36,160,128]{3,2,1,0:T(8,128)(2,1)} %collective-permute-done.10, bf16[2,36,160,128]{3,2,1,0:T(8,128)(2,1)S(1)} %shard_map.91.refs_8_, bf16[1,36,160,128]{3,2,1,0:T(8,128)(2,1)} %collective-permute-done.9, f32[160]{0:T(256)S(1)} %copy-done.6, f32[160]{0:T(256)S(1)} %copy-done.7, ...), kind=kLoop, calls=%fused_computation.19 | loop fusion | flops 38338560 | bytes 11799044 | tf_op jit(solution)/shard_map/jit(_where)/select_n | solution.py:270
  146.3 0.1 copy.24.refs_9_
  146.4 1.1 fusion.23
  147.5 1.1 copy.23
  148.5 1.4 reshape.111
  149.9 0.2 dynamic-slice_bitcast_fusion
  150.2 6.0 %collective-permute-done.11.refs_3_.refs_4_.refs_5_ = bf16[4,36,160,128]{3,2,1,0:T(8,128)(2,1)} collective-permute-done((bf16[4,36,160,128]{3,2,1,0:T(8,128)(2,1)}, bf16[4,36,160,128]{3,2,1,0:T(8,128)(2,1)}, u32[]{:S(2)}, u32[]{:S(2)}) %collective-permute-start.11) | collective-permute-done | bytes 5898272 | tf_op jit(solution)/shard_map/ppermute | solution.py:16
  156.2 16.0 %shard_map.92 = bf16[2,36,160,128]{3,2,1,0:T(8,128)(2,1)} custom-call(bf16[4,36,160,128]{3,2,1,0:T(8,128)(2,1)} %fusion.13.refs_0_.refs_1_.refs_2_, bf16[4,36,160,128]{3,2,1,0:T(8,128)(2,1)} %fusion.13.refs_0_.refs_1_.refs_2_, bf16[4,36,160,128]{3,2,1,0:T(8,128)(2,1)} %fusion.13.refs_0_.refs_1_.refs_2_, ...), custom_call_target="tpu_custom_call" | custom-call | flops 2831155200 | bytes 23900160 | tf_op jit(solution)/shard_map/pallas_call | solution.py:172
  (59 shorter events, 0.6 us)
Async XLA Ops:
  0.0 8.8 %copy-start = (bf16[2,36,160,128]{3,2,1,0:T(8,128)(2,1)S(1)}, bf16[2,36,160,128]{3,2,1,0:T(8,128)(2,1)}, u32[]{:S(2)}) copy-start(bf16[2,36,160,128]{3,2,1,0:T(8,128)(2,1)} %res_ref.1) | copy-start | bytes 8847364
  0.0 15.3 %copy-start.4 = (f32[160]{0:T(256)S(1)}, f32[160]{0:T(256)}, u32[]{:S(2)}) copy-start(f32[160]{0:T(256)} %param.11) | copy-start | bytes 1924
  0.0 15.3 %copy-start.5 = (f32[160]{0:T(256)S(1)}, f32[160]{0:T(256)}, u32[]{:S(2)}) copy-start(f32[160]{0:T(256)} %param.10) | copy-start | bytes 1924
  0.0 17.6 %collective-permute-start = (bf16[3,3,80,160]{3,2,1,0:T(8,128)(2,1)}, bf16[3,3,80,160]{3,2,1,0:T(8,128)(2,1)}, u32[]{:S(2)}, u32[]{:S(2)}) collective-permute-start(bf16[3,3,80,160]{3,2,1,0:T(8,128)(2,1)} %param.12), channel_id=1, source_target_pairs={{0,12},{4,0},{8,4},{12,8},{1,13},{5,1},{9,5},{13,9},{2,14},{6,2},{... | collective-permute-start | bytes 691208 | tf_op jit(solution)/shard_map/ppermute | solution.py:34
  5.1 32.8 %collective-permute-start.2 = (bf16[3,3,80,160]{3,2,1,0:T(8,128)(2,1)}, bf16[3,3,80,160]{3,2,1,0:T(8,128)(2,1)}, u32[]{:S(2)}, u32[]{:S(2)}) collective-permute-start(bf16[3,3,80,160]{3,2,1,0:T(8,128)(2,1)} %param.12), channel_id=1, source_target_pairs={{0,4},{4,8},{8,12},{12,0},{1,5},{5,9},{9,13},{13,1},{2,6},{6,10},{... | collective-permute-start | bytes 691208 | tf_op jit(solution)/shard_map/ppermute | solution.py:34
  5.1 31.8 %collective-permute-start.1 = (bf16[3,3,80,160]{3,2,1,0:T(8,128)(2,1)}, bf16[3,3,80,160]{3,2,1,0:T(8,128)(2,1)}, u32[]{:S(2)}, u32[]{:S(2)}) collective-permute-start(bf16[3,3,80,160]{3,2,1,0:T(8,128)(2,1)} %param.12), channel_id=1, source_target_pairs={{0,8},{4,12},{8,0},{12,4},{1,9},{5,13},{9,1},{13,5},{2,10},{6,14},... | collective-permute-start | bytes 691208 | tf_op jit(solution)/shard_map/ppermute | solution.py:34
  9.7 7.9 %copy-start.1 = (bf16[3,3,80,160]{3,2,1,0:T(8,128)(2,1)S(1)}, bf16[3,3,80,160]{3,2,1,0:T(8,128)(2,1)}, u32[]{:S(2)}) copy-start(bf16[3,3,80,160]{3,2,1,0:T(8,128)(2,1)} %param.12) | copy-start | bytes 691204
  42.1 5.4 %collective-permute-start.3 = (bf16[2,1,160,128]{3,2,1,0:T(8,128)(2,1)S(1)}, bf16[2,1,160,128]{3,2,1,0:T(8,128)(2,1)S(1)}, u32[]{:S(2)}, u32[]{:S(2)}) collective-permute-start(bf16[2,1,160,128]{3,2,1,0:T(8,128)(2,1)S(1)} %get-tuple-element.16), channel_id=1, source_target_pairs={{0,2},{1,3},{4,6},{5,7},{8,10},{9,11},{12,14},{13,15},{16,18},{17,... | collective-permute-start | bytes 245768 | tf_op jit(solution)/shard_map/ppermute | solution.py:23
  45.5 7.1 %copy-start.3 = (bf16[3,80,160]{2,1,0:T(8,128)(2,1)S(1)}, bf16[3,80,160]{2,1,0:T(8,128)(2,1)}, u32[]{:S(2)}) copy-start(bf16[3,80,160]{2,1,0:T(8,128)(2,1)} %param.16) | copy-start | bytes 230404
  45.5 10.4 %copy-start.8 = (f32[160]{0:T(256)S(1)}, f32[160]{0:T(256)}, u32[]{:S(2)}) copy-start(f32[160]{0:T(256)} %param.13) | copy-start | bytes 1924
  45.6 6.5 %collective-permute-start.4 = (bf16[2,1,160,128]{3,2,1,0:T(8,128)(2,1)S(1)}, bf16[2,1,160,128]{3,2,1,0:T(8,128)(2,1)S(1)}, u32[]{:S(2)}, u32[]{:S(2)}) collective-permute-start(bf16[2,1,160,128]{3,2,1,0:T(8,128)(2,1)S(1)} %get-tuple-element.15), channel_id=1, source_target_pairs={{2,0},{3,1},{6,4},{7,5},{10,8},{11,9},{14,12},{15,13},{18,16},{19,... | collective-permute-start | bytes 245768 | tf_op jit(solution)/shard_map/ppermute | solution.py:24
  52.7 18.2 %collective-permute-start.5 = (bf16[2,38,160,128]{3,2,1,0:T(8,128)(2,1)}, bf16[2,38,160,128]{3,2,1,0:T(8,128)(2,1)}, u32[]{:S(2)}, u32[]{:S(2)}) collective-permute-start(bf16[2,38,160,128]{3,2,1,0:T(8,128)(2,1)} %constant_dynamic-update-slice_fusion.xo_ref), channel_id=1, source_target_pairs={{0,1},{1,0},{2,3},{3,2},{4,5},{5,4},{6,7},{7,6},{8,9},{9,8},{10,11... | collective-permute-start | bytes 9338888 | tf_op jit(solution)/shard_map/ppermute | solution.py:16
  52.7 6.3 %collective-permute-start.6 = (bf16[3,80,160]{2,1,0:T(8,128)(2,1)S(1)}, bf16[3,80,160]{2,1,0:T(8,128)(2,1)S(1)}, u32[]{:S(2)}, u32[]{:S(2)}) collective-permute-start(bf16[3,80,160]{2,1,0:T(8,128)(2,1)S(1)} %copy-done.3), channel_id=1, source_target_pairs={{0,12},{4,0},{8,4},{12,8},{1,13},{5,1},{9,5},{13,9},{2,14},{6,2},{... | collective-permute-start | bytes 230408 | tf_op jit(solution)/shard_map/ppermute | solution.py:34
  55.3 11.6 %collective-permute-start.8 = (bf16[3,80,160]{2,1,0:T(8,128)(2,1)S(1)}, bf16[3,80,160]{2,1,0:T(8,128)(2,1)S(1)}, u32[]{:S(2)}, u32[]{:S(2)}) collective-permute-start(bf16[3,80,160]{2,1,0:T(8,128)(2,1)S(1)} %copy-done.3), channel_id=1, source_target_pairs={{0,4},{4,8},{8,12},{12,0},{1,5},{5,9},{9,13},{13,1},{2,6},{6,10},{... | collective-permute-start | bytes 230408 | tf_op jit(solution)/shard_map/ppermute | solution.py:34
  55.3 11.6 %collective-permute-start.7 = (bf16[3,80,160]{2,1,0:T(8,128)(2,1)S(1)}, bf16[3,80,160]{2,1,0:T(8,128)(2,1)S(1)}, u32[]{:S(2)}, u32[]{:S(2)}) collective-permute-start(bf16[3,80,160]{2,1,0:T(8,128)(2,1)S(1)} %copy-done.3), channel_id=1, source_target_pairs={{0,8},{4,12},{8,0},{12,4},{1,9},{5,13},{9,1},{13,5},{2,10},{6,14},... | collective-permute-start | bytes 230408 | tf_op jit(solution)/shard_map/ppermute | solution.py:34
  67.0 1.0 copy-start.2
  96.9 41.7 %copy-start.6 = (f32[160]{0:T(256)S(1)}, f32[160]{0:T(256)}, u32[]{:S(2)}) copy-start(f32[160]{0:T(256)} %param.15) | copy-start | bytes 1924
  96.9 41.7 %copy-start.7 = (f32[160]{0:T(256)S(1)}, f32[160]{0:T(256)}, u32[]{:S(2)}) copy-start(f32[160]{0:T(256)} %param.14) | copy-start | bytes 1924
  96.9 41.7 %collective-permute-start.9 = (bf16[1,36,160,128]{3,2,1,0:T(8,128)(2,1)}, bf16[1,36,160,128]{3,2,1,0:T(8,128)(2,1)}, u32[]{:S(2)}, u32[]{:S(2)}) collective-permute-start(bf16[1,36,160,128]{3,2,1,0:T(8,128)(2,1)} %get-tuple-element.13), channel_id=1, source_target_pairs={{0,4},{4,8},{8,12},{1,5},{5,9},{9,13},{2,6},{6,10},{10,14},{3,7},{... | collective-permute-start | bytes 4423688 | tf_op jit(solution)/shard_map/ppermute | solution.py:258
  99.5 39.1 %collective-permute-start.10 = (bf16[1,36,160,128]{3,2,1,0:T(8,128)(2,1)}, bf16[1,36,160,128]{3,2,1,0:T(8,128)(2,1)}, u32[]{:S(2)}, u32[]{:S(2)}) collective-permute-start(bf16[1,36,160,128]{3,2,1,0:T(8,128)(2,1)} %get-tuple-element.14), channel_id=1, source_target_pairs={{4,0},{8,4},{12,8},{5,1},{9,5},{13,9},{6,2},{10,6},{14,10},{7,3},{... | collective-permute-start | bytes 4423688 | tf_op jit(solution)/shard_map/ppermute | solution.py:259
  138.5 7.7 %copy-start.9 = (f32[160]{0:T(256)S(1)}, f32[160]{0:T(256)}, u32[]{:S(2)}) copy-start(f32[160]{0:T(256)} %param.17) | copy-start | bytes 1924
  146.3 9.9 %collective-permute-start.11 = (bf16[4,36,160,128]{3,2,1,0:T(8,128)(2,1)}, bf16[4,36,160,128]{3,2,1,0:T(8,128)(2,1)}, u32[]{:S(2)}, u32[]{:S(2)}) collective-permute-start(bf16[4,36,160,128]{3,2,1,0:T(8,128)(2,1)} %fusion.13.refs_0_.refs_1_.refs_2_), channel_id=1, source_target_pairs={{0,1},{1,0},{2,3},{3,2},{4,5},{5,4},{6,7},{7,6},{8,9},{9,8},{10,11... | collective-permute-start | bytes 17694728 | tf_op jit(solution)/shard_map/ppermute | solution.py:16

commit v9 on v7

--- a/solution.py
+++ b/solution.py
@@ -34,6 +34,18 @@
         pieces.append(lax.ppermute(piece, "tm", pairs))
     stacked = jnp.roll(jnp.stack(pieces), index, axis=0)
     return stacked
+
+
+def butterfly_sum(block, name):
+    count = lax.axis_size(name)
+    if count & (count - 1):
+        return lax.psum(block, name)
+    distance = 1
+    while distance < count:
+        pairs = [(i, i ^ distance) for i in range(count)]
+        block = block + lax.ppermute(block, name, pairs)
+        distance *= 2
+    return block
 
 
 def group_stats(grouped, axes, slot_axes):
@@ -53,7 +65,7 @@
     table = jnp.zeros((slots,) + mine.shape, jnp.float32)
     table = lax.dynamic_update_index_in_dim(table, mine, slot, 0)
     for name in reversed(slot_axes):
-        table = lax.psum(table, name)
+        table = butterfly_sum(table, name)
     means = table[:, 0]
     average = jnp.sum(means, axis=0) / slots
     spread = means - average

time: 169 us -> 172 us (1.018)
  blocking collectives: 72.2 us -> 32.5 us
  waiting for transfers between devices: 11.1 us -> 47 us
  starting transfers between devices: 16.5 us -> 22.7 us
    psum x3 -> x0, blocking collectives: 39.7 us -> none  [group_stats(): table = lax.psum(table, name)]
    ppermute x0 -> x4, waiting for transfers between devices: none -> 35.9 us  [butterfly_sum(): block = block + lax.ppermute(block, name, pairs)]
    ppermute x0 -> x4, starting transfers between devices: none -> 6.14 us  [butterfly_sum(): block = block + lax.ppermute(block, name, pairs)]
  transfers between devices with their start and end apart: 9 -> 13, of which waited for: 3 -> 7; matrix products, arithmetic and copies ran while one was open for 5% -> 4% of each run, Pallas kernels for 0% -> 0%
where the time goes in v9:
time: 172 us
  waiting for transfers between devices  47 us (27%)
  Pallas kernels  40.2 us (23%)
  blocking collectives  32.5 us (19%)
  starting transfers between devices  22.7 us (13%)
  other arithmetic  19.3 us (11%)
  local copies, waits for them, and re-layouts  9.82 us (6%)
    ppermute x4, waiting for transfers between devices, butterfly_sum(): block = block + lax.ppermute(block, name, pairs)  35.9 us
    all_gather x1, blocking collectives, body(): lax.all_gather(spatial_weight, 'tm', axis=2, tiled=True)  32.5 us
    pallas_call x1, Pallas kernels, spatial_call(): pl.pallas_call(spatial_kernel, out_shape=jax.ShapeDtypeStruct(residual.sh...  24.2 us
    pallas_call x1, Pallas kernels, temporal_call(): pl.pallas_call(temporal_kernel, out_shape=jax.ShapeDtypeStruct(residual.s...  16 us
    select_n x1, other arithmetic, body(): jnp.where(inside[:, None, None, None], act_two, jnp.zeros_like(act_two))  7.66 us
    ppermute x4, starting transfers between devices, butterfly_sum(): block = block + lax.ppermute(block, name, pairs)  6.14 us
    ppermute x2, waiting for transfers between devices, swap_chan(): return lax.ppermute(block, 'chan', [(0, 1), (1, 0)])  6.04 us
    ppermute x1, starting transfers between devices, body(): before = lax.ppermute(hidden[-1:], 'tm', forward)  5.41 us
  transfers between devices with their start and end apart: 13, of which 7 were waited for; matrix products, arithmetic and copies ran while one was open for 4% of the time, Pallas kernels for 0%

profile of v9, /device:TPU:0, one launch (start us, length us, event | category | flops | bytes accessed | tf_op | source)
XLA Modules:
  0.0 172.0 jit_solution(6002244262447114699)
XLA Ops:
  0.0 2.5 %convert_reduce_fusion = f32[2,160]{1,0:T(2,128)S(1)} fusion(bf16[2,36,160,128]{3,2,1,0:T(8,128)(2,1)} %res_ref.1), kind=kLoop, calls=%fused_computation.3 | loop fusion | flops 2948800 | bytes 2950400 | tf_op jit(solution)/shard_map/reduce_sum | solution.py:55
  2.5 0.1 reduce_sum.101
  2.5 0.1 reduce_sum.120
  2.6 0.1 sub.75
  2.7 0.1 sub.76
  2.8 2.7 %fusion.3 = f32[2,160]{1,0:T(2,128)S(1)} fusion(bf16[2,36,160,128]{3,2,1,0:T(8,128)(2,1)} %res_ref.1, f32[2,160]{1,0:T(2,128)S(1)} %sub.76), kind=kLoop, calls=%fused_computation.9 | loop fusion | flops 5897920 | bytes 2951680 | tf_op jit(solution)/shard_map/reduce_sum | solution.py:57
  5.6 0.1 reduce_sum.122
  5.7 0.1 reduce_sum.123
  5.8 3.0 %collective-permute-start = (f32[2,2,2,16]{3,2,1,0:T(2,128)S(1)}, f32[2,2,2,16]{3,2,1,0:T(2,128)S(1)}, u32[]{:S(2)}, u32[]{:S(2)}) collective-permute-start(f32[2,2,2,16]{3,2,1,0:T(2,128)S(1)} %constant_dynamic-update-slice_fusion.3), channel_id=1, source_target_pairs={{0,2},{2,0},{1,3},{3,1},{4,6},{6,4},{5,7},{7,5},{8,10},{10,8},{9,1... | collective-permute-start | bytes 1544 | tf_op jit(solution)/shard_map/ppermute | solution.py:46
  8.8 1.6 collective-permute-done
  10.4 0.1 mul.90
  10.5 0.1 mul.91
  10.6 0.1 sub.79
  10.7 0.1 sub.80
  10.8 0.0 copy-start.2
  10.8 0.0 copy-start.8
  10.8 0.0 copy-start.3
  10.8 2.3 %fusion.12 = bf16[2,36,160,128]{3,2,1,0:T(8,128)(2,1)S(1)} fusion(bf16[2,36,160,128]{3,2,1,0:T(8,128)(2,1)S(1)} %copy-done, f32[160]{0:T(256)S(1)} %copy-done.4, f32[160]{0:T(256)S(1)} %copy-done.5, f32[2,160]{1,0:T(2,128)S(1)} %mul.91, f32[2,160]{1,0:T(2,128)S(1)} %sub.80), kind=kLoop, calls=%fused_computation.18 | loop fusion | flops 14745600 | bytes 5902080 | tf_op jit(solution)/shard_map/convert_element_type | solution.py:85
  13.2 3.9 %collective-permute-start.1 = (bf16[2,1,160,128]{3,2,1,0:T(8,128)(2,1)S(1)}, bf16[2,1,160,128]{3,2,1,0:T(8,128)(2,1)S(1)}, u32[]{:S(2)}, u32[]{:S(2)}) collective-permute-start(bf16[2,1,160,128]{3,2,1,0:T(8,128)(2,1)S(1)} %get-tuple-element.11), channel_id=1, source_target_pairs={{0,2},{1,3},{4,6},{5,7},{8,10},{9,11},{12,14},{13,15},{16,18},{17,... | collective-permute-start | bytes 245768 | tf_op jit(solution)/shard_map/ppermute | solution.py:23
  17.1 1.3 collective-permute-start.2
  18.4 0.7 collective-permute-done.1
  19.2 4.3 %collective-permute-done.2 = bf16[2,1,160,128]{3,2,1,0:T(8,128)(2,1)S(1)} collective-permute-done((bf16[2,1,160,128]{3,2,1,0:T(8,128)(2,1)S(1)}, bf16[2,1,160,128]{3,2,1,0:T(8,128)(2,1)S(1)}, u32[]{:S(2)}, u32[]{:S(2)}) %collective-permute-start.2) | collective-permute-done | bytes 81952 | tf_op jit(solution)/shard_map/ppermute | solution.py:24
  23.5 2.1 %pad_maximum_fusion.xo_ref = bf16[2,38,160,128]{3,2,1,0:T(8,128)(2,1)} fusion(bf16[2,1,160,128]{3,2,1,0:T(8,128)(2,1)S(1)} %collective-permute-done.2, bf16[2,36,160,128]{3,2,1,0:T(8,128)(2,1)S(1)} %fusion.12, bf16[2,1,160,128]{3,2,1,0:T(8,128)(2,1)S(1)} %collective-permute-done.1), kind=kLoop, calls=%fused_computation.20 | loop fusion | flops 3112960 | bytes 6225920 | tf_op jit(solution)/shard_map/concatenate | solution.py:25
  25.5 3.6 %collective-permute-start.4 = (bf16[3,80,160]{2,1,0:T(8,128)(2,1)S(1)}, bf16[3,80,160]{2,1,0:T(8,128)(2,1)S(1)}, u32[]{:S(2)}, u32[]{:S(2)}) collective-permute-start(bf16[3,80,160]{2,1,0:T(8,128)(2,1)S(1)} %copy-done.2), channel_id=1, source_target_pairs={{0,12},{4,0},{8,4},{12,8},{1,13},{5,1},{9,5},{13,9},{2,14},{6,2},{... | collective-permute-start | bytes 230408 | tf_op jit(solution)/shard_map/ppermute | solution.py:34
  29.1 1.0 collective-permute-start.5
  30.1 0.1 copy.17.b_ref
  30.3 32.5 %all_gather.3 = bf16[3,3,320,160]{3,2,1,0:T(8,128)(2,1)S(1)} all-gather(bf16[3,3,80,160]{3,2,1,0:T(8,128)(2,1)S(1)} %copy-done.3), channel_id=1, replica_groups=mesh['groups'=2,'tm'=4,'height'=2,'chan'=2] {'tm'}, dimensions={2}, use_global_device_ids=true | all-gather | bytes 1152000 | tf_op jit(solution)/shard_map/all_gather | solution.py:243
  62.8 0.9 copy.16
  63.7 0.7 constant_dynamic-slice_fusion.2
  64.4 0.0 collective-permute-done.4
  64.6 0.9 copy-done.1
  65.6 24.2 %shard_map.91.refs_8_ = bf16[2,36,160,128]{3,2,1,0:T(8,128)(2,1)S(1)} custom-call(bf16[2,38,160,128]{3,2,1,0:T(8,128)(2,1)} %pad_maximum_fusion.xo_ref, bf16[2,38,160,128]{3,2,1,0:T(8,128)(2,1)} %collective-permute-done.3.xt_ref, bf16[3,480,160]{2,1,0:T(8,128)(2,1)S(1)} %get-tuple-element.14.wo_ref, bf16[3,480,160]{2,1,0:T(8,128)(2,1)S(1)} %get-tuple-element.13.wt_ref, ...), custom_call_target="tpu_custom_call" | custom-call | flops 8493465600 | bytes 13045760 | tf_op jit(solution)/shard_map/pallas_call | solution.py:130
  89.8 0.0 copy-start.6
  89.8 0.0 copy-start.7
  89.8 0.5 convert_reduce_fusion.1
  90.3 1.8 %fusion.20 = (bf16[1,36,160,128]{3,2,1,0:T(8,128)(2,1)}, bf16[1,36,160,128]{3,2,1,0:T(8,128)(2,1)}) fusion(bf16[2,36,160,128]{3,2,1,0:T(8,128)(2,1)S(1)} %shard_map.91.refs_8_), kind=kLoop, calls=%fused_computation.61 | loop fusion | bytes 5898240 | tf_op jit(solution)/shard_map/slice | solution.py:269
  92.1 0.1 reduce_sum.128
  92.2 0.1 reduce_sum.129
  92.3 5.4 %collective-permute-start.7 = (bf16[1,36,160,128]{3,2,1,0:T(8,128)(2,1)}, bf16[1,36,160,128]{3,2,1,0:T(8,128)(2,1)}, u32[]{:S(2)}, u32[]{:S(2)}) collective-permute-start(bf16[1,36,160,128]{3,2,1,0:T(8,128)(2,1)} %get-tuple-element.9), channel_id=1, source_target_pairs={{0,4},{4,8},{8,12},{1,5},{5,9},{9,13},{2,6},{6,10},{10,14},{3,7},{... | collective-permute-start | bytes 4423688 | tf_op jit(solution)/shard_map/ppermute | solution.py:269
  97.7 1.3 collective-permute-start.8
  99.0 0.1 sub.87
  99.1 0.1 sub.88
  99.2 0.9 fusion.1
  100.1 0.1 reduce_sum.131
  100.2 0.1 reduce_sum.132
  100.4 0.1 collective-permute-start.9
  100.4 3.6 %collective-permute-done.9 = f32[8,2,16]{2,1,0:T(2,128)S(1)} collective-permute-done((f32[8,2,16]{2,1,0:T(2,128)S(1)}, f32[8,2,16]{2,1,0:T(2,128)S(1)}, u32[]{:S(2)}, u32[]{:S(2)}) %collective-permute-start.9) | collective-permute-done | bytes 1056 | tf_op jit(solution)/shard_map/ppermute | solution.py:46
  104.1 2.7 %collective-permute-start.10 = (f32[8,2,16]{2,1,0:T(2,128)S(1)}, f32[8,2,16]{2,1,0:T(2,128)S(1)}, u32[]{:S(2)}, u32[]{:S(2)}) collective-permute-start(f32[8,2,16]{2,1,0:T(2,128)S(1)} %constant_dynamic-update-slice_fusion), channel_id=1, source_target_pairs={{0,4},{4,0},{8,12},{12,8},{1,5},{5,1},{9,13},{13,9},{2,6},{6,2},{1... | collective-permute-start | bytes 3080 | tf_op jit(solution)/shard_map/ppermute | solution.py:46
  106.8 26.5 %collective-permute-done.10 = f32[8,2,16]{2,1,0:T(2,128)S(1)} collective-permute-done((f32[8,2,16]{2,1,0:T(2,128)S(1)}, f32[8,2,16]{2,1,0:T(2,128)S(1)}, u32[]{:S(2)}, u32[]{:S(2)}) %collective-permute-start.10) | collective-permute-done | bytes 1056 | tf_op jit(solution)/shard_map/ppermute | solution.py:46
  133.3 0.3 collective-permute-start.11
  133.7 4.2 %collective-permute-done.11 = f32[8,2,16]{2,1,0:T(2,128)S(1)} collective-permute-done((f32[8,2,16]{2,1,0:T(2,128)S(1)}, f32[8,2,16]{2,1,0:T(2,128)S(1)}, u32[]{:S(2)}, u32[]{:S(2)}) %collective-permute-start.11) | collective-permute-done | bytes 1056 | tf_op jit(solution)/shard_map/ppermute | solution.py:46
  138.0 0.1 mul.103
  138.0 0.1 mul.104
  138.1 0.1 sub.91
  138.2 0.1 sub.92
  138.3 0.0 copy-start.9
  138.3 7.7 %fusion.13.refs_0_.refs_1_.refs_2_ = bf16[4,36,160,128]{3,2,1,0:T(8,128)(2,1)} fusion(bf16[1,36,160,128]{3,2,1,0:T(8,128)(2,1)} %collective-permute-done.8, bf16[2,36,160,128]{3,2,1,0:T(8,128)(2,1)S(1)} %shard_map.91.refs_8_, bf16[1,36,160,128]{3,2,1,0:T(8,128)(2,1)} %collective-permute-done.7, f32[160]{0:T(256)S(1)} %copy-done.6, f32[160]{0:T(256)S(1)} %copy-done.7, ...), kind=kLoop, calls=%fused_computation.19 | loop fusion | flops 38338560 | bytes 11799044 | tf_op jit(solution)/shard_map/jit(_where)/select_n | solution.py:281
  146.0 0.1 copy.19.refs_9_
  146.1 1.1 fusion.22
  147.2 1.1 copy.18
  148.3 1.4 reshape.107
  149.7 0.2 dynamic-slice_bitcast_fusion
  149.9 6.0 %collective-permute-done.12.refs_3_.refs_4_.refs_5_ = bf16[4,36,160,128]{3,2,1,0:T(8,128)(2,1)} collective-permute-done((bf16[4,36,160,128]{3,2,1,0:T(8,128)(2,1)}, bf16[4,36,160,128]{3,2,1,0:T(8,128)(2,1)}, u32[]{:S(2)}, u32[]{:S(2)}) %collective-permute-start.12) | collective-permute-done | bytes 5898272 | tf_op jit(solution)/shard_map/ppermute | solution.py:16
  155.9 16.0 %shard_map.92 = bf16[2,36,160,128]{3,2,1,0:T(8,128)(2,1)} custom-call(bf16[4,36,160,128]{3,2,1,0:T(8,128)(2,1)} %fusion.13.refs_0_.refs_1_.refs_2_, bf16[4,36,160,128]{3,2,1,0:T(8,128)(2,1)} %fusion.13.refs_0_.refs_1_.refs_2_, bf16[4,36,160,128]{3,2,1,0:T(8,128)(2,1)} %fusion.13.refs_0_.refs_1_.refs_2_, ...), custom_call_target="tpu_custom_call" | custom-call | flops 2831155200 | bytes 23900160 | tf_op jit(solution)/shard_map/pallas_call | solution.py:184
  (50 shorter events, 0.4 us)
Async XLA Ops:
  0.0 10.8 %copy-start = (bf16[2,36,160,128]{3,2,1,0:T(8,128)(2,1)S(1)}, bf16[2,36,160,128]{3,2,1,0:T(8,128)(2,1)}, u32[]{:S(2)}) copy-start(bf16[2,36,160,128]{3,2,1,0:T(8,128)(2,1)} %res_ref.1) | copy-start | bytes 8847364
  0.0 10.8 %copy-start.4 = (f32[160]{0:T(256)S(1)}, f32[160]{0:T(256)}, u32[]{:S(2)}) copy-start(f32[160]{0:T(256)} %param.11) | copy-start | bytes 1924
  0.0 10.8 %copy-start.5 = (f32[160]{0:T(256)S(1)}, f32[160]{0:T(256)}, u32[]{:S(2)}) copy-start(f32[160]{0:T(256)} %param.10) | copy-start | bytes 1924
  5.8 4.6 %collective-permute-start = (f32[2,2,2,16]{3,2,1,0:T(2,128)S(1)}, f32[2,2,2,16]{3,2,1,0:T(2,128)S(1)}, u32[]{:S(2)}, u32[]{:S(2)}) collective-permute-start(f32[2,2,2,16]{3,2,1,0:T(2,128)S(1)} %constant_dynamic-update-slice_fusion.3), channel_id=1, source_target_pairs={{0,2},{2,0},{1,3},{3,1},{4,6},{6,4},{5,7},{7,5},{8,10},{10,8},{9,1... | collective-permute-start | bytes 1544 | tf_op jit(solution)/shard_map/ppermute | solution.py:46
  10.8 14.7 %copy-start.2 = (bf16[3,80,160]{2,1,0:T(8,128)(2,1)S(1)}, bf16[3,80,160]{2,1,0:T(8,128)(2,1)}, u32[]{:S(2)}) copy-start(bf16[3,80,160]{2,1,0:T(8,128)(2,1)} %param.16) | copy-start | bytes 230404
  10.8 19.3 %copy-start.8 = (f32[160]{0:T(256)S(1)}, f32[160]{0:T(256)}, u32[]{:S(2)}) copy-start(f32[160]{0:T(256)} %param.13) | copy-start | bytes 1924
  10.8 19.4 %copy-start.3 = (bf16[3,3,80,160]{3,2,1,0:T(8,128)(2,1)S(1)}, bf16[3,3,80,160]{3,2,1,0:T(8,128)(2,1)}, u32[]{:S(2)}) copy-start(bf16[3,3,80,160]{3,2,1,0:T(8,128)(2,1)} %param.12) | copy-start | bytes 691204
  13.2 6.0 %collective-permute-start.1 = (bf16[2,1,160,128]{3,2,1,0:T(8,128)(2,1)S(1)}, bf16[2,1,160,128]{3,2,1,0:T(8,128)(2,1)S(1)}, u32[]{:S(2)}, u32[]{:S(2)}) collective-permute-start(bf16[2,1,160,128]{3,2,1,0:T(8,128)(2,1)S(1)} %get-tuple-element.11), channel_id=1, source_target_pairs={{0,2},{1,3},{4,6},{5,7},{8,10},{9,11},{12,14},{13,15},{16,18},{17,... | collective-permute-start | bytes 245768 | tf_op jit(solution)/shard_map/ppermute | solution.py:23
  17.1 6.3 %collective-permute-start.2 = (bf16[2,1,160,128]{3,2,1,0:T(8,128)(2,1)S(1)}, bf16[2,1,160,128]{3,2,1,0:T(8,128)(2,1)S(1)}, u32[]{:S(2)}, u32[]{:S(2)}) collective-permute-start(bf16[2,1,160,128]{3,2,1,0:T(8,128)(2,1)S(1)} %get-tuple-element.12), channel_id=1, source_target_pairs={{2,0},{3,1},{6,4},{7,5},{10,8},{11,9},{14,12},{15,13},{18,16},{19,... | collective-permute-start | bytes 245768 | tf_op jit(solution)/shard_map/ppermute | solution.py:24
  25.5 39.1 %collective-permute-start.3 = (bf16[2,38,160,128]{3,2,1,0:T(8,128)(2,1)}, bf16[2,38,160,128]{3,2,1,0:T(8,128)(2,1)}, u32[]{:S(2)}, u32[]{:S(2)}) collective-permute-start(bf16[2,38,160,128]{3,2,1,0:T(8,128)(2,1)} %pad_maximum_fusion.xo_ref), channel_id=1, source_target_pairs={{0,1},{1,0},{2,3},{3,2},{4,5},{5,4},{6,7},{7,6},{8,9},{9,8},{10,11... | collective-permute-start | bytes 9338888 | tf_op jit(solution)/shard_map/ppermute | solution.py:16
  25.5 38.9 %collective-permute-start.4 = (bf16[3,80,160]{2,1,0:T(8,128)(2,1)S(1)}, bf16[3,80,160]{2,1,0:T(8,128)(2,1)S(1)}, u32[]{:S(2)}, u32[]{:S(2)}) collective-permute-start(bf16[3,80,160]{2,1,0:T(8,128)(2,1)S(1)} %copy-done.2), channel_id=1, source_target_pairs={{0,12},{4,0},{8,4},{12,8},{1,13},{5,1},{9,5},{13,9},{2,14},{6,2},{... | collective-permute-start | bytes 230408 | tf_op jit(solution)/shard_map/ppermute | solution.py:34
  29.1 35.3 %collective-permute-start.6 = (bf16[3,80,160]{2,1,0:T(8,128)(2,1)S(1)}, bf16[3,80,160]{2,1,0:T(8,128)(2,1)S(1)}, u32[]{:S(2)}, u32[]{:S(2)}) collective-permute-start(bf16[3,80,160]{2,1,0:T(8,128)(2,1)S(1)} %copy-done.2), channel_id=1, source_target_pairs={{0,4},{4,8},{8,12},{12,0},{1,5},{5,9},{9,13},{13,1},{2,6},{6,10},{... | collective-permute-start | bytes 230408 | tf_op jit(solution)/shard_map/ppermute | solution.py:34
  29.1 35.3 %collective-permute-start.5 = (bf16[3,80,160]{2,1,0:T(8,128)(2,1)S(1)}, bf16[3,80,160]{2,1,0:T(8,128)(2,1)S(1)}, u32[]{:S(2)}, u32[]{:S(2)}) collective-permute-start(bf16[3,80,160]{2,1,0:T(8,128)(2,1)S(1)} %copy-done.2), channel_id=1, source_target_pairs={{0,8},{4,12},{8,0},{12,4},{1,9},{5,13},{9,1},{13,5},{2,10},{6,14},... | collective-permute-start | bytes 230408 | tf_op jit(solution)/shard_map/ppermute | solution.py:34
  64.6 1.0 copy-start.1
  89.8 48.6 %copy-start.6 = (f32[160]{0:T(256)S(1)}, f32[160]{0:T(256)}, u32[]{:S(2)}) copy-start(f32[160]{0:T(256)} %param.15) | copy-start | bytes 1924
  89.8 48.6 %copy-start.7 = (f32[160]{0:T(256)S(1)}, f32[160]{0:T(256)}, u32[]{:S(2)}) copy-start(f32[160]{0:T(256)} %param.14) | copy-start | bytes 1924
  92.3 46.0 %collective-permute-start.7 = (bf16[1,36,160,128]{3,2,1,0:T(8,128)(2,1)}, bf16[1,36,160,128]{3,2,1,0:T(8,128)(2,1)}, u32[]{:S(2)}, u32[]{:S(2)}) collective-permute-start(bf16[1,36,160,128]{3,2,1,0:T(8,128)(2,1)} %get-tuple-element.9), channel_id=1, source_target_pairs={{0,4},{4,8},{8,12},{1,5},{5,9},{9,13},{2,6},{6,10},{10,14},{3,7},{... | collective-permute-start | bytes 4423688 | tf_op jit(solution)/shard_map/ppermute | solution.py:269
  97.7 40.6 %collective-permute-start.8 = (bf16[1,36,160,128]{3,2,1,0:T(8,128)(2,1)}, bf16[1,36,160,128]{3,2,1,0:T(8,128)(2,1)}, u32[]{:S(2)}, u32[]{:S(2)}) collective-permute-start(bf16[1,36,160,128]{3,2,1,0:T(8,128)(2,1)} %get-tuple-element.10), channel_id=1, source_target_pairs={{4,0},{8,4},{12,8},{5,1},{9,5},{13,9},{6,2},{10,6},{14,10},{7,3},{... | collective-permute-start | bytes 4423688 | tf_op jit(solution)/shard_map/ppermute | solution.py:270
  100.4 3.7 %collective-permute-start.9 = (f32[8,2,16]{2,1,0:T(2,128)S(1)}, f32[8,2,16]{2,1,0:T(2,128)S(1)}, u32[]{:S(2)}, u32[]{:S(2)}) collective-permute-start(f32[8,2,16]{2,1,0:T(2,128)S(1)} %constant_dynamic-update-slice_fusion.1), channel_id=1, source_target_pairs={{0,2},{2,0},{1,3},{3,1},{4,6},{6,4},{5,7},{7,5},{8,10},{10,8},{9,1... | collective-permute-start | bytes 3080 | tf_op jit(solution)/shard_map/ppermute | solution.py:46
  104.1 29.2 %collective-permute-start.10 = (f32[8,2,16]{2,1,0:T(2,128)S(1)}, f32[8,2,16]{2,1,0:T(2,128)S(1)}, u32[]{:S(2)}, u32[]{:S(2)}) collective-permute-start(f32[8,2,16]{2,1,0:T(2,128)S(1)} %constant_dynamic-update-slice_fusion), channel_id=1, source_target_pairs={{0,4},{4,0},{8,12},{12,8},{1,5},{5,1},{9,13},{13,9},{2,6},{6,2},{1... | collective-permute-start | bytes 3080 | tf_op jit(solution)/shard_map/ppermute | solution.py:46
  133.3 4.5 %collective-permute-start.11 = (f32[8,2,16]{2,1,0:T(2,128)S(1)}, f32[8,2,16]{2,1,0:T(2,128)S(1)}, u32[]{:S(2)}, u32[]{:S(2)}) collective-permute-start(f32[8,2,16]{2,1,0:T(2,128)S(1)} %add.115), channel_id=1, source_target_pairs={{0,8},{4,12},{8,0},{12,4},{1,9},{5,13},{9,1},{13,5},{2,10},{6,14},... | collective-permute-start | bytes 3080 | tf_op jit(solution)/shard_map/ppermute | solution.py:46
  138.3 7.7 %copy-start.9 = (f32[160]{0:T(256)S(1)}, f32[160]{0:T(256)}, u32[]{:S(2)}) copy-start(f32[160]{0:T(256)} %param.17) | copy-start | bytes 1924
  146.0 9.9 %collective-permute-start.12 = (bf16[4,36,160,128]{3,2,1,0:T(8,128)(2,1)}, bf16[4,36,160,128]{3,2,1,0:T(8,128)(2,1)}, u32[]{:S(2)}, u32[]{:S(2)}) collective-permute-start(bf16[4,36,160,128]{3,2,1,0:T(8,128)(2,1)} %fusion.13.refs_0_.refs_1_.refs_2_), channel_id=1, source_target_pairs={{0,1},{1,0},{2,3},{3,2},{4,5},{5,4},{6,7},{7,6},{8,9},{9,8},{10,11... | collective-permute-start | bytes 17694728 | tf_op jit(solution)/shard_map/ppermute | solution.py:16

commit v10 on v6

--- a/solution.py
+++ b/solution.py
@@ -229,15 +229,25 @@
 
     piece = spatial_weight.shape[2]
     merged = jnp.concatenate([spatial_weight.reshape(9, piece, local_chan), temporal_weight], axis=0)
-    full_weight = lax.all_gather(merged, "tm", axis=1, tiled=True)
-    spatial_full = full_weight[:9]
-    temporal_full = full_weight[9:]
-    spatial_full = spatial_full.reshape(3, 3, C, local_chan)
+    sharers = lax.axis_size("groups") * lax.axis_size("height")
+    share = local_chan // sharers
+    slot = lax.axis_index("groups") * lax.axis_size("height") + lax.axis_index("height")
+    mine = lax.dynamic_slice_in_dim(merged, slot * share, share, axis=2)
+    along_tm = gather_tm(mine)
+    shared = [along_tm]
+    for shift in range(1, sharers):
+        pairs = [(i, (i - shift) % sharers) for i in range(sharers)]
+        shared.append(lax.ppermute(along_tm, ("groups", "height"), pairs))
+    shared = jnp.roll(jnp.stack(shared), slot, axis=0)
 
     values = video.astype(jnp.float32)
     grouped = values.reshape(frames, rows, local_groups, group_size, width)
     average, variance = group_stats(grouped, (1, 3, 4), ("height",))
     act_one = group_act(values, average, variance, norm1_gain, norm1_bias)
+    act_one, shared = lax.optimization_barrier((act_one, shared))
+    full_weight = jnp.transpose(shared, (2, 1, 3, 0, 4)).reshape(12, C, local_chan)
+    spatial_full = full_weight[:9].reshape(3, 3, C, local_chan)
+    temporal_full = full_weight[9:]
 
     with_rows = row_halo(act_one)
     own_start = chan_index * local_chan

time: 202 us -> 179 us (0.89)
  waiting for transfers between devices: 65.1 us -> 22.2 us
  local copies, waits for them, and re-layouts: 13.9 us -> 36.8 us
  between operations: 13.7 us -> 0.34 us
  starting transfers between devices: 9.27 us -> 20.5 us
    all_gather x1 -> x0, waiting for transfers between devices: 55.3 us -> none  [body(): full_weight = lax.all_gather(merged, 'tm', axis=1, tiled=True)]
    unnamed x21 -> x35, local copies, waits for them, and re-layouts: 6.08 us -> 20.2 us
    ppermute x0 -> x6, waiting for transfers between devices: none -> 13.6 us  [the longest x3 13.6 us: body(): shared.append(lax.ppermute(along_tm, ('groups', 'height'), pairs))]
    ppermute x0 -> x6, starting transfers between devices: none -> 9.61 us  [the longest x3 6.06 us: gather_tm(): pieces.append(lax.ppermute(piece, 'tm', pairs))]
    reshape x0 -> x1, local copies, waits for them, and re-layouts: none -> 2.81 us  [body(): spatial_full = full_weight[:9].reshape(3, 3, C, local_chan)]
    ppermute x1, waiting for transfers between devices: 4.3 us -> 1.54 us  [row_halo(): high = lax.ppermute(block[:, :1], 'height', backward)]
    concatenate x2 -> x0, other arithmetic: 2.15 us -> none  [the longest x1 2.06 us: row_halo(): return jnp.concatenate([low, block, high], axis=1)]
    dynamic_slice x0 -> x2, local copies, waits for them, and re-layouts: none -> 2.1 us  [the longest x1 1.88 us: body(): shared = jnp.roll(jnp.stack(shared), slot, axis=0)]
  transfers between devices with their start and end apart: 7 -> 12, of which waited for: 4 -> 6; matrix products, arithmetic and copies ran while one was open for 7% -> 15% of each run, Pallas kernels for 0% -> 0%
where the time goes in v10:
time: 179 us; the launch traced here: 178 us
  blocking collectives  40.2 us (22%)
  Pallas kernels  40.2 us (22%)
  local copies, waits for them, and re-layouts  36.8 us (21%)
  waiting for transfers between devices  22.2 us (12%)
  starting transfers between devices  20.5 us (11%)
  other arithmetic  17.7 us (10%)
    psum x3, blocking collectives, group_stats(): table = lax.psum(table, name)  40.2 us
    pallas_call x1, Pallas kernels, spatial_call(): pl.pallas_call(spatial_kernel, out_shape=jax.ShapeDtypeStruct(residual.sh...  24.2 us
    unnamed x35, local copies, waits for them, and re-layouts  20.2 us
    pallas_call x1, Pallas kernels, temporal_call(): pl.pallas_call(temporal_kernel, out_shape=jax.ShapeDtypeStruct(residual.s...  16 us
    ppermute x3, waiting for transfers between devices, body(): shared.append(lax.ppermute(along_tm, ('groups', 'height'), pairs))  13.6 us
    select_n x1, other arithmetic, body(): jnp.where(inside[:, None, None, None], act_two, jnp.zeros_like(act_two))  7.66 us
    ppermute x2, waiting for transfers between devices, swap_chan(): return lax.ppermute(block, 'chan', [(0, 1), (1, 0)])  6.39 us
    ppermute x3, starting transfers between devices, gather_tm(): pieces.append(lax.ppermute(piece, 'tm', pairs))  6.06 us
  transfers between devices with their start and end apart: 12, of which 6 were waited for; matrix products, arithmetic and copies ran while one was open for 15% of the time, Pallas kernels for 0%

profile of v10, /device:TPU:0, one launch (start us, length us, event | category | flops | bytes accessed | tf_op | source)
XLA Modules:
  0.0 177.9 jit_solution(16153069592387940364)
XLA Ops:
  0.0 1.8 %copy.39 = bf16[3,80,160]{1,2,0:T(8,128)(2,1)} copy(bf16[3,80,160]{2,1,0:T(8,128)(2,1)} %param.16) | data formatting | bytes 153600 | tf_op args[7]
  1.8 1.3 copy.38
  3.1 1.4 bitcast_dynamic-update-slice_fusion.14
  4.5 4.0 %collective-permute-start.1 = (bf16[12,80,40]{1,2,0:T(8,128)(2,1)S(1)}, bf16[12,80,40]{1,2,0:T(8,128)(2,1)S(1)}, u32[]{:S(2)}, u32[]{:S(2)}) collective-permute-start(bf16[12,80,40]{1,2,0:T(8,128)(2,1)S(1)} %get-tuple-element.16), channel_id=1, source_target_pairs={{0,8},{4,12},{8,0},{12,4},{1,9},{5,13},{9,1},{13,5},{2,10},{6,14},... | collective-permute-start | bytes 230408 | tf_op jit(solution)/shard_map/ppermute | solution.py:34
  8.6 1.3 collective-permute-start
  9.9 0.7 collective-permute-start.2
  10.6 2.3 %convert_reduce_fusion = f32[2,160]{1,0:T(2,128)S(1)} fusion(bf16[2,36,160,128]{3,2,1,0:T(8,128)(2,1)} %res_ref.1), kind=kLoop, calls=%fused_computation.3 | loop fusion | flops 2948800 | bytes 2950400 | tf_op jit(solution)/shard_map/reduce_sum | solution.py:43
  13.2 0.1 sub.80
  13.3 0.9 fusion.3
  14.4 4.9 %psum.21 = f32[2,2,2,16]{3,2,0,1:T(2,128)S(1)} all-reduce(f32[2,2,2,16]{3,2,0,1:T(2,128)S(1)} %constant_dynamic-update-slice_fusion.3), channel_id=1, replica_groups=mesh['groups'=2,'tm'=4,'height'=2,'chan'=2] {'height'}, use_global_device_ids=true, to_apply=%region_4.5 | all-reduce | flops 128 | bytes 1024 | tf_op jit(solution)/shard_map/psum | solution.py:56
  19.7 0.7 bitcast_dynamic-update-slice_fusion.12
  20.4 0.7 bitcast_dynamic-update-slice_fusion.10
  21.1 0.7 bitcast_dynamic-update-slice_fusion.8
  21.7 0.7 bitcast_dynamic-update-slice_fusion.15
  22.4 0.7 bitcast_dynamic-update-slice_fusion.13
  23.1 0.7 bitcast_dynamic-update-slice_fusion.11
  23.7 0.7 bitcast_dynamic-update-slice_fusion.9
  24.4 2.1 %bitcast_dynamic-update-slice_fusion.6 = (bf16[8,4,12,80,40]{3,4,2,1,0:T(8,128)(2,1)}, bf16[4,12,80,40]{2,3,1,0:T(8,128)(2,1)}) fusion(bf16[8,12,80,40]{2,3,1,0:T(8,128)(2,1)} %bitcast_dynamic-update-slice_fusion.9, s32[]{:T(128)S(6)} %select_n.49), kind=kLoop, calls=%fused_computation.28 | loop fusion | bytes 1290244
  26.5 1.5 collective-permute-start.4
  28.0 1.4 collective-permute-start.3
  29.4 3.4 %fusion.12 = bf16[2,36,160,128]{3,2,1,0:T(8,128)(2,1)} fusion(bf16[2,36,160,128]{3,2,1,0:T(8,128)(2,1)S(1)} %copy-done, f32[160]{0:T(256)S(1)} %copy-done.3, f32[160]{0:T(256)S(1)} %copy-done.4, f32[2,160]{1,0:T(2,128)S(1)} %mul.97, f32[2,160]{1,0:T(2,128)S(1)} %sub.84), kind=kLoop, calls=%fused_computation.18 | loop fusion | flops 14745600 | bytes 5902080 | tf_op jit(solution)/shard_map/convert_element_type | solution.py:73
  32.8 0.6 collective-permute-start.5
  33.4 9.1 %collective-permute-done.3 = bf16[4,12,80,40]{2,3,1,0:T(8,128)(2,1)} collective-permute-done((bf16[4,12,80,40]{2,3,1,0:T(8,128)(2,1)}, bf16[4,12,80,40]{2,3,1,0:T(8,128)(2,1)}, u32[]{:S(2)}, u32[]{:S(2)}) %collective-permute-start.3) | collective-permute-done | bytes 307232 | tf_op jit(solution)/shard_map/ppermute | solution.py:240
  42.5 1.9 %bitcast_dynamic-update-slice_fusion.4 = bf16[8,4,12,80,40]{3,4,2,1,0:T(8,128)(2,1)} fusion(bf16[8,4,12,80,40]{3,4,2,1,0:T(8,128)(2,1)} %get-tuple-element.13, bf16[4,12,80,40]{2,3,1,0:T(8,128)(2,1)} %collective-permute-done.3), kind=kLoop, calls=%fused_computation.26 | loop fusion | bytes 983040
  44.3 0.8 bitcast_dynamic-update-slice_fusion.2
  45.2 4.5 %collective-permute-done.5 = bf16[4,12,80,40]{2,3,1,0:T(8,128)(2,1)S(1)} collective-permute-done((bf16[4,12,80,40]{2,3,1,0:T(8,128)(2,1)}, bf16[4,12,80,40]{2,3,1,0:T(8,128)(2,1)S(1)}, u32[]{:S(2)}, u32[]{:S(2)}) %collective-permute-start.5) | collective-permute-done | bytes 307232 | tf_op jit(solution)/shard_map/ppermute | solution.py:240
  49.7 0.8 bitcast_dynamic-update-slice_fusion
  50.5 2.0 %bitcast_dynamic-update-slice_fusion.7 = bf16[8,4,12,80,40]{3,4,2,1,0:T(8,128)(2,1)} fusion(bf16[8,4,12,80,40]{3,4,2,1,0:T(8,128)(2,1)} %bitcast_dynamic-update-slice_fusion, bf16[4,12,80,40]{2,3,1,0:T(8,128)(2,1)} %get-tuple-element.14), kind=kLoop, calls=%fused_computation.29 | loop fusion | bytes 983040
  52.5 1.9 %bitcast_dynamic-update-slice_fusion.5 = bf16[8,4,12,80,40]{3,4,2,1,0:T(8,128)(2,1)} fusion(bf16[8,4,12,80,40]{3,4,2,1,0:T(8,128)(2,1)} %bitcast_dynamic-update-slice_fusion.7, bf16[4,12,80,40]{2,3,1,0:T(8,128)(2,1)} %collective-permute-done.3), kind=kLoop, calls=%fused_computation.27 | loop fusion | bytes 983040
  54.4 0.8 bitcast_dynamic-update-slice_fusion.3
  55.2 0.8 bitcast_dynamic-update-slice_fusion.1
  56.1 1.9 %constant_dynamic-slice_fusion.2 = bf16[4,4,12,80,40]{3,4,2,1,0:T(8,128)(2,1)S(1)} fusion(bf16[8,4,12,80,40]{3,4,2,1,0:T(8,128)(2,1)} %bitcast_dynamic-update-slice_fusion.1, s32[]{:T(128)S(6)} %select_n.51), kind=kLoop, calls=%fused_computation.51 | loop fusion | bytes 2457604 | tf_op jit(solution)/shard_map/jit(_roll_dynamic)/dynamic_slice | solution.py:241
  58.0 3.5 %collective-permute-start.6 = (bf16[2,1,160,128]{3,2,1,0:T(8,128)(2,1)S(1)}, bf16[2,1,160,128]{3,2,1,0:T(8,128)(2,1)S(1)}, u32[]{:S(2)}, u32[]{:S(2)}) collective-permute-start(bf16[2,1,160,128]{3,2,1,0:T(8,128)(2,1)S(1)} %get-tuple-element.20), channel_id=1, source_target_pairs={{0,2},{1,3},{4,6},{5,7},{8,10},{9,11},{12,14},{13,15},{16,18},{17,... | collective-permute-start | bytes 245768 | tf_op jit(solution)/shard_map/ppermute | solution.py:23
  61.5 1.3 collective-permute-start.7
  62.8 0.7 collective-permute-done.6
  63.5 0.6 constant_dynamic-update-slice_fusion.2
  64.1 2.1 %constant_dynamic-update-slice_fusion.1 = bf16[2,38,160,128]{3,2,1,0:T(8,128)(2,1)} fusion(bf16[2,38,160,128]{3,2,1,0:T(8,128)(2,1)} %constant_dynamic-update-slice_fusion.2, bf16[2,36,160,128]{3,2,1,0:T(8,128)(2,1)S(1)} %copy-done.1), kind=kLoop, calls=%fused_computation.42 | loop fusion | bytes 5898240
  66.3 1.5 collective-permute-done.7
  67.8 0.6 constant_dynamic-update-slice_fusion.xo_ref
  68.4 0.1 copy.41.b_ref
  68.6 0.3 slice.47
  68.8 1.8 copy.40
  70.6 2.8 %reshape.114 = bf16[3,3,320,160]{2,3,1,0:T(8,128)(2,1)S(1)} reshape(bf16[9,4,80,4,40]{2,1,4,3,0:T(4,128)(2,1)} %copy.40) | data formatting | bytes 1843200 | tf_op jit(solution)/shard_map/reshape | solution.py:249
  73.4 0.7 constant_dynamic-slice_fusion
  74.1 0.3 collective-permute-done.8.xt_ref
  74.4 24.2 %shard_map.91.refs_8_ = bf16[2,36,160,128]{3,2,1,0:T(8,128)(2,1)S(1)} custom-call(bf16[2,38,160,128]{3,2,1,0:T(8,128)(2,1)} %constant_dynamic-update-slice_fusion.xo_ref, bf16[2,38,160,128]{3,2,1,0:T(8,128)(2,1)} %collective-permute-done.8.xt_ref, bf16[3,480,160]{2,1,0:T(8,128)(2,1)S(1)} %get-tuple-element.22.wo_ref, ...), custom_call_target="tpu_custom_call" | custom-call | flops 8493465600 | bytes 13045760 | tf_op jit(solution)/shard_map/pallas_call | solution.py:118
  98.6 1.8 %fusion.22 = (bf16[1,36,160,128]{3,2,1,0:T(8,128)(2,1)}, bf16[1,36,160,128]{3,2,1,0:T(8,128)(2,1)}) fusion(bf16[2,36,160,128]{3,2,1,0:T(8,128)(2,1)S(1)} %shard_map.91.refs_8_), kind=kLoop, calls=%fused_computation.70 | loop fusion | bytes 5898240 | tf_op jit(solution)/shard_map/slice | solution.py:267
  100.4 4.8 %collective-permute-start.9 = (bf16[1,36,160,128]{3,2,1,0:T(8,128)(2,1)}, bf16[1,36,160,128]{3,2,1,0:T(8,128)(2,1)}, u32[]{:S(2)}, u32[]{:S(2)}) collective-permute-start(bf16[1,36,160,128]{3,2,1,0:T(8,128)(2,1)} %get-tuple-element.17), channel_id=1, source_target_pairs={{0,4},{4,8},{8,12},{1,5},{5,9},{9,13},{2,6},{6,10},{10,14},{3,7},{... | collective-permute-start | bytes 4423688 | tf_op jit(solution)/shard_map/ppermute | solution.py:267
  105.2 1.3 collective-permute-start.10
  106.5 0.5 convert_reduce_fusion.1
  107.1 0.1 reduce_sum.129
  107.3 0.1 sub.93
  107.4 0.9 fusion.1
  108.4 0.1 reduce_sum.132
  108.6 5.0 %psum.22 = f32[8,2,16]{2,0,1:T(8,128)S(1)} all-reduce(f32[8,2,16]{2,0,1:T(8,128)S(1)} %dynamic_update_slice.9), channel_id=1, replica_groups=mesh['groups'=2,'tm'=4,'height'=2,'chan'=2] {'height'}, use_global_device_ids=true, to_apply=%region_12.13 | all-reduce | flops 256 | bytes 2048 | tf_op jit(solution)/shard_map/psum | solution.py:56
  113.6 30.3 %psum.23 = f32[8,2,16]{2,0,1:T(8,128)S(1)} all-reduce(f32[8,2,16]{2,0,1:T(8,128)S(1)} %psum.22), channel_id=1, replica_groups=mesh['groups'=2,'tm'=4,'height'=2,'chan'=2] {'tm'}, use_global_device_ids=true, to_apply=%region_13.14 | all-reduce | flops 256 | bytes 2048 | tf_op jit(solution)/shard_map/psum | solution.py:56
  144.3 7.7 %fusion.13.refs_0_.refs_1_.refs_2_ = bf16[4,36,160,128]{3,2,1,0:T(8,128)(2,1)} fusion(bf16[1,36,160,128]{3,2,1,0:T(8,128)(2,1)} %collective-permute-done.10, bf16[2,36,160,128]{3,2,1,0:T(8,128)(2,1)S(1)} %shard_map.91.refs_8_, bf16[1,36,160,128]{3,2,1,0:T(8,128)(2,1)} %collective-permute-done.9, f32[160]{0:T(256)S(1)} %copy-done.5, f32[160]{0:T(256)S(1)} %copy-done.6, ...), kind=kLoop, calls=%fused_computation.19 | loop fusion | flops 38338560 | bytes 11799044 | tf_op jit(solution)/shard_map/jit(_where)/select_n | solution.py:279
  152.0 0.1 copy.44.refs_9_
  152.1 1.1 slice.52
  153.2 1.0 copy.43
  154.2 1.4 slice.44
  155.6 0.2 dynamic-slice_bitcast_fusion
  155.8 6.1 %collective-permute-done.11.refs_3_.refs_4_.refs_5_ = bf16[4,36,160,128]{3,2,1,0:T(8,128)(2,1)} collective-permute-done((bf16[4,36,160,128]{3,2,1,0:T(8,128)(2,1)}, bf16[4,36,160,128]{3,2,1,0:T(8,128)(2,1)}, u32[]{:S(2)}, u32[]{:S(2)}) %collective-permute-start.11) | collective-permute-done | bytes 5898272 | tf_op jit(solution)/shard_map/ppermute | solution.py:16
  161.9 16.0 %shard_map.92 = bf16[2,36,160,128]{3,2,1,0:T(8,128)(2,1)} custom-call(bf16[4,36,160,128]{3,2,1,0:T(8,128)(2,1)} %fusion.13.refs_0_.refs_1_.refs_2_, bf16[4,36,160,128]{3,2,1,0:T(8,128)(2,1)} %fusion.13.refs_0_.refs_1_.refs_2_, bf16[4,36,160,128]{3,2,1,0:T(8,128)(2,1)} %fusion.13.refs_0_.refs_1_.refs_2_, ...), custom_call_target="tpu_custom_call" | custom-call | flops 2831155200 | bytes 23900160 | tf_op jit(solution)/shard_map/pallas_call | solution.py:171
  (59 shorter events, 1.6 us)
Async XLA Ops:
  0.0 13.3 %copy-start = (bf16[2,36,160,128]{3,2,1,0:T(8,128)(2,1)S(1)}, bf16[2,36,160,128]{3,2,1,0:T(8,128)(2,1)}, u32[]{:S(2)}) copy-start(bf16[2,36,160,128]{3,2,1,0:T(8,128)(2,1)} %res_ref.1) | copy-start | bytes 8847364
  4.5 15.9 %collective-permute-start.1 = (bf16[12,80,40]{1,2,0:T(8,128)(2,1)S(1)}, bf16[12,80,40]{1,2,0:T(8,128)(2,1)S(1)}, u32[]{:S(2)}, u32[]{:S(2)}) collective-permute-start(bf16[12,80,40]{1,2,0:T(8,128)(2,1)S(1)} %get-tuple-element.16), channel_id=1, source_target_pairs={{0,8},{4,12},{8,0},{12,4},{1,9},{5,13},{9,1},{13,5},{2,10},{6,14},... | collective-permute-start | bytes 230408 | tf_op jit(solution)/shard_map/ppermute | solution.py:34
  8.6 11.2 %collective-permute-start = (bf16[12,80,40]{1,2,0:T(8,128)(2,1)S(1)}, bf16[12,80,40]{1,2,0:T(8,128)(2,1)S(1)}, u32[]{:S(2)}, u32[]{:S(2)}) collective-permute-start(bf16[12,80,40]{1,2,0:T(8,128)(2,1)S(1)} %get-tuple-element.16), channel_id=1, source_target_pairs={{0,12},{4,0},{8,4},{12,8},{1,13},{5,1},{9,5},{13,9},{2,14},{6,2},{... | collective-permute-start | bytes 230408 | tf_op jit(solution)/shard_map/ppermute | solution.py:34
  9.9 11.2 %collective-permute-start.2 = (bf16[12,80,40]{1,2,0:T(8,128)(2,1)S(1)}, bf16[12,80,40]{1,2,0:T(8,128)(2,1)S(1)}, u32[]{:S(2)}, u32[]{:S(2)}) collective-permute-start(bf16[12,80,40]{1,2,0:T(8,128)(2,1)S(1)} %get-tuple-element.16), channel_id=1, source_target_pairs={{0,4},{4,8},{8,12},{12,0},{1,5},{5,9},{9,13},{13,1},{2,6},{6,10},{... | collective-permute-start | bytes 230408 | tf_op jit(solution)/shard_map/ppermute | solution.py:34
  12.9 16.5 %copy-start.3 = (f32[160]{0:T(256)S(1)}, f32[160]{0:T(256)}, u32[]{:S(2)}) copy-start(f32[160]{0:T(256)} %param.11) | copy-start | bytes 1924
  12.9 16.5 %copy-start.4 = (f32[160]{0:T(256)S(1)}, f32[160]{0:T(256)}, u32[]{:S(2)}) copy-start(f32[160]{0:T(256)} %param.10) | copy-start | bytes 1924
  26.5 17.9 %collective-permute-start.4 = (bf16[4,12,80,40]{2,3,1,0:T(8,128)(2,1)}, bf16[4,12,80,40]{2,3,1,0:T(8,128)(2,1)S(1)}, u32[]{:S(2)}, u32[]{:S(2)}) collective-permute-start(bf16[4,12,80,40]{2,3,1,0:T(8,128)(2,1)} %get-tuple-element.14), channel_id=1, source_target_pairs={{0,16},{2,18},{16,0},{18,2},{1,17},{3,19},{17,1},{19,3},{4,20},{6,... | collective-permute-start | bytes 921608 | tf_op jit(solution)/shard_map/ppermute | solution.py:240
  28.0 14.5 %collective-permute-start.3 = (bf16[4,12,80,40]{2,3,1,0:T(8,128)(2,1)}, bf16[4,12,80,40]{2,3,1,0:T(8,128)(2,1)}, u32[]{:S(2)}, u32[]{:S(2)}) collective-permute-start(bf16[4,12,80,40]{2,3,1,0:T(8,128)(2,1)} %get-tuple-element.14), channel_id=1, source_target_pairs={{0,18},{2,0},{16,2},{18,16},{1,19},{3,1},{17,3},{19,17},{4,22},{6,... | collective-permute-start | bytes 921608 | tf_op jit(solution)/shard_map/ppermute | solution.py:240
  32.8 16.9 %collective-permute-start.5 = (bf16[4,12,80,40]{2,3,1,0:T(8,128)(2,1)}, bf16[4,12,80,40]{2,3,1,0:T(8,128)(2,1)S(1)}, u32[]{:S(2)}, u32[]{:S(2)}) collective-permute-start(bf16[4,12,80,40]{2,3,1,0:T(8,128)(2,1)} %get-tuple-element.14), channel_id=1, source_target_pairs={{0,2},{2,16},{16,18},{18,0},{1,3},{3,17},{17,19},{19,1},{4,6},{6,2... | collective-permute-start | bytes 921608 | tf_op jit(solution)/shard_map/ppermute | solution.py:240
  50.5 7.4 %copy-start.1 = (bf16[2,36,160,128]{3,2,1,0:T(8,128)(2,1)S(1)}, bf16[2,36,160,128]{3,2,1,0:T(8,128)(2,1)}, u32[]{:S(2)}) copy-start(bf16[2,36,160,128]{3,2,1,0:T(8,128)(2,1)} %fusion.12) | copy-start | bytes 8847364
  58.0 10.9 %copy-start.2 = (bf16[4,4,12,80,40]{3,4,2,1,0:T(8,128)(2,1)}, bf16[4,4,12,80,40]{3,4,2,1,0:T(8,128)(2,1)S(1)}, u32[]{:S(2)}) copy-start(bf16[4,4,12,80,40]{3,4,2,1,0:T(8,128)(2,1)S(1)} %constant_dynamic-slice_fusion.2) | copy-start | bytes 3686404
  58.0 10.5 %copy-start.7 = (f32[160]{0:T(256)S(1)}, f32[160]{0:T(256)}, u32[]{:S(2)}) copy-start(f32[160]{0:T(256)} %param.13) | copy-start | bytes 1924
  58.0 5.5 %collective-permute-start.6 = (bf16[2,1,160,128]{3,2,1,0:T(8,128)(2,1)S(1)}, bf16[2,1,160,128]{3,2,1,0:T(8,128)(2,1)S(1)}, u32[]{:S(2)}, u32[]{:S(2)}) collective-permute-start(bf16[2,1,160,128]{3,2,1,0:T(8,128)(2,1)S(1)} %get-tuple-element.20), channel_id=1, source_target_pairs={{0,2},{1,3},{4,6},{5,7},{8,10},{9,11},{12,14},{13,15},{16,18},{17,... | collective-permute-start | bytes 245768 | tf_op jit(solution)/shard_map/ppermute | solution.py:23
  61.5 6.3 %collective-permute-start.7 = (bf16[2,1,160,128]{3,2,1,0:T(8,128)(2,1)S(1)}, bf16[2,1,160,128]{3,2,1,0:T(8,128)(2,1)S(1)}, u32[]{:S(2)}, u32[]{:S(2)}) collective-permute-start(bf16[2,1,160,128]{3,2,1,0:T(8,128)(2,1)S(1)} %get-tuple-element.19), channel_id=1, source_target_pairs={{2,0},{3,1},{6,4},{7,5},{10,8},{11,9},{14,12},{15,13},{18,16},{19,... | collective-permute-start | bytes 245768 | tf_op jit(solution)/shard_map/ppermute | solution.py:24
  68.4 6.0 %collective-permute-start.8 = (bf16[2,38,160,128]{3,2,1,0:T(8,128)(2,1)}, bf16[2,38,160,128]{3,2,1,0:T(8,128)(2,1)}, u32[]{:S(2)}, u32[]{:S(2)}) collective-permute-start(bf16[2,38,160,128]{3,2,1,0:T(8,128)(2,1)} %constant_dynamic-update-slice_fusion.xo_ref), channel_id=1, source_target_pairs={{0,1},{1,0},{2,3},{3,2},{4,5},{5,4},{6,7},{7,6},{8,9},{9,8},{10,11... | collective-permute-start | bytes 9338888 | tf_op jit(solution)/shard_map/ppermute | solution.py:16
  100.4 43.9 %copy-start.5 = (f32[160]{0:T(256)S(1)}, f32[160]{0:T(256)}, u32[]{:S(2)}) copy-start(f32[160]{0:T(256)} %param.15) | copy-start | bytes 1924
  100.4 44.0 %copy-start.6 = (f32[160]{0:T(256)S(1)}, f32[160]{0:T(256)}, u32[]{:S(2)}) copy-start(f32[160]{0:T(256)} %param.14) | copy-start | bytes 1924
  100.4 43.9 %collective-permute-start.9 = (bf16[1,36,160,128]{3,2,1,0:T(8,128)(2,1)}, bf16[1,36,160,128]{3,2,1,0:T(8,128)(2,1)}, u32[]{:S(2)}, u32[]{:S(2)}) collective-permute-start(bf16[1,36,160,128]{3,2,1,0:T(8,128)(2,1)} %get-tuple-element.17), channel_id=1, source_target_pairs={{0,4},{4,8},{8,12},{1,5},{5,9},{9,13},{2,6},{6,10},{10,14},{3,7},{... | collective-permute-start | bytes 4423688 | tf_op jit(solution)/shard_map/ppermute | solution.py:267
  105.2 39.1 %collective-permute-start.10 = (bf16[1,36,160,128]{3,2,1,0:T(8,128)(2,1)}, bf16[1,36,160,128]{3,2,1,0:T(8,128)(2,1)}, u32[]{:S(2)}, u32[]{:S(2)}) collective-permute-start(bf16[1,36,160,128]{3,2,1,0:T(8,128)(2,1)} %get-tuple-element.18), channel_id=1, source_target_pairs={{4,0},{8,4},{12,8},{5,1},{9,5},{13,9},{6,2},{10,6},{14,10},{7,3},{... | collective-permute-start | bytes 4423688 | tf_op jit(solution)/shard_map/ppermute | solution.py:268
  144.3 7.7 %copy-start.8 = (f32[160]{0:T(256)S(1)}, f32[160]{0:T(256)}, u32[]{:S(2)}) copy-start(f32[160]{0:T(256)} %param.17) | copy-start | bytes 1924
  152.0 9.9 %collective-permute-start.11 = (bf16[4,36,160,128]{3,2,1,0:T(8,128)(2,1)}, bf16[4,36,160,128]{3,2,1,0:T(8,128)(2,1)}, u32[]{:S(2)}, u32[]{:S(2)}) collective-permute-start(bf16[4,36,160,128]{3,2,1,0:T(8,128)(2,1)} %fusion.13.refs_0_.refs_1_.refs_2_), channel_id=1, source_target_pairs={{0,1},{1,0},{2,3},{3,2},{4,5},{5,4},{6,7},{7,6},{8,9},{9,8},{10,11... | collective-permute-start | bytes 17694728 | tf_op jit(solution)/shard_map/ppermute | solution.py:16

commit v11 on v10

--- a/solution.py
+++ b/solution.py
@@ -244,12 +244,12 @@
     grouped = values.reshape(frames, rows, local_groups, group_size, width)
     average, variance = group_stats(grouped, (1, 3, 4), ("height",))
     act_one = group_act(values, average, variance, norm1_gain, norm1_bias)
-    act_one, shared = lax.optimization_barrier((act_one, shared))
+
+    with_rows = row_halo(act_one)
+    with_rows, shared = lax.optimization_barrier((with_rows, shared))
     full_weight = jnp.transpose(shared, (2, 1, 3, 0, 4)).reshape(12, C, local_chan)
     spatial_full = full_weight[:9].reshape(3, 3, C, local_chan)
     temporal_full = full_weight[9:]
-
-    with_rows = row_halo(act_one)
     own_start = chan_index * local_chan
     other_start = (1 - chan_index) * local_chan
     spatial_rows = jnp.transpose(spatial_full, (0, 1, 3, 2)).reshape(3, 3 * local_chan, C)

time: 179 us -> 176 us (0.983)
  local copies, waits for them, and re-layouts: 36.8 us -> 28.3 us
  other arithmetic: 17.7 us -> 20.7 us
  starting transfers between devices: 20.5 us -> 22.8 us
    unnamed x35, local copies, waits for them, and re-layouts: 20.2 us -> 10.7 us
    ppermute x3, starting transfers between devices: 3.55 us -> 7.21 us  [body(): shared.append(lax.ppermute(along_tm, ('groups', 'height'), pairs))]
    ppermute x1, waiting for transfers between devices: 0.74 us -> 4.01 us  [row_halo(): low = lax.ppermute(block[:, -1:], 'height', forward)]
    concatenate x0 -> x1, other arithmetic: none -> 3 us  [row_halo(): return jnp.concatenate([low, block, high], axis=1)]
  transfers between devices with their start and end apart: 12 -> 12, of which waited for: 6 -> 3; matrix products, arithmetic and copies ran while one was open for 15% -> 16% of each run, Pallas kernels for 0% -> 0%
where the time goes in v11:
time: 176 us; the launch traced here: 175 us
  blocking collectives  40.3 us (23%)
  Pallas kernels  40.2 us (23%)
  local copies, waits for them, and re-layouts  28.3 us (16%)
  starting transfers between devices  22.8 us (13%)
  waiting for transfers between devices  22.5 us (13%)
  other arithmetic  20.7 us (12%)
    psum x3, blocking collectives, group_stats(): table = lax.psum(table, name)  40.3 us
    pallas_call x1, Pallas kernels, spatial_call(): pl.pallas_call(spatial_kernel, out_shape=jax.ShapeDtypeStruct(residual.sh...  24.2 us
    pallas_call x1, Pallas kernels, temporal_call(): pl.pallas_call(temporal_kernel, out_shape=jax.ShapeDtypeStruct(residual.s...  16 us
    ppermute x3, waiting for transfers between devices, body(): shared.append(lax.ppermute(along_tm, ('groups', 'height'), pairs))  12.3 us
    unnamed x35, local copies, waits for them, and re-layouts  10.7 us
    select_n x1, other arithmetic, body(): jnp.where(inside[:, None, None, None], act_two, jnp.zeros_like(act_two))  7.66 us
    ppermute x3, starting transfers between devices, body(): shared.append(lax.ppermute(along_tm, ('groups', 'height'), pairs))  7.21 us
    ppermute x2, waiting for transfers between devices, swap_chan(): return lax.ppermute(block, 'chan', [(0, 1), (1, 0)])  6.12 us
  transfers between devices with their start and end apart: 12, of which 3 were waited for; matrix products, arithmetic and copies ran while one was open for 16% of the time, Pallas kernels for 0%

profile of v11, /device:TPU:0, one launch (start us, length us, event | category | flops | bytes accessed | tf_op | source)
XLA Modules:
  0.0 175.3 jit_solution(10911976597569702723)
XLA Ops:
  0.0 1.8 %copy.39 = bf16[3,80,160]{1,2,0:T(8,128)(2,1)} copy(bf16[3,80,160]{2,1,0:T(8,128)(2,1)} %param.16) | data formatting | bytes 153600 | tf_op args[7]
  1.8 1.3 copy.38
  3.1 1.4 bitcast_dynamic-update-slice_fusion.14
  4.5 4.0 %collective-permute-start.3 = (bf16[12,80,40]{1,2,0:T(8,128)(2,1)S(1)}, bf16[12,80,40]{1,2,0:T(8,128)(2,1)S(1)}, u32[]{:S(2)}, u32[]{:S(2)}) collective-permute-start(bf16[12,80,40]{1,2,0:T(8,128)(2,1)S(1)} %get-tuple-element.16), channel_id=1, source_target_pairs={{0,8},{4,12},{8,0},{12,4},{1,9},{5,13},{9,1},{13,5},{2,10},{6,14},... | collective-permute-start | bytes 230408 | tf_op jit(solution)/shard_map/ppermute | solution.py:34
  8.6 1.3 collective-permute-start.2
  9.9 0.7 collective-permute-start.4
  10.6 2.3 %convert_reduce_fusion = f32[2,160]{1,0:T(2,128)S(1)} fusion(bf16[2,36,160,128]{3,2,1,0:T(8,128)(2,1)} %res_ref.1), kind=kLoop, calls=%fused_computation.3 | loop fusion | flops 2948800 | bytes 2950400 | tf_op jit(solution)/shard_map/reduce_sum | solution.py:43
  12.9 0.1 reduce_sum.101
  13.0 0.1 reduce_sum.120
  13.2 0.1 sub.80
  13.3 0.9 fusion.3
  14.2 0.1 reduce_sum.122
  14.3 0.1 reduce_sum.123
  14.4 4.9 %psum.21 = f32[2,2,2,16]{3,2,0,1:T(2,128)S(1)} all-reduce(f32[2,2,2,16]{3,2,0,1:T(2,128)S(1)} %constant_dynamic-update-slice_fusion), channel_id=1, replica_groups=mesh['groups'=2,'tm'=4,'height'=2,'chan'=2] {'height'}, use_global_device_ids=true, to_apply=%region_4.5 | all-reduce | flops 128 | bytes 1024 | tf_op jit(solution)/shard_map/psum | solution.py:56
  19.5 0.1 mul.97
  19.6 0.1 sub.84
  19.7 3.4 %fusion.12 = bf16[2,36,160,128]{3,2,1,0:T(8,128)(2,1)} fusion(bf16[2,36,160,128]{3,2,1,0:T(8,128)(2,1)S(1)} %copy-done, f32[160]{0:T(256)S(1)} %copy-done.4, f32[160]{0:T(256)S(1)} %copy-done.5, f32[2,160]{1,0:T(2,128)S(1)} %mul.97, f32[2,160]{1,0:T(2,128)S(1)} %sub.84), kind=kLoop, calls=%fused_computation.18 | loop fusion | flops 14745600 | bytes 5902080 | tf_op jit(solution)/shard_map/convert_element_type | solution.py:73
  23.2 0.7 bitcast_dynamic-update-slice_fusion.12
  23.8 0.7 bitcast_dynamic-update-slice_fusion.10
  24.5 0.6 bitcast_dynamic-update-slice_fusion.8
  25.1 0.6 bitcast_dynamic-update-slice_fusion.15
  25.8 0.7 bitcast_dynamic-update-slice_fusion.13
  26.5 0.7 bitcast_dynamic-update-slice_fusion.11
  27.1 0.6 bitcast_dynamic-update-slice_fusion.9
  27.8 2.1 %bitcast_dynamic-update-slice_fusion.6 = (bf16[8,4,12,80,40]{3,4,2,1,0:T(8,128)(2,1)}, bf16[4,12,80,40]{2,3,1,0:T(8,128)(2,1)}) fusion(bf16[8,12,80,40]{2,3,1,0:T(8,128)(2,1)} %bitcast_dynamic-update-slice_fusion.9, s32[]{:T(128)S(6)} %select_n.49), kind=kLoop, calls=%fused_computation.29 | loop fusion | bytes 1290244
  29.9 2.5 %collective-permute-start.5 = (bf16[4,12,80,40]{2,3,1,0:T(8,128)(2,1)}, bf16[4,12,80,40]{2,3,1,0:T(8,128)(2,1)S(1)}, u32[]{:S(2)}, u32[]{:S(2)}) collective-permute-start(bf16[4,12,80,40]{2,3,1,0:T(8,128)(2,1)} %get-tuple-element.14), channel_id=1, source_target_pairs={{0,18},{2,0},{16,2},{18,16},{1,19},{3,1},{17,3},{19,17},{4,22},{6,... | collective-permute-start | bytes 921608 | tf_op jit(solution)/shard_map/ppermute | solution.py:240
  32.3 1.6 fusion.23
  33.9 2.1 %collective-permute-start = (bf16[2,1,160,128]{3,2,1,0:T(8,128)(2,1)}, bf16[2,1,160,128]{3,2,1,0:T(8,128)(2,1)}, u32[]{:S(2)}, u32[]{:S(2)}) collective-permute-start(bf16[2,1,160,128]{3,2,1,0:T(8,128)(2,1)} %get-tuple-element.19), channel_id=1, source_target_pairs={{0,2},{1,3},{4,6},{5,7},{8,10},{9,11},{12,14},{13,15},{16,18},{17,... | collective-permute-start | bytes 245768 | tf_op jit(solution)/shard_map/ppermute | solution.py:23
  36.0 1.3 collective-permute-start.1
  37.3 3.2 %collective-permute-start.7 = (bf16[4,12,80,40]{2,3,1,0:T(8,128)(2,1)}, bf16[4,12,80,40]{2,3,1,0:T(8,128)(2,1)S(1)}, u32[]{:S(2)}, u32[]{:S(2)}) collective-permute-start(bf16[4,12,80,40]{2,3,1,0:T(8,128)(2,1)} %get-tuple-element.14), channel_id=1, source_target_pairs={{0,2},{2,16},{16,18},{18,0},{1,3},{3,17},{17,19},{19,1},{4,6},{6,2... | collective-permute-start | bytes 921608 | tf_op jit(solution)/shard_map/ppermute | solution.py:240
  40.6 1.5 collective-permute-start.6
  42.1 4.0 %collective-permute-done = bf16[2,1,160,128]{3,2,1,0:T(8,128)(2,1)} collective-permute-done((bf16[2,1,160,128]{3,2,1,0:T(8,128)(2,1)}, bf16[2,1,160,128]{3,2,1,0:T(8,128)(2,1)}, u32[]{:S(2)}, u32[]{:S(2)}) %collective-permute-start) | collective-permute-done | bytes 81952 | tf_op jit(solution)/shard_map/ppermute | solution.py:23
  46.1 3.0 %pad_maximum_fusion.xo_ref = bf16[2,38,160,128]{3,2,1,0:T(8,128)(2,1)} fusion(bf16[2,1,160,128]{3,2,1,0:T(8,128)(2,1)} %collective-permute-done.1, bf16[2,36,160,128]{3,2,1,0:T(8,128)(2,1)S(1)} %copy-done.1, bf16[2,1,160,128]{3,2,1,0:T(8,128)(2,1)} %collective-permute-done), kind=kLoop, calls=%fused_computation.20 | loop fusion | flops 3112960 | bytes 6225920 | tf_op jit(solution)/shard_map/concatenate | solution.py:25
  49.2 12.3 %collective-permute-done.6 = bf16[4,12,80,40]{2,3,1,0:T(8,128)(2,1)S(1)} collective-permute-done((bf16[4,12,80,40]{2,3,1,0:T(8,128)(2,1)}, bf16[4,12,80,40]{2,3,1,0:T(8,128)(2,1)S(1)}, u32[]{:S(2)}, u32[]{:S(2)}) %collective-permute-start.6) | collective-permute-done | bytes 307232 | tf_op jit(solution)/shard_map/ppermute | solution.py:240
  61.7 1.1 bitcast_dynamic-update-slice_fusion.7
  63.1 0.3 constant_dynamic-slice_fusion.2
  63.6 0.1 copy.41.b_ref
  63.7 0.3 slice.49
  64.0 1.8 %copy.40 = bf16[9,4,80,4,40]{2,1,4,3,0:T(4,128)(2,1)} copy(bf16[9,4,80,4,40]{2,4,0,1,3:T(8,128)(2,1)S(1)} %slice.49) | data formatting | bytes 1843200 | tf_op jit(solution)/shard_map/slice | solution.py:251
  65.7 3.7 %reshape.114 = bf16[3,3,320,160]{2,3,1,0:T(8,128)(2,1)} reshape(bf16[9,4,80,4,40]{2,1,4,3,0:T(4,128)(2,1)} %copy.40) | data formatting | bytes 1843200 | tf_op jit(solution)/shard_map/reshape | solution.py:251
  69.4 2.2 %constant_dynamic-slice_fusion = (bf16[3,480,160]{2,1,0:T(8,128)(2,1)S(1)}, bf16[3,480,160]{2,1,0:T(8,128)(2,1)S(1)}) fusion(bf16[3,480,320]{2,1,0:T(8,128)(2,1)} %bitcast.68, s32[]{:T(128)S(6)} %select_n.53, s32[]{:T(128)S(6)} %select_n.52), kind=kLoop, calls=%fused_computation.47 | loop fusion | bytes 1843208 | tf_op jit(solution)/shard_map/dynamic_slice | solution.py:260
  71.6 24.2 %shard_map.91.refs_8_ = bf16[2,36,160,128]{3,2,1,0:T(8,128)(2,1)S(1)} custom-call(bf16[2,38,160,128]{3,2,1,0:T(8,128)(2,1)} %pad_maximum_fusion.xo_ref, bf16[2,38,160,128]{3,2,1,0:T(8,128)(2,1)} %collective-permute-done.8.xt_ref, bf16[3,480,160]{2,1,0:T(8,128)(2,1)S(1)} %get-tuple-element.22.wo_ref, bf16[3,480,160]{2,1,0:T(8,128)(2,1)S(1)} %get-tuple-element.21.wt_ref, ...), custom_call_target="tpu_custom_call" | custom-call | flops 8493465600 | bytes 13045760 | tf_op jit(solution)/shard_map/pallas_call | solution.py:118
  95.9 1.8 %fusion.22 = (bf16[1,36,160,128]{3,2,1,0:T(8,128)(2,1)}, bf16[1,36,160,128]{3,2,1,0:T(8,128)(2,1)}) fusion(bf16[2,36,160,128]{3,2,1,0:T(8,128)(2,1)S(1)} %shard_map.91.refs_8_), kind=kLoop, calls=%fused_computation.68 | loop fusion | bytes 5898240 | tf_op jit(solution)/shard_map/slice | solution.py:267
  97.6 4.8 %collective-permute-start.9 = (bf16[1,36,160,128]{3,2,1,0:T(8,128)(2,1)}, bf16[1,36,160,128]{3,2,1,0:T(8,128)(2,1)}, u32[]{:S(2)}, u32[]{:S(2)}) collective-permute-start(bf16[1,36,160,128]{3,2,1,0:T(8,128)(2,1)} %get-tuple-element.17), channel_id=1, source_target_pairs={{0,4},{4,8},{8,12},{1,5},{5,9},{9,13},{2,6},{6,10},{10,14},{3,7},{... | collective-permute-start | bytes 4423688 | tf_op jit(solution)/shard_map/ppermute | solution.py:267
  102.5 1.3 collective-permute-start.10
  103.7 0.5 convert_reduce_fusion.1
  104.3 0.1 reduce_sum.128
  104.3 0.1 reduce_sum.129
  104.5 0.1 sub.93
  104.6 0.9 fusion.1
  105.6 0.1 reduce_sum.131
  105.7 0.1 reduce_sum.132
  105.9 5.0 %psum.22 = f32[8,2,16]{2,0,1:T(8,128)S(1)} all-reduce(f32[8,2,16]{2,0,1:T(8,128)S(1)} %dynamic_update_slice.9), channel_id=1, replica_groups=mesh['groups'=2,'tm'=4,'height'=2,'chan'=2] {'height'}, use_global_device_ids=true, to_apply=%region_12.13 | all-reduce | flops 256 | bytes 2048 | tf_op jit(solution)/shard_map/psum | solution.py:56
  110.9 30.4 %psum.23 = f32[8,2,16]{2,0,1:T(8,128)S(1)} all-reduce(f32[8,2,16]{2,0,1:T(8,128)S(1)} %psum.22), channel_id=1, replica_groups=mesh['groups'=2,'tm'=4,'height'=2,'chan'=2] {'tm'}, use_global_device_ids=true, to_apply=%region_13.14 | all-reduce | flops 256 | bytes 2048 | tf_op jit(solution)/shard_map/psum | solution.py:56
  141.4 0.1 mul.112
  141.5 0.1 sub.97
  141.7 7.7 %fusion.13.refs_0_.refs_1_.refs_2_ = bf16[4,36,160,128]{3,2,1,0:T(8,128)(2,1)} fusion(bf16[1,36,160,128]{3,2,1,0:T(8,128)(2,1)} %collective-permute-done.10, bf16[2,36,160,128]{3,2,1,0:T(8,128)(2,1)S(1)} %shard_map.91.refs_8_, bf16[1,36,160,128]{3,2,1,0:T(8,128)(2,1)} %collective-permute-done.9, f32[160]{0:T(256)S(1)} %copy-done.6, f32[160]{0:T(256)S(1)} %copy-done.7, ...), kind=kLoop, calls=%fused_computation.19 | loop fusion | flops 38338560 | bytes 11799044 | tf_op jit(solution)/shard_map/jit(_where)/select_n | solution.py:279
  149.4 0.1 copy.44.refs_9_
  149.5 1.1 slice.54
  150.6 1.0 copy.43
  151.5 1.4 slice.44
  152.9 0.2 dynamic-slice_bitcast_fusion
  153.2 6.1 %collective-permute-done.11.refs_3_.refs_4_.refs_5_ = bf16[4,36,160,128]{3,2,1,0:T(8,128)(2,1)} collective-permute-done((bf16[4,36,160,128]{3,2,1,0:T(8,128)(2,1)}, bf16[4,36,160,128]{3,2,1,0:T(8,128)(2,1)}, u32[]{:S(2)}, u32[]{:S(2)}) %collective-permute-start.11) | collective-permute-done | bytes 5898272 | tf_op jit(solution)/shard_map/ppermute | solution.py:16
  159.3 16.0 %shard_map.92 = bf16[2,36,160,128]{3,2,1,0:T(8,128)(2,1)} custom-call(bf16[4,36,160,128]{3,2,1,0:T(8,128)(2,1)} %fusion.13.refs_0_.refs_1_.refs_2_, bf16[4,36,160,128]{3,2,1,0:T(8,128)(2,1)} %fusion.13.refs_0_.refs_1_.refs_2_, bf16[4,36,160,128]{3,2,1,0:T(8,128)(2,1)} %fusion.13.refs_0_.refs_1_.refs_2_, ...), custom_call_target="tpu_custom_call" | custom-call | flops 2831155200 | bytes 23900160 | tf_op jit(solution)/shard_map/pallas_call | solution.py:171
  (59 shorter events, 1.2 us)
Async XLA Ops:
  0.0 13.3 %copy-start = (bf16[2,36,160,128]{3,2,1,0:T(8,128)(2,1)S(1)}, bf16[2,36,160,128]{3,2,1,0:T(8,128)(2,1)}, u32[]{:S(2)}) copy-start(bf16[2,36,160,128]{3,2,1,0:T(8,128)(2,1)} %res_ref.1) | copy-start | bytes 8847364
  0.0 19.7 %copy-start.4 = (f32[160]{0:T(256)S(1)}, f32[160]{0:T(256)}, u32[]{:S(2)}) copy-start(f32[160]{0:T(256)} %param.11) | copy-start | bytes 1924
  0.0 19.7 %copy-start.5 = (f32[160]{0:T(256)S(1)}, f32[160]{0:T(256)}, u32[]{:S(2)}) copy-start(f32[160]{0:T(256)} %param.10) | copy-start | bytes 1924
  4.5 19.3 %collective-permute-start.3 = (bf16[12,80,40]{1,2,0:T(8,128)(2,1)S(1)}, bf16[12,80,40]{1,2,0:T(8,128)(2,1)S(1)}, u32[]{:S(2)}, u32[]{:S(2)}) collective-permute-start(bf16[12,80,40]{1,2,0:T(8,128)(2,1)S(1)} %get-tuple-element.16), channel_id=1, source_target_pairs={{0,8},{4,12},{8,0},{12,4},{1,9},{5,13},{9,1},{13,5},{2,10},{6,14},... | collective-permute-start | bytes 230408 | tf_op jit(solution)/shard_map/ppermute | solution.py:34
  8.6 14.6 %collective-permute-start.2 = (bf16[12,80,40]{1,2,0:T(8,128)(2,1)S(1)}, bf16[12,80,40]{1,2,0:T(8,128)(2,1)S(1)}, u32[]{:S(2)}, u32[]{:S(2)}) collective-permute-start(bf16[12,80,40]{1,2,0:T(8,128)(2,1)S(1)} %get-tuple-element.16), channel_id=1, source_target_pairs={{0,12},{4,0},{8,4},{12,8},{1,13},{5,1},{9,5},{13,9},{2,14},{6,2},{... | collective-permute-start | bytes 230408 | tf_op jit(solution)/shard_map/ppermute | solution.py:34
  9.9 14.6 %collective-permute-start.4 = (bf16[12,80,40]{1,2,0:T(8,128)(2,1)S(1)}, bf16[12,80,40]{1,2,0:T(8,128)(2,1)S(1)}, u32[]{:S(2)}, u32[]{:S(2)}) collective-permute-start(bf16[12,80,40]{1,2,0:T(8,128)(2,1)S(1)} %get-tuple-element.16), channel_id=1, source_target_pairs={{0,4},{4,8},{8,12},{12,0},{1,5},{5,9},{9,13},{13,1},{2,6},{6,10},{... | collective-permute-start | bytes 230408 | tf_op jit(solution)/shard_map/ppermute | solution.py:34
  23.1 23.0 %copy-start.1 = (bf16[2,36,160,128]{3,2,1,0:T(8,128)(2,1)S(1)}, bf16[2,36,160,128]{3,2,1,0:T(8,128)(2,1)}, u32[]{:S(2)}) copy-start(bf16[2,36,160,128]{3,2,1,0:T(8,128)(2,1)} %fusion.12) | copy-start | bytes 8847364
  29.9 19.2 %collective-permute-start.5 = (bf16[4,12,80,40]{2,3,1,0:T(8,128)(2,1)}, bf16[4,12,80,40]{2,3,1,0:T(8,128)(2,1)S(1)}, u32[]{:S(2)}, u32[]{:S(2)}) collective-permute-start(bf16[4,12,80,40]{2,3,1,0:T(8,128)(2,1)} %get-tuple-element.14), channel_id=1, source_target_pairs={{0,18},{2,0},{16,2},{18,16},{1,19},{3,1},{17,3},{19,17},{4,22},{6,... | collective-permute-start | bytes 921608 | tf_op jit(solution)/shard_map/ppermute | solution.py:240
  33.9 12.2 %collective-permute-start = (bf16[2,1,160,128]{3,2,1,0:T(8,128)(2,1)}, bf16[2,1,160,128]{3,2,1,0:T(8,128)(2,1)}, u32[]{:S(2)}, u32[]{:S(2)}) collective-permute-start(bf16[2,1,160,128]{3,2,1,0:T(8,128)(2,1)} %get-tuple-element.19), channel_id=1, source_target_pairs={{0,2},{1,3},{4,6},{5,7},{8,10},{9,11},{12,14},{13,15},{16,18},{17,... | collective-permute-start | bytes 245768 | tf_op jit(solution)/shard_map/ppermute | solution.py:23
  36.0 10.1 %collective-permute-start.1 = (bf16[2,1,160,128]{3,2,1,0:T(8,128)(2,1)S(1)}, bf16[2,1,160,128]{3,2,1,0:T(8,128)(2,1)}, u32[]{:S(2)}, u32[]{:S(2)}) collective-permute-start(bf16[2,1,160,128]{3,2,1,0:T(8,128)(2,1)S(1)} %get-tuple-element.20), channel_id=1, source_target_pairs={{2,0},{3,1},{6,4},{7,5},{10,8},{11,9},{14,12},{15,13},{18,16},{19,... | collective-permute-start | bytes 245768 | tf_op jit(solution)/shard_map/ppermute | solution.py:24
  37.3 11.8 %copy-start.3 = (bf16[8,4,12,80,40]{3,4,2,1,0:T(8,128)(2,1)S(1)}, bf16[8,4,12,80,40]{3,4,2,1,0:T(8,128)(2,1)}, u32[]{:S(2)}) copy-start(bf16[8,4,12,80,40]{3,4,2,1,0:T(8,128)(2,1)} %get-tuple-element.13) | copy-start | bytes 7372804
  37.3 24.3 %collective-permute-start.7 = (bf16[4,12,80,40]{2,3,1,0:T(8,128)(2,1)}, bf16[4,12,80,40]{2,3,1,0:T(8,128)(2,1)S(1)}, u32[]{:S(2)}, u32[]{:S(2)}) collective-permute-start(bf16[4,12,80,40]{2,3,1,0:T(8,128)(2,1)} %get-tuple-element.14), channel_id=1, source_target_pairs={{0,2},{2,16},{16,18},{18,0},{1,3},{3,17},{17,19},{19,1},{4,6},{6,2... | collective-permute-start | bytes 921608 | tf_op jit(solution)/shard_map/ppermute | solution.py:240
  40.6 21.0 %collective-permute-start.6 = (bf16[4,12,80,40]{2,3,1,0:T(8,128)(2,1)}, bf16[4,12,80,40]{2,3,1,0:T(8,128)(2,1)S(1)}, u32[]{:S(2)}, u32[]{:S(2)}) collective-permute-start(bf16[4,12,80,40]{2,3,1,0:T(8,128)(2,1)} %get-tuple-element.14), channel_id=1, source_target_pairs={{0,16},{2,18},{16,0},{18,2},{1,17},{3,19},{17,1},{19,3},{4,20},{6,... | collective-permute-start | bytes 921608 | tf_op jit(solution)/shard_map/ppermute | solution.py:240
  61.7 1.8 %copy-start.8 = (f32[160]{0:T(256)S(1)}, f32[160]{0:T(256)}, u32[]{:S(2)}) copy-start(f32[160]{0:T(256)} %param.13) | copy-start | bytes 1924
  63.5 5.9 %copy-start.2 = (bf16[4,4,12,80,40]{3,4,2,1,0:T(8,128)(2,1)}, bf16[4,4,12,80,40]{3,4,2,1,0:T(8,128)(2,1)S(1)}, u32[]{:S(2)}) copy-start(bf16[4,4,12,80,40]{3,4,2,1,0:T(8,128)(2,1)S(1)} %constant_dynamic-slice_fusion.2) | copy-start | bytes 3686404
  63.5 8.2 %collective-permute-start.8 = (bf16[2,38,160,128]{3,2,1,0:T(8,128)(2,1)}, bf16[2,38,160,128]{3,2,1,0:T(8,128)(2,1)}, u32[]{:S(2)}, u32[]{:S(2)}) collective-permute-start(bf16[2,38,160,128]{3,2,1,0:T(8,128)(2,1)} %pad_maximum_fusion.xo_ref), channel_id=1, source_target_pairs={{0,1},{1,0},{2,3},{3,2},{4,5},{5,4},{6,7},{7,6},{8,9},{9,8},{10,11... | collective-permute-start | bytes 9338888 | tf_op jit(solution)/shard_map/ppermute | solution.py:16
  97.6 44.0 %copy-start.6 = (f32[160]{0:T(256)S(1)}, f32[160]{0:T(256)}, u32[]{:S(2)}) copy-start(f32[160]{0:T(256)} %param.15) | copy-start | bytes 1924
  97.6 44.0 %copy-start.7 = (f32[160]{0:T(256)S(1)}, f32[160]{0:T(256)}, u32[]{:S(2)}) copy-start(f32[160]{0:T(256)} %param.14) | copy-start | bytes 1924
  97.6 44.0 %collective-permute-start.9 = (bf16[1,36,160,128]{3,2,1,0:T(8,128)(2,1)}, bf16[1,36,160,128]{3,2,1,0:T(8,128)(2,1)}, u32[]{:S(2)}, u32[]{:S(2)}) collective-permute-start(bf16[1,36,160,128]{3,2,1,0:T(8,128)(2,1)} %get-tuple-element.17), channel_id=1, source_target_pairs={{0,4},{4,8},{8,12},{1,5},{5,9},{9,13},{2,6},{6,10},{10,14},{3,7},{... | collective-permute-start | bytes 4423688 | tf_op jit(solution)/shard_map/ppermute | solution.py:267
  102.5 39.2 %collective-permute-start.10 = (bf16[1,36,160,128]{3,2,1,0:T(8,128)(2,1)}, bf16[1,36,160,128]{3,2,1,0:T(8,128)(2,1)}, u32[]{:S(2)}, u32[]{:S(2)}) collective-permute-start(bf16[1,36,160,128]{3,2,1,0:T(8,128)(2,1)} %get-tuple-element.18), channel_id=1, source_target_pairs={{4,0},{8,4},{12,8},{5,1},{9,5},{13,9},{6,2},{10,6},{14,10},{7,3},{... | collective-permute-start | bytes 4423688 | tf_op jit(solution)/shard_map/ppermute | solution.py:268
  141.6 7.7 %copy-start.9 = (f32[160]{0:T(256)S(1)}, f32[160]{0:T(256)}, u32[]{:S(2)}) copy-start(f32[160]{0:T(256)} %param.17) | copy-start | bytes 1924
  149.4 9.9 %collective-permute-start.11 = (bf16[4,36,160,128]{3,2,1,0:T(8,128)(2,1)}, bf16[4,36,160,128]{3,2,1,0:T(8,128)(2,1)}, u32[]{:S(2)}, u32[]{:S(2)}) collective-permute-start(bf16[4,36,160,128]{3,2,1,0:T(8,128)(2,1)} %fusion.13.refs_0_.refs_1_.refs_2_), channel_id=1, source_target_pairs={{0,1},{1,0},{2,3},{3,2},{4,5},{5,4},{6,7},{7,6},{8,9},{9,8},{10,11... | collective-permute-start | bytes 17694728 | tf_op jit(solution)/shard_map/ppermute | solution.py:16

commit v12 on v7

--- a/solution.py
+++ b/solution.py
@@ -80,8 +80,11 @@
     return lax.dynamic_update_slice_in_dim(joined, other, (1 - chan_index) * size, axis=2)
 
 
+STEP = 4
+
+
 def pair(ref, first):
-    return jnp.concatenate([ref[0, first], ref[0, first + 1]], axis=1)
+    return jnp.concatenate([ref[0, first + k] for k in range(STEP)], axis=1)
 
 
 def spatial_kernel(xo_ref, xt_ref, wo_ref, wt_ref, res_ref, b_ref, early_ref, o_ref):
@@ -90,13 +93,13 @@
     bias = b_ref[...]
 
     def two_rows(i, carry):
-        r = 2 * i
+        r = STEP * i
         y = jnp.dot(wo_ref[0], pair(xo_ref, r), preferred_element_type=jnp.float32)
         y = y + jnp.dot(wt_ref[0], pair(xt_ref, r), preferred_element_type=jnp.float32)
         for tap in (1, 2):
             y = y + jnp.dot(wo_ref[tap], pair(xo_ref, r + tap), preferred_element_type=jnp.float32)
             y = y + jnp.dot(wt_ref[tap], pair(xt_ref, r + tap), preferred_element_type=jnp.float32)
-        for half in range(2):
+        for half in range(STEP):
             part = y[:, half * width : (half + 1) * width]
             left = pltpu.roll(part[:local_chan], 1, 1)
             left = jnp.where(lane == 0, 0.0, left)
@@ -108,7 +111,7 @@
             )
         return carry
 
-    lax.fori_loop(0, rows // 2, two_rows, 0)
+    lax.fori_loop(0, rows // STEP, two_rows, 0)
 
 
 def spatial_call(own, other, weight_own, weight_other, residual, bias, early):
@@ -145,20 +148,20 @@
     bias = bias_ref[...]
 
     def two_rows(i, carry):
-        r = 2 * i
+        r = STEP * i
         y = jnp.dot(wo_ref[0], pair(own_refs[0], r), preferred_element_type=jnp.float32)
         y = y + jnp.dot(wt_ref[0], pair(other_refs[0], r), preferred_element_type=jnp.float32)
         for tap in (1, 2):
             y = y + jnp.dot(wo_ref[tap], pair(own_refs[tap], r), preferred_element_type=jnp.float32)
             y = y + jnp.dot(wt_ref[tap], pair(other_refs[tap], r), preferred_element_type=jnp.float32)
-        for half in range(2):
+        for half in range(STEP):
             part = y[:, half * width : (half + 1) * width]
             o_ref[0, r + half] = (res_ref[0, r + half].astype(jnp.float32) + part + bias).astype(
                 o_ref.dtype
             )
         return carry
 
-    lax.fori_loop(0, rows // 2, two_rows, 0)
+    lax.fori_loop(0, rows // STEP, two_rows, 0)
 
 
 def frame_spec(tap, rows, chans, width):

time: 169 us -> 163 us (0.964)
  Pallas kernels: 40.5 us -> 34.2 us
    pallas_call x1, Pallas kernels: 24.5 us -> 21.2 us  [spatial_call(): pl.pallas_call(spatial_kernel, out_shape=jax.ShapeDtypeStruct(residual.sh...]
    pallas_call x1, Pallas kernels: 16 us -> 13.1 us  [temporal_call(): pl.pallas_call(temporal_kernel, out_shape=jax.ShapeDtypeStruct(residual.s...]
where the time goes in v12:
time: 163 us
  blocking collectives  72.2 us (44%)
  Pallas kernels  34.2 us (21%)
  other arithmetic  19.2 us (12%)
  starting transfers between devices  16.5 us (10%)
  waiting for transfers between devices  11.1 us (7%)
  local copies, waits for them, and re-layouts  8.96 us (5%)
    psum x3, blocking collectives, group_stats(): table = lax.psum(table, name)  39.7 us
    all_gather x1, blocking collectives, body(): lax.all_gather(spatial_weight, 'tm', axis=2, tiled=True)  32.5 us
    pallas_call x1, Pallas kernels, spatial_call(): pl.pallas_call(spatial_kernel, out_shape=jax.ShapeDtypeStruct(residual.sh...  21.2 us
    pallas_call x1, Pallas kernels, temporal_call(): pl.pallas_call(temporal_kernel, out_shape=jax.ShapeDtypeStruct(residual.s...  13.1 us
    select_n x1, other arithmetic, body(): jnp.where(inside[:, None, None, None], act_two, jnp.zeros_like(act_two))  7.66 us
    ppermute x2, waiting for transfers between devices, swap_chan(): return lax.ppermute(block, 'chan', [(0, 1), (1, 0)])  6.04 us
    ppermute x1, starting transfers between devices, body(): before = lax.ppermute(hidden[-1:], 'tm', forward)  5.4 us
    ppermute x3, starting transfers between devices, gather_tm(): pieces.append(lax.ppermute(piece, 'tm', pairs))  4.62 us
  transfers between devices with their start and end apart: 9, of which 3 were waited for; matrix products, arithmetic and copies ran while one was open for 5% of the time, Pallas kernels for 0%

profile of v12, /device:TPU:0, one launch (start us, length us, event | category | flops | bytes accessed | tf_op | source)
XLA Modules:
  0.0 162.8 jit_solution(7143659137081087947)
XLA Ops:
  0.0 2.5 %convert_reduce_fusion = f32[2,160]{1,0:T(2,128)S(1)} fusion(bf16[2,36,160,128]{3,2,1,0:T(8,128)(2,1)} %res_ref.1), kind=kLoop, calls=%fused_computation.3 | loop fusion | flops 2948800 | bytes 2950400 | tf_op jit(solution)/shard_map/reduce_sum | solution.py:43
  2.5 0.1 reduce_sum.101
  2.5 0.1 reduce_sum.120
  2.6 0.1 sub.75
  2.7 0.1 sub.76
  2.8 2.7 %fusion.3 = f32[2,160]{1,0:T(2,128)S(1)} fusion(bf16[2,36,160,128]{3,2,1,0:T(8,128)(2,1)} %res_ref.1, f32[2,160]{1,0:T(2,128)S(1)} %sub.76), kind=kLoop, calls=%fused_computation.9 | loop fusion | flops 5897920 | bytes 2951680 | tf_op jit(solution)/shard_map/reduce_sum | solution.py:45
  5.6 0.1 reduce_sum.122
  5.7 0.1 reduce_sum.123
  5.8 5.9 %psum.21 = f32[2,2,2,16]{3,2,0,1:T(2,128)S(1)} all-reduce(f32[2,2,2,16]{3,2,0,1:T(2,128)S(1)} %fusion.16), channel_id=1, replica_groups=mesh['groups'=2,'tm'=4,'height'=2,'chan'=2] {'height'}, use_global_device_ids=true, to_apply=%region_4.5 | all-reduce | flops 128 | bytes 1024 | tf_op jit(solution)/shard_map/psum | solution.py:56
  11.7 0.1 mul.90
  11.7 0.1 mul.91
  11.8 0.1 sub.79
  11.9 0.1 sub.80
  12.0 0.0 copy-start.2
  12.1 0.0 copy-start.8
  12.1 0.0 copy-start.3
  12.1 2.3 %fusion.12 = bf16[2,36,160,128]{3,2,1,0:T(8,128)(2,1)S(1)} fusion(bf16[2,36,160,128]{3,2,1,0:T(8,128)(2,1)S(1)} %copy-done, f32[160]{0:T(256)S(1)} %copy-done.4, f32[160]{0:T(256)S(1)} %copy-done.5, f32[2,160]{1,0:T(2,128)S(1)} %mul.91, f32[2,160]{1,0:T(2,128)S(1)} %sub.80), kind=kLoop, calls=%fused_computation.18 | loop fusion | flops 14745600 | bytes 5902080 | tf_op jit(solution)/shard_map/convert_element_type | solution.py:73
  14.4 4.0 %collective-permute-start = (bf16[2,1,160,128]{3,2,1,0:T(8,128)(2,1)S(1)}, bf16[2,1,160,128]{3,2,1,0:T(8,128)(2,1)S(1)}, u32[]{:S(2)}, u32[]{:S(2)}) collective-permute-start(bf16[2,1,160,128]{3,2,1,0:T(8,128)(2,1)S(1)} %get-tuple-element.11), channel_id=1, source_target_pairs={{0,2},{1,3},{4,6},{5,7},{8,10},{9,11},{12,14},{13,15},{16,18},{17,... | collective-permute-start | bytes 245768 | tf_op jit(solution)/shard_map/ppermute | solution.py:23
  18.4 1.3 collective-permute-start.1
  19.7 0.7 collective-permute-done
  20.4 4.3 %collective-permute-done.1 = bf16[2,1,160,128]{3,2,1,0:T(8,128)(2,1)S(1)} collective-permute-done((bf16[2,1,160,128]{3,2,1,0:T(8,128)(2,1)S(1)}, bf16[2,1,160,128]{3,2,1,0:T(8,128)(2,1)S(1)}, u32[]{:S(2)}, u32[]{:S(2)}) %collective-permute-start.1) | collective-permute-done | bytes 81952 | tf_op jit(solution)/shard_map/ppermute | solution.py:24
  24.7 2.1 %pad_maximum_fusion.xo_ref = bf16[2,38,160,128]{3,2,1,0:T(8,128)(2,1)} fusion(bf16[2,1,160,128]{3,2,1,0:T(8,128)(2,1)S(1)} %collective-permute-done.1, bf16[2,36,160,128]{3,2,1,0:T(8,128)(2,1)S(1)} %fusion.12, bf16[2,1,160,128]{3,2,1,0:T(8,128)(2,1)S(1)} %collective-permute-done), kind=kLoop, calls=%fused_computation.20 | loop fusion | flops 3112960 | bytes 6225920 | tf_op jit(solution)/shard_map/concatenate | solution.py:25
  26.8 0.0 collective-permute-start.2
  26.8 3.6 %collective-permute-start.3 = (bf16[3,80,160]{2,1,0:T(8,128)(2,1)S(1)}, bf16[3,80,160]{2,1,0:T(8,128)(2,1)S(1)}, u32[]{:S(2)}, u32[]{:S(2)}) collective-permute-start(bf16[3,80,160]{2,1,0:T(8,128)(2,1)S(1)} %copy-done.2), channel_id=1, source_target_pairs={{0,12},{4,0},{8,4},{12,8},{1,13},{5,1},{9,5},{13,9},{2,14},{6,2},{... | collective-permute-start | bytes 230408 | tf_op jit(solution)/shard_map/ppermute | solution.py:34
  30.4 0.0 collective-permute-start.5
  30.4 1.0 collective-permute-start.4
  31.4 0.1 copy.22.b_ref
  31.5 32.5 %all_gather.3 = bf16[3,3,320,160]{3,2,1,0:T(8,128)(2,1)S(1)} all-gather(bf16[3,3,80,160]{3,2,1,0:T(8,128)(2,1)S(1)} %copy-done.3), channel_id=1, replica_groups=mesh['groups'=2,'tm'=4,'height'=2,'chan'=2] {'tm'}, dimensions={2}, use_global_device_ids=true | all-gather | bytes 1152000 | tf_op jit(solution)/shard_map/all_gather | solution.py:234
  64.0 0.9 copy.21
  65.0 0.7 constant_dynamic-slice_fusion.1
  65.7 0.0 collective-permute-done.3
  65.7 0.0 collective-permute-done.4
  65.8 0.0 collective-permute-done.5
  65.9 21.2 %shard_map.91.refs_8_ = bf16[2,36,160,128]{3,2,1,0:T(8,128)(2,1)S(1)} custom-call(bf16[2,38,160,128]{3,2,1,0:T(8,128)(2,1)} %pad_maximum_fusion.xo_ref, bf16[2,38,160,128]{3,2,1,0:T(8,128)(2,1)} %collective-permute-done.2.xt_ref, bf16[3,480,160]{2,1,0:T(8,128)(2,1)S(1)} %get-tuple-element.14.wo_ref, bf16[3,480,160]{2,1,0:T(8,128)(2,1)S(1)} %get-tuple-element.13.wt_ref, ...), custom_call_target="tpu_custom_call" | custom-call | flops 8493465600 | bytes 13045760 | tf_op jit(solution)/shard_map/pallas_call | solution.py:121
  87.1 0.0 copy-start.6
  87.1 0.0 copy-start.7
  87.1 1.8 %fusion.21 = (bf16[1,36,160,128]{3,2,1,0:T(8,128)(2,1)}, bf16[1,36,160,128]{3,2,1,0:T(8,128)(2,1)}) fusion(bf16[2,36,160,128]{3,2,1,0:T(8,128)(2,1)S(1)} %shard_map.91.refs_8_), kind=kLoop, calls=%fused_computation.56 | loop fusion | bytes 5898240 | tf_op jit(solution)/shard_map/slice | solution.py:260
  89.0 5.4 %collective-permute-start.6 = (bf16[1,36,160,128]{3,2,1,0:T(8,128)(2,1)}, bf16[1,36,160,128]{3,2,1,0:T(8,128)(2,1)}, u32[]{:S(2)}, u32[]{:S(2)}) collective-permute-start(bf16[1,36,160,128]{3,2,1,0:T(8,128)(2,1)} %get-tuple-element.9), channel_id=1, source_target_pairs={{0,4},{4,8},{8,12},{1,5},{5,9},{9,13},{2,6},{6,10},{10,14},{3,7},{... | collective-permute-start | bytes 4423688 | tf_op jit(solution)/shard_map/ppermute | solution.py:260
  94.4 1.3 collective-permute-start.7
  95.6 0.5 convert_reduce_fusion.1
  96.2 0.1 reduce_sum.128
  96.2 0.1 reduce_sum.129
  96.4 0.1 sub.87
  96.4 0.1 sub.88
  96.5 0.9 fusion.1
  97.5 0.1 reduce_sum.131
  97.6 0.1 reduce_sum.132
  97.8 5.0 %psum.22 = f32[8,2,16]{2,0,1:T(8,128)S(1)} all-reduce(f32[8,2,16]{2,0,1:T(8,128)S(1)} %dynamic_update_slice.9), channel_id=1, replica_groups=mesh['groups'=2,'tm'=4,'height'=2,'chan'=2] {'height'}, use_global_device_ids=true, to_apply=%region_12.13 | all-reduce | flops 256 | bytes 2048 | tf_op jit(solution)/shard_map/psum | solution.py:56
  102.8 28.9 %psum.23 = f32[8,2,16]{2,0,1:T(8,128)S(1)} all-reduce(f32[8,2,16]{2,0,1:T(8,128)S(1)} %psum.22), channel_id=1, replica_groups=mesh['groups'=2,'tm'=4,'height'=2,'chan'=2] {'tm'}, use_global_device_ids=true, to_apply=%region_13.14 | all-reduce | flops 256 | bytes 2048 | tf_op jit(solution)/shard_map/psum | solution.py:56
  131.7 0.1 mul.103
  131.8 0.1 mul.104
  131.9 0.1 sub.91
  131.9 0.1 sub.92
  132.0 0.0 copy-start.9
  132.1 0.0 collective-permute-done.7
  132.1 7.7 %fusion.13.refs_0_.refs_1_.refs_2_ = bf16[4,36,160,128]{3,2,1,0:T(8,128)(2,1)} fusion(bf16[1,36,160,128]{3,2,1,0:T(8,128)(2,1)} %collective-permute-done.7, bf16[2,36,160,128]{3,2,1,0:T(8,128)(2,1)S(1)} %shard_map.91.refs_8_, bf16[1,36,160,128]{3,2,1,0:T(8,128)(2,1)} %collective-permute-done.6, f32[160]{0:T(256)S(1)} %copy-done.6, f32[160]{0:T(256)S(1)} %copy-done.7, ...), kind=kLoop, calls=%fused_computation.19 | loop fusion | flops 38338560 | bytes 11799044 | tf_op jit(solution)/shard_map/jit(_where)/select_n | solution.py:272
  139.8 0.0 collective-permute-start.8
  139.8 0.1 copy.25.refs_9_
  139.9 1.1 fusion.23
  140.9 1.1 copy.24
  142.0 1.4 reshape.107
  143.4 0.2 dynamic-slice_bitcast_fusion
  143.7 6.0 %collective-permute-done.8.refs_3_.refs_4_.refs_5_ = bf16[4,36,160,128]{3,2,1,0:T(8,128)(2,1)} collective-permute-done((bf16[4,36,160,128]{3,2,1,0:T(8,128)(2,1)}, bf16[4,36,160,128]{3,2,1,0:T(8,128)(2,1)}, u32[]{:S(2)}, u32[]{:S(2)}) %collective-permute-start.8) | collective-permute-done | bytes 5898272 | tf_op jit(solution)/shard_map/ppermute | solution.py:16
  149.7 13.1 %shard_map.92 = bf16[2,36,160,128]{3,2,1,0:T(8,128)(2,1)} custom-call(bf16[4,36,160,128]{3,2,1,0:T(8,128)(2,1)} %fusion.13.refs_0_.refs_1_.refs_2_, bf16[4,36,160,128]{3,2,1,0:T(8,128)(2,1)} %fusion.13.refs_0_.refs_1_.refs_2_, bf16[4,36,160,128]{3,2,1,0:T(8,128)(2,1)} %fusion.13.refs_0_.refs_1_.refs_2_, ...), custom_call_target="tpu_custom_call" | custom-call | flops 2831155200 | bytes 23900160 | tf_op jit(solution)/shard_map/pallas_call | solution.py:175
  (42 shorter events, 0.4 us)
Async XLA Ops:
  0.0 12.0 %copy-start = (bf16[2,36,160,128]{3,2,1,0:T(8,128)(2,1)S(1)}, bf16[2,36,160,128]{3,2,1,0:T(8,128)(2,1)}, u32[]{:S(2)}) copy-start(bf16[2,36,160,128]{3,2,1,0:T(8,128)(2,1)} %res_ref.1) | copy-start | bytes 8847364
  0.0 12.0 %copy-start.4 = (f32[160]{0:T(256)S(1)}, f32[160]{0:T(256)}, u32[]{:S(2)}) copy-start(f32[160]{0:T(256)} %param.11) | copy-start | bytes 1924
  0.0 12.0 %copy-start.5 = (f32[160]{0:T(256)S(1)}, f32[160]{0:T(256)}, u32[]{:S(2)}) copy-start(f32[160]{0:T(256)} %param.10) | copy-start | bytes 1924
  12.0 14.8 %copy-start.2 = (bf16[3,80,160]{2,1,0:T(8,128)(2,1)S(1)}, bf16[3,80,160]{2,1,0:T(8,128)(2,1)}, u32[]{:S(2)}) copy-start(bf16[3,80,160]{2,1,0:T(8,128)(2,1)} %param.16) | copy-start | bytes 230404
  12.1 19.4 %copy-start.8 = (f32[160]{0:T(256)S(1)}, f32[160]{0:T(256)}, u32[]{:S(2)}) copy-start(f32[160]{0:T(256)} %param.13) | copy-start | bytes 1924
  12.1 19.5 %copy-start.3 = (bf16[3,3,80,160]{3,2,1,0:T(8,128)(2,1)S(1)}, bf16[3,3,80,160]{3,2,1,0:T(8,128)(2,1)}, u32[]{:S(2)}) copy-start(bf16[3,3,80,160]{3,2,1,0:T(8,128)(2,1)} %param.12) | copy-start | bytes 691204
  14.4 6.0 %collective-permute-start = (bf16[2,1,160,128]{3,2,1,0:T(8,128)(2,1)S(1)}, bf16[2,1,160,128]{3,2,1,0:T(8,128)(2,1)S(1)}, u32[]{:S(2)}, u32[]{:S(2)}) collective-permute-start(bf16[2,1,160,128]{3,2,1,0:T(8,128)(2,1)S(1)} %get-tuple-element.11), channel_id=1, source_target_pairs={{0,2},{1,3},{4,6},{5,7},{8,10},{9,11},{12,14},{13,15},{16,18},{17,... | collective-permute-start | bytes 245768 | tf_op jit(solution)/shard_map/ppermute | solution.py:23
  18.4 6.3 %collective-permute-start.1 = (bf16[2,1,160,128]{3,2,1,0:T(8,128)(2,1)S(1)}, bf16[2,1,160,128]{3,2,1,0:T(8,128)(2,1)S(1)}, u32[]{:S(2)}, u32[]{:S(2)}) collective-permute-start(bf16[2,1,160,128]{3,2,1,0:T(8,128)(2,1)S(1)} %get-tuple-element.12), channel_id=1, source_target_pairs={{2,0},{3,1},{6,4},{7,5},{10,8},{11,9},{14,12},{15,13},{18,16},{19,... | collective-permute-start | bytes 245768 | tf_op jit(solution)/shard_map/ppermute | solution.py:24
  26.8 39.1 %collective-permute-start.2 = (bf16[2,38,160,128]{3,2,1,0:T(8,128)(2,1)}, bf16[2,38,160,128]{3,2,1,0:T(8,128)(2,1)}, u32[]{:S(2)}, u32[]{:S(2)}) collective-permute-start(bf16[2,38,160,128]{3,2,1,0:T(8,128)(2,1)} %pad_maximum_fusion.xo_ref), channel_id=1, source_target_pairs={{0,1},{1,0},{2,3},{3,2},{4,5},{5,4},{6,7},{7,6},{8,9},{9,8},{10,11... | collective-permute-start | bytes 9338888 | tf_op jit(solution)/shard_map/ppermute | solution.py:16
  26.8 38.9 %collective-permute-start.3 = (bf16[3,80,160]{2,1,0:T(8,128)(2,1)S(1)}, bf16[3,80,160]{2,1,0:T(8,128)(2,1)S(1)}, u32[]{:S(2)}, u32[]{:S(2)}) collective-permute-start(bf16[3,80,160]{2,1,0:T(8,128)(2,1)S(1)} %copy-done.2), channel_id=1, source_target_pairs={{0,12},{4,0},{8,4},{12,8},{1,13},{5,1},{9,5},{13,9},{2,14},{6,2},{... | collective-permute-start | bytes 230408 | tf_op jit(solution)/shard_map/ppermute | solution.py:34
  30.4 35.4 %collective-permute-start.5 = (bf16[3,80,160]{2,1,0:T(8,128)(2,1)S(1)}, bf16[3,80,160]{2,1,0:T(8,128)(2,1)S(1)}, u32[]{:S(2)}, u32[]{:S(2)}) collective-permute-start(bf16[3,80,160]{2,1,0:T(8,128)(2,1)S(1)} %copy-done.2), channel_id=1, source_target_pairs={{0,4},{4,8},{8,12},{12,0},{1,5},{5,9},{9,13},{13,1},{2,6},{6,10},{... | collective-permute-start | bytes 230408 | tf_op jit(solution)/shard_map/ppermute | solution.py:34
  30.4 35.3 %collective-permute-start.4 = (bf16[3,80,160]{2,1,0:T(8,128)(2,1)S(1)}, bf16[3,80,160]{2,1,0:T(8,128)(2,1)S(1)}, u32[]{:S(2)}, u32[]{:S(2)}) collective-permute-start(bf16[3,80,160]{2,1,0:T(8,128)(2,1)S(1)} %copy-done.2), channel_id=1, source_target_pairs={{0,8},{4,12},{8,0},{12,4},{1,9},{5,13},{9,1},{13,5},{2,10},{6,14},... | collective-permute-start | bytes 230408 | tf_op jit(solution)/shard_map/ppermute | solution.py:34
  65.9 21.3 %copy-start.1 = (bf16[8,3,80,160]{3,2,1,0:T(8,128)(2,1)}, bf16[8,3,80,160]{3,2,1,0:T(8,128)(2,1)S(1)}, u32[]{:S(2)}) copy-start(bf16[8,3,80,160]{3,2,1,0:T(8,128)(2,1)S(1)} %bitcast_dynamic-update-slice_fusion.1) | copy-start | bytes 1843204
  87.1 44.9 %copy-start.6 = (f32[160]{0:T(256)S(1)}, f32[160]{0:T(256)}, u32[]{:S(2)}) copy-start(f32[160]{0:T(256)} %param.15) | copy-start | bytes 1924
  87.1 44.9 %copy-start.7 = (f32[160]{0:T(256)S(1)}, f32[160]{0:T(256)}, u32[]{:S(2)}) copy-start(f32[160]{0:T(256)} %param.14) | copy-start | bytes 1924
  89.0 43.1 %collective-permute-start.6 = (bf16[1,36,160,128]{3,2,1,0:T(8,128)(2,1)}, bf16[1,36,160,128]{3,2,1,0:T(8,128)(2,1)}, u32[]{:S(2)}, u32[]{:S(2)}) collective-permute-start(bf16[1,36,160,128]{3,2,1,0:T(8,128)(2,1)} %get-tuple-element.9), channel_id=1, source_target_pairs={{0,4},{4,8},{8,12},{1,5},{5,9},{9,13},{2,6},{6,10},{10,14},{3,7},{... | collective-permute-start | bytes 4423688 | tf_op jit(solution)/shard_map/ppermute | solution.py:260
  94.4 37.7 %collective-permute-start.7 = (bf16[1,36,160,128]{3,2,1,0:T(8,128)(2,1)}, bf16[1,36,160,128]{3,2,1,0:T(8,128)(2,1)}, u32[]{:S(2)}, u32[]{:S(2)}) collective-permute-start(bf16[1,36,160,128]{3,2,1,0:T(8,128)(2,1)} %get-tuple-element.10), channel_id=1, source_target_pairs={{4,0},{8,4},{12,8},{5,1},{9,5},{13,9},{6,2},{10,6},{14,10},{7,3},{... | collective-permute-start | bytes 4423688 | tf_op jit(solution)/shard_map/ppermute | solution.py:261
  132.0 7.7 %copy-start.9 = (f32[160]{0:T(256)S(1)}, f32[160]{0:T(256)}, u32[]{:S(2)}) copy-start(f32[160]{0:T(256)} %param.17) | copy-start | bytes 1924
  139.8 9.9 %collective-permute-start.8 = (bf16[4,36,160,128]{3,2,1,0:T(8,128)(2,1)}, bf16[4,36,160,128]{3,2,1,0:T(8,128)(2,1)}, u32[]{:S(2)}, u32[]{:S(2)}) collective-permute-start(bf16[4,36,160,128]{3,2,1,0:T(8,128)(2,1)} %fusion.13.refs_0_.refs_1_.refs_2_), channel_id=1, source_target_pairs={{0,1},{1,0},{2,3},{3,2},{4,5},{5,4},{6,7},{7,6},{8,9},{9,8},{10,11... | collective-permute-start | bytes 17694728 | tf_op jit(solution)/shard_map/ppermute | solution.py:16

commit v13 on v12

--- a/solution.py
+++ b/solution.py
@@ -80,7 +80,7 @@
     return lax.dynamic_update_slice_in_dim(joined, other, (1 - chan_index) * size, axis=2)
 
 
-STEP = 4
+STEP = 6
 
 
 def pair(ref, first):

time: 163 us -> 161 us (0.988)
  Pallas kernels: 34.2 us -> 31.9 us
where the time goes in v13:
time: 161 us; the launch traced here: 160 us
  blocking collectives  72.2 us (45%)
  Pallas kernels  31.9 us (20%)
  other arithmetic  19.2 us (12%)
  starting transfers between devices  16.5 us (10%)
  waiting for transfers between devices  11.1 us (7%)
  local copies, waits for them, and re-layouts  8.96 us (6%)
    psum x3, blocking collectives, group_stats(): table = lax.psum(table, name)  39.8 us
    all_gather x1, blocking collectives, body(): lax.all_gather(spatial_weight, 'tm', axis=2, tiled=True)  32.5 us
    pallas_call x1, Pallas kernels, spatial_call(): pl.pallas_call(spatial_kernel, out_shape=jax.ShapeDtypeStruct(residual.sh...  19.7 us
    pallas_call x1, Pallas kernels, temporal_call(): pl.pallas_call(temporal_kernel, out_shape=jax.ShapeDtypeStruct(residual.s...  12.2 us
    select_n x1, other arithmetic, body(): jnp.where(inside[:, None, None, None], act_two, jnp.zeros_like(act_two))  7.66 us
    ppermute x2, waiting for transfers between devices, swap_chan(): return lax.ppermute(block, 'chan', [(0, 1), (1, 0)])  6.04 us
    ppermute x1, starting transfers between devices, body(): before = lax.ppermute(hidden[-1:], 'tm', forward)  5.38 us
    ppermute x3, starting transfers between devices, gather_tm(): pieces.append(lax.ppermute(piece, 'tm', pairs))  4.62 us
  transfers between devices with their start and end apart: 9, of which 3 were waited for; matrix products, arithmetic and copies ran while one was open for 5% of the time, Pallas kernels for 0%

profile of v13, /device:TPU:0, one launch (start us, length us, event | category | flops | bytes accessed | tf_op | source)
XLA Modules:
  0.0 160.4 jit_solution(16415103005290011472)
XLA Ops:
  0.0 2.5 %convert_reduce_fusion = f32[2,160]{1,0:T(2,128)S(1)} fusion(bf16[2,36,160,128]{3,2,1,0:T(8,128)(2,1)} %res_ref.1), kind=kLoop, calls=%fused_computation.3 | loop fusion | flops 2948800 | bytes 2950400 | tf_op jit(solution)/shard_map/reduce_sum | solution.py:43
  2.5 0.1 reduce_sum.101
  2.5 0.1 reduce_sum.120
  2.6 0.1 sub.75
  2.7 0.1 sub.76
  2.8 2.7 %fusion.3 = f32[2,160]{1,0:T(2,128)S(1)} fusion(bf16[2,36,160,128]{3,2,1,0:T(8,128)(2,1)} %res_ref.1, f32[2,160]{1,0:T(2,128)S(1)} %sub.76), kind=kLoop, calls=%fused_computation.9 | loop fusion | flops 5897920 | bytes 2951680 | tf_op jit(solution)/shard_map/reduce_sum | solution.py:45
  5.6 0.1 reduce_sum.122
  5.7 0.1 reduce_sum.123
  5.8 5.9 %psum.21 = f32[2,2,2,16]{3,2,0,1:T(2,128)S(1)} all-reduce(f32[2,2,2,16]{3,2,0,1:T(2,128)S(1)} %fusion.16), channel_id=1, replica_groups=mesh['groups'=2,'tm'=4,'height'=2,'chan'=2] {'height'}, use_global_device_ids=true, to_apply=%region_4.5 | all-reduce | flops 128 | bytes 1024 | tf_op jit(solution)/shard_map/psum | solution.py:56
  11.7 0.1 mul.90
  11.7 0.1 mul.91
  11.8 0.1 sub.79
  11.9 0.1 sub.80
  12.0 0.0 copy-start.2
  12.1 0.0 copy-start.8
  12.1 0.0 copy-start.3
  12.1 2.3 %fusion.12 = bf16[2,36,160,128]{3,2,1,0:T(8,128)(2,1)S(1)} fusion(bf16[2,36,160,128]{3,2,1,0:T(8,128)(2,1)S(1)} %copy-done, f32[160]{0:T(256)S(1)} %copy-done.4, f32[160]{0:T(256)S(1)} %copy-done.5, f32[2,160]{1,0:T(2,128)S(1)} %mul.91, f32[2,160]{1,0:T(2,128)S(1)} %sub.80), kind=kLoop, calls=%fused_computation.18 | loop fusion | flops 14745600 | bytes 5902080 | tf_op jit(solution)/shard_map/convert_element_type | solution.py:73
  14.4 4.0 %collective-permute-start = (bf16[2,1,160,128]{3,2,1,0:T(8,128)(2,1)S(1)}, bf16[2,1,160,128]{3,2,1,0:T(8,128)(2,1)S(1)}, u32[]{:S(2)}, u32[]{:S(2)}) collective-permute-start(bf16[2,1,160,128]{3,2,1,0:T(8,128)(2,1)S(1)} %get-tuple-element.11), channel_id=1, source_target_pairs={{0,2},{1,3},{4,6},{5,7},{8,10},{9,11},{12,14},{13,15},{16,18},{17,... | collective-permute-start | bytes 245768 | tf_op jit(solution)/shard_map/ppermute | solution.py:23
  18.4 1.3 collective-permute-start.1
  19.7 0.7 collective-permute-done
  20.4 4.3 %collective-permute-done.1 = bf16[2,1,160,128]{3,2,1,0:T(8,128)(2,1)S(1)} collective-permute-done((bf16[2,1,160,128]{3,2,1,0:T(8,128)(2,1)S(1)}, bf16[2,1,160,128]{3,2,1,0:T(8,128)(2,1)S(1)}, u32[]{:S(2)}, u32[]{:S(2)}) %collective-permute-start.1) | collective-permute-done | bytes 81952 | tf_op jit(solution)/shard_map/ppermute | solution.py:24
  24.7 2.1 %pad_maximum_fusion.xo_ref = bf16[2,38,160,128]{3,2,1,0:T(8,128)(2,1)} fusion(bf16[2,1,160,128]{3,2,1,0:T(8,128)(2,1)S(1)} %collective-permute-done.1, bf16[2,36,160,128]{3,2,1,0:T(8,128)(2,1)S(1)} %fusion.12, bf16[2,1,160,128]{3,2,1,0:T(8,128)(2,1)S(1)} %collective-permute-done), kind=kLoop, calls=%fused_computation.20 | loop fusion | flops 3112960 | bytes 6225920 | tf_op jit(solution)/shard_map/concatenate | solution.py:25
  26.8 0.0 collective-permute-start.2
  26.8 3.6 %collective-permute-start.3 = (bf16[3,80,160]{2,1,0:T(8,128)(2,1)S(1)}, bf16[3,80,160]{2,1,0:T(8,128)(2,1)S(1)}, u32[]{:S(2)}, u32[]{:S(2)}) collective-permute-start(bf16[3,80,160]{2,1,0:T(8,128)(2,1)S(1)} %copy-done.2), channel_id=1, source_target_pairs={{0,12},{4,0},{8,4},{12,8},{1,13},{5,1},{9,5},{13,9},{2,14},{6,2},{... | collective-permute-start | bytes 230408 | tf_op jit(solution)/shard_map/ppermute | solution.py:34
  30.4 0.0 collective-permute-start.5
  30.4 1.0 collective-permute-start.4
  31.4 0.1 copy.22.b_ref
  31.5 32.5 %all_gather.3 = bf16[3,3,320,160]{3,2,1,0:T(8,128)(2,1)S(1)} all-gather(bf16[3,3,80,160]{3,2,1,0:T(8,128)(2,1)S(1)} %copy-done.3), channel_id=1, replica_groups=mesh['groups'=2,'tm'=4,'height'=2,'chan'=2] {'tm'}, dimensions={2}, use_global_device_ids=true | all-gather | bytes 1152000 | tf_op jit(solution)/shard_map/all_gather | solution.py:234
  64.0 0.9 copy.21
  65.0 0.7 constant_dynamic-slice_fusion.1
  65.7 0.0 collective-permute-done.3
  65.7 0.0 collective-permute-done.4
  65.8 0.0 collective-permute-done.5
  65.9 19.7 %shard_map.91.refs_8_ = bf16[2,36,160,128]{3,2,1,0:T(8,128)(2,1)S(1)} custom-call(bf16[2,38,160,128]{3,2,1,0:T(8,128)(2,1)} %pad_maximum_fusion.xo_ref, bf16[2,38,160,128]{3,2,1,0:T(8,128)(2,1)} %collective-permute-done.2.xt_ref, bf16[3,480,160]{2,1,0:T(8,128)(2,1)S(1)} %get-tuple-element.14.wo_ref, bf16[3,480,160]{2,1,0:T(8,128)(2,1)S(1)} %get-tuple-element.13.wt_ref, ...), custom_call_target="tpu_custom_call" | custom-call | flops 8493465600 | bytes 13045760 | tf_op jit(solution)/shard_map/pallas_call | solution.py:121
  85.7 0.0 copy-start.6
  85.7 0.0 copy-start.7
  85.7 1.8 %fusion.21 = (bf16[1,36,160,128]{3,2,1,0:T(8,128)(2,1)}, bf16[1,36,160,128]{3,2,1,0:T(8,128)(2,1)}) fusion(bf16[2,36,160,128]{3,2,1,0:T(8,128)(2,1)S(1)} %shard_map.91.refs_8_), kind=kLoop, calls=%fused_computation.56 | loop fusion | bytes 5898240 | tf_op jit(solution)/shard_map/slice | solution.py:260
  87.5 5.4 %collective-permute-start.6 = (bf16[1,36,160,128]{3,2,1,0:T(8,128)(2,1)}, bf16[1,36,160,128]{3,2,1,0:T(8,128)(2,1)}, u32[]{:S(2)}, u32[]{:S(2)}) collective-permute-start(bf16[1,36,160,128]{3,2,1,0:T(8,128)(2,1)} %get-tuple-element.9), channel_id=1, source_target_pairs={{0,4},{4,8},{8,12},{1,5},{5,9},{9,13},{2,6},{6,10},{10,14},{3,7},{... | collective-permute-start | bytes 4423688 | tf_op jit(solution)/shard_map/ppermute | solution.py:260
  92.9 1.3 collective-permute-start.7
  94.2 0.5 convert_reduce_fusion.1
  94.7 0.1 reduce_sum.128
  94.8 0.1 reduce_sum.129
  94.9 0.1 sub.87
  95.0 0.1 sub.88
  95.1 0.9 fusion.1
  96.0 0.1 reduce_sum.131
  96.1 0.1 reduce_sum.132
  96.3 5.0 %psum.22 = f32[8,2,16]{2,0,1:T(8,128)S(1)} all-reduce(f32[8,2,16]{2,0,1:T(8,128)S(1)} %dynamic_update_slice.9), channel_id=1, replica_groups=mesh['groups'=2,'tm'=4,'height'=2,'chan'=2] {'height'}, use_global_device_ids=true, to_apply=%region_12.13 | all-reduce | flops 256 | bytes 2048 | tf_op jit(solution)/shard_map/psum | solution.py:56
  101.3 28.9 %psum.23 = f32[8,2,16]{2,0,1:T(8,128)S(1)} all-reduce(f32[8,2,16]{2,0,1:T(8,128)S(1)} %psum.22), channel_id=1, replica_groups=mesh['groups'=2,'tm'=4,'height'=2,'chan'=2] {'tm'}, use_global_device_ids=true, to_apply=%region_13.14 | all-reduce | flops 256 | bytes 2048 | tf_op jit(solution)/shard_map/psum | solution.py:56
  130.3 0.1 mul.103
  130.3 0.1 mul.104
  130.4 0.1 sub.91
  130.5 0.1 sub.92
  130.6 0.0 copy-start.9
  130.6 0.0 collective-permute-done.7
  130.6 7.7 %fusion.13.refs_0_.refs_1_.refs_2_ = bf16[4,36,160,128]{3,2,1,0:T(8,128)(2,1)} fusion(bf16[1,36,160,128]{3,2,1,0:T(8,128)(2,1)} %collective-permute-done.7, bf16[2,36,160,128]{3,2,1,0:T(8,128)(2,1)S(1)} %shard_map.91.refs_8_, bf16[1,36,160,128]{3,2,1,0:T(8,128)(2,1)} %collective-permute-done.6, f32[160]{0:T(256)S(1)} %copy-done.6, f32[160]{0:T(256)S(1)} %copy-done.7, ...), kind=kLoop, calls=%fused_computation.19 | loop fusion | flops 38338560 | bytes 11799044 | tf_op jit(solution)/shard_map/jit(_where)/select_n | solution.py:272
  138.3 0.0 collective-permute-start.8
  138.3 0.1 copy.25.refs_9_
  138.4 1.1 fusion.23
  139.5 1.1 copy.24
  140.6 1.4 reshape.107
  142.0 0.2 dynamic-slice_bitcast_fusion
  142.2 6.0 %collective-permute-done.8.refs_3_.refs_4_.refs_5_ = bf16[4,36,160,128]{3,2,1,0:T(8,128)(2,1)} collective-permute-done((bf16[4,36,160,128]{3,2,1,0:T(8,128)(2,1)}, bf16[4,36,160,128]{3,2,1,0:T(8,128)(2,1)}, u32[]{:S(2)}, u32[]{:S(2)}) %collective-permute-start.8) | collective-permute-done | bytes 5898272 | tf_op jit(solution)/shard_map/ppermute | solution.py:16
  148.2 12.2 %shard_map.92 = bf16[2,36,160,128]{3,2,1,0:T(8,128)(2,1)} custom-call(bf16[4,36,160,128]{3,2,1,0:T(8,128)(2,1)} %fusion.13.refs_0_.refs_1_.refs_2_, bf16[4,36,160,128]{3,2,1,0:T(8,128)(2,1)} %fusion.13.refs_0_.refs_1_.refs_2_, bf16[4,36,160,128]{3,2,1,0:T(8,128)(2,1)} %fusion.13.refs_0_.refs_1_.refs_2_, ...), custom_call_target="tpu_custom_call" | custom-call | flops 2831155200 | bytes 23900160 | tf_op jit(solution)/shard_map/pallas_call | solution.py:175
  (42 shorter events, 0.4 us)
Async XLA Ops:
  0.0 12.0 %copy-start = (bf16[2,36,160,128]{3,2,1,0:T(8,128)(2,1)S(1)}, bf16[2,36,160,128]{3,2,1,0:T(8,128)(2,1)}, u32[]{:S(2)}) copy-start(bf16[2,36,160,128]{3,2,1,0:T(8,128)(2,1)} %res_ref.1) | copy-start | bytes 8847364
  0.0 12.0 %copy-start.4 = (f32[160]{0:T(256)S(1)}, f32[160]{0:T(256)}, u32[]{:S(2)}) copy-start(f32[160]{0:T(256)} %param.11) | copy-start | bytes 1924
  0.0 12.0 %copy-start.5 = (f32[160]{0:T(256)S(1)}, f32[160]{0:T(256)}, u32[]{:S(2)}) copy-start(f32[160]{0:T(256)} %param.10) | copy-start | bytes 1924
  12.0 14.8 %copy-start.2 = (bf16[3,80,160]{2,1,0:T(8,128)(2,1)S(1)}, bf16[3,80,160]{2,1,0:T(8,128)(2,1)}, u32[]{:S(2)}) copy-start(bf16[3,80,160]{2,1,0:T(8,128)(2,1)} %param.16) | copy-start | bytes 230404
  12.1 19.4 %copy-start.8 = (f32[160]{0:T(256)S(1)}, f32[160]{0:T(256)}, u32[]{:S(2)}) copy-start(f32[160]{0:T(256)} %param.13) | copy-start | bytes 1924
  12.1 19.5 %copy-start.3 = (bf16[3,3,80,160]{3,2,1,0:T(8,128)(2,1)S(1)}, bf16[3,3,80,160]{3,2,1,0:T(8,128)(2,1)}, u32[]{:S(2)}) copy-start(bf16[3,3,80,160]{3,2,1,0:T(8,128)(2,1)} %param.12) | copy-start | bytes 691204
  14.4 6.0 %collective-permute-start = (bf16[2,1,160,128]{3,2,1,0:T(8,128)(2,1)S(1)}, bf16[2,1,160,128]{3,2,1,0:T(8,128)(2,1)S(1)}, u32[]{:S(2)}, u32[]{:S(2)}) collective-permute-start(bf16[2,1,160,128]{3,2,1,0:T(8,128)(2,1)S(1)} %get-tuple-element.11), channel_id=1, source_target_pairs={{0,2},{1,3},{4,6},{5,7},{8,10},{9,11},{12,14},{13,15},{16,18},{17,... | collective-permute-start | bytes 245768 | tf_op jit(solution)/shard_map/ppermute | solution.py:23
  18.4 6.3 %collective-permute-start.1 = (bf16[2,1,160,128]{3,2,1,0:T(8,128)(2,1)S(1)}, bf16[2,1,160,128]{3,2,1,0:T(8,128)(2,1)S(1)}, u32[]{:S(2)}, u32[]{:S(2)}) collective-permute-start(bf16[2,1,160,128]{3,2,1,0:T(8,128)(2,1)S(1)} %get-tuple-element.12), channel_id=1, source_target_pairs={{2,0},{3,1},{6,4},{7,5},{10,8},{11,9},{14,12},{15,13},{18,16},{19,... | collective-permute-start | bytes 245768 | tf_op jit(solution)/shard_map/ppermute | solution.py:24
  26.8 39.1 %collective-permute-start.2 = (bf16[2,38,160,128]{3,2,1,0:T(8,128)(2,1)}, bf16[2,38,160,128]{3,2,1,0:T(8,128)(2,1)}, u32[]{:S(2)}, u32[]{:S(2)}) collective-permute-start(bf16[2,38,160,128]{3,2,1,0:T(8,128)(2,1)} %pad_maximum_fusion.xo_ref), channel_id=1, source_target_pairs={{0,1},{1,0},{2,3},{3,2},{4,5},{5,4},{6,7},{7,6},{8,9},{9,8},{10,11... | collective-permute-start | bytes 9338888 | tf_op jit(solution)/shard_map/ppermute | solution.py:16
  26.8 38.9 %collective-permute-start.3 = (bf16[3,80,160]{2,1,0:T(8,128)(2,1)S(1)}, bf16[3,80,160]{2,1,0:T(8,128)(2,1)S(1)}, u32[]{:S(2)}, u32[]{:S(2)}) collective-permute-start(bf16[3,80,160]{2,1,0:T(8,128)(2,1)S(1)} %copy-done.2), channel_id=1, source_target_pairs={{0,12},{4,0},{8,4},{12,8},{1,13},{5,1},{9,5},{13,9},{2,14},{6,2},{... | collective-permute-start | bytes 230408 | tf_op jit(solution)/shard_map/ppermute | solution.py:34
  30.4 35.4 %collective-permute-start.5 = (bf16[3,80,160]{2,1,0:T(8,128)(2,1)S(1)}, bf16[3,80,160]{2,1,0:T(8,128)(2,1)S(1)}, u32[]{:S(2)}, u32[]{:S(2)}) collective-permute-start(bf16[3,80,160]{2,1,0:T(8,128)(2,1)S(1)} %copy-done.2), channel_id=1, source_target_pairs={{0,4},{4,8},{8,12},{12,0},{1,5},{5,9},{9,13},{13,1},{2,6},{6,10},{... | collective-permute-start | bytes 230408 | tf_op jit(solution)/shard_map/ppermute | solution.py:34
  30.4 35.3 %collective-permute-start.4 = (bf16[3,80,160]{2,1,0:T(8,128)(2,1)S(1)}, bf16[3,80,160]{2,1,0:T(8,128)(2,1)S(1)}, u32[]{:S(2)}, u32[]{:S(2)}) collective-permute-start(bf16[3,80,160]{2,1,0:T(8,128)(2,1)S(1)} %copy-done.2), channel_id=1, source_target_pairs={{0,8},{4,12},{8,0},{12,4},{1,9},{5,13},{9,1},{13,5},{2,10},{6,14},... | collective-permute-start | bytes 230408 | tf_op jit(solution)/shard_map/ppermute | solution.py:34
  65.9 19.8 %copy-start.1 = (bf16[8,3,80,160]{3,2,1,0:T(8,128)(2,1)}, bf16[8,3,80,160]{3,2,1,0:T(8,128)(2,1)S(1)}, u32[]{:S(2)}) copy-start(bf16[8,3,80,160]{3,2,1,0:T(8,128)(2,1)S(1)} %bitcast_dynamic-update-slice_fusion.1) | copy-start | bytes 1843204
  85.7 44.9 %copy-start.6 = (f32[160]{0:T(256)S(1)}, f32[160]{0:T(256)}, u32[]{:S(2)}) copy-start(f32[160]{0:T(256)} %param.15) | copy-start | bytes 1924
  85.7 44.9 %copy-start.7 = (f32[160]{0:T(256)S(1)}, f32[160]{0:T(256)}, u32[]{:S(2)}) copy-start(f32[160]{0:T(256)} %param.14) | copy-start | bytes 1924
  87.5 43.1 %collective-permute-start.6 = (bf16[1,36,160,128]{3,2,1,0:T(8,128)(2,1)}, bf16[1,36,160,128]{3,2,1,0:T(8,128)(2,1)}, u32[]{:S(2)}, u32[]{:S(2)}) collective-permute-start(bf16[1,36,160,128]{3,2,1,0:T(8,128)(2,1)} %get-tuple-element.9), channel_id=1, source_target_pairs={{0,4},{4,8},{8,12},{1,5},{5,9},{9,13},{2,6},{6,10},{10,14},{3,7},{... | collective-permute-start | bytes 4423688 | tf_op jit(solution)/shard_map/ppermute | solution.py:260
  92.9 37.7 %collective-permute-start.7 = (bf16[1,36,160,128]{3,2,1,0:T(8,128)(2,1)}, bf16[1,36,160,128]{3,2,1,0:T(8,128)(2,1)}, u32[]{:S(2)}, u32[]{:S(2)}) collective-permute-start(bf16[1,36,160,128]{3,2,1,0:T(8,128)(2,1)} %get-tuple-element.10), channel_id=1, source_target_pairs={{4,0},{8,4},{12,8},{5,1},{9,5},{13,9},{6,2},{10,6},{14,10},{7,3},{... | collective-permute-start | bytes 4423688 | tf_op jit(solution)/shard_map/ppermute | solution.py:261
  130.6 7.7 %copy-start.9 = (f32[160]{0:T(256)S(1)}, f32[160]{0:T(256)}, u32[]{:S(2)}) copy-start(f32[160]{0:T(256)} %param.17) | copy-start | bytes 1924
  138.3 9.9 %collective-permute-start.8 = (bf16[4,36,160,128]{3,2,1,0:T(8,128)(2,1)}, bf16[4,36,160,128]{3,2,1,0:T(8,128)(2,1)}, u32[]{:S(2)}, u32[]{:S(2)}) collective-permute-start(bf16[4,36,160,128]{3,2,1,0:T(8,128)(2,1)} %fusion.13.refs_0_.refs_1_.refs_2_), channel_id=1, source_target_pairs={{0,1},{1,0},{2,3},{3,2},{4,5},{5,4},{6,7},{7,6},{8,9},{9,8},{10,11... | collective-permute-start | bytes 17694728 | tf_op jit(solution)/shard_map/ppermute | solution.py:16

commit v14 on v13

--- a/solution.py
+++ b/solution.py
@@ -80,7 +80,7 @@
     return lax.dynamic_update_slice_in_dim(joined, other, (1 - chan_index) * size, axis=2)
 
 
-STEP = 6
+STEP = 12
 
 
 def pair(ref, first):

time: 161 us -> 159 us (0.988)
  Pallas kernels: 31.9 us -> 30 us
where the time goes in v14:
time: 159 us
  blocking collectives  72.4 us (46%)
  Pallas kernels  30 us (19%)
  other arithmetic  19.2 us (12%)
  starting transfers between devices  16.5 us (10%)
  waiting for transfers between devices  11.1 us (7%)
  local copies, waits for them, and re-layouts  8.96 us (6%)
    psum x3, blocking collectives, group_stats(): table = lax.psum(table, name)  39.9 us
    all_gather x1, blocking collectives, body(): lax.all_gather(spatial_weight, 'tm', axis=2, tiled=True)  32.5 us
    pallas_call x1, Pallas kernels, spatial_call(): pl.pallas_call(spatial_kernel, out_shape=jax.ShapeDtypeStruct(residual.sh...  18.8 us
    pallas_call x1, Pallas kernels, temporal_call(): pl.pallas_call(temporal_kernel, out_shape=jax.ShapeDtypeStruct(residual.s...  11.2 us
    select_n x1, other arithmetic, body(): jnp.where(inside[:, None, None, None], act_two, jnp.zeros_like(act_two))  7.66 us
    ppermute x2, waiting for transfers between devices, swap_chan(): return lax.ppermute(block, 'chan', [(0, 1), (1, 0)])  6.04 us
    ppermute x1, starting transfers between devices, body(): before = lax.ppermute(hidden[-1:], 'tm', forward)  5.4 us
    ppermute x3, starting transfers between devices, gather_tm(): pieces.append(lax.ppermute(piece, 'tm', pairs))  4.62 us
  transfers between devices with their start and end apart: 9, of which 3 were waited for; matrix products, arithmetic and copies ran while one was open for 5% of the time, Pallas kernels for 0%

profile of v14, /device:TPU:0, one launch (start us, length us, event | category | flops | bytes accessed | tf_op | source)
XLA Modules:
  0.0 158.7 jit_solution(94772344197941224)
XLA Ops:
  0.0 2.5 %convert_reduce_fusion = f32[2,160]{1,0:T(2,128)S(1)} fusion(bf16[2,36,160,128]{3,2,1,0:T(8,128)(2,1)} %res_ref.1), kind=kLoop, calls=%fused_computation.3 | loop fusion | flops 2948800 | bytes 2950400 | tf_op jit(solution)/shard_map/reduce_sum | solution.py:43
  2.5 0.1 reduce_sum.101
  2.5 0.1 reduce_sum.120
  2.6 0.1 sub.75
  2.7 0.1 sub.76
  2.8 2.7 %fusion.3 = f32[2,160]{1,0:T(2,128)S(1)} fusion(bf16[2,36,160,128]{3,2,1,0:T(8,128)(2,1)} %res_ref.1, f32[2,160]{1,0:T(2,128)S(1)} %sub.76), kind=kLoop, calls=%fused_computation.9 | loop fusion | flops 5897920 | bytes 2951680 | tf_op jit(solution)/shard_map/reduce_sum | solution.py:45
  5.6 0.1 reduce_sum.122
  5.7 0.1 reduce_sum.123
  5.8 5.9 %psum.21 = f32[2,2,2,16]{3,2,0,1:T(2,128)S(1)} all-reduce(f32[2,2,2,16]{3,2,0,1:T(2,128)S(1)} %fusion.16), channel_id=1, replica_groups=mesh['groups'=2,'tm'=4,'height'=2,'chan'=2] {'height'}, use_global_device_ids=true, to_apply=%region_4.5 | all-reduce | flops 128 | bytes 1024 | tf_op jit(solution)/shard_map/psum | solution.py:56
  11.7 0.1 mul.90
  11.7 0.1 mul.91
  11.8 0.1 sub.79
  11.9 0.1 sub.80
  12.0 0.0 copy-start.2
  12.1 0.0 copy-start.8
  12.1 0.0 copy-start.3
  12.1 2.3 %fusion.12 = bf16[2,36,160,128]{3,2,1,0:T(8,128)(2,1)S(1)} fusion(bf16[2,36,160,128]{3,2,1,0:T(8,128)(2,1)S(1)} %copy-done, f32[160]{0:T(256)S(1)} %copy-done.4, f32[160]{0:T(256)S(1)} %copy-done.5, f32[2,160]{1,0:T(2,128)S(1)} %mul.91, f32[2,160]{1,0:T(2,128)S(1)} %sub.80), kind=kLoop, calls=%fused_computation.18 | loop fusion | flops 14745600 | bytes 5902080 | tf_op jit(solution)/shard_map/convert_element_type | solution.py:73
  14.4 4.0 %collective-permute-start = (bf16[2,1,160,128]{3,2,1,0:T(8,128)(2,1)S(1)}, bf16[2,1,160,128]{3,2,1,0:T(8,128)(2,1)S(1)}, u32[]{:S(2)}, u32[]{:S(2)}) collective-permute-start(bf16[2,1,160,128]{3,2,1,0:T(8,128)(2,1)S(1)} %get-tuple-element.11), channel_id=1, source_target_pairs={{0,2},{1,3},{4,6},{5,7},{8,10},{9,11},{12,14},{13,15},{16,18},{17,... | collective-permute-start | bytes 245768 | tf_op jit(solution)/shard_map/ppermute | solution.py:23
  18.4 1.3 collective-permute-start.1
  19.7 0.7 collective-permute-done
  20.4 4.3 %collective-permute-done.1 = bf16[2,1,160,128]{3,2,1,0:T(8,128)(2,1)S(1)} collective-permute-done((bf16[2,1,160,128]{3,2,1,0:T(8,128)(2,1)S(1)}, bf16[2,1,160,128]{3,2,1,0:T(8,128)(2,1)S(1)}, u32[]{:S(2)}, u32[]{:S(2)}) %collective-permute-start.1) | collective-permute-done | bytes 81952 | tf_op jit(solution)/shard_map/ppermute | solution.py:24
  24.7 2.1 %pad_maximum_fusion.xo_ref = bf16[2,38,160,128]{3,2,1,0:T(8,128)(2,1)} fusion(bf16[2,1,160,128]{3,2,1,0:T(8,128)(2,1)S(1)} %collective-permute-done.1, bf16[2,36,160,128]{3,2,1,0:T(8,128)(2,1)S(1)} %fusion.12, bf16[2,1,160,128]{3,2,1,0:T(8,128)(2,1)S(1)} %collective-permute-done), kind=kLoop, calls=%fused_computation.20 | loop fusion | flops 3112960 | bytes 6225920 | tf_op jit(solution)/shard_map/concatenate | solution.py:25
  26.8 0.0 collective-permute-start.2
  26.8 3.6 %collective-permute-start.3 = (bf16[3,80,160]{2,1,0:T(8,128)(2,1)S(1)}, bf16[3,80,160]{2,1,0:T(8,128)(2,1)S(1)}, u32[]{:S(2)}, u32[]{:S(2)}) collective-permute-start(bf16[3,80,160]{2,1,0:T(8,128)(2,1)S(1)} %copy-done.2), channel_id=1, source_target_pairs={{0,12},{4,0},{8,4},{12,8},{1,13},{5,1},{9,5},{13,9},{2,14},{6,2},{... | collective-permute-start | bytes 230408 | tf_op jit(solution)/shard_map/ppermute | solution.py:34
  30.4 0.0 collective-permute-start.5
  30.4 1.0 collective-permute-start.4
  31.4 0.1 copy.22.b_ref
  31.5 32.5 %all_gather.3 = bf16[3,3,320,160]{3,2,1,0:T(8,128)(2,1)S(1)} all-gather(bf16[3,3,80,160]{3,2,1,0:T(8,128)(2,1)S(1)} %copy-done.3), channel_id=1, replica_groups=mesh['groups'=2,'tm'=4,'height'=2,'chan'=2] {'tm'}, dimensions={2}, use_global_device_ids=true | all-gather | bytes 1152000 | tf_op jit(solution)/shard_map/all_gather | solution.py:234
  64.0 0.9 copy.21
  65.0 0.7 constant_dynamic-slice_fusion.1
  65.7 0.0 collective-permute-done.3
  65.7 0.0 collective-permute-done.4
  65.8 0.0 collective-permute-done.5
  65.9 18.8 %shard_map.91.refs_8_ = bf16[2,36,160,128]{3,2,1,0:T(8,128)(2,1)S(1)} custom-call(bf16[2,38,160,128]{3,2,1,0:T(8,128)(2,1)} %pad_maximum_fusion.xo_ref, bf16[2,38,160,128]{3,2,1,0:T(8,128)(2,1)} %collective-permute-done.2.xt_ref, bf16[3,480,160]{2,1,0:T(8,128)(2,1)S(1)} %get-tuple-element.14.wo_ref, bf16[3,480,160]{2,1,0:T(8,128)(2,1)S(1)} %get-tuple-element.13.wt_ref, ...), custom_call_target="tpu_custom_call" | custom-call | flops 8493465600 | bytes 13045760 | tf_op jit(solution)/shard_map/pallas_call | solution.py:121
  84.7 0.0 copy-start.6
  84.7 0.0 copy-start.7
  84.7 1.8 %fusion.21 = (bf16[1,36,160,128]{3,2,1,0:T(8,128)(2,1)}, bf16[1,36,160,128]{3,2,1,0:T(8,128)(2,1)}) fusion(bf16[2,36,160,128]{3,2,1,0:T(8,128)(2,1)S(1)} %shard_map.91.refs_8_), kind=kLoop, calls=%fused_computation.56 | loop fusion | bytes 5898240 | tf_op jit(solution)/shard_map/slice | solution.py:260
  86.5 5.4 %collective-permute-start.6 = (bf16[1,36,160,128]{3,2,1,0:T(8,128)(2,1)}, bf16[1,36,160,128]{3,2,1,0:T(8,128)(2,1)}, u32[]{:S(2)}, u32[]{:S(2)}) collective-permute-start(bf16[1,36,160,128]{3,2,1,0:T(8,128)(2,1)} %get-tuple-element.9), channel_id=1, source_target_pairs={{0,4},{4,8},{8,12},{1,5},{5,9},{9,13},{2,6},{6,10},{10,14},{3,7},{... | collective-permute-start | bytes 4423688 | tf_op jit(solution)/shard_map/ppermute | solution.py:260
  91.9 1.3 collective-permute-start.7
  93.2 0.5 convert_reduce_fusion.1
  93.7 0.1 reduce_sum.128
  93.8 0.1 reduce_sum.129
  94.0 0.1 sub.87
  94.0 0.1 sub.88
  94.1 0.9 fusion.1
  95.1 0.1 reduce_sum.131
  95.2 0.1 reduce_sum.132
  95.3 5.0 %psum.22 = f32[8,2,16]{2,0,1:T(8,128)S(1)} all-reduce(f32[8,2,16]{2,0,1:T(8,128)S(1)} %dynamic_update_slice.9), channel_id=1, replica_groups=mesh['groups'=2,'tm'=4,'height'=2,'chan'=2] {'height'}, use_global_device_ids=true, to_apply=%region_12.13 | all-reduce | flops 256 | bytes 2048 | tf_op jit(solution)/shard_map/psum | solution.py:56
  100.3 29.0 %psum.23 = f32[8,2,16]{2,0,1:T(8,128)S(1)} all-reduce(f32[8,2,16]{2,0,1:T(8,128)S(1)} %psum.22), channel_id=1, replica_groups=mesh['groups'=2,'tm'=4,'height'=2,'chan'=2] {'tm'}, use_global_device_ids=true, to_apply=%region_13.14 | all-reduce | flops 256 | bytes 2048 | tf_op jit(solution)/shard_map/psum | solution.py:56
  129.5 0.1 mul.103
  129.5 0.1 mul.104
  129.6 0.1 sub.91
  129.7 0.1 sub.92
  129.8 0.0 copy-start.9
  129.8 0.0 collective-permute-done.7
  129.9 7.7 %fusion.13.refs_0_.refs_1_.refs_2_ = bf16[4,36,160,128]{3,2,1,0:T(8,128)(2,1)} fusion(bf16[1,36,160,128]{3,2,1,0:T(8,128)(2,1)} %collective-permute-done.7, bf16[2,36,160,128]{3,2,1,0:T(8,128)(2,1)S(1)} %shard_map.91.refs_8_, bf16[1,36,160,128]{3,2,1,0:T(8,128)(2,1)} %collective-permute-done.6, f32[160]{0:T(256)S(1)} %copy-done.6, f32[160]{0:T(256)S(1)} %copy-done.7, ...), kind=kLoop, calls=%fused_computation.19 | loop fusion | flops 38338560 | bytes 11799044 | tf_op jit(solution)/shard_map/jit(_where)/select_n | solution.py:272
  137.5 0.0 collective-permute-start.8
  137.5 0.1 copy.25.refs_9_
  137.6 1.1 fusion.23
  138.7 1.1 copy.24
  139.8 1.4 reshape.107
  141.2 0.2 dynamic-slice_bitcast_fusion
  141.4 6.0 %collective-permute-done.8.refs_3_.refs_4_.refs_5_ = bf16[4,36,160,128]{3,2,1,0:T(8,128)(2,1)} collective-permute-done((bf16[4,36,160,128]{3,2,1,0:T(8,128)(2,1)}, bf16[4,36,160,128]{3,2,1,0:T(8,128)(2,1)}, u32[]{:S(2)}, u32[]{:S(2)}) %collective-permute-start.8) | collective-permute-done | bytes 5898272 | tf_op jit(solution)/shard_map/ppermute | solution.py:16
  147.5 11.2 %shard_map.92 = bf16[2,36,160,128]{3,2,1,0:T(8,128)(2,1)} custom-call(bf16[4,36,160,128]{3,2,1,0:T(8,128)(2,1)} %fusion.13.refs_0_.refs_1_.refs_2_, bf16[4,36,160,128]{3,2,1,0:T(8,128)(2,1)} %fusion.13.refs_0_.refs_1_.refs_2_, bf16[4,36,160,128]{3,2,1,0:T(8,128)(2,1)} %fusion.13.refs_0_.refs_1_.refs_2_, ...), custom_call_target="tpu_custom_call" | custom-call | flops 2831155200 | bytes 23900160 | tf_op jit(solution)/shard_map/pallas_call | solution.py:175
  (42 shorter events, 0.4 us)
Async XLA Ops:
  0.0 12.0 %copy-start = (bf16[2,36,160,128]{3,2,1,0:T(8,128)(2,1)S(1)}, bf16[2,36,160,128]{3,2,1,0:T(8,128)(2,1)}, u32[]{:S(2)}) copy-start(bf16[2,36,160,128]{3,2,1,0:T(8,128)(2,1)} %res_ref.1) | copy-start | bytes 8847364
  0.0 12.0 %copy-start.4 = (f32[160]{0:T(256)S(1)}, f32[160]{0:T(256)}, u32[]{:S(2)}) copy-start(f32[160]{0:T(256)} %param.11) | copy-start | bytes 1924
  0.0 12.0 %copy-start.5 = (f32[160]{0:T(256)S(1)}, f32[160]{0:T(256)}, u32[]{:S(2)}) copy-start(f32[160]{0:T(256)} %param.10) | copy-start | bytes 1924
  12.0 14.8 %copy-start.2 = (bf16[3,80,160]{2,1,0:T(8,128)(2,1)S(1)}, bf16[3,80,160]{2,1,0:T(8,128)(2,1)}, u32[]{:S(2)}) copy-start(bf16[3,80,160]{2,1,0:T(8,128)(2,1)} %param.16) | copy-start | bytes 230404
  12.1 19.4 %copy-start.8 = (f32[160]{0:T(256)S(1)}, f32[160]{0:T(256)}, u32[]{:S(2)}) copy-start(f32[160]{0:T(256)} %param.13) | copy-start | bytes 1924
  12.1 19.5 %copy-start.3 = (bf16[3,3,80,160]{3,2,1,0:T(8,128)(2,1)S(1)}, bf16[3,3,80,160]{3,2,1,0:T(8,128)(2,1)}, u32[]{:S(2)}) copy-start(bf16[3,3,80,160]{3,2,1,0:T(8,128)(2,1)} %param.12) | copy-start | bytes 691204
  14.4 6.0 %collective-permute-start = (bf16[2,1,160,128]{3,2,1,0:T(8,128)(2,1)S(1)}, bf16[2,1,160,128]{3,2,1,0:T(8,128)(2,1)S(1)}, u32[]{:S(2)}, u32[]{:S(2)}) collective-permute-start(bf16[2,1,160,128]{3,2,1,0:T(8,128)(2,1)S(1)} %get-tuple-element.11), channel_id=1, source_target_pairs={{0,2},{1,3},{4,6},{5,7},{8,10},{9,11},{12,14},{13,15},{16,18},{17,... | collective-permute-start | bytes 245768 | tf_op jit(solution)/shard_map/ppermute | solution.py:23
  18.4 6.3 %collective-permute-start.1 = (bf16[2,1,160,128]{3,2,1,0:T(8,128)(2,1)S(1)}, bf16[2,1,160,128]{3,2,1,0:T(8,128)(2,1)S(1)}, u32[]{:S(2)}, u32[]{:S(2)}) collective-permute-start(bf16[2,1,160,128]{3,2,1,0:T(8,128)(2,1)S(1)} %get-tuple-element.12), channel_id=1, source_target_pairs={{2,0},{3,1},{6,4},{7,5},{10,8},{11,9},{14,12},{15,13},{18,16},{19,... | collective-permute-start | bytes 245768 | tf_op jit(solution)/shard_map/ppermute | solution.py:24
  26.8 39.1 %collective-permute-start.2 = (bf16[2,38,160,128]{3,2,1,0:T(8,128)(2,1)}, bf16[2,38,160,128]{3,2,1,0:T(8,128)(2,1)}, u32[]{:S(2)}, u32[]{:S(2)}) collective-permute-start(bf16[2,38,160,128]{3,2,1,0:T(8,128)(2,1)} %pad_maximum_fusion.xo_ref), channel_id=1, source_target_pairs={{0,1},{1,0},{2,3},{3,2},{4,5},{5,4},{6,7},{7,6},{8,9},{9,8},{10,11... | collective-permute-start | bytes 9338888 | tf_op jit(solution)/shard_map/ppermute | solution.py:16
  26.8 38.9 %collective-permute-start.3 = (bf16[3,80,160]{2,1,0:T(8,128)(2,1)S(1)}, bf16[3,80,160]{2,1,0:T(8,128)(2,1)S(1)}, u32[]{:S(2)}, u32[]{:S(2)}) collective-permute-start(bf16[3,80,160]{2,1,0:T(8,128)(2,1)S(1)} %copy-done.2), channel_id=1, source_target_pairs={{0,12},{4,0},{8,4},{12,8},{1,13},{5,1},{9,5},{13,9},{2,14},{6,2},{... | collective-permute-start | bytes 230408 | tf_op jit(solution)/shard_map/ppermute | solution.py:34
  30.4 35.4 %collective-permute-start.5 = (bf16[3,80,160]{2,1,0:T(8,128)(2,1)S(1)}, bf16[3,80,160]{2,1,0:T(8,128)(2,1)S(1)}, u32[]{:S(2)}, u32[]{:S(2)}) collective-permute-start(bf16[3,80,160]{2,1,0:T(8,128)(2,1)S(1)} %copy-done.2), channel_id=1, source_target_pairs={{0,4},{4,8},{8,12},{12,0},{1,5},{5,9},{9,13},{13,1},{2,6},{6,10},{... | collective-permute-start | bytes 230408 | tf_op jit(solution)/shard_map/ppermute | solution.py:34
  30.4 35.3 %collective-permute-start.4 = (bf16[3,80,160]{2,1,0:T(8,128)(2,1)S(1)}, bf16[3,80,160]{2,1,0:T(8,128)(2,1)S(1)}, u32[]{:S(2)}, u32[]{:S(2)}) collective-permute-start(bf16[3,80,160]{2,1,0:T(8,128)(2,1)S(1)} %copy-done.2), channel_id=1, source_target_pairs={{0,8},{4,12},{8,0},{12,4},{1,9},{5,13},{9,1},{13,5},{2,10},{6,14},... | collective-permute-start | bytes 230408 | tf_op jit(solution)/shard_map/ppermute | solution.py:34
  65.9 18.8 %copy-start.1 = (bf16[8,3,80,160]{3,2,1,0:T(8,128)(2,1)}, bf16[8,3,80,160]{3,2,1,0:T(8,128)(2,1)S(1)}, u32[]{:S(2)}) copy-start(bf16[8,3,80,160]{3,2,1,0:T(8,128)(2,1)S(1)} %bitcast_dynamic-update-slice_fusion.1) | copy-start | bytes 1843204
  84.7 45.1 %copy-start.6 = (f32[160]{0:T(256)S(1)}, f32[160]{0:T(256)}, u32[]{:S(2)}) copy-start(f32[160]{0:T(256)} %param.15) | copy-start | bytes 1924
  84.7 45.1 %copy-start.7 = (f32[160]{0:T(256)S(1)}, f32[160]{0:T(256)}, u32[]{:S(2)}) copy-start(f32[160]{0:T(256)} %param.14) | copy-start | bytes 1924
  86.5 43.3 %collective-permute-start.6 = (bf16[1,36,160,128]{3,2,1,0:T(8,128)(2,1)}, bf16[1,36,160,128]{3,2,1,0:T(8,128)(2,1)}, u32[]{:S(2)}, u32[]{:S(2)}) collective-permute-start(bf16[1,36,160,128]{3,2,1,0:T(8,128)(2,1)} %get-tuple-element.9), channel_id=1, source_target_pairs={{0,4},{4,8},{8,12},{1,5},{5,9},{9,13},{2,6},{6,10},{10,14},{3,7},{... | collective-permute-start | bytes 4423688 | tf_op jit(solution)/shard_map/ppermute | solution.py:260
  91.9 37.9 %collective-permute-start.7 = (bf16[1,36,160,128]{3,2,1,0:T(8,128)(2,1)}, bf16[1,36,160,128]{3,2,1,0:T(8,128)(2,1)}, u32[]{:S(2)}, u32[]{:S(2)}) collective-permute-start(bf16[1,36,160,128]{3,2,1,0:T(8,128)(2,1)} %get-tuple-element.10), channel_id=1, source_target_pairs={{4,0},{8,4},{12,8},{5,1},{9,5},{13,9},{6,2},{10,6},{14,10},{7,3},{... | collective-permute-start | bytes 4423688 | tf_op jit(solution)/shard_map/ppermute | solution.py:261
  129.8 7.7 %copy-start.9 = (f32[160]{0:T(256)S(1)}, f32[160]{0:T(256)}, u32[]{:S(2)}) copy-start(f32[160]{0:T(256)} %param.17) | copy-start | bytes 1924
  137.5 9.9 %collective-permute-start.8 = (bf16[4,36,160,128]{3,2,1,0:T(8,128)(2,1)}, bf16[4,36,160,128]{3,2,1,0:T(8,128)(2,1)}, u32[]{:S(2)}, u32[]{:S(2)}) collective-permute-start(bf16[4,36,160,128]{3,2,1,0:T(8,128)(2,1)} %fusion.13.refs_0_.refs_1_.refs_2_), channel_id=1, source_target_pairs={{0,1},{1,0},{2,3},{3,2},{4,5},{5,4},{6,7},{7,6},{8,9},{9,8},{10,11... | collective-permute-start | bytes 17694728 | tf_op jit(solution)/shard_map/ppermute | solution.py:16

commit v15 on v14

--- a/solution.py
+++ b/solution.py
@@ -53,7 +53,10 @@
     table = jnp.zeros((slots,) + mine.shape, jnp.float32)
     table = lax.dynamic_update_index_in_dim(table, mine, slot, 0)
     for name in reversed(slot_axes):
-        table = lax.psum(table, name)
+        if lax.axis_size(name) == 2:
+            table = table + lax.ppermute(table, name, [(0, 1), (1, 0)])
+        else:
+            table = lax.psum(table, name)
     means = table[:, 0]
     average = jnp.sum(means, axis=0) / slots
     spread = means - average

time: 159 us -> 159 us (level)
  blocking collectives: 72.4 us -> 63.6 us
  waiting for transfers between devices: 11.1 us -> 16.3 us
  starting transfers between devices: 16.5 us -> 19.6 us
    psum x3 -> x1, blocking collectives: 39.9 us -> 31.1 us  [group_stats(): table = lax.psum(table, name)]
    ppermute x0 -> x2, waiting for transfers between devices: none -> 5.21 us  [group_stats(): table = table + lax.ppermute(table, name, [(0, 1), (1, 0)])]
    ppermute x0 -> x2, starting transfers between devices: none -> 3.09 us  [group_stats(): table = table + lax.ppermute(table, name, [(0, 1), (1, 0)])]
  transfers between devices with their start and end apart: 9 -> 11, of which waited for: 3 -> 5; matrix products, arithmetic and copies ran while one was open for 5% -> 5% of each run, Pallas kernels for 0% -> 0%
where the time goes in v15:
time: 159 us
  blocking collectives  63.6 us (40%)
  Pallas kernels  29.7 us (19%)
  starting transfers between devices  19.6 us (12%)
  other arithmetic  19.3 us (12%)
  waiting for transfers between devices  16.3 us (10%)
  local copies, waits for them, and re-layouts  9.82 us (6%)
    all_gather x1, blocking collectives, body(): lax.all_gather(spatial_weight, 'tm', axis=2, tiled=True)  32.5 us
    psum x1, blocking collectives, group_stats(): table = lax.psum(table, name)  31.1 us
    pallas_call x1, Pallas kernels, spatial_call(): pl.pallas_call(spatial_kernel, out_shape=jax.ShapeDtypeStruct(residual.sh...  18.5 us
    pallas_call x1, Pallas kernels, temporal_call(): pl.pallas_call(temporal_kernel, out_shape=jax.ShapeDtypeStruct(residual.s...  11.2 us
    select_n x1, other arithmetic, body(): jnp.where(inside[:, None, None, None], act_two, jnp.zeros_like(act_two))  7.66 us
    ppermute x2, waiting for transfers between devices, swap_chan(): return lax.ppermute(block, 'chan', [(0, 1), (1, 0)])  6.04 us
    ppermute x1, starting transfers between devices, body(): before = lax.ppermute(hidden[-1:], 'tm', forward)  5.41 us
    ppermute x2, waiting for transfers between devices, group_stats(): table = table + lax.ppermute(table, name, [(0, 1), (1, 0)])  5.21 us
  transfers between devices with their start and end apart: 11, of which 5 were waited for; matrix products, arithmetic and copies ran while one was open for 5% of the time, Pallas kernels for 0%

profile of v15, /device:TPU:0, one launch (start us, length us, event | category | flops | bytes accessed | tf_op | source)
XLA Modules:
  0.0 158.7 jit_solution(9890581208269552306)
XLA Ops:
  0.0 2.5 %convert_reduce_fusion = f32[2,160]{1,0:T(2,128)S(1)} fusion(bf16[2,36,160,128]{3,2,1,0:T(8,128)(2,1)} %res_ref.1), kind=kLoop, calls=%fused_computation.3 | loop fusion | flops 2948800 | bytes 2950400 | tf_op jit(solution)/shard_map/reduce_sum | solution.py:43
  2.5 0.1 reduce_sum.101
  2.5 0.1 reduce_sum.120
  2.6 0.1 sub.75
  2.7 0.1 sub.76
  2.8 2.7 %fusion.3 = f32[2,160]{1,0:T(2,128)S(1)} fusion(bf16[2,36,160,128]{3,2,1,0:T(8,128)(2,1)} %res_ref.1, f32[2,160]{1,0:T(2,128)S(1)} %sub.76), kind=kLoop, calls=%fused_computation.9 | loop fusion | flops 5897920 | bytes 2951680 | tf_op jit(solution)/shard_map/reduce_sum | solution.py:45
  5.6 0.1 reduce_sum.122
  5.7 0.1 reduce_sum.123
  5.8 3.0 %collective-permute-start = (f32[2,2,2,16]{3,2,1,0:T(2,128)S(1)}, f32[2,2,2,16]{3,2,1,0:T(2,128)S(1)}, u32[]{:S(2)}, u32[]{:S(2)}) collective-permute-start(f32[2,2,2,16]{3,2,1,0:T(2,128)S(1)} %constant_dynamic-update-slice_fusion.3), channel_id=1, source_target_pairs={{0,2},{2,0},{1,3},{3,1},{4,6},{6,4},{5,7},{7,5},{8,10},{10,8},{9,1... | collective-permute-start | bytes 1544 | tf_op jit(solution)/shard_map/ppermute | solution.py:57
  8.8 1.6 collective-permute-done
  10.4 0.1 mul.90
  10.5 0.1 mul.91
  10.6 0.1 sub.79
  10.7 0.1 sub.80
  10.8 0.0 copy-start.2
  10.8 0.0 copy-start.8
  10.8 0.0 copy-start.3
  10.8 2.3 %fusion.12 = bf16[2,36,160,128]{3,2,1,0:T(8,128)(2,1)S(1)} fusion(bf16[2,36,160,128]{3,2,1,0:T(8,128)(2,1)S(1)} %copy-done, f32[160]{0:T(256)S(1)} %copy-done.4, f32[160]{0:T(256)S(1)} %copy-done.5, f32[2,160]{1,0:T(2,128)S(1)} %mul.91, f32[2,160]{1,0:T(2,128)S(1)} %sub.80), kind=kLoop, calls=%fused_computation.18 | loop fusion | flops 14745600 | bytes 5902080 | tf_op jit(solution)/shard_map/convert_element_type | solution.py:76
  13.2 3.9 %collective-permute-start.1 = (bf16[2,1,160,128]{3,2,1,0:T(8,128)(2,1)S(1)}, bf16[2,1,160,128]{3,2,1,0:T(8,128)(2,1)S(1)}, u32[]{:S(2)}, u32[]{:S(2)}) collective-permute-start(bf16[2,1,160,128]{3,2,1,0:T(8,128)(2,1)S(1)} %get-tuple-element.11), channel_id=1, source_target_pairs={{0,2},{1,3},{4,6},{5,7},{8,10},{9,11},{12,14},{13,15},{16,18},{17,... | collective-permute-start | bytes 245768 | tf_op jit(solution)/shard_map/ppermute | solution.py:23
  17.1 1.3 collective-permute-start.2
  18.4 0.7 collective-permute-done.1
  19.2 4.3 %collective-permute-done.2 = bf16[2,1,160,128]{3,2,1,0:T(8,128)(2,1)S(1)} collective-permute-done((bf16[2,1,160,128]{3,2,1,0:T(8,128)(2,1)S(1)}, bf16[2,1,160,128]{3,2,1,0:T(8,128)(2,1)S(1)}, u32[]{:S(2)}, u32[]{:S(2)}) %collective-permute-start.2) | collective-permute-done | bytes 81952 | tf_op jit(solution)/shard_map/ppermute | solution.py:24
  23.5 2.1 %pad_maximum_fusion.xo_ref = bf16[2,38,160,128]{3,2,1,0:T(8,128)(2,1)} fusion(bf16[2,1,160,128]{3,2,1,0:T(8,128)(2,1)S(1)} %collective-permute-done.2, bf16[2,36,160,128]{3,2,1,0:T(8,128)(2,1)S(1)} %fusion.12, bf16[2,1,160,128]{3,2,1,0:T(8,128)(2,1)S(1)} %collective-permute-done.1), kind=kLoop, calls=%fused_computation.20 | loop fusion | flops 3112960 | bytes 6225920 | tf_op jit(solution)/shard_map/concatenate | solution.py:25
  25.5 0.0 collective-permute-start.3
  25.5 3.6 %collective-permute-start.4 = (bf16[3,80,160]{2,1,0:T(8,128)(2,1)S(1)}, bf16[3,80,160]{2,1,0:T(8,128)(2,1)S(1)}, u32[]{:S(2)}, u32[]{:S(2)}) collective-permute-start(bf16[3,80,160]{2,1,0:T(8,128)(2,1)S(1)} %copy-done.2), channel_id=1, source_target_pairs={{0,12},{4,0},{8,4},{12,8},{1,13},{5,1},{9,5},{13,9},{2,14},{6,2},{... | collective-permute-start | bytes 230408 | tf_op jit(solution)/shard_map/ppermute | solution.py:34
  29.1 0.0 collective-permute-start.6
  29.1 1.0 collective-permute-start.5
  30.1 0.1 copy.17.b_ref
  30.3 32.5 %all_gather.3 = bf16[3,3,320,160]{3,2,1,0:T(8,128)(2,1)S(1)} all-gather(bf16[3,3,80,160]{3,2,1,0:T(8,128)(2,1)S(1)} %copy-done.3), channel_id=1, replica_groups=mesh['groups'=2,'tm'=4,'height'=2,'chan'=2] {'tm'}, dimensions={2}, use_global_device_ids=true | all-gather | bytes 1152000 | tf_op jit(solution)/shard_map/all_gather | solution.py:237
  62.8 0.9 copy.16
  63.7 0.7 constant_dynamic-slice_fusion.2
  64.4 0.0 collective-permute-done.5
  64.6 0.9 copy-done.1
  65.6 18.5 %shard_map.91.refs_8_ = bf16[2,36,160,128]{3,2,1,0:T(8,128)(2,1)S(1)} custom-call(bf16[2,38,160,128]{3,2,1,0:T(8,128)(2,1)} %pad_maximum_fusion.xo_ref, bf16[2,38,160,128]{3,2,1,0:T(8,128)(2,1)} %collective-permute-done.3.xt_ref, bf16[3,480,160]{2,1,0:T(8,128)(2,1)S(1)} %get-tuple-element.14.wo_ref, bf16[3,480,160]{2,1,0:T(8,128)(2,1)S(1)} %get-tuple-element.13.wt_ref, ...), custom_call_target="tpu_custom_call" | custom-call | flops 8493465600 | bytes 13045760 | tf_op jit(solution)/shard_map/pallas_call | solution.py:124
  84.0 0.0 copy-start.6
  84.0 0.0 copy-start.7
  84.0 0.5 convert_reduce_fusion.1
  84.6 1.8 %fusion.20 = (bf16[1,36,160,128]{3,2,1,0:T(8,128)(2,1)}, bf16[1,36,160,128]{3,2,1,0:T(8,128)(2,1)}) fusion(bf16[2,36,160,128]{3,2,1,0:T(8,128)(2,1)S(1)} %shard_map.91.refs_8_), kind=kLoop, calls=%fused_computation.61 | loop fusion | bytes 5898240 | tf_op jit(solution)/shard_map/slice | solution.py:263
  86.4 0.1 reduce_sum.128
  86.4 0.1 reduce_sum.129
  86.6 5.4 %collective-permute-start.7 = (bf16[1,36,160,128]{3,2,1,0:T(8,128)(2,1)}, bf16[1,36,160,128]{3,2,1,0:T(8,128)(2,1)}, u32[]{:S(2)}, u32[]{:S(2)}) collective-permute-start(bf16[1,36,160,128]{3,2,1,0:T(8,128)(2,1)} %get-tuple-element.9), channel_id=1, source_target_pairs={{0,4},{4,8},{8,12},{1,5},{5,9},{9,13},{2,6},{6,10},{10,14},{3,7},{... | collective-permute-start | bytes 4423688 | tf_op jit(solution)/shard_map/ppermute | solution.py:263
  92.0 1.3 collective-permute-start.8
  93.3 0.1 sub.87
  93.4 0.1 sub.88
  93.4 0.9 fusion.1
  94.4 0.1 reduce_sum.131
  94.5 0.1 reduce_sum.132
  94.6 0.1 collective-permute-start.9
  94.7 3.6 %collective-permute-done.9 = f32[8,2,16]{2,1,0:T(2,128)S(1)} collective-permute-done((f32[8,2,16]{2,1,0:T(2,128)S(1)}, f32[8,2,16]{2,1,0:T(2,128)S(1)}, u32[]{:S(2)}, u32[]{:S(2)}) %collective-permute-start.9) | collective-permute-done | bytes 1056 | tf_op jit(solution)/shard_map/ppermute | solution.py:57
  98.4 31.1 %psum.7 = f32[8,2,16]{2,1,0:T(2,128)S(1)} all-reduce(f32[8,2,16]{2,1,0:T(2,128)S(1)} %constant_dynamic-update-slice_fusion), channel_id=1, replica_groups=mesh['groups'=2,'tm'=4,'height'=2,'chan'=2] {'tm'}, use_global_device_ids=true, to_apply=%region_11.12 | all-reduce | flops 256 | bytes 2048 | tf_op jit(solution)/shard_map/psum | solution.py:59
  129.5 0.1 mul.103
  129.6 0.1 mul.104
  129.7 0.1 sub.91
  129.8 0.1 sub.92
  129.9 0.0 copy-start.9
  129.9 0.0 collective-permute-done.7
  129.9 7.7 %fusion.13.refs_0_.refs_1_.refs_2_ = bf16[4,36,160,128]{3,2,1,0:T(8,128)(2,1)} fusion(bf16[1,36,160,128]{3,2,1,0:T(8,128)(2,1)} %collective-permute-done.8, bf16[2,36,160,128]{3,2,1,0:T(8,128)(2,1)S(1)} %shard_map.91.refs_8_, bf16[1,36,160,128]{3,2,1,0:T(8,128)(2,1)} %collective-permute-done.7, f32[160]{0:T(256)S(1)} %copy-done.6, f32[160]{0:T(256)S(1)} %copy-done.7, ...), kind=kLoop, calls=%fused_computation.19 | loop fusion | flops 38338560 | bytes 11799044 | tf_op jit(solution)/shard_map/jit(_where)/select_n | solution.py:275
  137.6 0.1 copy.19.refs_9_
  137.7 1.1 fusion.22
  138.8 1.1 copy.18
  139.8 1.4 reshape.107
  141.2 0.2 dynamic-slice_bitcast_fusion
  141.5 6.0 %collective-permute-done.10.refs_3_.refs_4_.refs_5_ = bf16[4,36,160,128]{3,2,1,0:T(8,128)(2,1)} collective-permute-done((bf16[4,36,160,128]{3,2,1,0:T(8,128)(2,1)}, bf16[4,36,160,128]{3,2,1,0:T(8,128)(2,1)}, u32[]{:S(2)}, u32[]{:S(2)}) %collective-permute-start.10) | collective-permute-done | bytes 5898272 | tf_op jit(solution)/shard_map/ppermute | solution.py:16
  147.5 11.2 %shard_map.92 = bf16[2,36,160,128]{3,2,1,0:T(8,128)(2,1)} custom-call(bf16[4,36,160,128]{3,2,1,0:T(8,128)(2,1)} %fusion.13.refs_0_.refs_1_.refs_2_, bf16[4,36,160,128]{3,2,1,0:T(8,128)(2,1)} %fusion.13.refs_0_.refs_1_.refs_2_, bf16[4,36,160,128]{3,2,1,0:T(8,128)(2,1)} %fusion.13.refs_0_.refs_1_.refs_2_, ...), custom_call_target="tpu_custom_call" | custom-call | flops 2831155200 | bytes 23900160 | tf_op jit(solution)/shard_map/pallas_call | solution.py:178
  (45 shorter events, 0.4 us)
Async XLA Ops:
  0.0 10.8 %copy-start = (bf16[2,36,160,128]{3,2,1,0:T(8,128)(2,1)S(1)}, bf16[2,36,160,128]{3,2,1,0:T(8,128)(2,1)}, u32[]{:S(2)}) copy-start(bf16[2,36,160,128]{3,2,1,0:T(8,128)(2,1)} %res_ref.1) | copy-start | bytes 8847364
  0.0 10.8 %copy-start.4 = (f32[160]{0:T(256)S(1)}, f32[160]{0:T(256)}, u32[]{:S(2)}) copy-start(f32[160]{0:T(256)} %param.11) | copy-start | bytes 1924
  0.0 10.8 %copy-start.5 = (f32[160]{0:T(256)S(1)}, f32[160]{0:T(256)}, u32[]{:S(2)}) copy-start(f32[160]{0:T(256)} %param.10) | copy-start | bytes 1924
  5.8 4.6 %collective-permute-start = (f32[2,2,2,16]{3,2,1,0:T(2,128)S(1)}, f32[2,2,2,16]{3,2,1,0:T(2,128)S(1)}, u32[]{:S(2)}, u32[]{:S(2)}) collective-permute-start(f32[2,2,2,16]{3,2,1,0:T(2,128)S(1)} %constant_dynamic-update-slice_fusion.3), channel_id=1, source_target_pairs={{0,2},{2,0},{1,3},{3,1},{4,6},{6,4},{5,7},{7,5},{8,10},{10,8},{9,1... | collective-permute-start | bytes 1544 | tf_op jit(solution)/shard_map/ppermute | solution.py:57
  10.8 14.7 %copy-start.2 = (bf16[3,80,160]{2,1,0:T(8,128)(2,1)S(1)}, bf16[3,80,160]{2,1,0:T(8,128)(2,1)}, u32[]{:S(2)}) copy-start(bf16[3,80,160]{2,1,0:T(8,128)(2,1)} %param.16) | copy-start | bytes 230404
  10.8 19.3 %copy-start.8 = (f32[160]{0:T(256)S(1)}, f32[160]{0:T(256)}, u32[]{:S(2)}) copy-start(f32[160]{0:T(256)} %param.13) | copy-start | bytes 1924
  10.8 19.4 %copy-start.3 = (bf16[3,3,80,160]{3,2,1,0:T(8,128)(2,1)S(1)}, bf16[3,3,80,160]{3,2,1,0:T(8,128)(2,1)}, u32[]{:S(2)}) copy-start(bf16[3,3,80,160]{3,2,1,0:T(8,128)(2,1)} %param.12) | copy-start | bytes 691204
  13.2 6.0 %collective-permute-start.1 = (bf16[2,1,160,128]{3,2,1,0:T(8,128)(2,1)S(1)}, bf16[2,1,160,128]{3,2,1,0:T(8,128)(2,1)S(1)}, u32[]{:S(2)}, u32[]{:S(2)}) collective-permute-start(bf16[2,1,160,128]{3,2,1,0:T(8,128)(2,1)S(1)} %get-tuple-element.11), channel_id=1, source_target_pairs={{0,2},{1,3},{4,6},{5,7},{8,10},{9,11},{12,14},{13,15},{16,18},{17,... | collective-permute-start | bytes 245768 | tf_op jit(solution)/shard_map/ppermute | solution.py:23
  17.1 6.3 %collective-permute-start.2 = (bf16[2,1,160,128]{3,2,1,0:T(8,128)(2,1)S(1)}, bf16[2,1,160,128]{3,2,1,0:T(8,128)(2,1)S(1)}, u32[]{:S(2)}, u32[]{:S(2)}) collective-permute-start(bf16[2,1,160,128]{3,2,1,0:T(8,128)(2,1)S(1)} %get-tuple-element.12), channel_id=1, source_target_pairs={{2,0},{3,1},{6,4},{7,5},{10,8},{11,9},{14,12},{15,13},{18,16},{19,... | collective-permute-start | bytes 245768 | tf_op jit(solution)/shard_map/ppermute | solution.py:24
  25.5 39.1 %collective-permute-start.3 = (bf16[2,38,160,128]{3,2,1,0:T(8,128)(2,1)}, bf16[2,38,160,128]{3,2,1,0:T(8,128)(2,1)}, u32[]{:S(2)}, u32[]{:S(2)}) collective-permute-start(bf16[2,38,160,128]{3,2,1,0:T(8,128)(2,1)} %pad_maximum_fusion.xo_ref), channel_id=1, source_target_pairs={{0,1},{1,0},{2,3},{3,2},{4,5},{5,4},{6,7},{7,6},{8,9},{9,8},{10,11... | collective-permute-start | bytes 9338888 | tf_op jit(solution)/shard_map/ppermute | solution.py:16
  25.5 38.9 %collective-permute-start.4 = (bf16[3,80,160]{2,1,0:T(8,128)(2,1)S(1)}, bf16[3,80,160]{2,1,0:T(8,128)(2,1)S(1)}, u32[]{:S(2)}, u32[]{:S(2)}) collective-permute-start(bf16[3,80,160]{2,1,0:T(8,128)(2,1)S(1)} %copy-done.2), channel_id=1, source_target_pairs={{0,12},{4,0},{8,4},{12,8},{1,13},{5,1},{9,5},{13,9},{2,14},{6,2},{... | collective-permute-start | bytes 230408 | tf_op jit(solution)/shard_map/ppermute | solution.py:34
  29.1 35.3 %collective-permute-start.6 = (bf16[3,80,160]{2,1,0:T(8,128)(2,1)S(1)}, bf16[3,80,160]{2,1,0:T(8,128)(2,1)S(1)}, u32[]{:S(2)}, u32[]{:S(2)}) collective-permute-start(bf16[3,80,160]{2,1,0:T(8,128)(2,1)S(1)} %copy-done.2), channel_id=1, source_target_pairs={{0,4},{4,8},{8,12},{12,0},{1,5},{5,9},{9,13},{13,1},{2,6},{6,10},{... | collective-permute-start | bytes 230408 | tf_op jit(solution)/shard_map/ppermute | solution.py:34
  29.1 35.3 %collective-permute-start.5 = (bf16[3,80,160]{2,1,0:T(8,128)(2,1)S(1)}, bf16[3,80,160]{2,1,0:T(8,128)(2,1)S(1)}, u32[]{:S(2)}, u32[]{:S(2)}) collective-permute-start(bf16[3,80,160]{2,1,0:T(8,128)(2,1)S(1)} %copy-done.2), channel_id=1, source_target_pairs={{0,8},{4,12},{8,0},{12,4},{1,9},{5,13},{9,1},{13,5},{2,10},{6,14},... | collective-permute-start | bytes 230408 | tf_op jit(solution)/shard_map/ppermute | solution.py:34
  64.6 1.0 copy-start.1
  84.0 45.9 %copy-start.6 = (f32[160]{0:T(256)S(1)}, f32[160]{0:T(256)}, u32[]{:S(2)}) copy-start(f32[160]{0:T(256)} %param.15) | copy-start | bytes 1924
  84.0 45.9 %copy-start.7 = (f32[160]{0:T(256)S(1)}, f32[160]{0:T(256)}, u32[]{:S(2)}) copy-start(f32[160]{0:T(256)} %param.14) | copy-start | bytes 1924
  86.6 43.3 %collective-permute-start.7 = (bf16[1,36,160,128]{3,2,1,0:T(8,128)(2,1)}, bf16[1,36,160,128]{3,2,1,0:T(8,128)(2,1)}, u32[]{:S(2)}, u32[]{:S(2)}) collective-permute-start(bf16[1,36,160,128]{3,2,1,0:T(8,128)(2,1)} %get-tuple-element.9), channel_id=1, source_target_pairs={{0,4},{4,8},{8,12},{1,5},{5,9},{9,13},{2,6},{6,10},{10,14},{3,7},{... | collective-permute-start | bytes 4423688 | tf_op jit(solution)/shard_map/ppermute | solution.py:263
  92.0 37.9 %collective-permute-start.8 = (bf16[1,36,160,128]{3,2,1,0:T(8,128)(2,1)}, bf16[1,36,160,128]{3,2,1,0:T(8,128)(2,1)}, u32[]{:S(2)}, u32[]{:S(2)}) collective-permute-start(bf16[1,36,160,128]{3,2,1,0:T(8,128)(2,1)} %get-tuple-element.10), channel_id=1, source_target_pairs={{4,0},{8,4},{12,8},{5,1},{9,5},{13,9},{6,2},{10,6},{14,10},{7,3},{... | collective-permute-start | bytes 4423688 | tf_op jit(solution)/shard_map/ppermute | solution.py:264
  94.6 3.7 %collective-permute-start.9 = (f32[8,2,16]{2,1,0:T(2,128)S(1)}, f32[8,2,16]{2,1,0:T(2,128)S(1)}, u32[]{:S(2)}, u32[]{:S(2)}) collective-permute-start(f32[8,2,16]{2,1,0:T(2,128)S(1)} %constant_dynamic-update-slice_fusion.1), channel_id=1, source_target_pairs={{0,2},{2,0},{1,3},{3,1},{4,6},{6,4},{5,7},{7,5},{8,10},{10,8},{9,1... | collective-permute-start | bytes 3080 | tf_op jit(solution)/shard_map/ppermute | solution.py:57
  129.9 7.7 %copy-start.9 = (f32[160]{0:T(256)S(1)}, f32[160]{0:T(256)}, u32[]{:S(2)}) copy-start(f32[160]{0:T(256)} %param.17) | copy-start | bytes 1924
  137.6 9.9 %collective-permute-start.10 = (bf16[4,36,160,128]{3,2,1,0:T(8,128)(2,1)}, bf16[4,36,160,128]{3,2,1,0:T(8,128)(2,1)}, u32[]{:S(2)}, u32[]{:S(2)}) collective-permute-start(bf16[4,36,160,128]{3,2,1,0:T(8,128)(2,1)} %fusion.13.refs_0_.refs_1_.refs_2_), channel_id=1, source_target_pairs={{0,1},{1,0},{2,3},{3,2},{4,5},{5,4},{6,7},{7,6},{8,9},{9,8},{10,11... | collective-permute-start | bytes 17694728 | tf_op jit(solution)/shard_map/ppermute | solution.py:16

commit v16 on v15

--- a/solution.py
+++ b/solution.py
@@ -83,7 +83,7 @@
     return lax.dynamic_update_slice_in_dim(joined, other, (1 - chan_index) * size, axis=2)
 
 
-STEP = 12
+STEP = 18
 
 
 def pair(ref, first):

time: 159 us -> 158 us (level)
  no operation moved by 1% of the time
where the time goes in v16:
time: 158 us
  blocking collectives  63.6 us (40%)
  Pallas kernels  29 us (18%)
  starting transfers between devices  19.6 us (12%)
  other arithmetic  19.3 us (12%)
  waiting for transfers between devices  16.3 us (10%)
  local copies, waits for them, and re-layouts  9.82 us (6%)
    all_gather x1, blocking collectives, body(): lax.all_gather(spatial_weight, 'tm', axis=2, tiled=True)  32.5 us
    psum x1, blocking collectives, group_stats(): table = lax.psum(table, name)  31.1 us
    pallas_call x1, Pallas kernels, spatial_call(): pl.pallas_call(spatial_kernel, out_shape=jax.ShapeDtypeStruct(residual.sh...  18.1 us
    pallas_call x1, Pallas kernels, temporal_call(): pl.pallas_call(temporal_kernel, out_shape=jax.ShapeDtypeStruct(residual.s...  10.9 us
    select_n x1, other arithmetic, body(): jnp.where(inside[:, None, None, None], act_two, jnp.zeros_like(act_two))  7.66 us
    ppermute x2, waiting for transfers between devices, swap_chan(): return lax.ppermute(block, 'chan', [(0, 1), (1, 0)])  6.04 us
    ppermute x1, starting transfers between devices, body(): before = lax.ppermute(hidden[-1:], 'tm', forward)  5.41 us
    ppermute x2, waiting for transfers between devices, group_stats(): table = table + lax.ppermute(table, name, [(0, 1), (1, 0)])  5.21 us
  transfers between devices with their start and end apart: 11, of which 5 were waited for; matrix products, arithmetic and copies ran while one was open for 5% of the time, Pallas kernels for 0%

profile of v16, /device:TPU:0, one launch (start us, length us, event | category | flops | bytes accessed | tf_op | source)
XLA Modules:
  0.0 158.0 jit_solution(15041764069116943573)
XLA Ops:
  0.0 2.5 %convert_reduce_fusion = f32[2,160]{1,0:T(2,128)S(1)} fusion(bf16[2,36,160,128]{3,2,1,0:T(8,128)(2,1)} %res_ref.1), kind=kLoop, calls=%fused_computation.3 | loop fusion | flops 2948800 | bytes 2950400 | tf_op jit(solution)/shard_map/reduce_sum | solution.py:43
  2.5 0.1 reduce_sum.101
  2.5 0.1 reduce_sum.120
  2.6 0.1 sub.75
  2.7 0.1 sub.76
  2.8 2.7 %fusion.3 = f32[2,160]{1,0:T(2,128)S(1)} fusion(bf16[2,36,160,128]{3,2,1,0:T(8,128)(2,1)} %res_ref.1, f32[2,160]{1,0:T(2,128)S(1)} %sub.76), kind=kLoop, calls=%fused_computation.9 | loop fusion | flops 5897920 | bytes 2951680 | tf_op jit(solution)/shard_map/reduce_sum | solution.py:45
  5.6 0.1 reduce_sum.122
  5.7 0.1 reduce_sum.123
  5.8 3.0 %collective-permute-start = (f32[2,2,2,16]{3,2,1,0:T(2,128)S(1)}, f32[2,2,2,16]{3,2,1,0:T(2,128)S(1)}, u32[]{:S(2)}, u32[]{:S(2)}) collective-permute-start(f32[2,2,2,16]{3,2,1,0:T(2,128)S(1)} %constant_dynamic-update-slice_fusion.3), channel_id=1, source_target_pairs={{0,2},{2,0},{1,3},{3,1},{4,6},{6,4},{5,7},{7,5},{8,10},{10,8},{9,1... | collective-permute-start | bytes 1544 | tf_op jit(solution)/shard_map/ppermute | solution.py:57
  8.8 1.6 %collective-permute-done = f32[2,2,2,16]{3,2,1,0:T(2,128)S(1)} collective-permute-done((f32[2,2,2,16]{3,2,1,0:T(2,128)S(1)}, f32[2,2,2,16]{3,2,1,0:T(2,128)S(1)}, u32[]{:S(2)}, u32[]{:S(2)}) %collective-permute-start) | collective-permute-done | bytes 544 | tf_op jit(solution)/shard_map/ppermute | solution.py:57
  10.4 0.1 mul.90
  10.5 0.1 mul.91
  10.6 0.1 sub.79
  10.7 0.1 sub.80
  10.8 0.0 copy-start.2
  10.8 0.0 copy-start.8
  10.8 0.0 copy-start.3
  10.8 2.3 %fusion.12 = bf16[2,36,160,128]{3,2,1,0:T(8,128)(2,1)S(1)} fusion(bf16[2,36,160,128]{3,2,1,0:T(8,128)(2,1)S(1)} %copy-done, f32[160]{0:T(256)S(1)} %copy-done.4, f32[160]{0:T(256)S(1)} %copy-done.5, f32[2,160]{1,0:T(2,128)S(1)} %mul.91, f32[2,160]{1,0:T(2,128)S(1)} %sub.80), kind=kLoop, calls=%fused_computation.18 | loop fusion | flops 14745600 | bytes 5902080 | tf_op jit(solution)/shard_map/convert_element_type | solution.py:76
  13.2 3.9 %collective-permute-start.1 = (bf16[2,1,160,128]{3,2,1,0:T(8,128)(2,1)S(1)}, bf16[2,1,160,128]{3,2,1,0:T(8,128)(2,1)S(1)}, u32[]{:S(2)}, u32[]{:S(2)}) collective-permute-start(bf16[2,1,160,128]{3,2,1,0:T(8,128)(2,1)S(1)} %get-tuple-element.11), channel_id=1, source_target_pairs={{0,2},{1,3},{4,6},{5,7},{8,10},{9,11},{12,14},{13,15},{16,18},{17,... | collective-permute-start | bytes 245768 | tf_op jit(solution)/shard_map/ppermute | solution.py:23
  17.1 1.3 collective-permute-start.2
  18.4 0.7 collective-permute-done.1
  19.2 4.3 %collective-permute-done.2 = bf16[2,1,160,128]{3,2,1,0:T(8,128)(2,1)S(1)} collective-permute-done((bf16[2,1,160,128]{3,2,1,0:T(8,128)(2,1)S(1)}, bf16[2,1,160,128]{3,2,1,0:T(8,128)(2,1)S(1)}, u32[]{:S(2)}, u32[]{:S(2)}) %collective-permute-start.2) | collective-permute-done | bytes 81952 | tf_op jit(solution)/shard_map/ppermute | solution.py:24
  23.5 2.1 %pad_maximum_fusion.xo_ref = bf16[2,38,160,128]{3,2,1,0:T(8,128)(2,1)} fusion(bf16[2,1,160,128]{3,2,1,0:T(8,128)(2,1)S(1)} %collective-permute-done.2, bf16[2,36,160,128]{3,2,1,0:T(8,128)(2,1)S(1)} %fusion.12, bf16[2,1,160,128]{3,2,1,0:T(8,128)(2,1)S(1)} %collective-permute-done.1), kind=kLoop, calls=%fused_computation.20 | loop fusion | flops 3112960 | bytes 6225920 | tf_op jit(solution)/shard_map/concatenate | solution.py:25
  25.5 3.6 %collective-permute-start.4 = (bf16[3,80,160]{2,1,0:T(8,128)(2,1)S(1)}, bf16[3,80,160]{2,1,0:T(8,128)(2,1)S(1)}, u32[]{:S(2)}, u32[]{:S(2)}) collective-permute-start(bf16[3,80,160]{2,1,0:T(8,128)(2,1)S(1)} %copy-done.2), channel_id=1, source_target_pairs={{0,12},{4,0},{8,4},{12,8},{1,13},{5,1},{9,5},{13,9},{2,14},{6,2},{... | collective-permute-start | bytes 230408 | tf_op jit(solution)/shard_map/ppermute | solution.py:34
  29.1 1.0 collective-permute-start.5
  30.1 0.1 copy.17.b_ref
  30.3 32.5 %all_gather.3 = bf16[3,3,320,160]{3,2,1,0:T(8,128)(2,1)S(1)} all-gather(bf16[3,3,80,160]{3,2,1,0:T(8,128)(2,1)S(1)} %copy-done.3), channel_id=1, replica_groups=mesh['groups'=2,'tm'=4,'height'=2,'chan'=2] {'tm'}, dimensions={2}, use_global_device_ids=true | all-gather | bytes 1152000 | tf_op jit(solution)/shard_map/all_gather | solution.py:237
  62.8 0.9 copy.16
  63.7 0.7 constant_dynamic-slice_fusion.2
  64.4 0.0 collective-permute-done.4
  64.5 0.0 collective-permute-done.6
  64.6 0.0 collective-permute-done.3.xt_ref
  64.6 0.9 copy-done.1
  65.6 18.1 %shard_map.91.refs_8_ = bf16[2,36,160,128]{3,2,1,0:T(8,128)(2,1)S(1)} custom-call(bf16[2,38,160,128]{3,2,1,0:T(8,128)(2,1)} %pad_maximum_fusion.xo_ref, bf16[2,38,160,128]{3,2,1,0:T(8,128)(2,1)} %collective-permute-done.3.xt_ref, bf16[3,480,160]{2,1,0:T(8,128)(2,1)S(1)} %get-tuple-element.14.wo_ref, bf16[3,480,160]{2,1,0:T(8,128)(2,1)S(1)} %get-tuple-element.13.wt_ref, ...), custom_call_target="tpu_custom_call" | custom-call | flops 8493465600 | bytes 13045760 | tf_op jit(solution)/shard_map/pallas_call | solution.py:124
  83.6 0.0 copy-start.6
  83.6 0.0 copy-start.7
  83.6 0.5 convert_reduce_fusion.1
  84.1 1.8 %fusion.20 = (bf16[1,36,160,128]{3,2,1,0:T(8,128)(2,1)}, bf16[1,36,160,128]{3,2,1,0:T(8,128)(2,1)}) fusion(bf16[2,36,160,128]{3,2,1,0:T(8,128)(2,1)S(1)} %shard_map.91.refs_8_), kind=kLoop, calls=%fused_computation.61 | loop fusion | bytes 5898240 | tf_op jit(solution)/shard_map/slice | solution.py:263
  86.0 0.1 reduce_sum.128
  86.0 0.1 reduce_sum.129
  86.2 5.4 %collective-permute-start.7 = (bf16[1,36,160,128]{3,2,1,0:T(8,128)(2,1)}, bf16[1,36,160,128]{3,2,1,0:T(8,128)(2,1)}, u32[]{:S(2)}, u32[]{:S(2)}) collective-permute-start(bf16[1,36,160,128]{3,2,1,0:T(8,128)(2,1)} %get-tuple-element.9), channel_id=1, source_target_pairs={{0,4},{4,8},{8,12},{1,5},{5,9},{9,13},{2,6},{6,10},{10,14},{3,7},{... | collective-permute-start | bytes 4423688 | tf_op jit(solution)/shard_map/ppermute | solution.py:263
  91.6 1.3 collective-permute-start.8
  92.9 0.1 sub.87
  92.9 0.1 sub.88
  93.0 0.9 fusion.1
  94.0 0.1 reduce_sum.131
  94.1 0.1 reduce_sum.132
  94.2 0.1 collective-permute-start.9
  94.3 3.6 %collective-permute-done.9 = f32[8,2,16]{2,1,0:T(2,128)S(1)} collective-permute-done((f32[8,2,16]{2,1,0:T(2,128)S(1)}, f32[8,2,16]{2,1,0:T(2,128)S(1)}, u32[]{:S(2)}, u32[]{:S(2)}) %collective-permute-start.9) | collective-permute-done | bytes 1056 | tf_op jit(solution)/shard_map/ppermute | solution.py:57
  97.9 31.1 %psum.7 = f32[8,2,16]{2,1,0:T(2,128)S(1)} all-reduce(f32[8,2,16]{2,1,0:T(2,128)S(1)} %constant_dynamic-update-slice_fusion), channel_id=1, replica_groups=mesh['groups'=2,'tm'=4,'height'=2,'chan'=2] {'tm'}, use_global_device_ids=true, to_apply=%region_11.12 | all-reduce | flops 256 | bytes 2048 | tf_op jit(solution)/shard_map/psum | solution.py:59
  129.1 0.1 mul.103
  129.2 0.1 mul.104
  129.3 0.1 sub.91
  129.3 0.1 sub.92
  129.4 0.0 copy-start.9
  129.5 0.0 collective-permute-done.7
  129.5 7.7 %fusion.13.refs_0_.refs_1_.refs_2_ = bf16[4,36,160,128]{3,2,1,0:T(8,128)(2,1)} fusion(bf16[1,36,160,128]{3,2,1,0:T(8,128)(2,1)} %collective-permute-done.8, bf16[2,36,160,128]{3,2,1,0:T(8,128)(2,1)S(1)} %shard_map.91.refs_8_, bf16[1,36,160,128]{3,2,1,0:T(8,128)(2,1)} %collective-permute-done.7, f32[160]{0:T(256)S(1)} %copy-done.6, f32[160]{0:T(256)S(1)} %copy-done.7, ...), kind=kLoop, calls=%fused_computation.19 | loop fusion | flops 38338560 | bytes 11799044 | tf_op jit(solution)/shard_map/jit(_where)/select_n | solution.py:275
  137.2 0.1 copy.19.refs_9_
  137.3 1.1 fusion.22
  138.4 1.1 copy.18
  139.4 1.4 reshape.107
  140.8 0.2 dynamic-slice_bitcast_fusion
  141.1 6.0 %collective-permute-done.10.refs_3_.refs_4_.refs_5_ = bf16[4,36,160,128]{3,2,1,0:T(8,128)(2,1)} collective-permute-done((bf16[4,36,160,128]{3,2,1,0:T(8,128)(2,1)}, bf16[4,36,160,128]{3,2,1,0:T(8,128)(2,1)}, u32[]{:S(2)}, u32[]{:S(2)}) %collective-permute-start.10) | collective-permute-done | bytes 5898272 | tf_op jit(solution)/shard_map/ppermute | solution.py:16
  147.1 10.9 %shard_map.92 = bf16[2,36,160,128]{3,2,1,0:T(8,128)(2,1)} custom-call(bf16[4,36,160,128]{3,2,1,0:T(8,128)(2,1)} %fusion.13.refs_0_.refs_1_.refs_2_, bf16[4,36,160,128]{3,2,1,0:T(8,128)(2,1)} %fusion.13.refs_0_.refs_1_.refs_2_, bf16[4,36,160,128]{3,2,1,0:T(8,128)(2,1)} %fusion.13.refs_0_.refs_1_.refs_2_, ...), custom_call_target="tpu_custom_call" | custom-call | flops 2831155200 | bytes 23900160 | tf_op jit(solution)/shard_map/pallas_call | solution.py:178
  (45 shorter events, 0.4 us)
Async XLA Ops:
  0.0 10.8 %copy-start = (bf16[2,36,160,128]{3,2,1,0:T(8,128)(2,1)S(1)}, bf16[2,36,160,128]{3,2,1,0:T(8,128)(2,1)}, u32[]{:S(2)}) copy-start(bf16[2,36,160,128]{3,2,1,0:T(8,128)(2,1)} %res_ref.1) | copy-start | bytes 8847364
  0.0 10.8 %copy-start.4 = (f32[160]{0:T(256)S(1)}, f32[160]{0:T(256)}, u32[]{:S(2)}) copy-start(f32[160]{0:T(256)} %param.11) | copy-start | bytes 1924
  0.0 10.8 %copy-start.5 = (f32[160]{0:T(256)S(1)}, f32[160]{0:T(256)}, u32[]{:S(2)}) copy-start(f32[160]{0:T(256)} %param.10) | copy-start | bytes 1924
  5.8 4.6 %collective-permute-start = (f32[2,2,2,16]{3,2,1,0:T(2,128)S(1)}, f32[2,2,2,16]{3,2,1,0:T(2,128)S(1)}, u32[]{:S(2)}, u32[]{:S(2)}) collective-permute-start(f32[2,2,2,16]{3,2,1,0:T(2,128)S(1)} %constant_dynamic-update-slice_fusion.3), channel_id=1, source_target_pairs={{0,2},{2,0},{1,3},{3,1},{4,6},{6,4},{5,7},{7,5},{8,10},{10,8},{9,1... | collective-permute-start | bytes 1544 | tf_op jit(solution)/shard_map/ppermute | solution.py:57
  10.8 14.7 %copy-start.2 = (bf16[3,80,160]{2,1,0:T(8,128)(2,1)S(1)}, bf16[3,80,160]{2,1,0:T(8,128)(2,1)}, u32[]{:S(2)}) copy-start(bf16[3,80,160]{2,1,0:T(8,128)(2,1)} %param.16) | copy-start | bytes 230404
  10.8 19.3 %copy-start.8 = (f32[160]{0:T(256)S(1)}, f32[160]{0:T(256)}, u32[]{:S(2)}) copy-start(f32[160]{0:T(256)} %param.13) | copy-start | bytes 1924
  10.8 19.4 %copy-start.3 = (bf16[3,3,80,160]{3,2,1,0:T(8,128)(2,1)S(1)}, bf16[3,3,80,160]{3,2,1,0:T(8,128)(2,1)}, u32[]{:S(2)}) copy-start(bf16[3,3,80,160]{3,2,1,0:T(8,128)(2,1)} %param.12) | copy-start | bytes 691204
  13.2 6.0 %collective-permute-start.1 = (bf16[2,1,160,128]{3,2,1,0:T(8,128)(2,1)S(1)}, bf16[2,1,160,128]{3,2,1,0:T(8,128)(2,1)S(1)}, u32[]{:S(2)}, u32[]{:S(2)}) collective-permute-start(bf16[2,1,160,128]{3,2,1,0:T(8,128)(2,1)S(1)} %get-tuple-element.11), channel_id=1, source_target_pairs={{0,2},{1,3},{4,6},{5,7},{8,10},{9,11},{12,14},{13,15},{16,18},{17,... | collective-permute-start | bytes 245768 | tf_op jit(solution)/shard_map/ppermute | solution.py:23
  17.1 6.3 %collective-permute-start.2 = (bf16[2,1,160,128]{3,2,1,0:T(8,128)(2,1)S(1)}, bf16[2,1,160,128]{3,2,1,0:T(8,128)(2,1)S(1)}, u32[]{:S(2)}, u32[]{:S(2)}) collective-permute-start(bf16[2,1,160,128]{3,2,1,0:T(8,128)(2,1)S(1)} %get-tuple-element.12), channel_id=1, source_target_pairs={{2,0},{3,1},{6,4},{7,5},{10,8},{11,9},{14,12},{15,13},{18,16},{19,... | collective-permute-start | bytes 245768 | tf_op jit(solution)/shard_map/ppermute | solution.py:24
  25.5 39.1 %collective-permute-start.3 = (bf16[2,38,160,128]{3,2,1,0:T(8,128)(2,1)}, bf16[2,38,160,128]{3,2,1,0:T(8,128)(2,1)}, u32[]{:S(2)}, u32[]{:S(2)}) collective-permute-start(bf16[2,38,160,128]{3,2,1,0:T(8,128)(2,1)} %pad_maximum_fusion.xo_ref), channel_id=1, source_target_pairs={{0,1},{1,0},{2,3},{3,2},{4,5},{5,4},{6,7},{7,6},{8,9},{9,8},{10,11... | collective-permute-start | bytes 9338888 | tf_op jit(solution)/shard_map/ppermute | solution.py:16
  25.5 38.9 %collective-permute-start.4 = (bf16[3,80,160]{2,1,0:T(8,128)(2,1)S(1)}, bf16[3,80,160]{2,1,0:T(8,128)(2,1)S(1)}, u32[]{:S(2)}, u32[]{:S(2)}) collective-permute-start(bf16[3,80,160]{2,1,0:T(8,128)(2,1)S(1)} %copy-done.2), channel_id=1, source_target_pairs={{0,12},{4,0},{8,4},{12,8},{1,13},{5,1},{9,5},{13,9},{2,14},{6,2},{... | collective-permute-start | bytes 230408 | tf_op jit(solution)/shard_map/ppermute | solution.py:34
  29.1 35.3 %collective-permute-start.6 = (bf16[3,80,160]{2,1,0:T(8,128)(2,1)S(1)}, bf16[3,80,160]{2,1,0:T(8,128)(2,1)S(1)}, u32[]{:S(2)}, u32[]{:S(2)}) collective-permute-start(bf16[3,80,160]{2,1,0:T(8,128)(2,1)S(1)} %copy-done.2), channel_id=1, source_target_pairs={{0,4},{4,8},{8,12},{12,0},{1,5},{5,9},{9,13},{13,1},{2,6},{6,10},{... | collective-permute-start | bytes 230408 | tf_op jit(solution)/shard_map/ppermute | solution.py:34
  29.1 35.3 %collective-permute-start.5 = (bf16[3,80,160]{2,1,0:T(8,128)(2,1)S(1)}, bf16[3,80,160]{2,1,0:T(8,128)(2,1)S(1)}, u32[]{:S(2)}, u32[]{:S(2)}) collective-permute-start(bf16[3,80,160]{2,1,0:T(8,128)(2,1)S(1)} %copy-done.2), channel_id=1, source_target_pairs={{0,8},{4,12},{8,0},{12,4},{1,9},{5,13},{9,1},{13,5},{2,10},{6,14},... | collective-permute-start | bytes 230408 | tf_op jit(solution)/shard_map/ppermute | solution.py:34
  64.6 1.0 copy-start.1
  83.6 45.9 %copy-start.6 = (f32[160]{0:T(256)S(1)}, f32[160]{0:T(256)}, u32[]{:S(2)}) copy-start(f32[160]{0:T(256)} %param.15) | copy-start | bytes 1924
  83.6 45.9 %copy-start.7 = (f32[160]{0:T(256)S(1)}, f32[160]{0:T(256)}, u32[]{:S(2)}) copy-start(f32[160]{0:T(256)} %param.14) | copy-start | bytes 1924
  86.2 43.3 %collective-permute-start.7 = (bf16[1,36,160,128]{3,2,1,0:T(8,128)(2,1)}, bf16[1,36,160,128]{3,2,1,0:T(8,128)(2,1)}, u32[]{:S(2)}, u32[]{:S(2)}) collective-permute-start(bf16[1,36,160,128]{3,2,1,0:T(8,128)(2,1)} %get-tuple-element.9), channel_id=1, source_target_pairs={{0,4},{4,8},{8,12},{1,5},{5,9},{9,13},{2,6},{6,10},{10,14},{3,7},{... | collective-permute-start | bytes 4423688 | tf_op jit(solution)/shard_map/ppermute | solution.py:263
  91.6 37.9 %collective-permute-start.8 = (bf16[1,36,160,128]{3,2,1,0:T(8,128)(2,1)}, bf16[1,36,160,128]{3,2,1,0:T(8,128)(2,1)}, u32[]{:S(2)}, u32[]{:S(2)}) collective-permute-start(bf16[1,36,160,128]{3,2,1,0:T(8,128)(2,1)} %get-tuple-element.10), channel_id=1, source_target_pairs={{4,0},{8,4},{12,8},{5,1},{9,5},{13,9},{6,2},{10,6},{14,10},{7,3},{... | collective-permute-start | bytes 4423688 | tf_op jit(solution)/shard_map/ppermute | solution.py:264
  94.2 3.7 %collective-permute-start.9 = (f32[8,2,16]{2,1,0:T(2,128)S(1)}, f32[8,2,16]{2,1,0:T(2,128)S(1)}, u32[]{:S(2)}, u32[]{:S(2)}) collective-permute-start(f32[8,2,16]{2,1,0:T(2,128)S(1)} %constant_dynamic-update-slice_fusion.1), channel_id=1, source_target_pairs={{0,2},{2,0},{1,3},{3,1},{4,6},{6,4},{5,7},{7,5},{8,10},{10,8},{9,1... | collective-permute-start | bytes 3080 | tf_op jit(solution)/shard_map/ppermute | solution.py:57
  129.4 7.7 %copy-start.9 = (f32[160]{0:T(256)S(1)}, f32[160]{0:T(256)}, u32[]{:S(2)}) copy-start(f32[160]{0:T(256)} %param.17) | copy-start | bytes 1924
  137.2 9.9 %collective-permute-start.10 = (bf16[4,36,160,128]{3,2,1,0:T(8,128)(2,1)}, bf16[4,36,160,128]{3,2,1,0:T(8,128)(2,1)}, u32[]{:S(2)}, u32[]{:S(2)}) collective-permute-start(bf16[4,36,160,128]{3,2,1,0:T(8,128)(2,1)} %fusion.13.refs_0_.refs_1_.refs_2_), channel_id=1, source_target_pairs={{0,1},{1,0},{2,3},{3,2},{4,5},{5,4},{6,7},{7,6},{8,9},{9,8},{10,11... | collective-permute-start | bytes 17694728 | tf_op jit(solution)/shard_map/ppermute | solution.py:16

commit v17 on v16

--- a/solution.py
+++ b/solution.py
@@ -18,6 +18,14 @@
 
 def row_halo(block):
     count = lax.axis_size("height")
+    if count == 2:
+        index = lax.axis_index("height")
+        edge = jnp.where(index == 0, block[:, -1:], block[:, :1])
+        received = lax.ppermute(edge, "height", [(0, 1), (1, 0)])
+        empty = jnp.zeros_like(received)
+        low = jnp.where(index == 1, received, empty)
+        high = jnp.where(index == 0, received, empty)
+        return jnp.concatenate([low, block, high], axis=1)
     forward = [(i, i + 1) for i in range(count - 1)]
     backward = [(target, source) for source, target in forward]
     low = lax.ppermute(block[:, -1:], "height", forward)

time: 158 us -> 157 us (level)
  waiting for transfers between devices: 16.3 us -> 12.2 us
  other arithmetic: 19.3 us -> 21.1 us
  local copies, waits for them, and re-layouts: 9.82 us -> 11.4 us
    ppermute x2 -> x1, starting transfers between devices: 5.22 us -> 2.09 us  [row_halo(): received = lax.ppermute(edge, 'height', [(0, 1), (1, 0)])]
    ppermute x2 -> x1, waiting for transfers between devices: 5.03 us -> 2.42 us  [row_halo(): received = lax.ppermute(edge, 'height', [(0, 1), (1, 0)])]
    concatenate x1, other arithmetic: 2.06 us -> 3.9 us  [row_halo(): return jnp.concatenate([low, block, high], axis=1)]
    unnamed x27 -> x29, local copies, waits for them, and re-layouts: 1.03 us -> 2.63 us
  transfers between devices with their start and end apart: 11 -> 10, of which waited for: 5 -> 4; matrix products, arithmetic and copies ran while one was open for 5% -> 5% of each run, Pallas kernels for 0% -> 0%
where the time goes in v17:
time: 157 us; the launch traced here: 156 us
  blocking collectives  63.6 us (41%)
  Pallas kernels  29 us (18%)
  other arithmetic  21.1 us (13%)
  starting transfers between devices  18.5 us (12%)
  waiting for transfers between devices  12.2 us (8%)
  local copies, waits for them, and re-layouts  11.4 us (7%)
    all_gather x1, blocking collectives, body(): lax.all_gather(spatial_weight, 'tm', axis=2, tiled=True)  32.5 us
    psum x1, blocking collectives, group_stats(): table = lax.psum(table, name)  31.1 us
    pallas_call x1, Pallas kernels, spatial_call(): pl.pallas_call(spatial_kernel, out_shape=jax.ShapeDtypeStruct(residual.sh...  18.1 us
    pallas_call x1, Pallas kernels, temporal_call(): pl.pallas_call(temporal_kernel, out_shape=jax.ShapeDtypeStruct(residual.s...  10.9 us
    select_n x1, other arithmetic, body(): jnp.where(inside[:, None, None, None], act_two, jnp.zeros_like(act_two))  7.66 us
    ppermute x2, waiting for transfers between devices, swap_chan(): return lax.ppermute(block, 'chan', [(0, 1), (1, 0)])  6.04 us
    ppermute x1, starting transfers between devices, body(): before = lax.ppermute(hidden[-1:], 'tm', forward)  5.41 us
    ppermute x3, starting transfers between devices, gather_tm(): pieces.append(lax.ppermute(piece, 'tm', pairs))  5.14 us
  transfers between devices with their start and end apart: 10, of which 4 were waited for; matrix products, arithmetic and copies ran while one was open for 5% of the time, Pallas kernels for 0%

profile of v17, /device:TPU:0, one launch (start us, length us, event | category | flops | bytes accessed | tf_op | source)
XLA Modules:
  0.0 156.2 jit_solution(15873121480686855540)
XLA Ops:
  0.0 2.5 %convert_reduce_fusion = f32[2,160]{1,0:T(2,128)S(1)} fusion(bf16[2,36,160,128]{3,2,1,0:T(8,128)(2,1)} %res_ref.1), kind=kLoop, calls=%fused_computation.3 | loop fusion | flops 2948800 | bytes 2950400 | tf_op jit(solution)/shard_map/reduce_sum | solution.py:51
  2.5 0.1 reduce_sum.101
  2.5 0.1 reduce_sum.120
  2.6 0.1 sub.75
  2.7 0.1 sub.76
  2.8 2.7 %fusion.3 = f32[2,160]{1,0:T(2,128)S(1)} fusion(bf16[2,36,160,128]{3,2,1,0:T(8,128)(2,1)} %res_ref.1, f32[2,160]{1,0:T(2,128)S(1)} %sub.76), kind=kLoop, calls=%fused_computation.9 | loop fusion | flops 5897920 | bytes 2951680 | tf_op jit(solution)/shard_map/reduce_sum | solution.py:53
  5.6 0.1 reduce_sum.122
  5.7 0.1 reduce_sum.123
  5.8 3.0 %collective-permute-start = (f32[2,2,2,16]{3,2,1,0:T(2,128)S(1)}, f32[2,2,2,16]{3,2,1,0:T(2,128)S(1)}, u32[]{:S(2)}, u32[]{:S(2)}) collective-permute-start(f32[2,2,2,16]{3,2,1,0:T(2,128)S(1)} %constant_dynamic-update-slice_fusion.3), channel_id=1, source_target_pairs={{0,2},{2,0},{1,3},{3,1},{4,6},{6,4},{5,7},{7,5},{8,10},{10,8},{9,1... | collective-permute-start | bytes 1544 | tf_op jit(solution)/shard_map/ppermute | solution.py:65
  8.8 1.6 %collective-permute-done = f32[2,2,2,16]{3,2,1,0:T(2,128)S(1)} collective-permute-done((f32[2,2,2,16]{3,2,1,0:T(2,128)S(1)}, f32[2,2,2,16]{3,2,1,0:T(2,128)S(1)}, u32[]{:S(2)}, u32[]{:S(2)}) %collective-permute-start) | collective-permute-done | bytes 544 | tf_op jit(solution)/shard_map/ppermute | solution.py:65
  10.4 0.1 mul.90
  10.5 0.1 mul.91
  10.6 0.1 sub.79
  10.7 0.1 sub.80
  10.8 0.0 copy-start.3
  10.8 0.0 copy-start.9
  10.8 0.0 copy-start.4
  10.8 2.3 %fusion.12 = bf16[2,36,160,128]{3,2,1,0:T(8,128)(2,1)S(1)} fusion(bf16[2,36,160,128]{3,2,1,0:T(8,128)(2,1)S(1)} %copy-done, f32[160]{0:T(256)S(1)} %copy-done.5, f32[160]{0:T(256)S(1)} %copy-done.6, f32[2,160]{1,0:T(2,128)S(1)} %mul.91, f32[2,160]{1,0:T(2,128)S(1)} %sub.80), kind=kLoop, calls=%fused_computation.18 | loop fusion | flops 14745600 | bytes 5902080 | tf_op jit(solution)/shard_map/convert_element_type | solution.py:84
  13.2 0.0 copy-start.1
  13.2 1.6 %copy-done.1 = bf16[2,36,160,128]{3,2,1,0:T(8,128)(2,1)} copy-done((bf16[2,36,160,128]{3,2,1,0:T(8,128)(2,1)}, bf16[2,36,160,128]{3,2,1,0:T(8,128)(2,1)S(1)}, u32[]{:S(2)}) %copy-start.1) | copy-done | bytes 2949144
  14.8 2.1 %collective-permute-start.1 = (bf16[2,1,160,128]{3,2,1,0:T(8,128)(2,1)S(1)}, bf16[2,1,160,128]{3,2,1,0:T(8,128)(2,1)S(1)}, u32[]{:S(2)}, u32[]{:S(2)}) collective-permute-start(bf16[2,1,160,128]{3,2,1,0:T(8,128)(2,1)S(1)} %slice_select_fusion), channel_id=1, source_target_pairs={{0,2},{2,0},{1,3},{3,1},{4,6},{6,4},{5,7},{7,5},{8,10},{10,8},{9,1... | collective-permute-start | bytes 245768 | tf_op jit(solution)/shard_map/ppermute | solution.py:24
  16.9 2.4 %collective-permute-done.1 = bf16[2,1,160,128]{3,2,1,0:T(8,128)(2,1)S(1)} collective-permute-done((bf16[2,1,160,128]{3,2,1,0:T(8,128)(2,1)S(1)}, bf16[2,1,160,128]{3,2,1,0:T(8,128)(2,1)S(1)}, u32[]{:S(2)}, u32[]{:S(2)}) %collective-permute-start.1) | collective-permute-done | bytes 81952 | tf_op jit(solution)/shard_map/ppermute | solution.py:24
  19.3 3.9 %pad_maximum_fusion.xo_ref = bf16[2,38,160,128]{3,2,1,0:T(8,128)(2,1)} fusion(bf16[2,1,160,128]{3,2,1,0:T(8,128)(2,1)S(1)} %get-tuple-element.16, bf16[2,36,160,128]{3,2,1,0:T(8,128)(2,1)} %copy-done.1, bf16[2,1,160,128]{3,2,1,0:T(8,128)(2,1)S(1)} %get-tuple-element.15), kind=kLoop, calls=%fused_computation.20 | loop fusion | flops 3112960 | bytes 6225920 | tf_op jit(solution)/shard_map/concatenate | solution.py:28
  23.2 0.0 collective-permute-start.2
  23.2 4.1 %collective-permute-start.3 = (bf16[3,80,160]{2,1,0:T(8,128)(2,1)S(1)}, bf16[3,80,160]{2,1,0:T(8,128)(2,1)S(1)}, u32[]{:S(2)}, u32[]{:S(2)}) collective-permute-start(bf16[3,80,160]{2,1,0:T(8,128)(2,1)S(1)} %copy-done.3), channel_id=1, source_target_pairs={{0,12},{4,0},{8,4},{12,8},{1,13},{5,1},{9,5},{13,9},{2,14},{6,2},{... | collective-permute-start | bytes 230408 | tf_op jit(solution)/shard_map/ppermute | solution.py:42
  27.3 1.0 collective-permute-start.4
  28.4 0.1 copy.17.b_ref
  28.5 32.5 %all_gather.3 = bf16[3,3,320,160]{3,2,1,0:T(8,128)(2,1)S(1)} all-gather(bf16[3,3,80,160]{3,2,1,0:T(8,128)(2,1)S(1)} %copy-done.4), channel_id=1, replica_groups=mesh['groups'=2,'tm'=4,'height'=2,'chan'=2] {'tm'}, dimensions={2}, use_global_device_ids=true | all-gather | bytes 1152000 | tf_op jit(solution)/shard_map/all_gather | solution.py:245
  61.0 0.9 copy.16
  61.9 0.7 constant_dynamic-slice_fusion.2
  62.6 0.0 collective-permute-done.3
  62.7 0.0 collective-permute-done.4
  62.8 0.0 collective-permute-done.2.xt_ref
  62.9 0.9 copy-done.2
  63.8 18.1 %shard_map.91.refs_8_ = bf16[2,36,160,128]{3,2,1,0:T(8,128)(2,1)S(1)} custom-call(bf16[2,38,160,128]{3,2,1,0:T(8,128)(2,1)} %pad_maximum_fusion.xo_ref, bf16[2,38,160,128]{3,2,1,0:T(8,128)(2,1)} %collective-permute-done.2.xt_ref, bf16[3,480,160]{2,1,0:T(8,128)(2,1)S(1)} %get-tuple-element.12.wo_ref, bf16[3,480,160]{2,1,0:T(8,128)(2,1)S(1)} %get-tuple-element.11.wt_ref, ...), custom_call_target="tpu_custom_call" | custom-call | flops 8493465600 | bytes 13045760 | tf_op jit(solution)/shard_map/pallas_call | solution.py:132
  81.8 0.0 copy-start.7
  81.8 0.0 copy-start.8
  81.9 0.5 convert_reduce_fusion.1
  82.4 1.8 %fusion.20 = (bf16[1,36,160,128]{3,2,1,0:T(8,128)(2,1)}, bf16[1,36,160,128]{3,2,1,0:T(8,128)(2,1)}) fusion(bf16[2,36,160,128]{3,2,1,0:T(8,128)(2,1)S(1)} %shard_map.91.refs_8_), kind=kLoop, calls=%fused_computation.64 | loop fusion | bytes 5898240 | tf_op jit(solution)/shard_map/slice | solution.py:271
  84.2 0.1 reduce_sum.128
  84.3 0.1 reduce_sum.129
  84.4 5.4 %collective-permute-start.6 = (bf16[1,36,160,128]{3,2,1,0:T(8,128)(2,1)}, bf16[1,36,160,128]{3,2,1,0:T(8,128)(2,1)}, u32[]{:S(2)}, u32[]{:S(2)}) collective-permute-start(bf16[1,36,160,128]{3,2,1,0:T(8,128)(2,1)} %get-tuple-element.9), channel_id=1, source_target_pairs={{0,4},{4,8},{8,12},{1,5},{5,9},{9,13},{2,6},{6,10},{10,14},{3,7},{... | collective-permute-start | bytes 4423688 | tf_op jit(solution)/shard_map/ppermute | solution.py:271
  89.8 1.3 collective-permute-start.7
  91.1 0.1 sub.87
  91.2 0.1 sub.88
  91.2 0.9 fusion.1
  92.2 0.1 reduce_sum.131
  92.3 0.1 reduce_sum.132
  92.4 1.6 collective-permute-start.8
  94.0 2.1 %collective-permute-done.8 = f32[8,2,16]{2,1,0:T(2,128)S(1)} collective-permute-done((f32[8,2,16]{2,1,0:T(2,128)S(1)}, f32[8,2,16]{2,1,0:T(2,128)S(1)}, u32[]{:S(2)}, u32[]{:S(2)}) %collective-permute-start.8) | collective-permute-done | bytes 1056 | tf_op jit(solution)/shard_map/ppermute | solution.py:65
  96.2 31.1 %psum.7 = f32[8,2,16]{2,1,0:T(2,128)S(1)} all-reduce(f32[8,2,16]{2,1,0:T(2,128)S(1)} %constant_dynamic-update-slice_fusion), channel_id=1, replica_groups=mesh['groups'=2,'tm'=4,'height'=2,'chan'=2] {'tm'}, use_global_device_ids=true, to_apply=%region_11.12 | all-reduce | flops 256 | bytes 2048 | tf_op jit(solution)/shard_map/psum | solution.py:67
  127.3 0.1 mul.103
  127.4 0.1 mul.104
  127.5 0.1 sub.91
  127.6 0.1 sub.92
  127.7 0.0 copy-start.10
  127.7 7.7 %fusion.13.refs_0_.refs_1_.refs_2_ = bf16[4,36,160,128]{3,2,1,0:T(8,128)(2,1)} fusion(bf16[1,36,160,128]{3,2,1,0:T(8,128)(2,1)} %collective-permute-done.7, bf16[2,36,160,128]{3,2,1,0:T(8,128)(2,1)S(1)} %shard_map.91.refs_8_, bf16[1,36,160,128]{3,2,1,0:T(8,128)(2,1)} %collective-permute-done.6, f32[160]{0:T(256)S(1)} %copy-done.7, f32[160]{0:T(256)S(1)} %copy-done.8, ...), kind=kLoop, calls=%fused_computation.19 | loop fusion | flops 38338560 | bytes 11799044 | tf_op jit(solution)/shard_map/jit(_where)/select_n | solution.py:283
  135.4 0.1 copy.19.refs_9_
  135.5 1.1 fusion.21
  136.6 1.1 copy.18
  137.6 1.4 reshape.107
  139.1 0.2 dynamic-slice_bitcast_fusion
  139.3 6.0 %collective-permute-done.9.refs_3_.refs_4_.refs_5_ = bf16[4,36,160,128]{3,2,1,0:T(8,128)(2,1)} collective-permute-done((bf16[4,36,160,128]{3,2,1,0:T(8,128)(2,1)}, bf16[4,36,160,128]{3,2,1,0:T(8,128)(2,1)}, u32[]{:S(2)}, u32[]{:S(2)}) %collective-permute-start.9) | collective-permute-done | bytes 5898272 | tf_op jit(solution)/shard_map/ppermute | solution.py:16
  145.3 10.9 %shard_map.92 = bf16[2,36,160,128]{3,2,1,0:T(8,128)(2,1)} custom-call(bf16[4,36,160,128]{3,2,1,0:T(8,128)(2,1)} %fusion.13.refs_0_.refs_1_.refs_2_, bf16[4,36,160,128]{3,2,1,0:T(8,128)(2,1)} %fusion.13.refs_0_.refs_1_.refs_2_, bf16[4,36,160,128]{3,2,1,0:T(8,128)(2,1)} %fusion.13.refs_0_.refs_1_.refs_2_, ...), custom_call_target="tpu_custom_call" | custom-call | flops 2831155200 | bytes 23900160 | tf_op jit(solution)/shard_map/pallas_call | solution.py:186
  (46 shorter events, 0.4 us)
Async XLA Ops:
  0.0 10.8 %copy-start = (bf16[2,36,160,128]{3,2,1,0:T(8,128)(2,1)S(1)}, bf16[2,36,160,128]{3,2,1,0:T(8,128)(2,1)}, u32[]{:S(2)}) copy-start(bf16[2,36,160,128]{3,2,1,0:T(8,128)(2,1)} %res_ref.1) | copy-start | bytes 8847364
  0.0 10.8 %copy-start.5 = (f32[160]{0:T(256)S(1)}, f32[160]{0:T(256)}, u32[]{:S(2)}) copy-start(f32[160]{0:T(256)} %param.11) | copy-start | bytes 1924
  0.0 10.8 %copy-start.6 = (f32[160]{0:T(256)S(1)}, f32[160]{0:T(256)}, u32[]{:S(2)}) copy-start(f32[160]{0:T(256)} %param.10) | copy-start | bytes 1924
  5.8 4.6 %collective-permute-start = (f32[2,2,2,16]{3,2,1,0:T(2,128)S(1)}, f32[2,2,2,16]{3,2,1,0:T(2,128)S(1)}, u32[]{:S(2)}, u32[]{:S(2)}) collective-permute-start(f32[2,2,2,16]{3,2,1,0:T(2,128)S(1)} %constant_dynamic-update-slice_fusion.3), channel_id=1, source_target_pairs={{0,2},{2,0},{1,3},{3,1},{4,6},{6,4},{5,7},{7,5},{8,10},{10,8},{9,1... | collective-permute-start | bytes 1544 | tf_op jit(solution)/shard_map/ppermute | solution.py:65
  10.8 12.4 %copy-start.3 = (bf16[3,80,160]{2,1,0:T(8,128)(2,1)S(1)}, bf16[3,80,160]{2,1,0:T(8,128)(2,1)}, u32[]{:S(2)}) copy-start(bf16[3,80,160]{2,1,0:T(8,128)(2,1)} %param.16) | copy-start | bytes 230404
  10.8 17.5 %copy-start.9 = (f32[160]{0:T(256)S(1)}, f32[160]{0:T(256)}, u32[]{:S(2)}) copy-start(f32[160]{0:T(256)} %param.13) | copy-start | bytes 1924
  10.8 17.7 %copy-start.4 = (bf16[3,3,80,160]{3,2,1,0:T(8,128)(2,1)S(1)}, bf16[3,3,80,160]{3,2,1,0:T(8,128)(2,1)}, u32[]{:S(2)}) copy-start(bf16[3,3,80,160]{3,2,1,0:T(8,128)(2,1)} %param.12) | copy-start | bytes 691204
  13.2 1.6 %copy-start.1 = (bf16[2,36,160,128]{3,2,1,0:T(8,128)(2,1)}, bf16[2,36,160,128]{3,2,1,0:T(8,128)(2,1)S(1)}, u32[]{:S(2)}) copy-start(bf16[2,36,160,128]{3,2,1,0:T(8,128)(2,1)S(1)} %fusion.12) | copy-start | bytes 8847364
  14.8 4.5 %collective-permute-start.1 = (bf16[2,1,160,128]{3,2,1,0:T(8,128)(2,1)S(1)}, bf16[2,1,160,128]{3,2,1,0:T(8,128)(2,1)S(1)}, u32[]{:S(2)}, u32[]{:S(2)}) collective-permute-start(bf16[2,1,160,128]{3,2,1,0:T(8,128)(2,1)S(1)} %slice_select_fusion), channel_id=1, source_target_pairs={{0,2},{2,0},{1,3},{3,1},{4,6},{6,4},{5,7},{7,5},{8,10},{10,8},{9,1... | collective-permute-start | bytes 245768 | tf_op jit(solution)/shard_map/ppermute | solution.py:24
  23.2 39.6 %collective-permute-start.2 = (bf16[2,38,160,128]{3,2,1,0:T(8,128)(2,1)}, bf16[2,38,160,128]{3,2,1,0:T(8,128)(2,1)}, u32[]{:S(2)}, u32[]{:S(2)}) collective-permute-start(bf16[2,38,160,128]{3,2,1,0:T(8,128)(2,1)} %pad_maximum_fusion.xo_ref), channel_id=1, source_target_pairs={{0,1},{1,0},{2,3},{3,2},{4,5},{5,4},{6,7},{7,6},{8,9},{9,8},{10,11... | collective-permute-start | bytes 9338888 | tf_op jit(solution)/shard_map/ppermute | solution.py:16
  23.2 39.4 %collective-permute-start.3 = (bf16[3,80,160]{2,1,0:T(8,128)(2,1)S(1)}, bf16[3,80,160]{2,1,0:T(8,128)(2,1)S(1)}, u32[]{:S(2)}, u32[]{:S(2)}) collective-permute-start(bf16[3,80,160]{2,1,0:T(8,128)(2,1)S(1)} %copy-done.3), channel_id=1, source_target_pairs={{0,12},{4,0},{8,4},{12,8},{1,13},{5,1},{9,5},{13,9},{2,14},{6,2},{... | collective-permute-start | bytes 230408 | tf_op jit(solution)/shard_map/ppermute | solution.py:42
  27.3 35.3 %collective-permute-start.5 = (bf16[3,80,160]{2,1,0:T(8,128)(2,1)S(1)}, bf16[3,80,160]{2,1,0:T(8,128)(2,1)S(1)}, u32[]{:S(2)}, u32[]{:S(2)}) collective-permute-start(bf16[3,80,160]{2,1,0:T(8,128)(2,1)S(1)} %copy-done.3), channel_id=1, source_target_pairs={{0,4},{4,8},{8,12},{12,0},{1,5},{5,9},{9,13},{13,1},{2,6},{6,10},{... | collective-permute-start | bytes 230408 | tf_op jit(solution)/shard_map/ppermute | solution.py:42
  27.3 35.3 %collective-permute-start.4 = (bf16[3,80,160]{2,1,0:T(8,128)(2,1)S(1)}, bf16[3,80,160]{2,1,0:T(8,128)(2,1)S(1)}, u32[]{:S(2)}, u32[]{:S(2)}) collective-permute-start(bf16[3,80,160]{2,1,0:T(8,128)(2,1)S(1)} %copy-done.3), channel_id=1, source_target_pairs={{0,8},{4,12},{8,0},{12,4},{1,9},{5,13},{9,1},{13,5},{2,10},{6,14},... | collective-permute-start | bytes 230408 | tf_op jit(solution)/shard_map/ppermute | solution.py:42
  62.8 1.0 copy-start.2
  81.8 45.9 %copy-start.7 = (f32[160]{0:T(256)S(1)}, f32[160]{0:T(256)}, u32[]{:S(2)}) copy-start(f32[160]{0:T(256)} %param.15) | copy-start | bytes 1924
  81.8 45.9 %copy-start.8 = (f32[160]{0:T(256)S(1)}, f32[160]{0:T(256)}, u32[]{:S(2)}) copy-start(f32[160]{0:T(256)} %param.14) | copy-start | bytes 1924
  84.4 43.3 %collective-permute-start.6 = (bf16[1,36,160,128]{3,2,1,0:T(8,128)(2,1)}, bf16[1,36,160,128]{3,2,1,0:T(8,128)(2,1)}, u32[]{:S(2)}, u32[]{:S(2)}) collective-permute-start(bf16[1,36,160,128]{3,2,1,0:T(8,128)(2,1)} %get-tuple-element.9), channel_id=1, source_target_pairs={{0,4},{4,8},{8,12},{1,5},{5,9},{9,13},{2,6},{6,10},{10,14},{3,7},{... | collective-permute-start | bytes 4423688 | tf_op jit(solution)/shard_map/ppermute | solution.py:271
  89.8 37.9 %collective-permute-start.7 = (bf16[1,36,160,128]{3,2,1,0:T(8,128)(2,1)}, bf16[1,36,160,128]{3,2,1,0:T(8,128)(2,1)}, u32[]{:S(2)}, u32[]{:S(2)}) collective-permute-start(bf16[1,36,160,128]{3,2,1,0:T(8,128)(2,1)} %get-tuple-element.10), channel_id=1, source_target_pairs={{4,0},{8,4},{12,8},{5,1},{9,5},{13,9},{6,2},{10,6},{14,10},{7,3},{... | collective-permute-start | bytes 4423688 | tf_op jit(solution)/shard_map/ppermute | solution.py:272
  92.4 3.7 %collective-permute-start.8 = (f32[8,2,16]{2,1,0:T(2,128)S(1)}, f32[8,2,16]{2,1,0:T(2,128)S(1)}, u32[]{:S(2)}, u32[]{:S(2)}) collective-permute-start(f32[8,2,16]{2,1,0:T(2,128)S(1)} %constant_dynamic-update-slice_fusion.1), channel_id=1, source_target_pairs={{0,2},{2,0},{1,3},{3,1},{4,6},{6,4},{5,7},{7,5},{8,10},{10,8},{9,1... | collective-permute-start | bytes 3080 | tf_op jit(solution)/shard_map/ppermute | solution.py:65
  127.7 7.7 %copy-start.10 = (f32[160]{0:T(256)S(1)}, f32[160]{0:T(256)}, u32[]{:S(2)}) copy-start(f32[160]{0:T(256)} %param.17) | copy-start | bytes 1924
  135.4 9.9 %collective-permute-start.9 = (bf16[4,36,160,128]{3,2,1,0:T(8,128)(2,1)}, bf16[4,36,160,128]{3,2,1,0:T(8,128)(2,1)}, u32[]{:S(2)}, u32[]{:S(2)}) collective-permute-start(bf16[4,36,160,128]{3,2,1,0:T(8,128)(2,1)} %fusion.13.refs_0_.refs_1_.refs_2_), channel_id=1, source_target_pairs={{0,1},{1,0},{2,3},{3,2},{4,5},{5,4},{6,7},{7,6},{8,9},{9,8},{10,11... | collective-permute-start | bytes 17694728 | tf_op jit(solution)/shard_map/ppermute | solution.py:16

commit v18 on v17

--- a/solution.py
+++ b/solution.py
@@ -122,7 +122,7 @@
             )
         return carry
 
-    lax.fori_loop(0, rows // STEP, two_rows, 0)
+    lax.fori_loop(0, rows // STEP, two_rows, 0, unroll=True)
 
 
 def spatial_call(own, other, weight_own, weight_other, residual, bias, early):
@@ -172,7 +172,7 @@
             )
         return carry
 
-    lax.fori_loop(0, rows // STEP, two_rows, 0)
+    lax.fori_loop(0, rows // STEP, two_rows, 0, unroll=True)
 
 
 def frame_spec(tap, rows, chans, width):

time: 157 us -> 155 us (0.987)
  no operation moved by 1% of the time
where the time goes in v18:
time: 155 us
  blocking collectives  63.6 us (41%)
  Pallas kernels  27.6 us (18%)
  other arithmetic  21.2 us (14%)
  starting transfers between devices  18.5 us (12%)
  waiting for transfers between devices  12.2 us (8%)
  local copies, waits for them, and re-layouts  11.4 us (7%)
    all_gather x1, blocking collectives, body(): lax.all_gather(spatial_weight, 'tm', axis=2, tiled=True)  32.5 us
    psum x1, blocking collectives, group_stats(): table = lax.psum(table, name)  31.1 us
    pallas_call x1, Pallas kernels, spatial_call(): pl.pallas_call(spatial_kernel, out_shape=jax.ShapeDtypeStruct(residual.sh...  17 us
    pallas_call x1, Pallas kernels, temporal_call(): pl.pallas_call(temporal_kernel, out_shape=jax.ShapeDtypeStruct(residual.s...  10.6 us
    select_n x1, other arithmetic, body(): jnp.where(inside[:, None, None, None], act_two, jnp.zeros_like(act_two))  7.66 us
    ppermute x2, waiting for transfers between devices, swap_chan(): return lax.ppermute(block, 'chan', [(0, 1), (1, 0)])  6.04 us
    ppermute x1, starting transfers between devices, body(): before = lax.ppermute(hidden[-1:], 'tm', forward)  5.41 us
    ppermute x3, starting transfers between devices, gather_tm(): pieces.append(lax.ppermute(piece, 'tm', pairs))  5.14 us
  transfers between devices with their start and end apart: 10, of which 4 were waited for; matrix products, arithmetic and copies ran while one was open for 5% of the time, Pallas kernels for 0%

profile of v18, /device:TPU:0, one launch (start us, length us, event | category | flops | bytes accessed | tf_op | source)
XLA Modules:
  0.0 154.9 jit_solution(8598071587485835483)
XLA Ops:
  0.0 2.5 %convert_reduce_fusion = f32[2,160]{1,0:T(2,128)S(1)} fusion(bf16[2,36,160,128]{3,2,1,0:T(8,128)(2,1)} %res_ref.1), kind=kLoop, calls=%fused_computation.3 | loop fusion | flops 2948800 | bytes 2950400 | tf_op jit(solution)/shard_map/reduce_sum | solution.py:51
  2.5 0.1 reduce_sum.101
  2.5 0.1 reduce_sum.120
  2.6 0.1 sub.75
  2.7 0.1 sub.76
  2.8 2.7 %fusion.3 = f32[2,160]{1,0:T(2,128)S(1)} fusion(bf16[2,36,160,128]{3,2,1,0:T(8,128)(2,1)} %res_ref.1, f32[2,160]{1,0:T(2,128)S(1)} %sub.76), kind=kLoop, calls=%fused_computation.9 | loop fusion | flops 5897920 | bytes 2951680 | tf_op jit(solution)/shard_map/reduce_sum | solution.py:53
  5.6 0.1 reduce_sum.122
  5.7 0.1 reduce_sum.123
  5.8 3.0 %collective-permute-start = (f32[2,2,2,16]{3,2,1,0:T(2,128)S(1)}, f32[2,2,2,16]{3,2,1,0:T(2,128)S(1)}, u32[]{:S(2)}, u32[]{:S(2)}) collective-permute-start(f32[2,2,2,16]{3,2,1,0:T(2,128)S(1)} %constant_dynamic-update-slice_fusion.3), channel_id=1, source_target_pairs={{0,2},{2,0},{1,3},{3,1},{4,6},{6,4},{5,7},{7,5},{8,10},{10,8},{9,1... | collective-permute-start | bytes 1544 | tf_op jit(solution)/shard_map/ppermute | solution.py:65
  8.8 1.6 %collective-permute-done = f32[2,2,2,16]{3,2,1,0:T(2,128)S(1)} collective-permute-done((f32[2,2,2,16]{3,2,1,0:T(2,128)S(1)}, f32[2,2,2,16]{3,2,1,0:T(2,128)S(1)}, u32[]{:S(2)}, u32[]{:S(2)}) %collective-permute-start) | collective-permute-done | bytes 544 | tf_op jit(solution)/shard_map/ppermute | solution.py:65
  10.4 0.1 mul.90
  10.5 0.1 mul.91
  10.6 0.1 sub.79
  10.7 0.1 sub.80
  10.8 0.0 copy-start.3
  10.8 0.0 copy-start.9
  10.8 0.0 copy-start.4
  10.8 2.3 %fusion.12 = bf16[2,36,160,128]{3,2,1,0:T(8,128)(2,1)S(1)} fusion(bf16[2,36,160,128]{3,2,1,0:T(8,128)(2,1)S(1)} %copy-done, f32[160]{0:T(256)S(1)} %copy-done.5, f32[160]{0:T(256)S(1)} %copy-done.6, f32[2,160]{1,0:T(2,128)S(1)} %mul.91, f32[2,160]{1,0:T(2,128)S(1)} %sub.80), kind=kLoop, calls=%fused_computation.18 | loop fusion | flops 14745600 | bytes 5902080 | tf_op jit(solution)/shard_map/convert_element_type | solution.py:84
  13.2 0.0 copy-start.1
  13.2 1.6 %copy-done.1 = bf16[2,36,160,128]{3,2,1,0:T(8,128)(2,1)} copy-done((bf16[2,36,160,128]{3,2,1,0:T(8,128)(2,1)}, bf16[2,36,160,128]{3,2,1,0:T(8,128)(2,1)S(1)}, u32[]{:S(2)}) %copy-start.1) | copy-done | bytes 2949144
  14.8 2.1 %collective-permute-start.1 = (bf16[2,1,160,128]{3,2,1,0:T(8,128)(2,1)S(1)}, bf16[2,1,160,128]{3,2,1,0:T(8,128)(2,1)S(1)}, u32[]{:S(2)}, u32[]{:S(2)}) collective-permute-start(bf16[2,1,160,128]{3,2,1,0:T(8,128)(2,1)S(1)} %slice_select_fusion), channel_id=1, source_target_pairs={{0,2},{2,0},{1,3},{3,1},{4,6},{6,4},{5,7},{7,5},{8,10},{10,8},{9,1... | collective-permute-start | bytes 245768 | tf_op jit(solution)/shard_map/ppermute | solution.py:24
  16.9 2.4 %collective-permute-done.1 = bf16[2,1,160,128]{3,2,1,0:T(8,128)(2,1)S(1)} collective-permute-done((bf16[2,1,160,128]{3,2,1,0:T(8,128)(2,1)S(1)}, bf16[2,1,160,128]{3,2,1,0:T(8,128)(2,1)S(1)}, u32[]{:S(2)}, u32[]{:S(2)}) %collective-permute-start.1) | collective-permute-done | bytes 81952 | tf_op jit(solution)/shard_map/ppermute | solution.py:24
  19.3 3.9 %pad_maximum_fusion.xo_ref = bf16[2,38,160,128]{3,2,1,0:T(8,128)(2,1)} fusion(bf16[2,1,160,128]{3,2,1,0:T(8,128)(2,1)S(1)} %get-tuple-element.16, bf16[2,36,160,128]{3,2,1,0:T(8,128)(2,1)} %copy-done.1, bf16[2,1,160,128]{3,2,1,0:T(8,128)(2,1)S(1)} %get-tuple-element.15), kind=kLoop, calls=%fused_computation.20 | loop fusion | flops 3112960 | bytes 6225920 | tf_op jit(solution)/shard_map/concatenate | solution.py:28
  23.2 0.0 collective-permute-start.2
  23.2 4.1 %collective-permute-start.3 = (bf16[3,80,160]{2,1,0:T(8,128)(2,1)S(1)}, bf16[3,80,160]{2,1,0:T(8,128)(2,1)S(1)}, u32[]{:S(2)}, u32[]{:S(2)}) collective-permute-start(bf16[3,80,160]{2,1,0:T(8,128)(2,1)S(1)} %copy-done.3), channel_id=1, source_target_pairs={{0,12},{4,0},{8,4},{12,8},{1,13},{5,1},{9,5},{13,9},{2,14},{6,2},{... | collective-permute-start | bytes 230408 | tf_op jit(solution)/shard_map/ppermute | solution.py:42
  27.3 0.0 collective-permute-start.5
  27.3 1.0 collective-permute-start.4
  28.4 0.1 copy.17.b_ref
  28.5 32.5 %all_gather.3 = bf16[3,3,320,160]{3,2,1,0:T(8,128)(2,1)S(1)} all-gather(bf16[3,3,80,160]{3,2,1,0:T(8,128)(2,1)S(1)} %copy-done.4), channel_id=1, replica_groups=mesh['groups'=2,'tm'=4,'height'=2,'chan'=2] {'tm'}, dimensions={2}, use_global_device_ids=true | all-gather | bytes 1152000 | tf_op jit(solution)/shard_map/all_gather | solution.py:245
  61.0 0.9 copy.16
  61.9 0.7 constant_dynamic-slice_fusion.2
  62.7 0.0 collective-permute-done.4
  62.9 0.9 copy-done.2
  63.8 17.0 %shard_map.91.refs_8_ = bf16[2,36,160,128]{3,2,1,0:T(8,128)(2,1)S(1)} custom-call(bf16[2,38,160,128]{3,2,1,0:T(8,128)(2,1)} %pad_maximum_fusion.xo_ref, bf16[2,38,160,128]{3,2,1,0:T(8,128)(2,1)} %collective-permute-done.2.xt_ref, bf16[3,480,160]{2,1,0:T(8,128)(2,1)S(1)} %get-tuple-element.12.wo_ref, bf16[3,480,160]{2,1,0:T(8,128)(2,1)S(1)} %get-tuple-element.11.wt_ref, ...), custom_call_target="tpu_custom_call" | custom-call | flops 8493465600 | bytes 13045760 | tf_op jit(solution)/shard_map/pallas_call | solution.py:132
  80.7 0.0 copy-start.7
  80.8 0.0 copy-start.8
  80.8 0.5 convert_reduce_fusion.1
  81.3 1.8 %fusion.20 = (bf16[1,36,160,128]{3,2,1,0:T(8,128)(2,1)}, bf16[1,36,160,128]{3,2,1,0:T(8,128)(2,1)}) fusion(bf16[2,36,160,128]{3,2,1,0:T(8,128)(2,1)S(1)} %shard_map.91.refs_8_), kind=kLoop, calls=%fused_computation.64 | loop fusion | bytes 5898240 | tf_op jit(solution)/shard_map/slice | solution.py:271
  83.1 0.1 reduce_sum.128
  83.2 0.1 reduce_sum.129
  83.3 5.4 %collective-permute-start.6 = (bf16[1,36,160,128]{3,2,1,0:T(8,128)(2,1)}, bf16[1,36,160,128]{3,2,1,0:T(8,128)(2,1)}, u32[]{:S(2)}, u32[]{:S(2)}) collective-permute-start(bf16[1,36,160,128]{3,2,1,0:T(8,128)(2,1)} %get-tuple-element.9), channel_id=1, source_target_pairs={{0,4},{4,8},{8,12},{1,5},{5,9},{9,13},{2,6},{6,10},{10,14},{3,7},{... | collective-permute-start | bytes 4423688 | tf_op jit(solution)/shard_map/ppermute | solution.py:271
  88.7 1.3 collective-permute-start.7
  90.0 0.1 sub.87
  90.1 0.1 sub.88
  90.2 0.9 fusion.1
  91.1 0.1 reduce_sum.131
  91.2 0.1 reduce_sum.132
  91.3 1.6 %collective-permute-start.8 = (f32[8,2,16]{2,1,0:T(2,128)S(1)}, f32[8,2,16]{2,1,0:T(2,128)S(1)}, u32[]{:S(2)}, u32[]{:S(2)}) collective-permute-start(f32[8,2,16]{2,1,0:T(2,128)S(1)} %constant_dynamic-update-slice_fusion.1), channel_id=1, source_target_pairs={{0,2},{2,0},{1,3},{3,1},{4,6},{6,4},{5,7},{7,5},{8,10},{10,8},{9,1... | collective-permute-start | bytes 3080 | tf_op jit(solution)/shard_map/ppermute | solution.py:65
  92.9 2.2 %collective-permute-done.8 = f32[8,2,16]{2,1,0:T(2,128)S(1)} collective-permute-done((f32[8,2,16]{2,1,0:T(2,128)S(1)}, f32[8,2,16]{2,1,0:T(2,128)S(1)}, u32[]{:S(2)}, u32[]{:S(2)}) %collective-permute-start.8) | collective-permute-done | bytes 1056 | tf_op jit(solution)/shard_map/ppermute | solution.py:65
  95.1 31.1 %psum.7 = f32[8,2,16]{2,1,0:T(2,128)S(1)} all-reduce(f32[8,2,16]{2,1,0:T(2,128)S(1)} %constant_dynamic-update-slice_fusion), channel_id=1, replica_groups=mesh['groups'=2,'tm'=4,'height'=2,'chan'=2] {'tm'}, use_global_device_ids=true, to_apply=%region_11.12 | all-reduce | flops 256 | bytes 2048 | tf_op jit(solution)/shard_map/psum | solution.py:67
  126.3 0.1 mul.103
  126.3 0.1 mul.104
  126.4 0.1 sub.91
  126.5 0.1 sub.92
  126.6 0.0 copy-start.10
  126.6 0.0 collective-permute-done.6
  126.7 7.7 %fusion.13.refs_0_.refs_1_.refs_2_ = bf16[4,36,160,128]{3,2,1,0:T(8,128)(2,1)} fusion(bf16[1,36,160,128]{3,2,1,0:T(8,128)(2,1)} %collective-permute-done.7, bf16[2,36,160,128]{3,2,1,0:T(8,128)(2,1)S(1)} %shard_map.91.refs_8_, bf16[1,36,160,128]{3,2,1,0:T(8,128)(2,1)} %collective-permute-done.6, f32[160]{0:T(256)S(1)} %copy-done.7, f32[160]{0:T(256)S(1)} %copy-done.8, ...), kind=kLoop, calls=%fused_computation.19 | loop fusion | flops 38338560 | bytes 11799044 | tf_op jit(solution)/shard_map/jit(_where)/select_n | solution.py:283
  134.3 0.1 copy.19.refs_9_
  134.4 1.1 fusion.21
  135.5 1.1 copy.18
  136.6 1.4 reshape.107
  138.0 0.2 dynamic-slice_bitcast_fusion
  138.2 6.0 %collective-permute-done.9.refs_3_.refs_4_.refs_5_ = bf16[4,36,160,128]{3,2,1,0:T(8,128)(2,1)} collective-permute-done((bf16[4,36,160,128]{3,2,1,0:T(8,128)(2,1)}, bf16[4,36,160,128]{3,2,1,0:T(8,128)(2,1)}, u32[]{:S(2)}, u32[]{:S(2)}) %collective-permute-start.9) | collective-permute-done | bytes 5898272 | tf_op jit(solution)/shard_map/ppermute | solution.py:16
  144.3 10.6 %shard_map.92 = bf16[2,36,160,128]{3,2,1,0:T(8,128)(2,1)} custom-call(bf16[4,36,160,128]{3,2,1,0:T(8,128)(2,1)} %fusion.13.refs_0_.refs_1_.refs_2_, bf16[4,36,160,128]{3,2,1,0:T(8,128)(2,1)} %fusion.13.refs_0_.refs_1_.refs_2_, bf16[4,36,160,128]{3,2,1,0:T(8,128)(2,1)} %fusion.13.refs_0_.refs_1_.refs_2_, ...), custom_call_target="tpu_custom_call" | custom-call | flops 2831155200 | bytes 23900160 | tf_op jit(solution)/shard_map/pallas_call | solution.py:186
  (46 shorter events, 0.4 us)
Async XLA Ops:
  0.0 10.8 %copy-start = (bf16[2,36,160,128]{3,2,1,0:T(8,128)(2,1)S(1)}, bf16[2,36,160,128]{3,2,1,0:T(8,128)(2,1)}, u32[]{:S(2)}) copy-start(bf16[2,36,160,128]{3,2,1,0:T(8,128)(2,1)} %res_ref.1) | copy-start | bytes 8847364
  0.0 10.8 %copy-start.5 = (f32[160]{0:T(256)S(1)}, f32[160]{0:T(256)}, u32[]{:S(2)}) copy-start(f32[160]{0:T(256)} %param.11) | copy-start | bytes 1924
  0.0 10.8 %copy-start.6 = (f32[160]{0:T(256)S(1)}, f32[160]{0:T(256)}, u32[]{:S(2)}) copy-start(f32[160]{0:T(256)} %param.10) | copy-start | bytes 1924
  5.8 4.6 %collective-permute-start = (f32[2,2,2,16]{3,2,1,0:T(2,128)S(1)}, f32[2,2,2,16]{3,2,1,0:T(2,128)S(1)}, u32[]{:S(2)}, u32[]{:S(2)}) collective-permute-start(f32[2,2,2,16]{3,2,1,0:T(2,128)S(1)} %constant_dynamic-update-slice_fusion.3), channel_id=1, source_target_pairs={{0,2},{2,0},{1,3},{3,1},{4,6},{6,4},{5,7},{7,5},{8,10},{10,8},{9,1... | collective-permute-start | bytes 1544 | tf_op jit(solution)/shard_map/ppermute | solution.py:65
  10.8 12.4 %copy-start.3 = (bf16[3,80,160]{2,1,0:T(8,128)(2,1)S(1)}, bf16[3,80,160]{2,1,0:T(8,128)(2,1)}, u32[]{:S(2)}) copy-start(bf16[3,80,160]{2,1,0:T(8,128)(2,1)} %param.16) | copy-start | bytes 230404
  10.8 17.5 %copy-start.9 = (f32[160]{0:T(256)S(1)}, f32[160]{0:T(256)}, u32[]{:S(2)}) copy-start(f32[160]{0:T(256)} %param.13) | copy-start | bytes 1924
  10.8 17.7 %copy-start.4 = (bf16[3,3,80,160]{3,2,1,0:T(8,128)(2,1)S(1)}, bf16[3,3,80,160]{3,2,1,0:T(8,128)(2,1)}, u32[]{:S(2)}) copy-start(bf16[3,3,80,160]{3,2,1,0:T(8,128)(2,1)} %param.12) | copy-start | bytes 691204
  13.2 1.6 %copy-start.1 = (bf16[2,36,160,128]{3,2,1,0:T(8,128)(2,1)}, bf16[2,36,160,128]{3,2,1,0:T(8,128)(2,1)S(1)}, u32[]{:S(2)}) copy-start(bf16[2,36,160,128]{3,2,1,0:T(8,128)(2,1)S(1)} %fusion.12) | copy-start | bytes 8847364
  14.8 4.5 %collective-permute-start.1 = (bf16[2,1,160,128]{3,2,1,0:T(8,128)(2,1)S(1)}, bf16[2,1,160,128]{3,2,1,0:T(8,128)(2,1)S(1)}, u32[]{:S(2)}, u32[]{:S(2)}) collective-permute-start(bf16[2,1,160,128]{3,2,1,0:T(8,128)(2,1)S(1)} %slice_select_fusion), channel_id=1, source_target_pairs={{0,2},{2,0},{1,3},{3,1},{4,6},{6,4},{5,7},{7,5},{8,10},{10,8},{9,1... | collective-permute-start | bytes 245768 | tf_op jit(solution)/shard_map/ppermute | solution.py:24
  23.2 39.6 %collective-permute-start.2 = (bf16[2,38,160,128]{3,2,1,0:T(8,128)(2,1)}, bf16[2,38,160,128]{3,2,1,0:T(8,128)(2,1)}, u32[]{:S(2)}, u32[]{:S(2)}) collective-permute-start(bf16[2,38,160,128]{3,2,1,0:T(8,128)(2,1)} %pad_maximum_fusion.xo_ref), channel_id=1, source_target_pairs={{0,1},{1,0},{2,3},{3,2},{4,5},{5,4},{6,7},{7,6},{8,9},{9,8},{10,11... | collective-permute-start | bytes 9338888 | tf_op jit(solution)/shard_map/ppermute | solution.py:16
  23.2 39.4 %collective-permute-start.3 = (bf16[3,80,160]{2,1,0:T(8,128)(2,1)S(1)}, bf16[3,80,160]{2,1,0:T(8,128)(2,1)S(1)}, u32[]{:S(2)}, u32[]{:S(2)}) collective-permute-start(bf16[3,80,160]{2,1,0:T(8,128)(2,1)S(1)} %copy-done.3), channel_id=1, source_target_pairs={{0,12},{4,0},{8,4},{12,8},{1,13},{5,1},{9,5},{13,9},{2,14},{6,2},{... | collective-permute-start | bytes 230408 | tf_op jit(solution)/shard_map/ppermute | solution.py:42
  27.3 35.3 %collective-permute-start.5 = (bf16[3,80,160]{2,1,0:T(8,128)(2,1)S(1)}, bf16[3,80,160]{2,1,0:T(8,128)(2,1)S(1)}, u32[]{:S(2)}, u32[]{:S(2)}) collective-permute-start(bf16[3,80,160]{2,1,0:T(8,128)(2,1)S(1)} %copy-done.3), channel_id=1, source_target_pairs={{0,4},{4,8},{8,12},{12,0},{1,5},{5,9},{9,13},{13,1},{2,6},{6,10},{... | collective-permute-start | bytes 230408 | tf_op jit(solution)/shard_map/ppermute | solution.py:42
  27.3 35.3 %collective-permute-start.4 = (bf16[3,80,160]{2,1,0:T(8,128)(2,1)S(1)}, bf16[3,80,160]{2,1,0:T(8,128)(2,1)S(1)}, u32[]{:S(2)}, u32[]{:S(2)}) collective-permute-start(bf16[3,80,160]{2,1,0:T(8,128)(2,1)S(1)} %copy-done.3), channel_id=1, source_target_pairs={{0,8},{4,12},{8,0},{12,4},{1,9},{5,13},{9,1},{13,5},{2,10},{6,14},... | collective-permute-start | bytes 230408 | tf_op jit(solution)/shard_map/ppermute | solution.py:42
  62.8 1.0 copy-start.2
  80.7 45.9 %copy-start.7 = (f32[160]{0:T(256)S(1)}, f32[160]{0:T(256)}, u32[]{:S(2)}) copy-start(f32[160]{0:T(256)} %param.15) | copy-start | bytes 1924
  80.8 45.9 %copy-start.8 = (f32[160]{0:T(256)S(1)}, f32[160]{0:T(256)}, u32[]{:S(2)}) copy-start(f32[160]{0:T(256)} %param.14) | copy-start | bytes 1924
  83.3 43.3 %collective-permute-start.6 = (bf16[1,36,160,128]{3,2,1,0:T(8,128)(2,1)}, bf16[1,36,160,128]{3,2,1,0:T(8,128)(2,1)}, u32[]{:S(2)}, u32[]{:S(2)}) collective-permute-start(bf16[1,36,160,128]{3,2,1,0:T(8,128)(2,1)} %get-tuple-element.9), channel_id=1, source_target_pairs={{0,4},{4,8},{8,12},{1,5},{5,9},{9,13},{2,6},{6,10},{10,14},{3,7},{... | collective-permute-start | bytes 4423688 | tf_op jit(solution)/shard_map/ppermute | solution.py:271
  88.7 37.9 %collective-permute-start.7 = (bf16[1,36,160,128]{3,2,1,0:T(8,128)(2,1)}, bf16[1,36,160,128]{3,2,1,0:T(8,128)(2,1)}, u32[]{:S(2)}, u32[]{:S(2)}) collective-permute-start(bf16[1,36,160,128]{3,2,1,0:T(8,128)(2,1)} %get-tuple-element.10), channel_id=1, source_target_pairs={{4,0},{8,4},{12,8},{5,1},{9,5},{13,9},{6,2},{10,6},{14,10},{7,3},{... | collective-permute-start | bytes 4423688 | tf_op jit(solution)/shard_map/ppermute | solution.py:272
  91.3 3.7 %collective-permute-start.8 = (f32[8,2,16]{2,1,0:T(2,128)S(1)}, f32[8,2,16]{2,1,0:T(2,128)S(1)}, u32[]{:S(2)}, u32[]{:S(2)}) collective-permute-start(f32[8,2,16]{2,1,0:T(2,128)S(1)} %constant_dynamic-update-slice_fusion.1), channel_id=1, source_target_pairs={{0,2},{2,0},{1,3},{3,1},{4,6},{6,4},{5,7},{7,5},{8,10},{10,8},{9,1... | collective-permute-start | bytes 3080 | tf_op jit(solution)/shard_map/ppermute | solution.py:65
  126.6 7.7 %copy-start.10 = (f32[160]{0:T(256)S(1)}, f32[160]{0:T(256)}, u32[]{:S(2)}) copy-start(f32[160]{0:T(256)} %param.17) | copy-start | bytes 1924
  134.3 9.9 %collective-permute-start.9 = (bf16[4,36,160,128]{3,2,1,0:T(8,128)(2,1)}, bf16[4,36,160,128]{3,2,1,0:T(8,128)(2,1)}, u32[]{:S(2)}, u32[]{:S(2)}) collective-permute-start(bf16[4,36,160,128]{3,2,1,0:T(8,128)(2,1)} %fusion.13.refs_0_.refs_1_.refs_2_), channel_id=1, source_target_pairs={{0,1},{1,0},{2,3},{3,2},{4,5},{5,4},{6,7},{7,6},{8,9},{9,8},{10,11... | collective-permute-start | bytes 17694728 | tf_op jit(solution)/shard_map/ppermute | solution.py:16

commit v19 on v18

--- a/solution.py
+++ b/solution.py
@@ -91,7 +91,7 @@
     return lax.dynamic_update_slice_in_dim(joined, other, (1 - chan_index) * size, axis=2)
 
 
-STEP = 18
+STEP = 12
 
 
 def pair(ref, first):

time: 155 us -> 155 us (level)
  no operation moved by 1% of the time
where the time goes in v19:
time: 155 us
  blocking collectives  63.2 us (41%)
  Pallas kernels  27.7 us (18%)
  other arithmetic  21.2 us (14%)
  starting transfers between devices  18.7 us (12%)
  waiting for transfers between devices  12.2 us (8%)
  local copies, waits for them, and re-layouts  11.4 us (7%)
    all_gather x1, blocking collectives, body(): lax.all_gather(spatial_weight, 'tm', axis=2, tiled=True)  32.5 us
    psum x1, blocking collectives, group_stats(): table = lax.psum(table, name)  30.7 us
    pallas_call x1, Pallas kernels, spatial_call(): pl.pallas_call(spatial_kernel, out_shape=jax.ShapeDtypeStruct(residual.sh...  17.1 us
    pallas_call x1, Pallas kernels, temporal_call(): pl.pallas_call(temporal_kernel, out_shape=jax.ShapeDtypeStruct(residual.s...  10.6 us
    select_n x1, other arithmetic, body(): jnp.where(inside[:, None, None, None], act_two, jnp.zeros_like(act_two))  7.66 us
    ppermute x2, waiting for transfers between devices, swap_chan(): return lax.ppermute(block, 'chan', [(0, 1), (1, 0)])  6.04 us
    ppermute x1, starting transfers between devices, body(): before = lax.ppermute(hidden[-1:], 'tm', forward)  5.41 us
    ppermute x3, starting transfers between devices, gather_tm(): pieces.append(lax.ppermute(piece, 'tm', pairs))  5.14 us
  transfers between devices with their start and end apart: 10, of which 4 were waited for; matrix products, arithmetic and copies ran while one was open for 5% of the time, Pallas kernels for 0%

profile of v19, /device:TPU:0, one launch (start us, length us, event | category | flops | bytes accessed | tf_op | source)
XLA Modules:
  0.0 154.8 jit_solution(11352635833530850497)
XLA Ops:
  0.0 2.5 %convert_reduce_fusion = f32[2,160]{1,0:T(2,128)S(1)} fusion(bf16[2,36,160,128]{3,2,1,0:T(8,128)(2,1)} %res_ref.1), kind=kLoop, calls=%fused_computation.3 | loop fusion | flops 2948800 | bytes 2950400 | tf_op jit(solution)/shard_map/reduce_sum | solution.py:51
  2.5 0.1 reduce_sum.101
  2.5 0.1 reduce_sum.120
  2.6 0.1 sub.75
  2.7 0.1 sub.76
  2.8 2.7 %fusion.3 = f32[2,160]{1,0:T(2,128)S(1)} fusion(bf16[2,36,160,128]{3,2,1,0:T(8,128)(2,1)} %res_ref.1, f32[2,160]{1,0:T(2,128)S(1)} %sub.76), kind=kLoop, calls=%fused_computation.9 | loop fusion | flops 5897920 | bytes 2951680 | tf_op jit(solution)/shard_map/reduce_sum | solution.py:53
  5.6 0.1 reduce_sum.122
  5.7 0.1 reduce_sum.123
  5.8 3.0 %collective-permute-start = (f32[2,2,2,16]{3,2,1,0:T(2,128)S(1)}, f32[2,2,2,16]{3,2,1,0:T(2,128)S(1)}, u32[]{:S(2)}, u32[]{:S(2)}) collective-permute-start(f32[2,2,2,16]{3,2,1,0:T(2,128)S(1)} %constant_dynamic-update-slice_fusion.3), channel_id=1, source_target_pairs={{0,2},{2,0},{1,3},{3,1},{4,6},{6,4},{5,7},{7,5},{8,10},{10,8},{9,1... | collective-permute-start | bytes 1544 | tf_op jit(solution)/shard_map/ppermute | solution.py:65
  8.8 1.6 %collective-permute-done = f32[2,2,2,16]{3,2,1,0:T(2,128)S(1)} collective-permute-done((f32[2,2,2,16]{3,2,1,0:T(2,128)S(1)}, f32[2,2,2,16]{3,2,1,0:T(2,128)S(1)}, u32[]{:S(2)}, u32[]{:S(2)}) %collective-permute-start) | collective-permute-done | bytes 544 | tf_op jit(solution)/shard_map/ppermute | solution.py:65
  10.4 0.1 mul.90
  10.5 0.1 mul.91
  10.6 0.1 sub.79
  10.7 0.1 sub.80
  10.8 0.0 copy-start.3
  10.8 0.0 copy-start.9
  10.8 0.0 copy-start.4
  10.8 2.3 %fusion.12 = bf16[2,36,160,128]{3,2,1,0:T(8,128)(2,1)S(1)} fusion(bf16[2,36,160,128]{3,2,1,0:T(8,128)(2,1)S(1)} %copy-done, f32[160]{0:T(256)S(1)} %copy-done.5, f32[160]{0:T(256)S(1)} %copy-done.6, f32[2,160]{1,0:T(2,128)S(1)} %mul.91, f32[2,160]{1,0:T(2,128)S(1)} %sub.80), kind=kLoop, calls=%fused_computation.18 | loop fusion | flops 14745600 | bytes 5902080 | tf_op jit(solution)/shard_map/convert_element_type | solution.py:84
  13.2 0.0 copy-start.1
  13.2 1.6 %copy-done.1 = bf16[2,36,160,128]{3,2,1,0:T(8,128)(2,1)} copy-done((bf16[2,36,160,128]{3,2,1,0:T(8,128)(2,1)}, bf16[2,36,160,128]{3,2,1,0:T(8,128)(2,1)S(1)}, u32[]{:S(2)}) %copy-start.1) | copy-done | bytes 2949144
  14.8 2.1 %collective-permute-start.1 = (bf16[2,1,160,128]{3,2,1,0:T(8,128)(2,1)S(1)}, bf16[2,1,160,128]{3,2,1,0:T(8,128)(2,1)S(1)}, u32[]{:S(2)}, u32[]{:S(2)}) collective-permute-start(bf16[2,1,160,128]{3,2,1,0:T(8,128)(2,1)S(1)} %slice_select_fusion), channel_id=1, source_target_pairs={{0,2},{2,0},{1,3},{3,1},{4,6},{6,4},{5,7},{7,5},{8,10},{10,8},{9,1... | collective-permute-start | bytes 245768 | tf_op jit(solution)/shard_map/ppermute | solution.py:24
  16.9 2.4 %collective-permute-done.1 = bf16[2,1,160,128]{3,2,1,0:T(8,128)(2,1)S(1)} collective-permute-done((bf16[2,1,160,128]{3,2,1,0:T(8,128)(2,1)S(1)}, bf16[2,1,160,128]{3,2,1,0:T(8,128)(2,1)S(1)}, u32[]{:S(2)}, u32[]{:S(2)}) %collective-permute-start.1) | collective-permute-done | bytes 81952 | tf_op jit(solution)/shard_map/ppermute | solution.py:24
  19.3 3.9 %pad_maximum_fusion.xo_ref = bf16[2,38,160,128]{3,2,1,0:T(8,128)(2,1)} fusion(bf16[2,1,160,128]{3,2,1,0:T(8,128)(2,1)S(1)} %get-tuple-element.16, bf16[2,36,160,128]{3,2,1,0:T(8,128)(2,1)} %copy-done.1, bf16[2,1,160,128]{3,2,1,0:T(8,128)(2,1)S(1)} %get-tuple-element.15), kind=kLoop, calls=%fused_computation.20 | loop fusion | flops 3112960 | bytes 6225920 | tf_op jit(solution)/shard_map/concatenate | solution.py:28
  23.2 4.1 %collective-permute-start.3 = (bf16[3,80,160]{2,1,0:T(8,128)(2,1)S(1)}, bf16[3,80,160]{2,1,0:T(8,128)(2,1)S(1)}, u32[]{:S(2)}, u32[]{:S(2)}) collective-permute-start(bf16[3,80,160]{2,1,0:T(8,128)(2,1)S(1)} %copy-done.3), channel_id=1, source_target_pairs={{0,12},{4,0},{8,4},{12,8},{1,13},{5,1},{9,5},{13,9},{2,14},{6,2},{... | collective-permute-start | bytes 230408 | tf_op jit(solution)/shard_map/ppermute | solution.py:42
  27.3 0.0 collective-permute-start.5
  27.3 1.0 collective-permute-start.4
  28.4 0.1 copy.17.b_ref
  28.5 32.5 %all_gather.3 = bf16[3,3,320,160]{3,2,1,0:T(8,128)(2,1)S(1)} all-gather(bf16[3,3,80,160]{3,2,1,0:T(8,128)(2,1)S(1)} %copy-done.4), channel_id=1, replica_groups=mesh['groups'=2,'tm'=4,'height'=2,'chan'=2] {'tm'}, dimensions={2}, use_global_device_ids=true | all-gather | bytes 1152000 | tf_op jit(solution)/shard_map/all_gather | solution.py:245
  61.0 0.9 copy.16
  61.9 0.7 constant_dynamic-slice_fusion.2
  62.7 0.0 collective-permute-done.4
  62.7 0.0 collective-permute-done.5
  62.9 0.9 copy-done.2
  63.8 17.1 %shard_map.91.refs_8_ = bf16[2,36,160,128]{3,2,1,0:T(8,128)(2,1)S(1)} custom-call(bf16[2,38,160,128]{3,2,1,0:T(8,128)(2,1)} %pad_maximum_fusion.xo_ref, bf16[2,38,160,128]{3,2,1,0:T(8,128)(2,1)} %collective-permute-done.2.xt_ref, bf16[3,480,160]{2,1,0:T(8,128)(2,1)S(1)} %get-tuple-element.12.wo_ref, bf16[3,480,160]{2,1,0:T(8,128)(2,1)S(1)} %get-tuple-element.11.wt_ref, ...), custom_call_target="tpu_custom_call" | custom-call | flops 8493465600 | bytes 13045760 | tf_op jit(solution)/shard_map/pallas_call | solution.py:132
  80.9 0.0 copy-start.7
  80.9 0.0 copy-start.8
  80.9 0.5 convert_reduce_fusion.1
  81.4 1.8 %fusion.20 = (bf16[1,36,160,128]{3,2,1,0:T(8,128)(2,1)}, bf16[1,36,160,128]{3,2,1,0:T(8,128)(2,1)}) fusion(bf16[2,36,160,128]{3,2,1,0:T(8,128)(2,1)S(1)} %shard_map.91.refs_8_), kind=kLoop, calls=%fused_computation.64 | loop fusion | bytes 5898240 | tf_op jit(solution)/shard_map/slice | solution.py:271
  83.2 0.1 reduce_sum.128
  83.3 0.1 reduce_sum.129
  83.4 5.4 %collective-permute-start.6 = (bf16[1,36,160,128]{3,2,1,0:T(8,128)(2,1)}, bf16[1,36,160,128]{3,2,1,0:T(8,128)(2,1)}, u32[]{:S(2)}, u32[]{:S(2)}) collective-permute-start(bf16[1,36,160,128]{3,2,1,0:T(8,128)(2,1)} %get-tuple-element.9), channel_id=1, source_target_pairs={{0,4},{4,8},{8,12},{1,5},{5,9},{9,13},{2,6},{6,10},{10,14},{3,7},{... | collective-permute-start | bytes 4423688 | tf_op jit(solution)/shard_map/ppermute | solution.py:271
  88.9 1.5 collective-permute-start.7
  90.3 0.1 sub.87
  90.4 0.1 sub.88
  90.5 0.9 fusion.1
  91.4 0.1 reduce_sum.131
  91.5 0.1 reduce_sum.132
  91.7 1.6 %collective-permute-start.8 = (f32[8,2,16]{2,1,0:T(2,128)S(1)}, f32[8,2,16]{2,1,0:T(2,128)S(1)}, u32[]{:S(2)}, u32[]{:S(2)}) collective-permute-start(f32[8,2,16]{2,1,0:T(2,128)S(1)} %constant_dynamic-update-slice_fusion.1), channel_id=1, source_target_pairs={{0,2},{2,0},{1,3},{3,1},{4,6},{6,4},{5,7},{7,5},{8,10},{10,8},{9,1... | collective-permute-start | bytes 3080 | tf_op jit(solution)/shard_map/ppermute | solution.py:65
  93.2 2.2 %collective-permute-done.8 = f32[8,2,16]{2,1,0:T(2,128)S(1)} collective-permute-done((f32[8,2,16]{2,1,0:T(2,128)S(1)}, f32[8,2,16]{2,1,0:T(2,128)S(1)}, u32[]{:S(2)}, u32[]{:S(2)}) %collective-permute-start.8) | collective-permute-done | bytes 1056 | tf_op jit(solution)/shard_map/ppermute | solution.py:65
  95.4 30.7 %psum.7 = f32[8,2,16]{2,1,0:T(2,128)S(1)} all-reduce(f32[8,2,16]{2,1,0:T(2,128)S(1)} %constant_dynamic-update-slice_fusion), channel_id=1, replica_groups=mesh['groups'=2,'tm'=4,'height'=2,'chan'=2] {'tm'}, use_global_device_ids=true, to_apply=%region_11.12 | all-reduce | flops 256 | bytes 2048 | tf_op jit(solution)/shard_map/psum | solution.py:67
  126.2 0.1 mul.103
  126.3 0.1 mul.104
  126.4 0.1 sub.91
  126.4 0.1 sub.92
  126.5 0.0 copy-start.10
  126.6 0.0 collective-permute-done.6
  126.6 7.7 %fusion.13.refs_0_.refs_1_.refs_2_ = bf16[4,36,160,128]{3,2,1,0:T(8,128)(2,1)} fusion(bf16[1,36,160,128]{3,2,1,0:T(8,128)(2,1)} %collective-permute-done.7, bf16[2,36,160,128]{3,2,1,0:T(8,128)(2,1)S(1)} %shard_map.91.refs_8_, bf16[1,36,160,128]{3,2,1,0:T(8,128)(2,1)} %collective-permute-done.6, f32[160]{0:T(256)S(1)} %copy-done.7, f32[160]{0:T(256)S(1)} %copy-done.8, ...), kind=kLoop, calls=%fused_computation.19 | loop fusion | flops 38338560 | bytes 11799044 | tf_op jit(solution)/shard_map/jit(_where)/select_n | solution.py:283
  134.3 0.1 copy.19.refs_9_
  134.4 1.1 fusion.21
  135.5 1.1 copy.18
  136.5 1.4 reshape.107
  137.9 0.2 dynamic-slice_bitcast_fusion
  138.2 6.0 %collective-permute-done.9.refs_3_.refs_4_.refs_5_ = bf16[4,36,160,128]{3,2,1,0:T(8,128)(2,1)} collective-permute-done((bf16[4,36,160,128]{3,2,1,0:T(8,128)(2,1)}, bf16[4,36,160,128]{3,2,1,0:T(8,128)(2,1)}, u32[]{:S(2)}, u32[]{:S(2)}) %collective-permute-start.9) | collective-permute-done | bytes 5898272 | tf_op jit(solution)/shard_map/ppermute | solution.py:16
  144.2 10.6 %shard_map.92 = bf16[2,36,160,128]{3,2,1,0:T(8,128)(2,1)} custom-call(bf16[4,36,160,128]{3,2,1,0:T(8,128)(2,1)} %fusion.13.refs_0_.refs_1_.refs_2_, bf16[4,36,160,128]{3,2,1,0:T(8,128)(2,1)} %fusion.13.refs_0_.refs_1_.refs_2_, bf16[4,36,160,128]{3,2,1,0:T(8,128)(2,1)} %fusion.13.refs_0_.refs_1_.refs_2_, ...), custom_call_target="tpu_custom_call" | custom-call | flops 2831155200 | bytes 23900160 | tf_op jit(solution)/shard_map/pallas_call | solution.py:186
  (46 shorter events, 0.4 us)
Async XLA Ops:
  0.0 10.8 %copy-start = (bf16[2,36,160,128]{3,2,1,0:T(8,128)(2,1)S(1)}, bf16[2,36,160,128]{3,2,1,0:T(8,128)(2,1)}, u32[]{:S(2)}) copy-start(bf16[2,36,160,128]{3,2,1,0:T(8,128)(2,1)} %res_ref.1) | copy-start | bytes 8847364
  0.0 10.8 %copy-start.5 = (f32[160]{0:T(256)S(1)}, f32[160]{0:T(256)}, u32[]{:S(2)}) copy-start(f32[160]{0:T(256)} %param.11) | copy-start | bytes 1924
  0.0 10.8 %copy-start.6 = (f32[160]{0:T(256)S(1)}, f32[160]{0:T(256)}, u32[]{:S(2)}) copy-start(f32[160]{0:T(256)} %param.10) | copy-start | bytes 1924
  5.8 4.6 %collective-permute-start = (f32[2,2,2,16]{3,2,1,0:T(2,128)S(1)}, f32[2,2,2,16]{3,2,1,0:T(2,128)S(1)}, u32[]{:S(2)}, u32[]{:S(2)}) collective-permute-start(f32[2,2,2,16]{3,2,1,0:T(2,128)S(1)} %constant_dynamic-update-slice_fusion.3), channel_id=1, source_target_pairs={{0,2},{2,0},{1,3},{3,1},{4,6},{6,4},{5,7},{7,5},{8,10},{10,8},{9,1... | collective-permute-start | bytes 1544 | tf_op jit(solution)/shard_map/ppermute | solution.py:65
  10.8 12.4 %copy-start.3 = (bf16[3,80,160]{2,1,0:T(8,128)(2,1)S(1)}, bf16[3,80,160]{2,1,0:T(8,128)(2,1)}, u32[]{:S(2)}) copy-start(bf16[3,80,160]{2,1,0:T(8,128)(2,1)} %param.16) | copy-start | bytes 230404
  10.8 17.5 %copy-start.9 = (f32[160]{0:T(256)S(1)}, f32[160]{0:T(256)}, u32[]{:S(2)}) copy-start(f32[160]{0:T(256)} %param.13) | copy-start | bytes 1924
  10.8 17.7 %copy-start.4 = (bf16[3,3,80,160]{3,2,1,0:T(8,128)(2,1)S(1)}, bf16[3,3,80,160]{3,2,1,0:T(8,128)(2,1)}, u32[]{:S(2)}) copy-start(bf16[3,3,80,160]{3,2,1,0:T(8,128)(2,1)} %param.12) | copy-start | bytes 691204
  13.2 1.6 %copy-start.1 = (bf16[2,36,160,128]{3,2,1,0:T(8,128)(2,1)}, bf16[2,36,160,128]{3,2,1,0:T(8,128)(2,1)S(1)}, u32[]{:S(2)}) copy-start(bf16[2,36,160,128]{3,2,1,0:T(8,128)(2,1)S(1)} %fusion.12) | copy-start | bytes 8847364
  14.8 4.5 %collective-permute-start.1 = (bf16[2,1,160,128]{3,2,1,0:T(8,128)(2,1)S(1)}, bf16[2,1,160,128]{3,2,1,0:T(8,128)(2,1)S(1)}, u32[]{:S(2)}, u32[]{:S(2)}) collective-permute-start(bf16[2,1,160,128]{3,2,1,0:T(8,128)(2,1)S(1)} %slice_select_fusion), channel_id=1, source_target_pairs={{0,2},{2,0},{1,3},{3,1},{4,6},{6,4},{5,7},{7,5},{8,10},{10,8},{9,1... | collective-permute-start | bytes 245768 | tf_op jit(solution)/shard_map/ppermute | solution.py:24
  23.2 39.6 %collective-permute-start.2 = (bf16[2,38,160,128]{3,2,1,0:T(8,128)(2,1)}, bf16[2,38,160,128]{3,2,1,0:T(8,128)(2,1)}, u32[]{:S(2)}, u32[]{:S(2)}) collective-permute-start(bf16[2,38,160,128]{3,2,1,0:T(8,128)(2,1)} %pad_maximum_fusion.xo_ref), channel_id=1, source_target_pairs={{0,1},{1,0},{2,3},{3,2},{4,5},{5,4},{6,7},{7,6},{8,9},{9,8},{10,11... | collective-permute-start | bytes 9338888 | tf_op jit(solution)/shard_map/ppermute | solution.py:16
  23.2 39.4 %collective-permute-start.3 = (bf16[3,80,160]{2,1,0:T(8,128)(2,1)S(1)}, bf16[3,80,160]{2,1,0:T(8,128)(2,1)S(1)}, u32[]{:S(2)}, u32[]{:S(2)}) collective-permute-start(bf16[3,80,160]{2,1,0:T(8,128)(2,1)S(1)} %copy-done.3), channel_id=1, source_target_pairs={{0,12},{4,0},{8,4},{12,8},{1,13},{5,1},{9,5},{13,9},{2,14},{6,2},{... | collective-permute-start | bytes 230408 | tf_op jit(solution)/shard_map/ppermute | solution.py:42
  27.3 35.3 %collective-permute-start.5 = (bf16[3,80,160]{2,1,0:T(8,128)(2,1)S(1)}, bf16[3,80,160]{2,1,0:T(8,128)(2,1)S(1)}, u32[]{:S(2)}, u32[]{:S(2)}) collective-permute-start(bf16[3,80,160]{2,1,0:T(8,128)(2,1)S(1)} %copy-done.3), channel_id=1, source_target_pairs={{0,4},{4,8},{8,12},{12,0},{1,5},{5,9},{9,13},{13,1},{2,6},{6,10},{... | collective-permute-start | bytes 230408 | tf_op jit(solution)/shard_map/ppermute | solution.py:42
  27.3 35.3 %collective-permute-start.4 = (bf16[3,80,160]{2,1,0:T(8,128)(2,1)S(1)}, bf16[3,80,160]{2,1,0:T(8,128)(2,1)S(1)}, u32[]{:S(2)}, u32[]{:S(2)}) collective-permute-start(bf16[3,80,160]{2,1,0:T(8,128)(2,1)S(1)} %copy-done.3), channel_id=1, source_target_pairs={{0,8},{4,12},{8,0},{12,4},{1,9},{5,13},{9,1},{13,5},{2,10},{6,14},... | collective-permute-start | bytes 230408 | tf_op jit(solution)/shard_map/ppermute | solution.py:42
  62.8 1.0 copy-start.2
  80.9 45.7 %copy-start.7 = (f32[160]{0:T(256)S(1)}, f32[160]{0:T(256)}, u32[]{:S(2)}) copy-start(f32[160]{0:T(256)} %param.15) | copy-start | bytes 1924
  80.9 45.7 %copy-start.8 = (f32[160]{0:T(256)S(1)}, f32[160]{0:T(256)}, u32[]{:S(2)}) copy-start(f32[160]{0:T(256)} %param.14) | copy-start | bytes 1924
  83.4 43.1 %collective-permute-start.6 = (bf16[1,36,160,128]{3,2,1,0:T(8,128)(2,1)}, bf16[1,36,160,128]{3,2,1,0:T(8,128)(2,1)}, u32[]{:S(2)}, u32[]{:S(2)}) collective-permute-start(bf16[1,36,160,128]{3,2,1,0:T(8,128)(2,1)} %get-tuple-element.9), channel_id=1, source_target_pairs={{0,4},{4,8},{8,12},{1,5},{5,9},{9,13},{2,6},{6,10},{10,14},{3,7},{... | collective-permute-start | bytes 4423688 | tf_op jit(solution)/shard_map/ppermute | solution.py:271
  88.9 37.7 %collective-permute-start.7 = (bf16[1,36,160,128]{3,2,1,0:T(8,128)(2,1)}, bf16[1,36,160,128]{3,2,1,0:T(8,128)(2,1)}, u32[]{:S(2)}, u32[]{:S(2)}) collective-permute-start(bf16[1,36,160,128]{3,2,1,0:T(8,128)(2,1)} %get-tuple-element.10), channel_id=1, source_target_pairs={{4,0},{8,4},{12,8},{5,1},{9,5},{13,9},{6,2},{10,6},{14,10},{7,3},{... | collective-permute-start | bytes 4423688 | tf_op jit(solution)/shard_map/ppermute | solution.py:272
  91.7 3.7 %collective-permute-start.8 = (f32[8,2,16]{2,1,0:T(2,128)S(1)}, f32[8,2,16]{2,1,0:T(2,128)S(1)}, u32[]{:S(2)}, u32[]{:S(2)}) collective-permute-start(f32[8,2,16]{2,1,0:T(2,128)S(1)} %constant_dynamic-update-slice_fusion.1), channel_id=1, source_target_pairs={{0,2},{2,0},{1,3},{3,1},{4,6},{6,4},{5,7},{7,5},{8,10},{10,8},{9,1... | collective-permute-start | bytes 3080 | tf_op jit(solution)/shard_map/ppermute | solution.py:65
  126.5 7.7 %copy-start.10 = (f32[160]{0:T(256)S(1)}, f32[160]{0:T(256)}, u32[]{:S(2)}) copy-start(f32[160]{0:T(256)} %param.17) | copy-start | bytes 1924
  134.3 9.9 %collective-permute-start.9 = (bf16[4,36,160,128]{3,2,1,0:T(8,128)(2,1)}, bf16[4,36,160,128]{3,2,1,0:T(8,128)(2,1)}, u32[]{:S(2)}, u32[]{:S(2)}) collective-permute-start(bf16[4,36,160,128]{3,2,1,0:T(8,128)(2,1)} %fusion.13.refs_0_.refs_1_.refs_2_), channel_id=1, source_target_pairs={{0,1},{1,0},{2,3},{3,2},{4,5},{5,4},{6,7},{7,6},{8,9},{9,8},{10,11... | collective-permute-start | bytes 17694728 | tf_op jit(solution)/shard_map/ppermute | solution.py:16

commit v20 on v19

--- a/solution.py
+++ b/solution.py
@@ -91,7 +91,7 @@
     return lax.dynamic_update_slice_in_dim(joined, other, (1 - chan_index) * size, axis=2)
 
 
-STEP = 12
+STEP = 6
 
 
 def pair(ref, first):

time: 155 us -> 155 us (level)
  no operation moved by 1% of the time
where the time goes in v20:
time: 155 us
  blocking collectives  63.6 us (41%)
  Pallas kernels  27.7 us (18%)
  other arithmetic  21.2 us (14%)
  starting transfers between devices  18.5 us (12%)
  waiting for transfers between devices  12.2 us (8%)
  local copies, waits for them, and re-layouts  11.4 us (7%)
    all_gather x1, blocking collectives, body(): lax.all_gather(spatial_weight, 'tm', axis=2, tiled=True)  32.5 us
    psum x1, blocking collectives, group_stats(): table = lax.psum(table, name)  31.1 us
    pallas_call x1, Pallas kernels, spatial_call(): pl.pallas_call(spatial_kernel, out_shape=jax.ShapeDtypeStruct(residual.sh...  17.1 us
    pallas_call x1, Pallas kernels, temporal_call(): pl.pallas_call(temporal_kernel, out_shape=jax.ShapeDtypeStruct(residual.s...  10.6 us
    select_n x1, other arithmetic, body(): jnp.where(inside[:, None, None, None], act_two, jnp.zeros_like(act_two))  7.66 us
    ppermute x2, waiting for transfers between devices, swap_chan(): return lax.ppermute(block, 'chan', [(0, 1), (1, 0)])  6.04 us
    ppermute x1, starting transfers between devices, body(): before = lax.ppermute(hidden[-1:], 'tm', forward)  5.41 us
    ppermute x3, starting transfers between devices, gather_tm(): pieces.append(lax.ppermute(piece, 'tm', pairs))  5.14 us
  transfers between devices with their start and end apart: 10, of which 4 were waited for; matrix products, arithmetic and copies ran while one was open for 5% of the time, Pallas kernels for 0%

profile of v20, /device:TPU:0, one launch (start us, length us, event | category | flops | bytes accessed | tf_op | source)
XLA Modules:
  0.0 155.0 jit_solution(6822972633033138290)
XLA Ops:
  0.0 2.5 %convert_reduce_fusion = f32[2,160]{1,0:T(2,128)S(1)} fusion(bf16[2,36,160,128]{3,2,1,0:T(8,128)(2,1)} %res_ref.1), kind=kLoop, calls=%fused_computation.3 | loop fusion | flops 2948800 | bytes 2950400 | tf_op jit(solution)/shard_map/reduce_sum | solution.py:51
  2.5 0.1 reduce_sum.101
  2.5 0.1 reduce_sum.120
  2.6 0.1 sub.75
  2.7 0.1 sub.76
  2.8 2.7 %fusion.3 = f32[2,160]{1,0:T(2,128)S(1)} fusion(bf16[2,36,160,128]{3,2,1,0:T(8,128)(2,1)} %res_ref.1, f32[2,160]{1,0:T(2,128)S(1)} %sub.76), kind=kLoop, calls=%fused_computation.9 | loop fusion | flops 5897920 | bytes 2951680 | tf_op jit(solution)/shard_map/reduce_sum | solution.py:53
  5.6 0.1 reduce_sum.122
  5.7 0.1 reduce_sum.123
  5.8 3.0 %collective-permute-start = (f32[2,2,2,16]{3,2,1,0:T(2,128)S(1)}, f32[2,2,2,16]{3,2,1,0:T(2,128)S(1)}, u32[]{:S(2)}, u32[]{:S(2)}) collective-permute-start(f32[2,2,2,16]{3,2,1,0:T(2,128)S(1)} %constant_dynamic-update-slice_fusion.3), channel_id=1, source_target_pairs={{0,2},{2,0},{1,3},{3,1},{4,6},{6,4},{5,7},{7,5},{8,10},{10,8},{9,1... | collective-permute-start | bytes 1544 | tf_op jit(solution)/shard_map/ppermute | solution.py:65
  8.8 1.6 %collective-permute-done = f32[2,2,2,16]{3,2,1,0:T(2,128)S(1)} collective-permute-done((f32[2,2,2,16]{3,2,1,0:T(2,128)S(1)}, f32[2,2,2,16]{3,2,1,0:T(2,128)S(1)}, u32[]{:S(2)}, u32[]{:S(2)}) %collective-permute-start) | collective-permute-done | bytes 544 | tf_op jit(solution)/shard_map/ppermute | solution.py:65
  10.4 0.1 mul.90
  10.5 0.1 mul.91
  10.6 0.1 sub.79
  10.7 0.1 sub.80
  10.8 0.0 copy-start.3
  10.8 0.0 copy-start.9
  10.8 0.0 copy-start.4
  10.8 2.3 %fusion.12 = bf16[2,36,160,128]{3,2,1,0:T(8,128)(2,1)S(1)} fusion(bf16[2,36,160,128]{3,2,1,0:T(8,128)(2,1)S(1)} %copy-done, f32[160]{0:T(256)S(1)} %copy-done.5, f32[160]{0:T(256)S(1)} %copy-done.6, f32[2,160]{1,0:T(2,128)S(1)} %mul.91, f32[2,160]{1,0:T(2,128)S(1)} %sub.80), kind=kLoop, calls=%fused_computation.18 | loop fusion | flops 14745600 | bytes 5902080 | tf_op jit(solution)/shard_map/convert_element_type | solution.py:84
  13.2 0.0 copy-start.1
  13.2 1.6 %copy-done.1 = bf16[2,36,160,128]{3,2,1,0:T(8,128)(2,1)} copy-done((bf16[2,36,160,128]{3,2,1,0:T(8,128)(2,1)}, bf16[2,36,160,128]{3,2,1,0:T(8,128)(2,1)S(1)}, u32[]{:S(2)}) %copy-start.1) | copy-done | bytes 2949144
  14.8 2.1 %collective-permute-start.1 = (bf16[2,1,160,128]{3,2,1,0:T(8,128)(2,1)S(1)}, bf16[2,1,160,128]{3,2,1,0:T(8,128)(2,1)S(1)}, u32[]{:S(2)}, u32[]{:S(2)}) collective-permute-start(bf16[2,1,160,128]{3,2,1,0:T(8,128)(2,1)S(1)} %slice_select_fusion), channel_id=1, source_target_pairs={{0,2},{2,0},{1,3},{3,1},{4,6},{6,4},{5,7},{7,5},{8,10},{10,8},{9,1... | collective-permute-start | bytes 245768 | tf_op jit(solution)/shard_map/ppermute | solution.py:24
  16.9 2.4 %collective-permute-done.1 = bf16[2,1,160,128]{3,2,1,0:T(8,128)(2,1)S(1)} collective-permute-done((bf16[2,1,160,128]{3,2,1,0:T(8,128)(2,1)S(1)}, bf16[2,1,160,128]{3,2,1,0:T(8,128)(2,1)S(1)}, u32[]{:S(2)}, u32[]{:S(2)}) %collective-permute-start.1) | collective-permute-done | bytes 81952 | tf_op jit(solution)/shard_map/ppermute | solution.py:24
  19.3 3.9 %pad_maximum_fusion.xo_ref = bf16[2,38,160,128]{3,2,1,0:T(8,128)(2,1)} fusion(bf16[2,1,160,128]{3,2,1,0:T(8,128)(2,1)S(1)} %get-tuple-element.16, bf16[2,36,160,128]{3,2,1,0:T(8,128)(2,1)} %copy-done.1, bf16[2,1,160,128]{3,2,1,0:T(8,128)(2,1)S(1)} %get-tuple-element.15), kind=kLoop, calls=%fused_computation.20 | loop fusion | flops 3112960 | bytes 6225920 | tf_op jit(solution)/shard_map/concatenate | solution.py:28
  23.2 4.1 %collective-permute-start.3 = (bf16[3,80,160]{2,1,0:T(8,128)(2,1)S(1)}, bf16[3,80,160]{2,1,0:T(8,128)(2,1)S(1)}, u32[]{:S(2)}, u32[]{:S(2)}) collective-permute-start(bf16[3,80,160]{2,1,0:T(8,128)(2,1)S(1)} %copy-done.3), channel_id=1, source_target_pairs={{0,12},{4,0},{8,4},{12,8},{1,13},{5,1},{9,5},{13,9},{2,14},{6,2},{... | collective-permute-start | bytes 230408 | tf_op jit(solution)/shard_map/ppermute | solution.py:42
  27.3 0.0 collective-permute-start.5
  27.3 1.0 collective-permute-start.4
  28.4 0.1 copy.17.b_ref
  28.5 32.5 %all_gather.3 = bf16[3,3,320,160]{3,2,1,0:T(8,128)(2,1)S(1)} all-gather(bf16[3,3,80,160]{3,2,1,0:T(8,128)(2,1)S(1)} %copy-done.4), channel_id=1, replica_groups=mesh['groups'=2,'tm'=4,'height'=2,'chan'=2] {'tm'}, dimensions={2}, use_global_device_ids=true | all-gather | bytes 1152000 | tf_op jit(solution)/shard_map/all_gather | solution.py:245
  61.0 0.9 copy.16
  61.9 0.7 constant_dynamic-slice_fusion.2
  62.6 0.0 collective-permute-done.3
  62.7 0.0 collective-permute-done.5
  62.8 0.0 collective-permute-done.2.xt_ref
  62.9 0.9 copy-done.2
  63.8 17.1 %shard_map.91.refs_8_ = bf16[2,36,160,128]{3,2,1,0:T(8,128)(2,1)S(1)} custom-call(bf16[2,38,160,128]{3,2,1,0:T(8,128)(2,1)} %pad_maximum_fusion.xo_ref, bf16[2,38,160,128]{3,2,1,0:T(8,128)(2,1)} %collective-permute-done.2.xt_ref, bf16[3,480,160]{2,1,0:T(8,128)(2,1)S(1)} %get-tuple-element.12.wo_ref, bf16[3,480,160]{2,1,0:T(8,128)(2,1)S(1)} %get-tuple-element.11.wt_ref, ...), custom_call_target="tpu_custom_call" | custom-call | flops 8493465600 | bytes 13045760 | tf_op jit(solution)/shard_map/pallas_call | solution.py:132
  80.9 0.0 copy-start.7
  80.9 0.0 copy-start.8
  80.9 0.5 convert_reduce_fusion.1
  81.4 1.8 %fusion.20 = (bf16[1,36,160,128]{3,2,1,0:T(8,128)(2,1)}, bf16[1,36,160,128]{3,2,1,0:T(8,128)(2,1)}) fusion(bf16[2,36,160,128]{3,2,1,0:T(8,128)(2,1)S(1)} %shard_map.91.refs_8_), kind=kLoop, calls=%fused_computation.64 | loop fusion | bytes 5898240 | tf_op jit(solution)/shard_map/slice | solution.py:271
  83.2 0.1 reduce_sum.128
  83.3 0.1 reduce_sum.129
  83.4 5.4 %collective-permute-start.6 = (bf16[1,36,160,128]{3,2,1,0:T(8,128)(2,1)}, bf16[1,36,160,128]{3,2,1,0:T(8,128)(2,1)}, u32[]{:S(2)}, u32[]{:S(2)}) collective-permute-start(bf16[1,36,160,128]{3,2,1,0:T(8,128)(2,1)} %get-tuple-element.9), channel_id=1, source_target_pairs={{0,4},{4,8},{8,12},{1,5},{5,9},{9,13},{2,6},{6,10},{10,14},{3,7},{... | collective-permute-start | bytes 4423688 | tf_op jit(solution)/shard_map/ppermute | solution.py:271
  88.8 1.3 collective-permute-start.7
  90.1 0.1 sub.87
  90.2 0.1 sub.88
  90.3 0.9 fusion.1
  91.2 0.1 reduce_sum.131
  91.3 0.1 reduce_sum.132
  91.5 1.6 %collective-permute-start.8 = (f32[8,2,16]{2,1,0:T(2,128)S(1)}, f32[8,2,16]{2,1,0:T(2,128)S(1)}, u32[]{:S(2)}, u32[]{:S(2)}) collective-permute-start(f32[8,2,16]{2,1,0:T(2,128)S(1)} %constant_dynamic-update-slice_fusion.1), channel_id=1, source_target_pairs={{0,2},{2,0},{1,3},{3,1},{4,6},{6,4},{5,7},{7,5},{8,10},{10,8},{9,1... | collective-permute-start | bytes 3080 | tf_op jit(solution)/shard_map/ppermute | solution.py:65
  93.0 2.2 %collective-permute-done.8 = f32[8,2,16]{2,1,0:T(2,128)S(1)} collective-permute-done((f32[8,2,16]{2,1,0:T(2,128)S(1)}, f32[8,2,16]{2,1,0:T(2,128)S(1)}, u32[]{:S(2)}, u32[]{:S(2)}) %collective-permute-start.8) | collective-permute-done | bytes 1056 | tf_op jit(solution)/shard_map/ppermute | solution.py:65
  95.2 31.1 %psum.7 = f32[8,2,16]{2,1,0:T(2,128)S(1)} all-reduce(f32[8,2,16]{2,1,0:T(2,128)S(1)} %constant_dynamic-update-slice_fusion), channel_id=1, replica_groups=mesh['groups'=2,'tm'=4,'height'=2,'chan'=2] {'tm'}, use_global_device_ids=true, to_apply=%region_11.12 | all-reduce | flops 256 | bytes 2048 | tf_op jit(solution)/shard_map/psum | solution.py:67
  126.4 0.1 mul.103
  126.5 0.1 mul.104
  126.6 0.1 sub.91
  126.6 0.1 sub.92
  126.7 0.0 copy-start.10
  126.8 7.7 %fusion.13.refs_0_.refs_1_.refs_2_ = bf16[4,36,160,128]{3,2,1,0:T(8,128)(2,1)} fusion(bf16[1,36,160,128]{3,2,1,0:T(8,128)(2,1)} %collective-permute-done.7, bf16[2,36,160,128]{3,2,1,0:T(8,128)(2,1)S(1)} %shard_map.91.refs_8_, bf16[1,36,160,128]{3,2,1,0:T(8,128)(2,1)} %collective-permute-done.6, f32[160]{0:T(256)S(1)} %copy-done.7, f32[160]{0:T(256)S(1)} %copy-done.8, ...), kind=kLoop, calls=%fused_computation.19 | loop fusion | flops 38338560 | bytes 11799044 | tf_op jit(solution)/shard_map/jit(_where)/select_n | solution.py:283
  134.5 0.1 copy.19.refs_9_
  134.6 1.1 fusion.21
  135.7 1.1 copy.18
  136.7 1.4 reshape.107
  138.1 0.2 dynamic-slice_bitcast_fusion
  138.4 6.0 %collective-permute-done.9.refs_3_.refs_4_.refs_5_ = bf16[4,36,160,128]{3,2,1,0:T(8,128)(2,1)} collective-permute-done((bf16[4,36,160,128]{3,2,1,0:T(8,128)(2,1)}, bf16[4,36,160,128]{3,2,1,0:T(8,128)(2,1)}, u32[]{:S(2)}, u32[]{:S(2)}) %collective-permute-start.9) | collective-permute-done | bytes 5898272 | tf_op jit(solution)/shard_map/ppermute | solution.py:16
  144.4 10.6 %shard_map.92 = bf16[2,36,160,128]{3,2,1,0:T(8,128)(2,1)} custom-call(bf16[4,36,160,128]{3,2,1,0:T(8,128)(2,1)} %fusion.13.refs_0_.refs_1_.refs_2_, bf16[4,36,160,128]{3,2,1,0:T(8,128)(2,1)} %fusion.13.refs_0_.refs_1_.refs_2_, bf16[4,36,160,128]{3,2,1,0:T(8,128)(2,1)} %fusion.13.refs_0_.refs_1_.refs_2_, ...), custom_call_target="tpu_custom_call" | custom-call | flops 2831155200 | bytes 23900160 | tf_op jit(solution)/shard_map/pallas_call | solution.py:186
  (46 shorter events, 0.4 us)
Async XLA Ops:
  0.0 10.8 %copy-start = (bf16[2,36,160,128]{3,2,1,0:T(8,128)(2,1)S(1)}, bf16[2,36,160,128]{3,2,1,0:T(8,128)(2,1)}, u32[]{:S(2)}) copy-start(bf16[2,36,160,128]{3,2,1,0:T(8,128)(2,1)} %res_ref.1) | copy-start | bytes 8847364
  0.0 10.8 %copy-start.5 = (f32[160]{0:T(256)S(1)}, f32[160]{0:T(256)}, u32[]{:S(2)}) copy-start(f32[160]{0:T(256)} %param.11) | copy-start | bytes 1924
  0.0 10.8 %copy-start.6 = (f32[160]{0:T(256)S(1)}, f32[160]{0:T(256)}, u32[]{:S(2)}) copy-start(f32[160]{0:T(256)} %param.10) | copy-start | bytes 1924
  5.8 4.6 %collective-permute-start = (f32[2,2,2,16]{3,2,1,0:T(2,128)S(1)}, f32[2,2,2,16]{3,2,1,0:T(2,128)S(1)}, u32[]{:S(2)}, u32[]{:S(2)}) collective-permute-start(f32[2,2,2,16]{3,2,1,0:T(2,128)S(1)} %constant_dynamic-update-slice_fusion.3), channel_id=1, source_target_pairs={{0,2},{2,0},{1,3},{3,1},{4,6},{6,4},{5,7},{7,5},{8,10},{10,8},{9,1... | collective-permute-start | bytes 1544 | tf_op jit(solution)/shard_map/ppermute | solution.py:65
  10.8 12.4 %copy-start.3 = (bf16[3,80,160]{2,1,0:T(8,128)(2,1)S(1)}, bf16[3,80,160]{2,1,0:T(8,128)(2,1)}, u32[]{:S(2)}) copy-start(bf16[3,80,160]{2,1,0:T(8,128)(2,1)} %param.16) | copy-start | bytes 230404
  10.8 17.5 %copy-start.9 = (f32[160]{0:T(256)S(1)}, f32[160]{0:T(256)}, u32[]{:S(2)}) copy-start(f32[160]{0:T(256)} %param.13) | copy-start | bytes 1924
  10.8 17.7 %copy-start.4 = (bf16[3,3,80,160]{3,2,1,0:T(8,128)(2,1)S(1)}, bf16[3,3,80,160]{3,2,1,0:T(8,128)(2,1)}, u32[]{:S(2)}) copy-start(bf16[3,3,80,160]{3,2,1,0:T(8,128)(2,1)} %param.12) | copy-start | bytes 691204
  13.2 1.6 %copy-start.1 = (bf16[2,36,160,128]{3,2,1,0:T(8,128)(2,1)}, bf16[2,36,160,128]{3,2,1,0:T(8,128)(2,1)S(1)}, u32[]{:S(2)}) copy-start(bf16[2,36,160,128]{3,2,1,0:T(8,128)(2,1)S(1)} %fusion.12) | copy-start | bytes 8847364
  14.8 4.5 %collective-permute-start.1 = (bf16[2,1,160,128]{3,2,1,0:T(8,128)(2,1)S(1)}, bf16[2,1,160,128]{3,2,1,0:T(8,128)(2,1)S(1)}, u32[]{:S(2)}, u32[]{:S(2)}) collective-permute-start(bf16[2,1,160,128]{3,2,1,0:T(8,128)(2,1)S(1)} %slice_select_fusion), channel_id=1, source_target_pairs={{0,2},{2,0},{1,3},{3,1},{4,6},{6,4},{5,7},{7,5},{8,10},{10,8},{9,1... | collective-permute-start | bytes 245768 | tf_op jit(solution)/shard_map/ppermute | solution.py:24
  23.2 39.6 %collective-permute-start.2 = (bf16[2,38,160,128]{3,2,1,0:T(8,128)(2,1)}, bf16[2,38,160,128]{3,2,1,0:T(8,128)(2,1)}, u32[]{:S(2)}, u32[]{:S(2)}) collective-permute-start(bf16[2,38,160,128]{3,2,1,0:T(8,128)(2,1)} %pad_maximum_fusion.xo_ref), channel_id=1, source_target_pairs={{0,1},{1,0},{2,3},{3,2},{4,5},{5,4},{6,7},{7,6},{8,9},{9,8},{10,11... | collective-permute-start | bytes 9338888 | tf_op jit(solution)/shard_map/ppermute | solution.py:16
  23.2 39.4 %collective-permute-start.3 = (bf16[3,80,160]{2,1,0:T(8,128)(2,1)S(1)}, bf16[3,80,160]{2,1,0:T(8,128)(2,1)S(1)}, u32[]{:S(2)}, u32[]{:S(2)}) collective-permute-start(bf16[3,80,160]{2,1,0:T(8,128)(2,1)S(1)} %copy-done.3), channel_id=1, source_target_pairs={{0,12},{4,0},{8,4},{12,8},{1,13},{5,1},{9,5},{13,9},{2,14},{6,2},{... | collective-permute-start | bytes 230408 | tf_op jit(solution)/shard_map/ppermute | solution.py:42
  27.3 35.3 %collective-permute-start.5 = (bf16[3,80,160]{2,1,0:T(8,128)(2,1)S(1)}, bf16[3,80,160]{2,1,0:T(8,128)(2,1)S(1)}, u32[]{:S(2)}, u32[]{:S(2)}) collective-permute-start(bf16[3,80,160]{2,1,0:T(8,128)(2,1)S(1)} %copy-done.3), channel_id=1, source_target_pairs={{0,4},{4,8},{8,12},{12,0},{1,5},{5,9},{9,13},{13,1},{2,6},{6,10},{... | collective-permute-start | bytes 230408 | tf_op jit(solution)/shard_map/ppermute | solution.py:42
  27.3 35.3 %collective-permute-start.4 = (bf16[3,80,160]{2,1,0:T(8,128)(2,1)S(1)}, bf16[3,80,160]{2,1,0:T(8,128)(2,1)S(1)}, u32[]{:S(2)}, u32[]{:S(2)}) collective-permute-start(bf16[3,80,160]{2,1,0:T(8,128)(2,1)S(1)} %copy-done.3), channel_id=1, source_target_pairs={{0,8},{4,12},{8,0},{12,4},{1,9},{5,13},{9,1},{13,5},{2,10},{6,14},... | collective-permute-start | bytes 230408 | tf_op jit(solution)/shard_map/ppermute | solution.py:42
  62.8 1.0 copy-start.2
  80.9 45.9 %copy-start.7 = (f32[160]{0:T(256)S(1)}, f32[160]{0:T(256)}, u32[]{:S(2)}) copy-start(f32[160]{0:T(256)} %param.15) | copy-start | bytes 1924
  80.9 45.9 %copy-start.8 = (f32[160]{0:T(256)S(1)}, f32[160]{0:T(256)}, u32[]{:S(2)}) copy-start(f32[160]{0:T(256)} %param.14) | copy-start | bytes 1924
  83.4 43.3 %collective-permute-start.6 = (bf16[1,36,160,128]{3,2,1,0:T(8,128)(2,1)}, bf16[1,36,160,128]{3,2,1,0:T(8,128)(2,1)}, u32[]{:S(2)}, u32[]{:S(2)}) collective-permute-start(bf16[1,36,160,128]{3,2,1,0:T(8,128)(2,1)} %get-tuple-element.9), channel_id=1, source_target_pairs={{0,4},{4,8},{8,12},{1,5},{5,9},{9,13},{2,6},{6,10},{10,14},{3,7},{... | collective-permute-start | bytes 4423688 | tf_op jit(solution)/shard_map/ppermute | solution.py:271
  88.8 37.9 %collective-permute-start.7 = (bf16[1,36,160,128]{3,2,1,0:T(8,128)(2,1)}, bf16[1,36,160,128]{3,2,1,0:T(8,128)(2,1)}, u32[]{:S(2)}, u32[]{:S(2)}) collective-permute-start(bf16[1,36,160,128]{3,2,1,0:T(8,128)(2,1)} %get-tuple-element.10), channel_id=1, source_target_pairs={{4,0},{8,4},{12,8},{5,1},{9,5},{13,9},{6,2},{10,6},{14,10},{7,3},{... | collective-permute-start | bytes 4423688 | tf_op jit(solution)/shard_map/ppermute | solution.py:272
  91.5 3.7 %collective-permute-start.8 = (f32[8,2,16]{2,1,0:T(2,128)S(1)}, f32[8,2,16]{2,1,0:T(2,128)S(1)}, u32[]{:S(2)}, u32[]{:S(2)}) collective-permute-start(f32[8,2,16]{2,1,0:T(2,128)S(1)} %constant_dynamic-update-slice_fusion.1), channel_id=1, source_target_pairs={{0,2},{2,0},{1,3},{3,1},{4,6},{6,4},{5,7},{7,5},{8,10},{10,8},{9,1... | collective-permute-start | bytes 3080 | tf_op jit(solution)/shard_map/ppermute | solution.py:65
  126.7 7.7 %copy-start.10 = (f32[160]{0:T(256)S(1)}, f32[160]{0:T(256)}, u32[]{:S(2)}) copy-start(f32[160]{0:T(256)} %param.17) | copy-start | bytes 1924
  134.5 9.9 %collective-permute-start.9 = (bf16[4,36,160,128]{3,2,1,0:T(8,128)(2,1)}, bf16[4,36,160,128]{3,2,1,0:T(8,128)(2,1)}, u32[]{:S(2)}, u32[]{:S(2)}) collective-permute-start(bf16[4,36,160,128]{3,2,1,0:T(8,128)(2,1)} %fusion.13.refs_0_.refs_1_.refs_2_), channel_id=1, source_target_pairs={{0,1},{1,0},{2,3},{3,2},{4,5},{5,4},{6,7},{7,6},{8,9},{9,8},{10,11... | collective-permute-start | bytes 17694728 | tf_op jit(solution)/shard_map/ppermute | solution.py:16

commit v21 on v19

--- a/solution.py
+++ b/solution.py
@@ -242,7 +242,8 @@
     tm_index = lax.axis_index("tm")
     tm_count = lax.axis_size("tm")
 
-    spatial_full = lax.all_gather(spatial_weight, "tm", axis=2, tiled=True).reshape(9, C, local_chan)
+    spatial_stack = lax.all_gather(spatial_weight, "tm", axis=0)
+    spatial_full = jnp.moveaxis(spatial_stack, 0, 2).reshape(9, C, local_chan)
     temporal_pieces = gather_tm(temporal_weight)
     temporal_full = jnp.moveaxis(temporal_pieces, 0, 1).reshape(3, C, local_chan)
     spatial_full = spatial_full.reshape(3, 3, C, local_chan)

time: 155 us -> 158 us (1.019)
  local copies, waits for them, and re-layouts: 11.4 us -> 14.2 us
    transpose x1, local copies, waits for them, and re-layouts: 0.93 us -> 2.7 us  [body(): spatial_full = jnp.moveaxis(spatial_stack, 0, 2).reshape(9, C, local_chan)]
  transfers between devices with their start and end apart: 10 -> 10, of which waited for: 4 -> 4; matrix products, arithmetic and copies ran while one was open for 5% -> 6% of each run, Pallas kernels for 0% -> 0%
where the time goes in v21:
time: 158 us
  blocking collectives  63.9 us (40%)
  Pallas kernels  27.7 us (18%)
  other arithmetic  21.1 us (13%)
  starting transfers between devices  18.3 us (12%)
  local copies, waits for them, and re-layouts  14.2 us (9%)
  waiting for transfers between devices  12.2 us (8%)
    all_gather x1, blocking collectives, body(): spatial_stack = lax.all_gather(spatial_weight, 'tm', axis=0)  32.8 us
    psum x1, blocking collectives, group_stats(): table = lax.psum(table, name)  31.1 us
    pallas_call x1, Pallas kernels, spatial_call(): pl.pallas_call(spatial_kernel, out_shape=jax.ShapeDtypeStruct(residual.sh...  17.1 us
    pallas_call x1, Pallas kernels, temporal_call(): pl.pallas_call(temporal_kernel, out_shape=jax.ShapeDtypeStruct(residual.s...  10.6 us
    select_n x1, other arithmetic, body(): jnp.where(inside[:, None, None, None], act_two, jnp.zeros_like(act_two))  7.66 us
    ppermute x2, waiting for transfers between devices, swap_chan(): return lax.ppermute(block, 'chan', [(0, 1), (1, 0)])  6.04 us
    ppermute x1, starting transfers between devices, body(): before = lax.ppermute(hidden[-1:], 'tm', forward)  5.25 us
    ppermute x3, starting transfers between devices, gather_tm(): pieces.append(lax.ppermute(piece, 'tm', pairs))  5.14 us
  transfers between devices with their start and end apart: 10, of which 4 were waited for; matrix products, arithmetic and copies ran while one was open for 6% of the time, Pallas kernels for 0%

profile of v21, /device:TPU:0, one launch (start us, length us, event | category | flops | bytes accessed | tf_op | source)
XLA Modules:
  0.0 157.9 jit_solution(14438007263883707577)
XLA Ops:
  0.0 2.5 %convert_reduce_fusion = f32[2,160]{1,0:T(2,128)S(1)} fusion(bf16[2,36,160,128]{3,2,1,0:T(8,128)(2,1)} %res_ref.1), kind=kLoop, calls=%fused_computation.3 | loop fusion | flops 2948800 | bytes 2950400 | tf_op jit(solution)/shard_map/reduce_sum | solution.py:51
  2.5 0.1 reduce_sum.101
  2.5 0.1 reduce_sum.120
  2.6 0.1 sub.75
  2.7 0.1 sub.76
  2.8 2.7 %fusion.3 = f32[2,160]{1,0:T(2,128)S(1)} fusion(bf16[2,36,160,128]{3,2,1,0:T(8,128)(2,1)} %res_ref.1, f32[2,160]{1,0:T(2,128)S(1)} %sub.76), kind=kLoop, calls=%fused_computation.9 | loop fusion | flops 5897920 | bytes 2951680 | tf_op jit(solution)/shard_map/reduce_sum | solution.py:53
  5.6 0.1 reduce_sum.122
  5.7 0.1 reduce_sum.123
  5.8 3.0 %collective-permute-start = (f32[2,2,2,16]{3,2,1,0:T(2,128)S(1)}, f32[2,2,2,16]{3,2,1,0:T(2,128)S(1)}, u32[]{:S(2)}, u32[]{:S(2)}) collective-permute-start(f32[2,2,2,16]{3,2,1,0:T(2,128)S(1)} %constant_dynamic-update-slice_fusion.3), channel_id=1, source_target_pairs={{0,2},{2,0},{1,3},{3,1},{4,6},{6,4},{5,7},{7,5},{8,10},{10,8},{9,1... | collective-permute-start | bytes 1544 | tf_op jit(solution)/shard_map/ppermute | solution.py:65
  8.8 1.6 %collective-permute-done = f32[2,2,2,16]{3,2,1,0:T(2,128)S(1)} collective-permute-done((f32[2,2,2,16]{3,2,1,0:T(2,128)S(1)}, f32[2,2,2,16]{3,2,1,0:T(2,128)S(1)}, u32[]{:S(2)}, u32[]{:S(2)}) %collective-permute-start) | collective-permute-done | bytes 544 | tf_op jit(solution)/shard_map/ppermute | solution.py:65
  10.4 0.1 mul.90
  10.5 0.1 mul.91
  10.6 0.1 sub.79
  10.7 0.1 sub.80
  10.8 0.0 copy-start.3
  10.8 0.0 copy-start.9
  10.8 0.0 copy-start.4
  10.8 2.3 %fusion.12 = bf16[2,36,160,128]{3,2,1,0:T(8,128)(2,1)S(1)} fusion(bf16[2,36,160,128]{3,2,1,0:T(8,128)(2,1)S(1)} %copy-done, f32[160]{0:T(256)S(1)} %copy-done.5, f32[160]{0:T(256)S(1)} %copy-done.6, f32[2,160]{1,0:T(2,128)S(1)} %mul.91, f32[2,160]{1,0:T(2,128)S(1)} %sub.80), kind=kLoop, calls=%fused_computation.18 | loop fusion | flops 14745600 | bytes 5902080 | tf_op jit(solution)/shard_map/convert_element_type | solution.py:84
  13.2 0.0 copy-start.1
  13.2 1.6 %copy-done.1 = bf16[2,36,160,128]{3,2,1,0:T(8,128)(2,1)} copy-done((bf16[2,36,160,128]{3,2,1,0:T(8,128)(2,1)}, bf16[2,36,160,128]{3,2,1,0:T(8,128)(2,1)S(1)}, u32[]{:S(2)}) %copy-start.1) | copy-done | bytes 2949144
  14.8 2.1 %collective-permute-start.1 = (bf16[2,1,160,128]{3,2,1,0:T(8,128)(2,1)S(1)}, bf16[2,1,160,128]{3,2,1,0:T(8,128)(2,1)S(1)}, u32[]{:S(2)}, u32[]{:S(2)}) collective-permute-start(bf16[2,1,160,128]{3,2,1,0:T(8,128)(2,1)S(1)} %slice_select_fusion), channel_id=1, source_target_pairs={{0,2},{2,0},{1,3},{3,1},{4,6},{6,4},{5,7},{7,5},{8,10},{10,8},{9,1... | collective-permute-start | bytes 245768 | tf_op jit(solution)/shard_map/ppermute | solution.py:24
  16.9 2.4 %collective-permute-done.1 = bf16[2,1,160,128]{3,2,1,0:T(8,128)(2,1)S(1)} collective-permute-done((bf16[2,1,160,128]{3,2,1,0:T(8,128)(2,1)S(1)}, bf16[2,1,160,128]{3,2,1,0:T(8,128)(2,1)S(1)}, u32[]{:S(2)}, u32[]{:S(2)}) %collective-permute-start.1) | collective-permute-done | bytes 81952 | tf_op jit(solution)/shard_map/ppermute | solution.py:24
  19.3 3.9 %pad_maximum_fusion.xo_ref = bf16[2,38,160,128]{3,2,1,0:T(8,128)(2,1)} fusion(bf16[2,1,160,128]{3,2,1,0:T(8,128)(2,1)S(1)} %get-tuple-element.16, bf16[2,36,160,128]{3,2,1,0:T(8,128)(2,1)} %copy-done.1, bf16[2,1,160,128]{3,2,1,0:T(8,128)(2,1)S(1)} %get-tuple-element.15), kind=kLoop, calls=%fused_computation.20 | loop fusion | flops 3112960 | bytes 6225920 | tf_op jit(solution)/shard_map/concatenate | solution.py:28
  23.2 4.1 %collective-permute-start.3 = (bf16[3,80,160]{2,1,0:T(8,128)(2,1)S(1)}, bf16[3,80,160]{2,1,0:T(8,128)(2,1)S(1)}, u32[]{:S(2)}, u32[]{:S(2)}) collective-permute-start(bf16[3,80,160]{2,1,0:T(8,128)(2,1)S(1)} %copy-done.3), channel_id=1, source_target_pairs={{0,12},{4,0},{8,4},{12,8},{1,13},{5,1},{9,5},{13,9},{2,14},{6,2},{... | collective-permute-start | bytes 230408 | tf_op jit(solution)/shard_map/ppermute | solution.py:42
  27.3 0.0 collective-permute-start.5
  27.3 1.0 collective-permute-start.4
  28.4 0.1 copy.21.b_ref
  28.5 32.8 %all-gather = bf16[12,3,80,160]{3,2,1,0:T(8,128)(2,1)} all-gather(bf16[3,3,80,160]{3,2,1,0:T(8,128)(2,1)S(1)} %copy-done.4), channel_id=2, replica_groups=mesh['groups'=2,'tm'=4,'height'=2,'chan'=2] {'tm'}, dimensions={0}, use_global_device_ids=true | all-gather | bytes 1152000 | tf_op jit(solution)/shard_map/all_gather | solution.py:245
  61.2 2.7 %copy.20 = bf16[3,3,4,80,160]{3,2,4,1,0:T(4,128)(2,1)S(1)} copy(bf16[3,3,4,80,160]{4,3,1,0,2:T(8,128)(2,1)} %bitcast.56) | data formatting | bytes 1843200 | tf_op jit(solution)/shard_map/transpose | solution.py:246
  63.9 1.0 reshape_reshape.3
  65.0 0.7 constant_dynamic-slice_fusion.2
  65.7 0.0 collective-permute-done.3
  65.7 0.0 collective-permute-done.4
  65.9 0.9 copy-done.2
  66.8 17.1 %shard_map.91.refs_8_ = bf16[2,36,160,128]{3,2,1,0:T(8,128)(2,1)S(1)} custom-call(bf16[2,38,160,128]{3,2,1,0:T(8,128)(2,1)} %pad_maximum_fusion.xo_ref, bf16[2,38,160,128]{3,2,1,0:T(8,128)(2,1)} %collective-permute-done.2.xt_ref, bf16[3,480,160]{2,1,0:T(8,128)(2,1)S(1)} %get-tuple-element.12.wo_ref, bf16[3,480,160]{2,1,0:T(8,128)(2,1)S(1)} %get-tuple-element.11.wt_ref, ...), custom_call_target="tpu_custom_call" | custom-call | flops 8493465600 | bytes 13045760 | tf_op jit(solution)/shard_map/pallas_call | solution.py:132
  84.0 0.0 copy-start.7
  84.0 0.0 copy-start.8
  84.0 0.5 convert_reduce_fusion.1
  84.5 1.8 %fusion.20 = (bf16[1,36,160,128]{3,2,1,0:T(8,128)(2,1)}, bf16[1,36,160,128]{3,2,1,0:T(8,128)(2,1)}) fusion(bf16[2,36,160,128]{3,2,1,0:T(8,128)(2,1)S(1)} %shard_map.91.refs_8_), kind=kLoop, calls=%fused_computation.64 | loop fusion | bytes 5898240 | tf_op jit(solution)/shard_map/slice | solution.py:272
  86.3 0.1 reduce_sum.128
  86.4 0.1 reduce_sum.129
  86.5 5.3 %collective-permute-start.6 = (bf16[1,36,160,128]{3,2,1,0:T(8,128)(2,1)}, bf16[1,36,160,128]{3,2,1,0:T(8,128)(2,1)}, u32[]{:S(2)}, u32[]{:S(2)}) collective-permute-start(bf16[1,36,160,128]{3,2,1,0:T(8,128)(2,1)} %get-tuple-element.9), channel_id=1, source_target_pairs={{0,4},{4,8},{8,12},{1,5},{5,9},{9,13},{2,6},{6,10},{10,14},{3,7},{... | collective-permute-start | bytes 4423688 | tf_op jit(solution)/shard_map/ppermute | solution.py:272
  91.8 1.3 collective-permute-start.7
  93.1 0.1 sub.87
  93.1 0.1 sub.88
  93.2 0.9 fusion.1
  94.2 0.1 reduce_sum.131
  94.2 0.1 reduce_sum.132
  94.4 1.6 collective-permute-start.8
  96.0 2.1 %collective-permute-done.8 = f32[8,2,16]{2,1,0:T(2,128)S(1)} collective-permute-done((f32[8,2,16]{2,1,0:T(2,128)S(1)}, f32[8,2,16]{2,1,0:T(2,128)S(1)}, u32[]{:S(2)}, u32[]{:S(2)}) %collective-permute-start.8) | collective-permute-done | bytes 1056 | tf_op jit(solution)/shard_map/ppermute | solution.py:65
  98.1 31.1 %psum.7 = f32[8,2,16]{2,1,0:T(2,128)S(1)} all-reduce(f32[8,2,16]{2,1,0:T(2,128)S(1)} %constant_dynamic-update-slice_fusion), channel_id=1, replica_groups=mesh['groups'=2,'tm'=4,'height'=2,'chan'=2] {'tm'}, use_global_device_ids=true, to_apply=%region_11.12 | all-reduce | flops 256 | bytes 2048 | tf_op jit(solution)/shard_map/psum | solution.py:67
  129.3 0.1 mul.103
  129.4 0.1 mul.104
  129.5 0.1 sub.91
  129.6 0.1 sub.92
  129.7 0.0 copy-start.10
  129.7 7.7 %fusion.13.refs_0_.refs_1_.refs_2_ = bf16[4,36,160,128]{3,2,1,0:T(8,128)(2,1)} fusion(bf16[1,36,160,128]{3,2,1,0:T(8,128)(2,1)} %collective-permute-done.7, bf16[2,36,160,128]{3,2,1,0:T(8,128)(2,1)S(1)} %shard_map.91.refs_8_, bf16[1,36,160,128]{3,2,1,0:T(8,128)(2,1)} %collective-permute-done.6, f32[160]{0:T(256)S(1)} %copy-done.7, f32[160]{0:T(256)S(1)} %copy-done.8, ...), kind=kLoop, calls=%fused_computation.19 | loop fusion | flops 38338560 | bytes 11799044 | tf_op jit(solution)/shard_map/jit(_where)/select_n | solution.py:284
  137.4 0.1 copy.23.refs_9_
  137.5 1.1 fusion.21
  138.6 1.1 copy.22
  139.7 1.4 reshape.107
  141.1 0.2 dynamic-slice_bitcast_fusion
  141.3 6.0 %collective-permute-done.9.refs_3_.refs_4_.refs_5_ = bf16[4,36,160,128]{3,2,1,0:T(8,128)(2,1)} collective-permute-done((bf16[4,36,160,128]{3,2,1,0:T(8,128)(2,1)}, bf16[4,36,160,128]{3,2,1,0:T(8,128)(2,1)}, u32[]{:S(2)}, u32[]{:S(2)}) %collective-permute-start.9) | collective-permute-done | bytes 5898272 | tf_op jit(solution)/shard_map/ppermute | solution.py:16
  147.3 10.6 %shard_map.92 = bf16[2,36,160,128]{3,2,1,0:T(8,128)(2,1)} custom-call(bf16[4,36,160,128]{3,2,1,0:T(8,128)(2,1)} %fusion.13.refs_0_.refs_1_.refs_2_, bf16[4,36,160,128]{3,2,1,0:T(8,128)(2,1)} %fusion.13.refs_0_.refs_1_.refs_2_, bf16[4,36,160,128]{3,2,1,0:T(8,128)(2,1)} %fusion.13.refs_0_.refs_1_.refs_2_, ...), custom_call_target="tpu_custom_call" | custom-call | flops 2831155200 | bytes 23900160 | tf_op jit(solution)/shard_map/pallas_call | solution.py:186
  (47 shorter events, 0.4 us)
Async XLA Ops:
  0.0 10.8 %copy-start = (bf16[2,36,160,128]{3,2,1,0:T(8,128)(2,1)S(1)}, bf16[2,36,160,128]{3,2,1,0:T(8,128)(2,1)}, u32[]{:S(2)}) copy-start(bf16[2,36,160,128]{3,2,1,0:T(8,128)(2,1)} %res_ref.1) | copy-start | bytes 8847364
  0.0 10.8 %copy-start.5 = (f32[160]{0:T(256)S(1)}, f32[160]{0:T(256)}, u32[]{:S(2)}) copy-start(f32[160]{0:T(256)} %param.11) | copy-start | bytes 1924
  0.0 10.8 %copy-start.6 = (f32[160]{0:T(256)S(1)}, f32[160]{0:T(256)}, u32[]{:S(2)}) copy-start(f32[160]{0:T(256)} %param.10) | copy-start | bytes 1924
  5.8 4.6 %collective-permute-start = (f32[2,2,2,16]{3,2,1,0:T(2,128)S(1)}, f32[2,2,2,16]{3,2,1,0:T(2,128)S(1)}, u32[]{:S(2)}, u32[]{:S(2)}) collective-permute-start(f32[2,2,2,16]{3,2,1,0:T(2,128)S(1)} %constant_dynamic-update-slice_fusion.3), channel_id=1, source_target_pairs={{0,2},{2,0},{1,3},{3,1},{4,6},{6,4},{5,7},{7,5},{8,10},{10,8},{9,1... | collective-permute-start | bytes 1544 | tf_op jit(solution)/shard_map/ppermute | solution.py:65
  10.8 12.4 %copy-start.3 = (bf16[3,80,160]{2,1,0:T(8,128)(2,1)S(1)}, bf16[3,80,160]{2,1,0:T(8,128)(2,1)}, u32[]{:S(2)}) copy-start(bf16[3,80,160]{2,1,0:T(8,128)(2,1)} %param.16) | copy-start | bytes 230404
  10.8 17.5 %copy-start.9 = (f32[160]{0:T(256)S(1)}, f32[160]{0:T(256)}, u32[]{:S(2)}) copy-start(f32[160]{0:T(256)} %param.13) | copy-start | bytes 1924
  10.8 17.7 %copy-start.4 = (bf16[3,3,80,160]{3,2,1,0:T(8,128)(2,1)S(1)}, bf16[3,3,80,160]{3,2,1,0:T(8,128)(2,1)}, u32[]{:S(2)}) copy-start(bf16[3,3,80,160]{3,2,1,0:T(8,128)(2,1)} %param.12) | copy-start | bytes 691204
  13.2 1.6 %copy-start.1 = (bf16[2,36,160,128]{3,2,1,0:T(8,128)(2,1)}, bf16[2,36,160,128]{3,2,1,0:T(8,128)(2,1)S(1)}, u32[]{:S(2)}) copy-start(bf16[2,36,160,128]{3,2,1,0:T(8,128)(2,1)S(1)} %fusion.12) | copy-start | bytes 8847364
  14.8 4.5 %collective-permute-start.1 = (bf16[2,1,160,128]{3,2,1,0:T(8,128)(2,1)S(1)}, bf16[2,1,160,128]{3,2,1,0:T(8,128)(2,1)S(1)}, u32[]{:S(2)}, u32[]{:S(2)}) collective-permute-start(bf16[2,1,160,128]{3,2,1,0:T(8,128)(2,1)S(1)} %slice_select_fusion), channel_id=1, source_target_pairs={{0,2},{2,0},{1,3},{3,1},{4,6},{6,4},{5,7},{7,5},{8,10},{10,8},{9,1... | collective-permute-start | bytes 245768 | tf_op jit(solution)/shard_map/ppermute | solution.py:24
  23.2 42.7 %collective-permute-start.2 = (bf16[2,38,160,128]{3,2,1,0:T(8,128)(2,1)}, bf16[2,38,160,128]{3,2,1,0:T(8,128)(2,1)}, u32[]{:S(2)}, u32[]{:S(2)}) collective-permute-start(bf16[2,38,160,128]{3,2,1,0:T(8,128)(2,1)} %pad_maximum_fusion.xo_ref), channel_id=1, source_target_pairs={{0,1},{1,0},{2,3},{3,2},{4,5},{5,4},{6,7},{7,6},{8,9},{9,8},{10,11... | collective-permute-start | bytes 9338888 | tf_op jit(solution)/shard_map/ppermute | solution.py:16
  23.2 42.5 %collective-permute-start.3 = (bf16[3,80,160]{2,1,0:T(8,128)(2,1)S(1)}, bf16[3,80,160]{2,1,0:T(8,128)(2,1)S(1)}, u32[]{:S(2)}, u32[]{:S(2)}) collective-permute-start(bf16[3,80,160]{2,1,0:T(8,128)(2,1)S(1)} %copy-done.3), channel_id=1, source_target_pairs={{0,12},{4,0},{8,4},{12,8},{1,13},{5,1},{9,5},{13,9},{2,14},{6,2},{... | collective-permute-start | bytes 230408 | tf_op jit(solution)/shard_map/ppermute | solution.py:42
  27.3 38.4 %collective-permute-start.5 = (bf16[3,80,160]{2,1,0:T(8,128)(2,1)S(1)}, bf16[3,80,160]{2,1,0:T(8,128)(2,1)S(1)}, u32[]{:S(2)}, u32[]{:S(2)}) collective-permute-start(bf16[3,80,160]{2,1,0:T(8,128)(2,1)S(1)} %copy-done.3), channel_id=1, source_target_pairs={{0,4},{4,8},{8,12},{12,0},{1,5},{5,9},{9,13},{13,1},{2,6},{6,10},{... | collective-permute-start | bytes 230408 | tf_op jit(solution)/shard_map/ppermute | solution.py:42
  27.3 38.4 %collective-permute-start.4 = (bf16[3,80,160]{2,1,0:T(8,128)(2,1)S(1)}, bf16[3,80,160]{2,1,0:T(8,128)(2,1)S(1)}, u32[]{:S(2)}, u32[]{:S(2)}) collective-permute-start(bf16[3,80,160]{2,1,0:T(8,128)(2,1)S(1)} %copy-done.3), channel_id=1, source_target_pairs={{0,8},{4,12},{8,0},{12,4},{1,9},{5,13},{9,1},{13,5},{2,10},{6,14},... | collective-permute-start | bytes 230408 | tf_op jit(solution)/shard_map/ppermute | solution.py:42
  65.9 1.0 copy-start.2
  84.0 45.7 %copy-start.7 = (f32[160]{0:T(256)S(1)}, f32[160]{0:T(256)}, u32[]{:S(2)}) copy-start(f32[160]{0:T(256)} %param.15) | copy-start | bytes 1924
  84.0 45.7 %copy-start.8 = (f32[160]{0:T(256)S(1)}, f32[160]{0:T(256)}, u32[]{:S(2)}) copy-start(f32[160]{0:T(256)} %param.14) | copy-start | bytes 1924
  86.5 43.2 %collective-permute-start.6 = (bf16[1,36,160,128]{3,2,1,0:T(8,128)(2,1)}, bf16[1,36,160,128]{3,2,1,0:T(8,128)(2,1)}, u32[]{:S(2)}, u32[]{:S(2)}) collective-permute-start(bf16[1,36,160,128]{3,2,1,0:T(8,128)(2,1)} %get-tuple-element.9), channel_id=1, source_target_pairs={{0,4},{4,8},{8,12},{1,5},{5,9},{9,13},{2,6},{6,10},{10,14},{3,7},{... | collective-permute-start | bytes 4423688 | tf_op jit(solution)/shard_map/ppermute | solution.py:272
  91.8 37.9 %collective-permute-start.7 = (bf16[1,36,160,128]{3,2,1,0:T(8,128)(2,1)}, bf16[1,36,160,128]{3,2,1,0:T(8,128)(2,1)}, u32[]{:S(2)}, u32[]{:S(2)}) collective-permute-start(bf16[1,36,160,128]{3,2,1,0:T(8,128)(2,1)} %get-tuple-element.10), channel_id=1, source_target_pairs={{4,0},{8,4},{12,8},{5,1},{9,5},{13,9},{6,2},{10,6},{14,10},{7,3},{... | collective-permute-start | bytes 4423688 | tf_op jit(solution)/shard_map/ppermute | solution.py:273
  94.4 3.7 %collective-permute-start.8 = (f32[8,2,16]{2,1,0:T(2,128)S(1)}, f32[8,2,16]{2,1,0:T(2,128)S(1)}, u32[]{:S(2)}, u32[]{:S(2)}) collective-permute-start(f32[8,2,16]{2,1,0:T(2,128)S(1)} %constant_dynamic-update-slice_fusion.1), channel_id=1, source_target_pairs={{0,2},{2,0},{1,3},{3,1},{4,6},{6,4},{5,7},{7,5},{8,10},{10,8},{9,1... | collective-permute-start | bytes 3080 | tf_op jit(solution)/shard_map/ppermute | solution.py:65
  129.7 7.7 %copy-start.10 = (f32[160]{0:T(256)S(1)}, f32[160]{0:T(256)}, u32[]{:S(2)}) copy-start(f32[160]{0:T(256)} %param.17) | copy-start | bytes 1924
  137.4 9.9 %collective-permute-start.9 = (bf16[4,36,160,128]{3,2,1,0:T(8,128)(2,1)}, bf16[4,36,160,128]{3,2,1,0:T(8,128)(2,1)}, u32[]{:S(2)}, u32[]{:S(2)}) collective-permute-start(bf16[4,36,160,128]{3,2,1,0:T(8,128)(2,1)} %fusion.13.refs_0_.refs_1_.refs_2_), channel_id=1, source_target_pairs={{0,1},{1,0},{2,3},{3,2},{4,5},{5,4},{6,7},{7,6},{8,9},{9,8},{10,11... | collective-permute-start | bytes 17694728 | tf_op jit(solution)/shard_map/ppermute | solution.py:16

commit v22 on v19

--- a/solution.py
+++ b/solution.py
@@ -25,12 +25,12 @@
         empty = jnp.zeros_like(received)
         low = jnp.where(index == 1, received, empty)
         high = jnp.where(index == 0, received, empty)
-        return jnp.concatenate([low, block, high], axis=1)
+        return jnp.concatenate([low, high], axis=1)
     forward = [(i, i + 1) for i in range(count - 1)]
     backward = [(target, source) for source, target in forward]
     low = lax.ppermute(block[:, -1:], "height", forward)
     high = lax.ppermute(block[:, :1], "height", backward)
-    return jnp.concatenate([low, block, high], axis=1)
+    return jnp.concatenate([low, high], axis=1)
 
 
 def gather_tm(piece):
@@ -98,18 +98,35 @@
     return jnp.concatenate([ref[0, first + k] for k in range(STEP)], axis=1)
 
 
-def spatial_kernel(xo_ref, xt_ref, wo_ref, wt_ref, res_ref, b_ref, early_ref, o_ref):
+def halo_rows(ref, edge_ref, first):
+    rows = ref.shape[1]
+    picked = []
+    for q in range(first, first + STEP):
+        if q == 0:
+            picked.append(edge_ref[0, 0])
+        elif q == rows + 1:
+            picked.append(edge_ref[0, 1])
+        else:
+            picked.append(ref[0, q - 1])
+    return jnp.concatenate(picked, axis=1)
+
+
+def spatial_kernel(xo_ref, eo_ref, xt_ref, et_ref, wo_ref, wt_ref, res_ref, b_ref, early_ref, o_ref):
     rows, local_chan, width = o_ref.shape[1], o_ref.shape[2], o_ref.shape[3]
     lane = lax.broadcasted_iota(jnp.int32, (local_chan, width), 1)
     bias = b_ref[...]
 
-    def two_rows(i, carry):
+    for i in range(rows // STEP):
         r = STEP * i
-        y = jnp.dot(wo_ref[0], pair(xo_ref, r), preferred_element_type=jnp.float32)
-        y = y + jnp.dot(wt_ref[0], pair(xt_ref, r), preferred_element_type=jnp.float32)
+        y = jnp.dot(wo_ref[0], halo_rows(xo_ref, eo_ref, r), preferred_element_type=jnp.float32)
+        y = y + jnp.dot(wt_ref[0], halo_rows(xt_ref, et_ref, r), preferred_element_type=jnp.float32)
         for tap in (1, 2):
-            y = y + jnp.dot(wo_ref[tap], pair(xo_ref, r + tap), preferred_element_type=jnp.float32)
-            y = y + jnp.dot(wt_ref[tap], pair(xt_ref, r + tap), preferred_element_type=jnp.float32)
+            y = y + jnp.dot(
+                wo_ref[tap], halo_rows(xo_ref, eo_ref, r + tap), preferred_element_type=jnp.float32
+            )
+            y = y + jnp.dot(
+                wt_ref[tap], halo_rows(xt_ref, et_ref, r + tap), preferred_element_type=jnp.float32
+            )
         for half in range(STEP):
             part = y[:, half * width : (half + 1) * width]
             left = pltpu.roll(part[:local_chan], 1, 1)
@@ -120,14 +137,12 @@
             o_ref[0, r + half] = (res_ref[0, r + half].astype(jnp.float32) + total + bias).astype(
                 o_ref.dtype
             )
-        return carry
-
-    lax.fori_loop(0, rows // STEP, two_rows, 0, unroll=True)
-
-
-def spatial_call(own, other, weight_own, weight_other, residual, bias, early):
+
+
+def spatial_call(own, own_edges, other, other_edges, weight_own, weight_other, residual, bias, early):
     frames, rows, local_chan, width = residual.shape
-    act_spec = pl.BlockSpec((1, rows + 2, local_chan, width), lambda f: (f, 0, 0, 0))
+    act_spec = pl.BlockSpec((1, rows, local_chan, width), lambda f: (f, 0, 0, 0))
+    edge_spec = pl.BlockSpec((1, 2, local_chan, width), lambda f: (f, 0, 0, 0))
     weight_spec = pl.BlockSpec((3, 3 * local_chan, local_chan), lambda f: (0, 0, 0))
     return pl.pallas_call(
         spatial_kernel,
@@ -135,7 +150,9 @@
         grid=(frames,),
         in_specs=[
             act_spec,
+            edge_spec,
             act_spec,
+            edge_spec,
             weight_spec,
             weight_spec,
             pl.BlockSpec((1, rows, local_chan, width), lambda f: (f, 0, 0, 0)),
@@ -149,7 +166,7 @@
             transcendentals=0,
             bytes_accessed=4 * own.size + 4 * weight_own.size + 4 * residual.size,
         ),
-    )(own, other, weight_own, weight_other, residual, bias, early)
+    )(own, own_edges, other, other_edges, weight_own, weight_other, residual, bias, early)
 
 
 def temporal_kernel(*refs):
@@ -252,13 +269,15 @@
     average, variance = group_stats(grouped, (1, 3, 4), ("height",))
     act_one = group_act(values, average, variance, norm1_gain, norm1_bias)
 
-    with_rows = row_halo(act_one)
+    edges = row_halo(act_one)
     own_start = chan_index * local_chan
     other_start = (1 - chan_index) * local_chan
     spatial_rows = jnp.transpose(spatial_full, (0, 1, 3, 2)).reshape(3, 3 * local_chan, C)
     hidden = spatial_call(
-        with_rows,
-        swap_chan(with_rows),
+        act_one,
+        edges,
+        swap_chan(act_one),
+        swap_chan(edges),
         lax.dynamic_slice_in_dim(spatial_rows, own_start, local_chan, axis=2),
         lax.dynamic_slice_in_dim(spatial_rows, other_start, local_chan, axis=2),
         video,

time: 155 us -> 149 us (0.961)
  local copies, waits for them, and re-layouts: 11.4 us -> 8.9 us
  waiting for transfers between devices: 12.2 us -> 14.3 us
  other arithmetic: 21.2 us -> 19.1 us
  starting transfers between devices: 18.7 us -> 16.6 us
    concatenate x1, other arithmetic: 3.9 us -> 0.02 us  [row_halo(): return jnp.concatenate([low, high], axis=1)]
    all_gather x1, blocking collectives: 32.5 us -> 29.1 us  [body(): lax.all_gather(spatial_weight, 'tm', axis=2, tiled=True)]
    unnamed x29 -> x27, local copies, waits for them, and re-layouts: 2.63 us -> 0.12 us
    psum x1, blocking collectives: 30.7 us -> 32.5 us  [group_stats(): table = lax.psum(table, name)]
    ppermute x2 -> x3, waiting for transfers between devices: 6.04 us -> 7.34 us  [swap_chan(): return lax.ppermute(block, 'chan', [(0, 1), (1, 0)])]
  transfers between devices with their start and end apart: 10 -> 11, of which waited for: 4 -> 5; matrix products, arithmetic and copies ran while one was open for 5% -> 12% of each run, Pallas kernels for 0% -> 0%
where the time goes in v22:
time: 149 us
  blocking collectives  61.7 us (41%)
  Pallas kernels  27.6 us (19%)
  other arithmetic  19.1 us (13%)
  starting transfers between devices  16.6 us (11%)
  waiting for transfers between devices  14.3 us (10%)
  local copies, waits for them, and re-layouts  8.9 us (6%)
    psum x1, blocking collectives, group_stats(): table = lax.psum(table, name)  32.5 us
    all_gather x1, blocking collectives, body(): lax.all_gather(spatial_weight, 'tm', axis=2, tiled=True)  29.1 us
    pallas_call x1, Pallas kernels, spatial_call(): pl.pallas_call(spatial_kernel, out_shape=jax.ShapeDtypeStruct(residual.sh...  17.1 us
    pallas_call x1, Pallas kernels, temporal_call(): pl.pallas_call(temporal_kernel, out_shape=jax.ShapeDtypeStruct(residual.s...  10.6 us
    select_n x1, other arithmetic, body(): jnp.where(inside[:, None, None, None], act_two, jnp.zeros_like(act_two))  7.66 us
    ppermute x3, waiting for transfers between devices, swap_chan(): return lax.ppermute(block, 'chan', [(0, 1), (1, 0)])  7.34 us
    ppermute x3, starting transfers between devices, gather_tm(): pieces.append(lax.ppermute(piece, 'tm', pairs))  6.13 us
    ppermute x1, starting transfers between devices, body(): before = lax.ppermute(hidden[-1:], 'tm', forward)  4.23 us
  transfers between devices with their start and end apart: 11, of which 5 were waited for; matrix products, arithmetic and copies ran while one was open for 12% of the time, Pallas kernels for 0%

profile of v22, /device:TPU:0, one launch (start us, length us, event | category | flops | bytes accessed | tf_op | source)
XLA Modules:
  0.0 148.6 jit_solution(17386019536311315733)
XLA Ops:
  0.0 5.1 %collective-permute-start.4 = (bf16[3,80,160]{2,1,0:T(8,128)(2,1)}, bf16[3,80,160]{2,1,0:T(8,128)(2,1)S(1)}, u32[]{:S(2)}, u32[]{:S(2)}) collective-permute-start(bf16[3,80,160]{2,1,0:T(8,128)(2,1)} %param.16), channel_id=1, source_target_pairs={{0,12},{4,0},{8,4},{12,8},{1,13},{5,1},{9,5},{13,9},{2,14},{6,2},{... | collective-permute-start | bytes 230408 | tf_op jit(solution)/shard_map/ppermute | solution.py:42
  5.1 0.0 collective-permute-start.6
  5.1 1.0 collective-permute-start.5
  6.1 2.3 %convert_reduce_fusion = f32[2,160]{1,0:T(2,128)S(1)} fusion(bf16[2,36,160,128]{3,2,1,0:T(8,128)(2,1)} %res_ref.1), kind=kLoop, calls=%fused_computation.3 | loop fusion | flops 2948800 | bytes 2950400 | tf_op jit(solution)/shard_map/reduce_sum | solution.py:51
  8.4 0.1 reduce_sum.101
  8.5 0.1 reduce_sum.120
  8.6 0.1 sub.75
  8.7 0.1 sub.76
  8.8 2.7 %fusion.3 = f32[2,160]{1,0:T(2,128)S(1)} fusion(bf16[2,36,160,128]{3,2,1,0:T(8,128)(2,1)} %res_ref.1, f32[2,160]{1,0:T(2,128)S(1)} %sub.76), kind=kLoop, calls=%fused_computation.9 | loop fusion | flops 5897920 | bytes 2951680 | tf_op jit(solution)/shard_map/reduce_sum | solution.py:53
  11.5 0.1 reduce_sum.122
  11.6 0.1 reduce_sum.123
  11.7 1.6 %collective-permute-start = (f32[2,2,2,16]{3,2,1,0:T(2,128)S(1)}, f32[2,2,2,16]{3,2,1,0:T(2,128)S(1)}, u32[]{:S(2)}, u32[]{:S(2)}) collective-permute-start(f32[2,2,2,16]{3,2,1,0:T(2,128)S(1)} %constant_dynamic-update-slice_fusion.3), channel_id=1, source_target_pairs={{0,2},{2,0},{1,3},{3,1},{4,6},{6,4},{5,7},{7,5},{8,10},{10,8},{9,1... | collective-permute-start | bytes 1544 | tf_op jit(solution)/shard_map/ppermute | solution.py:65
  13.3 0.1 copy.17.b_ref
  13.4 2.0 %collective-permute-done = f32[2,2,2,16]{3,2,1,0:T(2,128)S(1)} collective-permute-done((f32[2,2,2,16]{3,2,1,0:T(2,128)S(1)}, f32[2,2,2,16]{3,2,1,0:T(2,128)S(1)}, u32[]{:S(2)}, u32[]{:S(2)}) %collective-permute-start) | collective-permute-done | bytes 544 | tf_op jit(solution)/shard_map/ppermute | solution.py:65
  15.5 0.1 mul.90
  15.6 0.1 mul.91
  15.7 0.1 sub.79
  15.7 0.1 sub.80
  15.8 0.0 copy-start.3
  15.9 0.0 copy-start.2
  15.9 3.4 %fusion.12.xo_ref = bf16[2,36,160,128]{3,2,1,0:T(8,128)(2,1)} fusion(bf16[2,36,160,128]{3,2,1,0:T(8,128)(2,1)S(1)} %copy-done, f32[160]{0:T(256)S(1)} %copy-done.4, f32[160]{0:T(256)S(1)} %copy-done.5, f32[2,160]{1,0:T(2,128)S(1)} %mul.91, f32[2,160]{1,0:T(2,128)S(1)} %sub.80), kind=kLoop, calls=%fused_computation.18 | loop fusion | flops 14745600 | bytes 5902080 | tf_op jit(solution)/shard_map/convert_element_type | solution.py:84
  19.3 0.0 collective-permute-start.2
  19.3 29.1 %all_gather.3 = bf16[3,3,320,160]{3,2,1,0:T(8,128)(2,1)S(1)} all-gather(bf16[3,3,80,160]{3,2,1,0:T(8,128)(2,1)S(1)} %copy-done.3), channel_id=1, replica_groups=mesh['groups'=2,'tm'=4,'height'=2,'chan'=2] {'tm'}, dimensions={2}, use_global_device_ids=true | all-gather | bytes 1152000 | tf_op jit(solution)/shard_map/all_gather | solution.py:262
  48.4 0.9 copy.16
  49.3 0.7 constant_dynamic-slice_fusion.2
  50.0 0.9 slice_select_fusion
  51.0 1.6 %collective-permute-start.1 = (bf16[2,1,160,128]{3,2,1,0:T(8,128)(2,1)S(1)}, bf16[2,1,160,128]{3,2,1,0:T(8,128)(2,1)S(1)}, u32[]{:S(2)}, u32[]{:S(2)}) collective-permute-start(bf16[2,1,160,128]{3,2,1,0:T(8,128)(2,1)S(1)} %slice_select_fusion), channel_id=1, source_target_pairs={{0,2},{2,0},{1,3},{3,1},{4,6},{6,4},{5,7},{7,5},{8,10},{10,8},{9,1... | collective-permute-start | bytes 245768 | tf_op jit(solution)/shard_map/ppermute | solution.py:24
  52.6 0.0 collective-permute-done.4
  52.6 0.0 collective-permute-done.5
  52.6 0.0 collective-permute-done.6
  52.7 2.8 %collective-permute-done.1 = bf16[2,1,160,128]{3,2,1,0:T(8,128)(2,1)S(1)} collective-permute-done((bf16[2,1,160,128]{3,2,1,0:T(8,128)(2,1)S(1)}, bf16[2,1,160,128]{3,2,1,0:T(8,128)(2,1)S(1)}, u32[]{:S(2)}, u32[]{:S(2)}) %collective-permute-start.1) | collective-permute-done | bytes 81952 | tf_op jit(solution)/shard_map/ppermute | solution.py:24
  55.6 0.1 collective-permute-start.3
  55.7 1.3 collective-permute-done.3.et_ref
  57.0 17.1 %shard_map.91.refs_8_ = bf16[2,36,160,128]{3,2,1,0:T(8,128)(2,1)S(1)} custom-call(bf16[2,36,160,128]{3,2,1,0:T(8,128)(2,1)} %fusion.12.xo_ref, bf16[2,2,160,128]{3,2,1,0:T(8,128)(2,1)S(1)} %pad_maximum_fusion.eo_ref, bf16[2,36,160,128]{3,2,1,0:T(8,128)(2,1)} %collective-permute-done.2.xt_ref, bf16[2,2,160,128]{3,2,1,0:T(8,128)(2,1)S(1)} %collective-permute-done.3.et_ref, ...), custom_call_target="tpu_custom_call" | custom-call | flops 8493465600 | bytes 12718080 | tf_op jit(solution)/shard_map/pallas_call | solution.py:147
  74.1 0.0 copy-start.6
  74.1 0.0 copy-start.7
  74.1 0.5 convert_reduce_fusion.1
  74.6 1.8 %fusion.20 = (bf16[1,36,160,128]{3,2,1,0:T(8,128)(2,1)}, bf16[1,36,160,128]{3,2,1,0:T(8,128)(2,1)}) fusion(bf16[2,36,160,128]{3,2,1,0:T(8,128)(2,1)S(1)} %shard_map.91.refs_8_), kind=kLoop, calls=%fused_computation.64 | loop fusion | bytes 5898240 | tf_op jit(solution)/shard_map/slice | solution.py:290
  76.4 0.1 reduce_sum.128
  76.5 0.1 reduce_sum.129
  76.6 4.2 %collective-permute-start.7 = (bf16[1,36,160,128]{3,2,1,0:T(8,128)(2,1)}, bf16[1,36,160,128]{3,2,1,0:T(8,128)(2,1)}, u32[]{:S(2)}, u32[]{:S(2)}) collective-permute-start(bf16[1,36,160,128]{3,2,1,0:T(8,128)(2,1)} %get-tuple-element.9), channel_id=1, source_target_pairs={{0,4},{4,8},{8,12},{1,5},{5,9},{9,13},{2,6},{6,10},{10,14},{3,7},{... | collective-permute-start | bytes 4423688 | tf_op jit(solution)/shard_map/ppermute | solution.py:290
  80.9 1.5 collective-permute-start.8
  82.3 0.1 sub.87
  82.4 0.1 sub.88
  82.5 0.9 fusion.1
  83.4 0.1 reduce_sum.131
  83.5 0.1 reduce_sum.132
  83.7 1.6 %collective-permute-start.9 = (f32[8,2,16]{2,1,0:T(2,128)S(1)}, f32[8,2,16]{2,1,0:T(2,128)S(1)}, u32[]{:S(2)}, u32[]{:S(2)}) collective-permute-start(f32[8,2,16]{2,1,0:T(2,128)S(1)} %constant_dynamic-update-slice_fusion.1), channel_id=1, source_target_pairs={{0,2},{2,0},{1,3},{3,1},{4,6},{6,4},{5,7},{7,5},{8,10},{10,8},{9,1... | collective-permute-start | bytes 3080 | tf_op jit(solution)/shard_map/ppermute | solution.py:65
  85.3 2.2 %collective-permute-done.9 = f32[8,2,16]{2,1,0:T(2,128)S(1)} collective-permute-done((f32[8,2,16]{2,1,0:T(2,128)S(1)}, f32[8,2,16]{2,1,0:T(2,128)S(1)}, u32[]{:S(2)}, u32[]{:S(2)}) %collective-permute-start.9) | collective-permute-done | bytes 1056 | tf_op jit(solution)/shard_map/ppermute | solution.py:65
  87.4 32.5 %psum.7 = f32[8,2,16]{2,1,0:T(2,128)S(1)} all-reduce(f32[8,2,16]{2,1,0:T(2,128)S(1)} %constant_dynamic-update-slice_fusion), channel_id=1, replica_groups=mesh['groups'=2,'tm'=4,'height'=2,'chan'=2] {'tm'}, use_global_device_ids=true, to_apply=%region_11.12 | all-reduce | flops 256 | bytes 2048 | tf_op jit(solution)/shard_map/psum | solution.py:67
  120.1 0.1 mul.103
  120.1 0.1 mul.104
  120.2 0.1 sub.91
  120.3 0.1 sub.92
  120.4 0.0 copy-start.9
  120.4 0.0 collective-permute-done.7
  120.4 7.7 %fusion.13.refs_0_.refs_1_.refs_2_ = bf16[4,36,160,128]{3,2,1,0:T(8,128)(2,1)} fusion(bf16[1,36,160,128]{3,2,1,0:T(8,128)(2,1)} %collective-permute-done.8, bf16[2,36,160,128]{3,2,1,0:T(8,128)(2,1)S(1)} %shard_map.91.refs_8_, bf16[1,36,160,128]{3,2,1,0:T(8,128)(2,1)} %collective-permute-done.7, f32[160]{0:T(256)S(1)} %copy-done.6, f32[160]{0:T(256)S(1)} %copy-done.7, ...), kind=kLoop, calls=%fused_computation.19 | loop fusion | flops 38338560 | bytes 11799044 | tf_op jit(solution)/shard_map/jit(_where)/select_n | solution.py:302
  128.1 0.1 copy.19.refs_9_
  128.2 1.1 fusion.21
  129.3 1.1 copy.18
  130.4 1.4 reshape.107
  131.8 0.2 dynamic-slice_bitcast_fusion
  132.0 6.0 %collective-permute-done.10.refs_3_.refs_4_.refs_5_ = bf16[4,36,160,128]{3,2,1,0:T(8,128)(2,1)} collective-permute-done((bf16[4,36,160,128]{3,2,1,0:T(8,128)(2,1)}, bf16[4,36,160,128]{3,2,1,0:T(8,128)(2,1)}, u32[]{:S(2)}, u32[]{:S(2)}) %collective-permute-start.10) | collective-permute-done | bytes 5898272 | tf_op jit(solution)/shard_map/ppermute | solution.py:16
  138.0 10.6 %shard_map.92 = bf16[2,36,160,128]{3,2,1,0:T(8,128)(2,1)} custom-call(bf16[4,36,160,128]{3,2,1,0:T(8,128)(2,1)} %fusion.13.refs_0_.refs_1_.refs_2_, bf16[4,36,160,128]{3,2,1,0:T(8,128)(2,1)} %fusion.13.refs_0_.refs_1_.refs_2_, bf16[4,36,160,128]{3,2,1,0:T(8,128)(2,1)} %fusion.13.refs_0_.refs_1_.refs_2_, ...), custom_call_target="tpu_custom_call" | custom-call | flops 2831155200 | bytes 23900160 | tf_op jit(solution)/shard_map/pallas_call | solution.py:203
  (46 shorter events, 0.4 us)
Async XLA Ops:
  0.0 15.8 %copy-start = (bf16[2,36,160,128]{3,2,1,0:T(8,128)(2,1)S(1)}, bf16[2,36,160,128]{3,2,1,0:T(8,128)(2,1)}, u32[]{:S(2)}) copy-start(bf16[2,36,160,128]{3,2,1,0:T(8,128)(2,1)} %res_ref.1) | copy-start | bytes 8847364
  0.0 13.3 %copy-start.8 = (f32[160]{0:T(256)S(1)}, f32[160]{0:T(256)}, u32[]{:S(2)}) copy-start(f32[160]{0:T(256)} %param.13) | copy-start | bytes 1924
  0.0 15.8 %copy-start.4 = (f32[160]{0:T(256)S(1)}, f32[160]{0:T(256)}, u32[]{:S(2)}) copy-start(f32[160]{0:T(256)} %param.11) | copy-start | bytes 1924
  0.0 15.8 %copy-start.5 = (f32[160]{0:T(256)S(1)}, f32[160]{0:T(256)}, u32[]{:S(2)}) copy-start(f32[160]{0:T(256)} %param.10) | copy-start | bytes 1924
  0.0 52.5 %collective-permute-start.4 = (bf16[3,80,160]{2,1,0:T(8,128)(2,1)}, bf16[3,80,160]{2,1,0:T(8,128)(2,1)S(1)}, u32[]{:S(2)}, u32[]{:S(2)}) collective-permute-start(bf16[3,80,160]{2,1,0:T(8,128)(2,1)} %param.16), channel_id=1, source_target_pairs={{0,12},{4,0},{8,4},{12,8},{1,13},{5,1},{9,5},{13,9},{2,14},{6,2},{... | collective-permute-start | bytes 230408 | tf_op jit(solution)/shard_map/ppermute | solution.py:42
  5.1 47.5 %collective-permute-start.6 = (bf16[3,80,160]{2,1,0:T(8,128)(2,1)}, bf16[3,80,160]{2,1,0:T(8,128)(2,1)S(1)}, u32[]{:S(2)}, u32[]{:S(2)}) collective-permute-start(bf16[3,80,160]{2,1,0:T(8,128)(2,1)} %param.16), channel_id=1, source_target_pairs={{0,4},{4,8},{8,12},{12,0},{1,5},{5,9},{9,13},{13,1},{2,6},{6,10},{... | collective-permute-start | bytes 230408 | tf_op jit(solution)/shard_map/ppermute | solution.py:42
  5.1 47.5 %collective-permute-start.5 = (bf16[3,80,160]{2,1,0:T(8,128)(2,1)}, bf16[3,80,160]{2,1,0:T(8,128)(2,1)S(1)}, u32[]{:S(2)}, u32[]{:S(2)}) collective-permute-start(bf16[3,80,160]{2,1,0:T(8,128)(2,1)} %param.16), channel_id=1, source_target_pairs={{0,8},{4,12},{8,0},{12,4},{1,9},{5,13},{9,1},{13,5},{2,10},{6,14},... | collective-permute-start | bytes 230408 | tf_op jit(solution)/shard_map/ppermute | solution.py:42
  11.7 3.7 %collective-permute-start = (f32[2,2,2,16]{3,2,1,0:T(2,128)S(1)}, f32[2,2,2,16]{3,2,1,0:T(2,128)S(1)}, u32[]{:S(2)}, u32[]{:S(2)}) collective-permute-start(f32[2,2,2,16]{3,2,1,0:T(2,128)S(1)} %constant_dynamic-update-slice_fusion.3), channel_id=1, source_target_pairs={{0,2},{2,0},{1,3},{3,1},{4,6},{6,4},{5,7},{7,5},{8,10},{10,8},{9,1... | collective-permute-start | bytes 1544 | tf_op jit(solution)/shard_map/ppermute | solution.py:65
  15.8 3.4 %copy-start.3 = (bf16[3,3,80,160]{3,2,1,0:T(8,128)(2,1)S(1)}, bf16[3,3,80,160]{3,2,1,0:T(8,128)(2,1)}, u32[]{:S(2)}) copy-start(bf16[3,3,80,160]{3,2,1,0:T(8,128)(2,1)} %param.12) | copy-start | bytes 691204
  15.9 34.2 %copy-start.2 = (bf16[3,80,160]{2,1,0:T(8,128)(2,1)S(1)}, bf16[3,80,160]{2,1,0:T(8,128)(2,1)}, u32[]{:S(2)}) copy-start(bf16[3,80,160]{2,1,0:T(8,128)(2,1)} %param.16) | copy-start | bytes 230404
  19.3 37.7 %collective-permute-start.2 = (bf16[2,36,160,128]{3,2,1,0:T(8,128)(2,1)}, bf16[2,36,160,128]{3,2,1,0:T(8,128)(2,1)}, u32[]{:S(2)}, u32[]{:S(2)}) collective-permute-start(bf16[2,36,160,128]{3,2,1,0:T(8,128)(2,1)} %fusion.12.xo_ref), channel_id=1, source_target_pairs={{0,1},{1,0},{2,3},{3,2},{4,5},{5,4},{6,7},{7,6},{8,9},{9,8},{10,11... | collective-permute-start | bytes 8847368 | tf_op jit(solution)/shard_map/ppermute | solution.py:16
  51.0 4.5 %collective-permute-start.1 = (bf16[2,1,160,128]{3,2,1,0:T(8,128)(2,1)S(1)}, bf16[2,1,160,128]{3,2,1,0:T(8,128)(2,1)S(1)}, u32[]{:S(2)}, u32[]{:S(2)}) collective-permute-start(bf16[2,1,160,128]{3,2,1,0:T(8,128)(2,1)S(1)} %slice_select_fusion), channel_id=1, source_target_pairs={{0,2},{2,0},{1,3},{3,1},{4,6},{6,4},{5,7},{7,5},{8,10},{10,8},{9,1... | collective-permute-start | bytes 245768 | tf_op jit(solution)/shard_map/ppermute | solution.py:24
  55.6 1.5 collective-permute-start.3
  55.6 18.4 %copy-start.1 = (bf16[8,3,80,160]{3,2,1,0:T(8,128)(2,1)}, bf16[8,3,80,160]{3,2,1,0:T(8,128)(2,1)S(1)}, u32[]{:S(2)}) copy-start(bf16[8,3,80,160]{3,2,1,0:T(8,128)(2,1)S(1)} %bitcast_dynamic-update-slice_fusion.1) | copy-start | bytes 1843204
  74.1 46.3 %copy-start.6 = (f32[160]{0:T(256)S(1)}, f32[160]{0:T(256)}, u32[]{:S(2)}) copy-start(f32[160]{0:T(256)} %param.15) | copy-start | bytes 1924
  74.1 46.3 %copy-start.7 = (f32[160]{0:T(256)S(1)}, f32[160]{0:T(256)}, u32[]{:S(2)}) copy-start(f32[160]{0:T(256)} %param.14) | copy-start | bytes 1924
  76.6 43.8 %collective-permute-start.7 = (bf16[1,36,160,128]{3,2,1,0:T(8,128)(2,1)}, bf16[1,36,160,128]{3,2,1,0:T(8,128)(2,1)}, u32[]{:S(2)}, u32[]{:S(2)}) collective-permute-start(bf16[1,36,160,128]{3,2,1,0:T(8,128)(2,1)} %get-tuple-element.9), channel_id=1, source_target_pairs={{0,4},{4,8},{8,12},{1,5},{5,9},{9,13},{2,6},{6,10},{10,14},{3,7},{... | collective-permute-start | bytes 4423688 | tf_op jit(solution)/shard_map/ppermute | solution.py:290
  80.9 39.5 %collective-permute-start.8 = (bf16[1,36,160,128]{3,2,1,0:T(8,128)(2,1)}, bf16[1,36,160,128]{3,2,1,0:T(8,128)(2,1)}, u32[]{:S(2)}, u32[]{:S(2)}) collective-permute-start(bf16[1,36,160,128]{3,2,1,0:T(8,128)(2,1)} %get-tuple-element.10), channel_id=1, source_target_pairs={{4,0},{8,4},{12,8},{5,1},{9,5},{13,9},{6,2},{10,6},{14,10},{7,3},{... | collective-permute-start | bytes 4423688 | tf_op jit(solution)/shard_map/ppermute | solution.py:291
  83.7 3.7 %collective-permute-start.9 = (f32[8,2,16]{2,1,0:T(2,128)S(1)}, f32[8,2,16]{2,1,0:T(2,128)S(1)}, u32[]{:S(2)}, u32[]{:S(2)}) collective-permute-start(f32[8,2,16]{2,1,0:T(2,128)S(1)} %constant_dynamic-update-slice_fusion.1), channel_id=1, source_target_pairs={{0,2},{2,0},{1,3},{3,1},{4,6},{6,4},{5,7},{7,5},{8,10},{10,8},{9,1... | collective-permute-start | bytes 3080 | tf_op jit(solution)/shard_map/ppermute | solution.py:65
  120.4 7.7 %copy-start.9 = (f32[160]{0:T(256)S(1)}, f32[160]{0:T(256)}, u32[]{:S(2)}) copy-start(f32[160]{0:T(256)} %param.17) | copy-start | bytes 1924
  128.1 9.9 %collective-permute-start.10 = (bf16[4,36,160,128]{3,2,1,0:T(8,128)(2,1)}, bf16[4,36,160,128]{3,2,1,0:T(8,128)(2,1)}, u32[]{:S(2)}, u32[]{:S(2)}) collective-permute-start(bf16[4,36,160,128]{3,2,1,0:T(8,128)(2,1)} %fusion.13.refs_0_.refs_1_.refs_2_), channel_id=1, source_target_pairs={{0,1},{1,0},{2,3},{3,2},{4,5},{5,4},{6,7},{7,6},{8,9},{9,8},{10,11... | collective-permute-start | bytes 17694728 | tf_op jit(solution)/shard_map/ppermute | solution.py:16

commit v23 on v22

--- a/solution.py
+++ b/solution.py
@@ -259,15 +259,15 @@
     tm_index = lax.axis_index("tm")
     tm_count = lax.axis_size("tm")
 
-    spatial_full = lax.all_gather(spatial_weight, "tm", axis=2, tiled=True).reshape(9, C, local_chan)
     temporal_pieces = gather_tm(temporal_weight)
     temporal_full = jnp.moveaxis(temporal_pieces, 0, 1).reshape(3, C, local_chan)
-    spatial_full = spatial_full.reshape(3, 3, C, local_chan)
 
     values = video.astype(jnp.float32)
     grouped = values.reshape(frames, rows, local_groups, group_size, width)
     average, variance = group_stats(grouped, (1, 3, 4), ("height",))
     act_one = group_act(values, average, variance, norm1_gain, norm1_bias)
+    act_one, spatial_weight = lax.optimization_barrier((act_one, spatial_weight))
+    spatial_full = lax.all_gather(spatial_weight, "tm", axis=2, tiled=True)
 
     edges = row_halo(act_one)
     own_start = chan_index * local_chan

time: 149 us -> 151 us (1.013)
  local copies, waits for them, and re-layouts: 8.9 us -> 15.1 us
  waiting for transfers between devices: 14.3 us -> 11.2 us
    unnamed x27 -> x25, local copies, waits for them, and re-layouts: 0.12 us -> 4.66 us
    ppermute x1, waiting for transfers between devices: 2.82 us -> 0.01 us  [row_halo(): received = lax.ppermute(edge, 'height', [(0, 1), (1, 0)])]
  transfers between devices with their start and end apart: 11 -> 11, of which waited for: 5 -> 3; matrix products, arithmetic and copies ran while one was open for 12% -> 16% of each run, Pallas kernels for 0% -> 0%
where the time goes in v23:
time: 151 us
  blocking collectives  61.6 us (41%)
  Pallas kernels  27.6 us (18%)
  other arithmetic  19.2 us (13%)
  starting transfers between devices  15.7 us (10%)
  local copies, waits for them, and re-layouts  15.1 us (10%)
  waiting for transfers between devices  11.2 us (7%)
    psum x1, blocking collectives, group_stats(): table = lax.psum(table, name)  32.8 us
    all_gather x1, blocking collectives, body(): spatial_full = lax.all_gather(spatial_weight, 'tm', axis=2, tiled=True)  28.8 us
    pallas_call x1, Pallas kernels, spatial_call(): pl.pallas_call(spatial_kernel, out_shape=jax.ShapeDtypeStruct(residual.sh...  17.1 us
    pallas_call x1, Pallas kernels, temporal_call(): pl.pallas_call(temporal_kernel, out_shape=jax.ShapeDtypeStruct(residual.s...  10.6 us
    select_n x1, other arithmetic, body(): jnp.where(inside[:, None, None, None], act_two, jnp.zeros_like(act_two))  7.66 us
    ppermute x3, starting transfers between devices, gather_tm(): pieces.append(lax.ppermute(piece, 'tm', pairs))  6.13 us
    ppermute x3, waiting for transfers between devices, swap_chan(): return lax.ppermute(block, 'chan', [(0, 1), (1, 0)])  6.04 us
    ppermute x2, waiting for transfers between devices, group_stats(): table = table + lax.ppermute(table, name, [(0, 1), (1, 0)])  5.1 us
  transfers between devices with their start and end apart: 11, of which 3 were waited for; matrix products, arithmetic and copies ran while one was open for 16% of the time, Pallas kernels for 0%

profile of v23, /device:TPU:0, one launch (start us, length us, event | category | flops | bytes accessed | tf_op | source)
XLA Modules:
  0.0 150.7 jit_solution(15264136630775099949)
XLA Ops:
  0.0 5.1 %collective-permute-start.4 = (bf16[3,80,160]{2,1,0:T(8,128)(2,1)}, bf16[3,80,160]{2,1,0:T(8,128)(2,1)S(1)}, u32[]{:S(2)}, u32[]{:S(2)}) collective-permute-start(bf16[3,80,160]{2,1,0:T(8,128)(2,1)} %param.16), channel_id=1, source_target_pairs={{0,12},{4,0},{8,4},{12,8},{1,13},{5,1},{9,5},{13,9},{2,14},{6,2},{... | collective-permute-start | bytes 230408 | tf_op jit(solution)/shard_map/ppermute | solution.py:42
  5.1 1.0 collective-permute-start.5
  6.1 2.3 %convert_reduce_fusion = f32[2,160]{1,0:T(2,128)S(1)} fusion(bf16[2,36,160,128]{3,2,1,0:T(8,128)(2,1)} %res_ref.1), kind=kLoop, calls=%fused_computation.3 | loop fusion | flops 2948800 | bytes 2950400 | tf_op jit(solution)/shard_map/reduce_sum | solution.py:51
  8.5 0.1 reduce_sum.101
  8.6 0.1 reduce_sum.120
  8.7 0.1 sub.75
  8.7 0.1 sub.76
  8.8 2.7 %fusion.3 = f32[2,160]{1,0:T(2,128)S(1)} fusion(bf16[2,36,160,128]{3,2,1,0:T(8,128)(2,1)} %res_ref.1, f32[2,160]{1,0:T(2,128)S(1)} %sub.76), kind=kLoop, calls=%fused_computation.9 | loop fusion | flops 5897920 | bytes 2951680 | tf_op jit(solution)/shard_map/reduce_sum | solution.py:53
  11.6 0.1 reduce_sum.122
  11.7 0.1 reduce_sum.123
  11.8 1.6 %collective-permute-start = (f32[2,2,2,16]{3,2,1,0:T(2,128)S(1)}, f32[2,2,2,16]{3,2,1,0:T(2,128)S(1)}, u32[]{:S(2)}, u32[]{:S(2)}) collective-permute-start(f32[2,2,2,16]{3,2,1,0:T(2,128)S(1)} %constant_dynamic-update-slice_fusion.3), channel_id=1, source_target_pairs={{0,2},{2,0},{1,3},{3,1},{4,6},{6,4},{5,7},{7,5},{8,10},{10,8},{9,1... | collective-permute-start | bytes 1544 | tf_op jit(solution)/shard_map/ppermute | solution.py:65
  13.3 0.1 copy.17.b_ref
  13.5 2.0 %collective-permute-done = f32[2,2,2,16]{3,2,1,0:T(2,128)S(1)} collective-permute-done((f32[2,2,2,16]{3,2,1,0:T(2,128)S(1)}, f32[2,2,2,16]{3,2,1,0:T(2,128)S(1)}, u32[]{:S(2)}, u32[]{:S(2)}) %collective-permute-start) | collective-permute-done | bytes 544 | tf_op jit(solution)/shard_map/ppermute | solution.py:65
  15.5 0.1 mul.90
  15.6 0.1 mul.91
  15.7 0.1 sub.79
  15.8 0.1 sub.80
  15.9 0.0 copy-start.2
  15.9 3.4 %fusion.12.xo_ref = bf16[2,36,160,128]{3,2,1,0:T(8,128)(2,1)} fusion(bf16[2,36,160,128]{3,2,1,0:T(8,128)(2,1)S(1)} %copy-done, f32[160]{0:T(256)S(1)} %copy-done.3, f32[160]{0:T(256)S(1)} %copy-done.4, f32[2,160]{1,0:T(2,128)S(1)} %mul.91, f32[2,160]{1,0:T(2,128)S(1)} %sub.80), kind=kLoop, calls=%fused_computation.18 | loop fusion | flops 14745600 | bytes 5902080 | tf_op jit(solution)/shard_map/convert_element_type | solution.py:84
  19.3 0.7 bitcast_dynamic-update-slice_fusion.6
  20.0 0.9 slice_select_fusion
  20.9 1.6 %collective-permute-start.1 = (bf16[2,1,160,128]{3,2,1,0:T(8,128)(2,1)S(1)}, bf16[2,1,160,128]{3,2,1,0:T(8,128)(2,1)S(1)}, u32[]{:S(2)}, u32[]{:S(2)}) collective-permute-start(bf16[2,1,160,128]{3,2,1,0:T(8,128)(2,1)S(1)} %slice_select_fusion), channel_id=1, source_target_pairs={{0,2},{2,0},{1,3},{3,1},{4,6},{6,4},{5,7},{7,5},{8,10},{10,8},{9,1... | collective-permute-start | bytes 245768 | tf_op jit(solution)/shard_map/ppermute | solution.py:24
  22.5 28.8 %all_gather.3 = bf16[3,3,320,160]{3,2,1,0:T(8,128)(2,1)S(1)} all-gather(bf16[3,3,80,160]{3,2,1,0:T(8,128)(2,1)S(1)} %copy-done.2), channel_id=1, replica_groups=mesh['groups'=2,'tm'=4,'height'=2,'chan'=2] {'tm'}, dimensions={2}, use_global_device_ids=true | all-gather | bytes 1152000 | tf_op jit(solution)/shard_map/all_gather | solution.py:270
  51.3 0.9 copy.16
  52.2 0.7 constant_dynamic-slice_fusion.2
  52.9 0.7 bitcast_dynamic-update-slice_fusion.4
  53.6 0.7 bitcast_dynamic-update-slice_fusion.2
  54.2 0.7 bitcast_dynamic-update-slice_fusion
  54.9 0.7 bitcast_dynamic-update-slice_fusion.7
  55.6 0.7 bitcast_dynamic-update-slice_fusion.5
  56.2 0.7 bitcast_dynamic-update-slice_fusion.3
  56.9 0.1 collective-permute-start.3
  57.0 0.7 bitcast_dynamic-update-slice_fusion.1
  57.7 1.1 constant_dynamic-slice_fusion.1.early_ref
  58.8 17.1 %shard_map.91.refs_8_ = bf16[2,36,160,128]{3,2,1,0:T(8,128)(2,1)S(1)} custom-call(bf16[2,36,160,128]{3,2,1,0:T(8,128)(2,1)} %fusion.12.xo_ref, bf16[2,2,160,128]{3,2,1,0:T(8,128)(2,1)S(1)} %pad_maximum_fusion.eo_ref, bf16[2,36,160,128]{3,2,1,0:T(8,128)(2,1)} %collective-permute-done.2.xt_ref, bf16[2,2,160,128]{3,2,1,0:T(8,128)(2,1)S(1)} %collective-permute-done.3.et_ref, ...), custom_call_target="tpu_custom_call" | custom-call | flops 8493465600 | bytes 12718080 | tf_op jit(solution)/shard_map/pallas_call | solution.py:147
  75.9 0.0 copy-start.5
  75.9 0.0 copy-start.6
  75.9 0.5 convert_reduce_fusion.1
  76.4 1.8 %fusion.20 = (bf16[1,36,160,128]{3,2,1,0:T(8,128)(2,1)}, bf16[1,36,160,128]{3,2,1,0:T(8,128)(2,1)}) fusion(bf16[2,36,160,128]{3,2,1,0:T(8,128)(2,1)S(1)} %shard_map.91.refs_8_), kind=kLoop, calls=%fused_computation.64 | loop fusion | bytes 5898240 | tf_op jit(solution)/shard_map/slice | solution.py:290
  78.2 0.1 reduce_sum.128
  78.3 0.1 reduce_sum.129
  78.4 4.3 %collective-permute-start.7 = (bf16[1,36,160,128]{3,2,1,0:T(8,128)(2,1)}, bf16[1,36,160,128]{3,2,1,0:T(8,128)(2,1)}, u32[]{:S(2)}, u32[]{:S(2)}) collective-permute-start(bf16[1,36,160,128]{3,2,1,0:T(8,128)(2,1)} %get-tuple-element.13), channel_id=1, source_target_pairs={{0,4},{4,8},{8,12},{1,5},{5,9},{9,13},{2,6},{6,10},{10,14},{3,7},{... | collective-permute-start | bytes 4423688 | tf_op jit(solution)/shard_map/ppermute | solution.py:290
  82.7 1.5 collective-permute-start.8
  84.2 0.1 sub.87
  84.3 0.1 sub.88
  84.4 0.9 fusion.1
  85.3 0.1 reduce_sum.131
  85.4 0.1 reduce_sum.132
  85.6 0.6 collective-permute-start.9
  86.2 3.1 %collective-permute-done.9 = f32[8,2,16]{2,1,0:T(2,128)S(1)} collective-permute-done((f32[8,2,16]{2,1,0:T(2,128)S(1)}, f32[8,2,16]{2,1,0:T(2,128)S(1)}, u32[]{:S(2)}, u32[]{:S(2)}) %collective-permute-start.9) | collective-permute-done | bytes 1056 | tf_op jit(solution)/shard_map/ppermute | solution.py:65
  89.3 32.8 %psum.7 = f32[8,2,16]{2,1,0:T(2,128)S(1)} all-reduce(f32[8,2,16]{2,1,0:T(2,128)S(1)} %constant_dynamic-update-slice_fusion), channel_id=1, replica_groups=mesh['groups'=2,'tm'=4,'height'=2,'chan'=2] {'tm'}, use_global_device_ids=true, to_apply=%region_11.12 | all-reduce | flops 256 | bytes 2048 | tf_op jit(solution)/shard_map/psum | solution.py:67
  122.2 0.1 mul.103
  122.2 0.1 mul.104
  122.3 0.1 sub.91
  122.4 0.1 sub.92
  122.5 0.0 copy-start.8
  122.6 7.7 %fusion.13.refs_0_.refs_1_.refs_2_ = bf16[4,36,160,128]{3,2,1,0:T(8,128)(2,1)} fusion(bf16[1,36,160,128]{3,2,1,0:T(8,128)(2,1)} %collective-permute-done.8, bf16[2,36,160,128]{3,2,1,0:T(8,128)(2,1)S(1)} %shard_map.91.refs_8_, bf16[1,36,160,128]{3,2,1,0:T(8,128)(2,1)} %collective-permute-done.7, f32[160]{0:T(256)S(1)} %copy-done.5, f32[160]{0:T(256)S(1)} %copy-done.6, ...), kind=kLoop, calls=%fused_computation.19 | loop fusion | flops 38338560 | bytes 11799044 | tf_op jit(solution)/shard_map/jit(_where)/select_n | solution.py:302
  130.2 0.1 copy.19.refs_9_
  130.3 1.1 fusion.21
  131.4 1.1 copy.18
  132.5 1.4 reshape.107
  133.9 0.2 dynamic-slice_bitcast_fusion
  134.1 6.0 %collective-permute-done.10.refs_3_.refs_4_.refs_5_ = bf16[4,36,160,128]{3,2,1,0:T(8,128)(2,1)} collective-permute-done((bf16[4,36,160,128]{3,2,1,0:T(8,128)(2,1)}, bf16[4,36,160,128]{3,2,1,0:T(8,128)(2,1)}, u32[]{:S(2)}, u32[]{:S(2)}) %collective-permute-start.10) | collective-permute-done | bytes 5898272 | tf_op jit(solution)/shard_map/ppermute | solution.py:16
  140.2 10.6 %shard_map.92 = bf16[2,36,160,128]{3,2,1,0:T(8,128)(2,1)} custom-call(bf16[4,36,160,128]{3,2,1,0:T(8,128)(2,1)} %fusion.13.refs_0_.refs_1_.refs_2_, bf16[4,36,160,128]{3,2,1,0:T(8,128)(2,1)} %fusion.13.refs_0_.refs_1_.refs_2_, bf16[4,36,160,128]{3,2,1,0:T(8,128)(2,1)} %fusion.13.refs_0_.refs_1_.refs_2_, ...), custom_call_target="tpu_custom_call" | custom-call | flops 2831155200 | bytes 23900160 | tf_op jit(solution)/shard_map/pallas_call | solution.py:203
  (44 shorter events, 0.3 us)
Async XLA Ops:
  0.0 15.9 %copy-start = (bf16[2,36,160,128]{3,2,1,0:T(8,128)(2,1)S(1)}, bf16[2,36,160,128]{3,2,1,0:T(8,128)(2,1)}, u32[]{:S(2)}) copy-start(bf16[2,36,160,128]{3,2,1,0:T(8,128)(2,1)} %res_ref.1) | copy-start | bytes 8847364
  0.0 13.3 %copy-start.7 = (f32[160]{0:T(256)S(1)}, f32[160]{0:T(256)}, u32[]{:S(2)}) copy-start(f32[160]{0:T(256)} %param.13) | copy-start | bytes 1924
  0.0 15.9 %copy-start.3 = (f32[160]{0:T(256)S(1)}, f32[160]{0:T(256)}, u32[]{:S(2)}) copy-start(f32[160]{0:T(256)} %param.11) | copy-start | bytes 1924
  0.0 15.9 %copy-start.4 = (f32[160]{0:T(256)S(1)}, f32[160]{0:T(256)}, u32[]{:S(2)}) copy-start(f32[160]{0:T(256)} %param.10) | copy-start | bytes 1924
  0.0 52.9 %collective-permute-start.4 = (bf16[3,80,160]{2,1,0:T(8,128)(2,1)}, bf16[3,80,160]{2,1,0:T(8,128)(2,1)S(1)}, u32[]{:S(2)}, u32[]{:S(2)}) collective-permute-start(bf16[3,80,160]{2,1,0:T(8,128)(2,1)} %param.16), channel_id=1, source_target_pairs={{0,12},{4,0},{8,4},{12,8},{1,13},{5,1},{9,5},{13,9},{2,14},{6,2},{... | collective-permute-start | bytes 230408 | tf_op jit(solution)/shard_map/ppermute | solution.py:42
  5.1 49.1 %collective-permute-start.6 = (bf16[3,80,160]{2,1,0:T(8,128)(2,1)}, bf16[3,80,160]{2,1,0:T(8,128)(2,1)S(1)}, u32[]{:S(2)}, u32[]{:S(2)}) collective-permute-start(bf16[3,80,160]{2,1,0:T(8,128)(2,1)} %param.16), channel_id=1, source_target_pairs={{0,4},{4,8},{8,12},{12,0},{1,5},{5,9},{9,13},{13,1},{2,6},{6,10},{... | collective-permute-start | bytes 230408 | tf_op jit(solution)/shard_map/ppermute | solution.py:42
  5.1 48.5 %collective-permute-start.5 = (bf16[3,80,160]{2,1,0:T(8,128)(2,1)}, bf16[3,80,160]{2,1,0:T(8,128)(2,1)S(1)}, u32[]{:S(2)}, u32[]{:S(2)}) collective-permute-start(bf16[3,80,160]{2,1,0:T(8,128)(2,1)} %param.16), channel_id=1, source_target_pairs={{0,8},{4,12},{8,0},{12,4},{1,9},{5,13},{9,1},{13,5},{2,10},{6,14},... | collective-permute-start | bytes 230408 | tf_op jit(solution)/shard_map/ppermute | solution.py:42
  6.1 13.2 %copy-start.1 = (bf16[3,80,160]{2,1,0:T(8,128)(2,1)S(1)}, bf16[3,80,160]{2,1,0:T(8,128)(2,1)}, u32[]{:S(2)}) copy-start(bf16[3,80,160]{2,1,0:T(8,128)(2,1)} %param.16) | copy-start | bytes 230404
  11.8 3.7 %collective-permute-start = (f32[2,2,2,16]{3,2,1,0:T(2,128)S(1)}, f32[2,2,2,16]{3,2,1,0:T(2,128)S(1)}, u32[]{:S(2)}, u32[]{:S(2)}) collective-permute-start(f32[2,2,2,16]{3,2,1,0:T(2,128)S(1)} %constant_dynamic-update-slice_fusion.3), channel_id=1, source_target_pairs={{0,2},{2,0},{1,3},{3,1},{4,6},{6,4},{5,7},{7,5},{8,10},{10,8},{9,1... | collective-permute-start | bytes 1544 | tf_op jit(solution)/shard_map/ppermute | solution.py:65
  15.9 6.6 %copy-start.2 = (bf16[3,3,80,160]{3,2,1,0:T(8,128)(2,1)S(1)}, bf16[3,3,80,160]{3,2,1,0:T(8,128)(2,1)}, u32[]{:S(2)}) copy-start(bf16[3,3,80,160]{3,2,1,0:T(8,128)(2,1)} %param.12) | copy-start | bytes 691204
  19.3 39.5 %collective-permute-start.2 = (bf16[2,36,160,128]{3,2,1,0:T(8,128)(2,1)}, bf16[2,36,160,128]{3,2,1,0:T(8,128)(2,1)}, u32[]{:S(2)}, u32[]{:S(2)}) collective-permute-start(bf16[2,36,160,128]{3,2,1,0:T(8,128)(2,1)} %fusion.12.xo_ref), channel_id=1, source_target_pairs={{0,1},{1,0},{2,3},{3,2},{4,5},{5,4},{6,7},{7,6},{8,9},{9,8},{10,11... | collective-permute-start | bytes 8847368 | tf_op jit(solution)/shard_map/ppermute | solution.py:16
  20.9 36.0 %collective-permute-start.1 = (bf16[2,1,160,128]{3,2,1,0:T(8,128)(2,1)S(1)}, bf16[2,1,160,128]{3,2,1,0:T(8,128)(2,1)S(1)}, u32[]{:S(2)}, u32[]{:S(2)}) collective-permute-start(bf16[2,1,160,128]{3,2,1,0:T(8,128)(2,1)S(1)} %slice_select_fusion), channel_id=1, source_target_pairs={{0,2},{2,0},{1,3},{3,1},{4,6},{6,4},{5,7},{7,5},{8,10},{10,8},{9,1... | collective-permute-start | bytes 245768 | tf_op jit(solution)/shard_map/ppermute | solution.py:24
  56.9 1.8 %collective-permute-start.3 = (bf16[2,2,160,128]{3,2,1,0:T(8,128)(2,1)S(1)}, bf16[2,2,160,128]{3,2,1,0:T(8,128)(2,1)S(1)}, u32[]{:S(2)}, u32[]{:S(2)}) collective-permute-start(bf16[2,2,160,128]{3,2,1,0:T(8,128)(2,1)S(1)} %pad_maximum_fusion.eo_ref), channel_id=1, source_target_pairs={{0,1},{1,0},{2,3},{3,2},{4,5},{5,4},{6,7},{7,6},{8,9},{9,8},{10,11... | collective-permute-start | bytes 491528 | tf_op jit(solution)/shard_map/ppermute | solution.py:16
  75.9 46.7 %copy-start.5 = (f32[160]{0:T(256)S(1)}, f32[160]{0:T(256)}, u32[]{:S(2)}) copy-start(f32[160]{0:T(256)} %param.15) | copy-start | bytes 1924
  75.9 46.7 %copy-start.6 = (f32[160]{0:T(256)S(1)}, f32[160]{0:T(256)}, u32[]{:S(2)}) copy-start(f32[160]{0:T(256)} %param.14) | copy-start | bytes 1924
  78.4 44.1 %collective-permute-start.7 = (bf16[1,36,160,128]{3,2,1,0:T(8,128)(2,1)}, bf16[1,36,160,128]{3,2,1,0:T(8,128)(2,1)}, u32[]{:S(2)}, u32[]{:S(2)}) collective-permute-start(bf16[1,36,160,128]{3,2,1,0:T(8,128)(2,1)} %get-tuple-element.13), channel_id=1, source_target_pairs={{0,4},{4,8},{8,12},{1,5},{5,9},{9,13},{2,6},{6,10},{10,14},{3,7},{... | collective-permute-start | bytes 4423688 | tf_op jit(solution)/shard_map/ppermute | solution.py:290
  82.7 39.8 %collective-permute-start.8 = (bf16[1,36,160,128]{3,2,1,0:T(8,128)(2,1)}, bf16[1,36,160,128]{3,2,1,0:T(8,128)(2,1)}, u32[]{:S(2)}, u32[]{:S(2)}) collective-permute-start(bf16[1,36,160,128]{3,2,1,0:T(8,128)(2,1)} %get-tuple-element.14), channel_id=1, source_target_pairs={{4,0},{8,4},{12,8},{5,1},{9,5},{13,9},{6,2},{10,6},{14,10},{7,3},{... | collective-permute-start | bytes 4423688 | tf_op jit(solution)/shard_map/ppermute | solution.py:291
  85.6 3.7 %collective-permute-start.9 = (f32[8,2,16]{2,1,0:T(2,128)S(1)}, f32[8,2,16]{2,1,0:T(2,128)S(1)}, u32[]{:S(2)}, u32[]{:S(2)}) collective-permute-start(f32[8,2,16]{2,1,0:T(2,128)S(1)} %constant_dynamic-update-slice_fusion.1), channel_id=1, source_target_pairs={{0,2},{2,0},{1,3},{3,1},{4,6},{6,4},{5,7},{7,5},{8,10},{10,8},{9,1... | collective-permute-start | bytes 3080 | tf_op jit(solution)/shard_map/ppermute | solution.py:65
  122.5 7.7 %copy-start.8 = (f32[160]{0:T(256)S(1)}, f32[160]{0:T(256)}, u32[]{:S(2)}) copy-start(f32[160]{0:T(256)} %param.17) | copy-start | bytes 1924
  130.2 9.9 %collective-permute-start.10 = (bf16[4,36,160,128]{3,2,1,0:T(8,128)(2,1)}, bf16[4,36,160,128]{3,2,1,0:T(8,128)(2,1)}, u32[]{:S(2)}, u32[]{:S(2)}) collective-permute-start(bf16[4,36,160,128]{3,2,1,0:T(8,128)(2,1)} %fusion.13.refs_0_.refs_1_.refs_2_), channel_id=1, source_target_pairs={{0,1},{1,0},{2,3},{3,2},{4,5},{5,4},{6,7},{7,6},{8,9},{9,8},{10,11... | collective-permute-start | bytes 17694728 | tf_op jit(solution)/shard_map/ppermute | solution.py:16

commit v24 on v22

--- a/solution.py
+++ b/solution.py
@@ -193,26 +193,27 @@
 
 
 def frame_spec(tap, rows, chans, width):
-    return pl.BlockSpec((1, rows, chans, width), lambda f: (f + tap, 0, 0, 0))
+    return pl.BlockSpec((1, rows, chans, width), lambda f, j: (f + tap, j, 0, 0))
 
 
 def temporal_call(own, other, weight_own, weight_other, residual, bias):
     frames, rows, local_chan, width = residual.shape
-    taps = [frame_spec(tap, rows, local_chan, width) for tap in range(3)]
-    weight_spec = pl.BlockSpec((3, local_chan, local_chan), lambda f: (0, 0, 0))
+    taps = [frame_spec(tap, STEP, local_chan, width) for tap in range(3)]
+    weight_spec = pl.BlockSpec((3, local_chan, local_chan), lambda f, j: (0, 0, 0))
+    row_spec = pl.BlockSpec((1, STEP, local_chan, width), lambda f, j: (f, j, 0, 0))
     return pl.pallas_call(
         temporal_kernel,
         out_shape=jax.ShapeDtypeStruct(residual.shape, jnp.bfloat16),
-        grid=(frames,),
+        grid=(frames, rows // STEP),
         in_specs=taps
         + taps
         + [
             weight_spec,
             weight_spec,
-            pl.BlockSpec((1, rows, local_chan, width), lambda f: (f, 0, 0, 0)),
-            pl.BlockSpec((local_chan, 1), lambda f: (0, 0)),
+            row_spec,
+            pl.BlockSpec((local_chan, 1), lambda f, j: (0, 0)),
         ],
-        out_specs=pl.BlockSpec((1, rows, local_chan, width), lambda f: (f, 0, 0, 0)),
+        out_specs=row_spec,
         compiler_params=pltpu.CompilerParams(vmem_limit_bytes=48 * 1024 * 1024),
         cost_estimate=pl.CostEstimate(
             flops=2 * frames * rows * width * 6 * local_chan * local_chan,

time: 149 us -> 149 us (level)
  no operation moved by 1% of the time
where the time goes in v24:
time: 149 us
  blocking collectives  61.7 us (41%)
  Pallas kernels  27.8 us (19%)
  other arithmetic  19.1 us (13%)
  starting transfers between devices  16.6 us (11%)
  waiting for transfers between devices  14.3 us (10%)
  local copies, waits for them, and re-layouts  8.9 us (6%)
    psum x1, blocking collectives, group_stats(): table = lax.psum(table, name)  32.5 us
    all_gather x1, blocking collectives, body(): lax.all_gather(spatial_weight, 'tm', axis=2, tiled=True)  29.1 us
    pallas_call x1, Pallas kernels, spatial_call(): pl.pallas_call(spatial_kernel, out_shape=jax.ShapeDtypeStruct(residual.sh...  17.1 us
    pallas_call x1, Pallas kernels, temporal_call(): pl.pallas_call(temporal_kernel, out_shape=jax.ShapeDtypeStruct(residual.s...  10.7 us
    select_n x1, other arithmetic, body(): jnp.where(inside[:, None, None, None], act_two, jnp.zeros_like(act_two))  7.66 us
    ppermute x3, waiting for transfers between devices, swap_chan(): return lax.ppermute(block, 'chan', [(0, 1), (1, 0)])  7.34 us
    ppermute x3, starting transfers between devices, gather_tm(): pieces.append(lax.ppermute(piece, 'tm', pairs))  6.13 us
    ppermute x1, starting transfers between devices, body(): before = lax.ppermute(hidden[-1:], 'tm', forward)  4.23 us
  transfers between devices with their start and end apart: 11, of which 5 were waited for; matrix products, arithmetic and copies ran while one was open for 12% of the time, Pallas kernels for 0%

profile of v24, /device:TPU:0, one launch (start us, length us, event | category | flops | bytes accessed | tf_op | source)
XLA Modules:
  0.0 148.7 jit_solution(10103613860275229029)
XLA Ops:
  0.0 5.1 %collective-permute-start.4 = (bf16[3,80,160]{2,1,0:T(8,128)(2,1)}, bf16[3,80,160]{2,1,0:T(8,128)(2,1)S(1)}, u32[]{:S(2)}, u32[]{:S(2)}) collective-permute-start(bf16[3,80,160]{2,1,0:T(8,128)(2,1)} %param.16), channel_id=1, source_target_pairs={{0,12},{4,0},{8,4},{12,8},{1,13},{5,1},{9,5},{13,9},{2,14},{6,2},{... | collective-permute-start | bytes 230408 | tf_op jit(solution)/shard_map/ppermute | solution.py:42
  5.1 0.0 collective-permute-start.6
  5.1 1.0 collective-permute-start.5
  6.1 2.3 %convert_reduce_fusion = f32[2,160]{1,0:T(2,128)S(1)} fusion(bf16[2,36,160,128]{3,2,1,0:T(8,128)(2,1)} %res_ref.1), kind=kLoop, calls=%fused_computation.3 | loop fusion | flops 2948800 | bytes 2950400 | tf_op jit(solution)/shard_map/reduce_sum | solution.py:51
  8.4 0.1 reduce_sum.101
  8.5 0.1 reduce_sum.120
  8.6 0.1 sub.75
  8.7 0.1 sub.76
  8.8 2.7 %fusion.3 = f32[2,160]{1,0:T(2,128)S(1)} fusion(bf16[2,36,160,128]{3,2,1,0:T(8,128)(2,1)} %res_ref.1, f32[2,160]{1,0:T(2,128)S(1)} %sub.76), kind=kLoop, calls=%fused_computation.9 | loop fusion | flops 5897920 | bytes 2951680 | tf_op jit(solution)/shard_map/reduce_sum | solution.py:53
  11.5 0.1 reduce_sum.122
  11.6 0.1 reduce_sum.123
  11.7 1.6 %collective-permute-start = (f32[2,2,2,16]{3,2,1,0:T(2,128)S(1)}, f32[2,2,2,16]{3,2,1,0:T(2,128)S(1)}, u32[]{:S(2)}, u32[]{:S(2)}) collective-permute-start(f32[2,2,2,16]{3,2,1,0:T(2,128)S(1)} %constant_dynamic-update-slice_fusion.3), channel_id=1, source_target_pairs={{0,2},{2,0},{1,3},{3,1},{4,6},{6,4},{5,7},{7,5},{8,10},{10,8},{9,1... | collective-permute-start | bytes 1544 | tf_op jit(solution)/shard_map/ppermute | solution.py:65
  13.3 0.1 copy.17.b_ref
  13.4 2.0 %collective-permute-done = f32[2,2,2,16]{3,2,1,0:T(2,128)S(1)} collective-permute-done((f32[2,2,2,16]{3,2,1,0:T(2,128)S(1)}, f32[2,2,2,16]{3,2,1,0:T(2,128)S(1)}, u32[]{:S(2)}, u32[]{:S(2)}) %collective-permute-start) | collective-permute-done | bytes 544 | tf_op jit(solution)/shard_map/ppermute | solution.py:65
  15.5 0.1 mul.90
  15.6 0.1 mul.91
  15.7 0.1 sub.79
  15.7 0.1 sub.80
  15.8 0.0 copy-start.3
  15.9 0.0 copy-start.2
  15.9 3.4 %fusion.12.xo_ref = bf16[2,36,160,128]{3,2,1,0:T(8,128)(2,1)} fusion(bf16[2,36,160,128]{3,2,1,0:T(8,128)(2,1)S(1)} %copy-done, f32[160]{0:T(256)S(1)} %copy-done.4, f32[160]{0:T(256)S(1)} %copy-done.5, f32[2,160]{1,0:T(2,128)S(1)} %mul.91, f32[2,160]{1,0:T(2,128)S(1)} %sub.80), kind=kLoop, calls=%fused_computation.18 | loop fusion | flops 14745600 | bytes 5902080 | tf_op jit(solution)/shard_map/convert_element_type | solution.py:84
  19.3 29.1 %all_gather.3 = bf16[3,3,320,160]{3,2,1,0:T(8,128)(2,1)S(1)} all-gather(bf16[3,3,80,160]{3,2,1,0:T(8,128)(2,1)S(1)} %copy-done.3), channel_id=1, replica_groups=mesh['groups'=2,'tm'=4,'height'=2,'chan'=2] {'tm'}, dimensions={2}, use_global_device_ids=true | all-gather | bytes 1152000 | tf_op jit(solution)/shard_map/all_gather | solution.py:263
  48.4 0.9 copy.16
  49.3 0.7 constant_dynamic-slice_fusion.2
  50.0 0.9 slice_select_fusion
  51.0 1.6 %collective-permute-start.1 = (bf16[2,1,160,128]{3,2,1,0:T(8,128)(2,1)S(1)}, bf16[2,1,160,128]{3,2,1,0:T(8,128)(2,1)S(1)}, u32[]{:S(2)}, u32[]{:S(2)}) collective-permute-start(bf16[2,1,160,128]{3,2,1,0:T(8,128)(2,1)S(1)} %slice_select_fusion), channel_id=1, source_target_pairs={{0,2},{2,0},{1,3},{3,1},{4,6},{6,4},{5,7},{7,5},{8,10},{10,8},{9,1... | collective-permute-start | bytes 245768 | tf_op jit(solution)/shard_map/ppermute | solution.py:24
  52.6 0.0 collective-permute-done.4
  52.6 0.0 collective-permute-done.5
  52.7 2.8 %collective-permute-done.1 = bf16[2,1,160,128]{3,2,1,0:T(8,128)(2,1)S(1)} collective-permute-done((bf16[2,1,160,128]{3,2,1,0:T(8,128)(2,1)S(1)}, bf16[2,1,160,128]{3,2,1,0:T(8,128)(2,1)S(1)}, u32[]{:S(2)}, u32[]{:S(2)}) %collective-permute-start.1) | collective-permute-done | bytes 81952 | tf_op jit(solution)/shard_map/ppermute | solution.py:24
  55.6 0.1 collective-permute-start.3
  55.7 1.3 collective-permute-done.3.et_ref
  57.0 0.0 collective-permute-done.2.xt_ref
  57.0 17.1 %shard_map.91.refs_8_ = bf16[2,36,160,128]{3,2,1,0:T(8,128)(2,1)S(1)} custom-call(bf16[2,36,160,128]{3,2,1,0:T(8,128)(2,1)} %fusion.12.xo_ref, bf16[2,2,160,128]{3,2,1,0:T(8,128)(2,1)S(1)} %pad_maximum_fusion.eo_ref, bf16[2,36,160,128]{3,2,1,0:T(8,128)(2,1)} %collective-permute-done.2.xt_ref, bf16[2,2,160,128]{3,2,1,0:T(8,128)(2,1)S(1)} %collective-permute-done.3.et_ref, ...), custom_call_target="tpu_custom_call" | custom-call | flops 8493465600 | bytes 12718080 | tf_op jit(solution)/shard_map/pallas_call | solution.py:147
  74.1 0.0 copy-start.6
  74.1 0.0 copy-start.7
  74.1 0.5 convert_reduce_fusion.1
  74.6 1.8 %fusion.20 = (bf16[1,36,160,128]{3,2,1,0:T(8,128)(2,1)}, bf16[1,36,160,128]{3,2,1,0:T(8,128)(2,1)}) fusion(bf16[2,36,160,128]{3,2,1,0:T(8,128)(2,1)S(1)} %shard_map.91.refs_8_), kind=kLoop, calls=%fused_computation.64 | loop fusion | bytes 5898240 | tf_op jit(solution)/shard_map/slice | solution.py:291
  76.4 0.1 reduce_sum.128
  76.5 0.1 reduce_sum.129
  76.6 4.2 %collective-permute-start.7 = (bf16[1,36,160,128]{3,2,1,0:T(8,128)(2,1)}, bf16[1,36,160,128]{3,2,1,0:T(8,128)(2,1)}, u32[]{:S(2)}, u32[]{:S(2)}) collective-permute-start(bf16[1,36,160,128]{3,2,1,0:T(8,128)(2,1)} %get-tuple-element.9), channel_id=1, source_target_pairs={{0,4},{4,8},{8,12},{1,5},{5,9},{9,13},{2,6},{6,10},{10,14},{3,7},{... | collective-permute-start | bytes 4423688 | tf_op jit(solution)/shard_map/ppermute | solution.py:291
  80.9 1.5 collective-permute-start.8
  82.3 0.1 sub.87
  82.4 0.1 sub.88
  82.5 0.9 fusion.1
  83.4 0.1 reduce_sum.131
  83.5 0.1 reduce_sum.132
  83.7 1.6 %collective-permute-start.9 = (f32[8,2,16]{2,1,0:T(2,128)S(1)}, f32[8,2,16]{2,1,0:T(2,128)S(1)}, u32[]{:S(2)}, u32[]{:S(2)}) collective-permute-start(f32[8,2,16]{2,1,0:T(2,128)S(1)} %constant_dynamic-update-slice_fusion.1), channel_id=1, source_target_pairs={{0,2},{2,0},{1,3},{3,1},{4,6},{6,4},{5,7},{7,5},{8,10},{10,8},{9,1... | collective-permute-start | bytes 3080 | tf_op jit(solution)/shard_map/ppermute | solution.py:65
  85.3 2.2 %collective-permute-done.9 = f32[8,2,16]{2,1,0:T(2,128)S(1)} collective-permute-done((f32[8,2,16]{2,1,0:T(2,128)S(1)}, f32[8,2,16]{2,1,0:T(2,128)S(1)}, u32[]{:S(2)}, u32[]{:S(2)}) %collective-permute-start.9) | collective-permute-done | bytes 1056 | tf_op jit(solution)/shard_map/ppermute | solution.py:65
  87.4 32.5 %psum.7 = f32[8,2,16]{2,1,0:T(2,128)S(1)} all-reduce(f32[8,2,16]{2,1,0:T(2,128)S(1)} %constant_dynamic-update-slice_fusion), channel_id=1, replica_groups=mesh['groups'=2,'tm'=4,'height'=2,'chan'=2] {'tm'}, use_global_device_ids=true, to_apply=%region_11.12 | all-reduce | flops 256 | bytes 2048 | tf_op jit(solution)/shard_map/psum | solution.py:67
  120.1 0.1 mul.103
  120.1 0.1 mul.104
  120.2 0.1 sub.91
  120.3 0.1 sub.92
  120.4 0.0 copy-start.9
  120.4 0.0 collective-permute-done.8
  120.4 7.7 %fusion.13.refs_0_.refs_1_.refs_2_ = bf16[4,36,160,128]{3,2,1,0:T(8,128)(2,1)} fusion(bf16[1,36,160,128]{3,2,1,0:T(8,128)(2,1)} %collective-permute-done.8, bf16[2,36,160,128]{3,2,1,0:T(8,128)(2,1)S(1)} %shard_map.91.refs_8_, bf16[1,36,160,128]{3,2,1,0:T(8,128)(2,1)} %collective-permute-done.7, f32[160]{0:T(256)S(1)} %copy-done.6, f32[160]{0:T(256)S(1)} %copy-done.7, ...), kind=kLoop, calls=%fused_computation.19 | loop fusion | flops 38338560 | bytes 11799044 | tf_op jit(solution)/shard_map/jit(_where)/select_n | solution.py:303
  128.1 0.0 collective-permute-start.10
  128.1 0.1 copy.19.refs_9_
  128.2 1.1 fusion.21
  129.3 1.1 copy.18
  130.4 1.4 reshape.107
  131.8 0.2 dynamic-slice_bitcast_fusion
  132.0 6.0 %collective-permute-done.10.refs_3_.refs_4_.refs_5_ = bf16[4,36,160,128]{3,2,1,0:T(8,128)(2,1)} collective-permute-done((bf16[4,36,160,128]{3,2,1,0:T(8,128)(2,1)}, bf16[4,36,160,128]{3,2,1,0:T(8,128)(2,1)}, u32[]{:S(2)}, u32[]{:S(2)}) %collective-permute-start.10) | collective-permute-done | bytes 5898272 | tf_op jit(solution)/shard_map/ppermute | solution.py:16
  138.0 10.7 %shard_map.92 = bf16[2,36,160,128]{3,2,1,0:T(8,128)(2,1)} custom-call(bf16[4,36,160,128]{3,2,1,0:T(8,128)(2,1)} %fusion.13.refs_0_.refs_1_.refs_2_, bf16[4,36,160,128]{3,2,1,0:T(8,128)(2,1)} %fusion.13.refs_0_.refs_1_.refs_2_, bf16[4,36,160,128]{3,2,1,0:T(8,128)(2,1)} %fusion.13.refs_0_.refs_1_.refs_2_, ...), custom_call_target="tpu_custom_call" | custom-call | flops 2831155200 | bytes 23900160 | tf_op jit(solution)/shard_map/pallas_call | solution.py:204
  (46 shorter events, 0.4 us)
Async XLA Ops:
  0.0 15.8 %copy-start = (bf16[2,36,160,128]{3,2,1,0:T(8,128)(2,1)S(1)}, bf16[2,36,160,128]{3,2,1,0:T(8,128)(2,1)}, u32[]{:S(2)}) copy-start(bf16[2,36,160,128]{3,2,1,0:T(8,128)(2,1)} %res_ref.1) | copy-start | bytes 8847364
  0.0 13.3 %copy-start.8 = (f32[160]{0:T(256)S(1)}, f32[160]{0:T(256)}, u32[]{:S(2)}) copy-start(f32[160]{0:T(256)} %param.13) | copy-start | bytes 1924
  0.0 15.8 %copy-start.4 = (f32[160]{0:T(256)S(1)}, f32[160]{0:T(256)}, u32[]{:S(2)}) copy-start(f32[160]{0:T(256)} %param.11) | copy-start | bytes 1924
  0.0 15.8 %copy-start.5 = (f32[160]{0:T(256)S(1)}, f32[160]{0:T(256)}, u32[]{:S(2)}) copy-start(f32[160]{0:T(256)} %param.10) | copy-start | bytes 1924
  0.0 52.5 %collective-permute-start.4 = (bf16[3,80,160]{2,1,0:T(8,128)(2,1)}, bf16[3,80,160]{2,1,0:T(8,128)(2,1)S(1)}, u32[]{:S(2)}, u32[]{:S(2)}) collective-permute-start(bf16[3,80,160]{2,1,0:T(8,128)(2,1)} %param.16), channel_id=1, source_target_pairs={{0,12},{4,0},{8,4},{12,8},{1,13},{5,1},{9,5},{13,9},{2,14},{6,2},{... | collective-permute-start | bytes 230408 | tf_op jit(solution)/shard_map/ppermute | solution.py:42
  5.1 47.5 %collective-permute-start.6 = (bf16[3,80,160]{2,1,0:T(8,128)(2,1)}, bf16[3,80,160]{2,1,0:T(8,128)(2,1)S(1)}, u32[]{:S(2)}, u32[]{:S(2)}) collective-permute-start(bf16[3,80,160]{2,1,0:T(8,128)(2,1)} %param.16), channel_id=1, source_target_pairs={{0,4},{4,8},{8,12},{12,0},{1,5},{5,9},{9,13},{13,1},{2,6},{6,10},{... | collective-permute-start | bytes 230408 | tf_op jit(solution)/shard_map/ppermute | solution.py:42
  5.1 47.5 %collective-permute-start.5 = (bf16[3,80,160]{2,1,0:T(8,128)(2,1)}, bf16[3,80,160]{2,1,0:T(8,128)(2,1)S(1)}, u32[]{:S(2)}, u32[]{:S(2)}) collective-permute-start(bf16[3,80,160]{2,1,0:T(8,128)(2,1)} %param.16), channel_id=1, source_target_pairs={{0,8},{4,12},{8,0},{12,4},{1,9},{5,13},{9,1},{13,5},{2,10},{6,14},... | collective-permute-start | bytes 230408 | tf_op jit(solution)/shard_map/ppermute | solution.py:42
  11.7 3.7 %collective-permute-start = (f32[2,2,2,16]{3,2,1,0:T(2,128)S(1)}, f32[2,2,2,16]{3,2,1,0:T(2,128)S(1)}, u32[]{:S(2)}, u32[]{:S(2)}) collective-permute-start(f32[2,2,2,16]{3,2,1,0:T(2,128)S(1)} %constant_dynamic-update-slice_fusion.3), channel_id=1, source_target_pairs={{0,2},{2,0},{1,3},{3,1},{4,6},{6,4},{5,7},{7,5},{8,10},{10,8},{9,1... | collective-permute-start | bytes 1544 | tf_op jit(solution)/shard_map/ppermute | solution.py:65
  15.8 3.4 %copy-start.3 = (bf16[3,3,80,160]{3,2,1,0:T(8,128)(2,1)S(1)}, bf16[3,3,80,160]{3,2,1,0:T(8,128)(2,1)}, u32[]{:S(2)}) copy-start(bf16[3,3,80,160]{3,2,1,0:T(8,128)(2,1)} %param.12) | copy-start | bytes 691204
  15.9 34.2 %copy-start.2 = (bf16[3,80,160]{2,1,0:T(8,128)(2,1)S(1)}, bf16[3,80,160]{2,1,0:T(8,128)(2,1)}, u32[]{:S(2)}) copy-start(bf16[3,80,160]{2,1,0:T(8,128)(2,1)} %param.16) | copy-start | bytes 230404
  19.3 37.7 %collective-permute-start.2 = (bf16[2,36,160,128]{3,2,1,0:T(8,128)(2,1)}, bf16[2,36,160,128]{3,2,1,0:T(8,128)(2,1)}, u32[]{:S(2)}, u32[]{:S(2)}) collective-permute-start(bf16[2,36,160,128]{3,2,1,0:T(8,128)(2,1)} %fusion.12.xo_ref), channel_id=1, source_target_pairs={{0,1},{1,0},{2,3},{3,2},{4,5},{5,4},{6,7},{7,6},{8,9},{9,8},{10,11... | collective-permute-start | bytes 8847368 | tf_op jit(solution)/shard_map/ppermute | solution.py:16
  51.0 4.5 %collective-permute-start.1 = (bf16[2,1,160,128]{3,2,1,0:T(8,128)(2,1)S(1)}, bf16[2,1,160,128]{3,2,1,0:T(8,128)(2,1)S(1)}, u32[]{:S(2)}, u32[]{:S(2)}) collective-permute-start(bf16[2,1,160,128]{3,2,1,0:T(8,128)(2,1)S(1)} %slice_select_fusion), channel_id=1, source_target_pairs={{0,2},{2,0},{1,3},{3,1},{4,6},{6,4},{5,7},{7,5},{8,10},{10,8},{9,1... | collective-permute-start | bytes 245768 | tf_op jit(solution)/shard_map/ppermute | solution.py:24
  55.6 1.5 collective-permute-start.3
  55.6 18.4 %copy-start.1 = (bf16[8,3,80,160]{3,2,1,0:T(8,128)(2,1)}, bf16[8,3,80,160]{3,2,1,0:T(8,128)(2,1)S(1)}, u32[]{:S(2)}) copy-start(bf16[8,3,80,160]{3,2,1,0:T(8,128)(2,1)S(1)} %bitcast_dynamic-update-slice_fusion.1) | copy-start | bytes 1843204
  74.1 46.3 %copy-start.6 = (f32[160]{0:T(256)S(1)}, f32[160]{0:T(256)}, u32[]{:S(2)}) copy-start(f32[160]{0:T(256)} %param.15) | copy-start | bytes 1924
  74.1 46.3 %copy-start.7 = (f32[160]{0:T(256)S(1)}, f32[160]{0:T(256)}, u32[]{:S(2)}) copy-start(f32[160]{0:T(256)} %param.14) | copy-start | bytes 1924
  76.6 43.8 %collective-permute-start.7 = (bf16[1,36,160,128]{3,2,1,0:T(8,128)(2,1)}, bf16[1,36,160,128]{3,2,1,0:T(8,128)(2,1)}, u32[]{:S(2)}, u32[]{:S(2)}) collective-permute-start(bf16[1,36,160,128]{3,2,1,0:T(8,128)(2,1)} %get-tuple-element.9), channel_id=1, source_target_pairs={{0,4},{4,8},{8,12},{1,5},{5,9},{9,13},{2,6},{6,10},{10,14},{3,7},{... | collective-permute-start | bytes 4423688 | tf_op jit(solution)/shard_map/ppermute | solution.py:291
  80.9 39.5 %collective-permute-start.8 = (bf16[1,36,160,128]{3,2,1,0:T(8,128)(2,1)}, bf16[1,36,160,128]{3,2,1,0:T(8,128)(2,1)}, u32[]{:S(2)}, u32[]{:S(2)}) collective-permute-start(bf16[1,36,160,128]{3,2,1,0:T(8,128)(2,1)} %get-tuple-element.10), channel_id=1, source_target_pairs={{4,0},{8,4},{12,8},{5,1},{9,5},{13,9},{6,2},{10,6},{14,10},{7,3},{... | collective-permute-start | bytes 4423688 | tf_op jit(solution)/shard_map/ppermute | solution.py:292
  83.7 3.7 %collective-permute-start.9 = (f32[8,2,16]{2,1,0:T(2,128)S(1)}, f32[8,2,16]{2,1,0:T(2,128)S(1)}, u32[]{:S(2)}, u32[]{:S(2)}) collective-permute-start(f32[8,2,16]{2,1,0:T(2,128)S(1)} %constant_dynamic-update-slice_fusion.1), channel_id=1, source_target_pairs={{0,2},{2,0},{1,3},{3,1},{4,6},{6,4},{5,7},{7,5},{8,10},{10,8},{9,1... | collective-permute-start | bytes 3080 | tf_op jit(solution)/shard_map/ppermute | solution.py:65
  120.4 7.7 %copy-start.9 = (f32[160]{0:T(256)S(1)}, f32[160]{0:T(256)}, u32[]{:S(2)}) copy-start(f32[160]{0:T(256)} %param.17) | copy-start | bytes 1924
  128.1 9.9 %collective-permute-start.10 = (bf16[4,36,160,128]{3,2,1,0:T(8,128)(2,1)}, bf16[4,36,160,128]{3,2,1,0:T(8,128)(2,1)}, u32[]{:S(2)}, u32[]{:S(2)}) collective-permute-start(bf16[4,36,160,128]{3,2,1,0:T(8,128)(2,1)} %fusion.13.refs_0_.refs_1_.refs_2_), channel_id=1, source_target_pairs={{0,1},{1,0},{2,3},{3,2},{4,5},{5,4},{6,7},{7,6},{8,9},{9,8},{10,11... | collective-permute-start | bytes 17694728 | tf_op jit(solution)/shard_map/ppermute | solution.py:16

commit v25 on v22

--- a/solution.py
+++ b/solution.py
@@ -91,7 +91,7 @@
     return lax.dynamic_update_slice_in_dim(joined, other, (1 - chan_index) * size, axis=2)
 
 
-STEP = 12
+STEP = 18
 
 
 def pair(ref, first):

time: 149 us -> 149 us (level)
  no operation moved by 1% of the time
where the time goes in v25:
time: 149 us
  blocking collectives  62.2 us (42%)
  Pallas kernels  27.5 us (18%)
  other arithmetic  19.1 us (13%)
  starting transfers between devices  16.4 us (11%)
  waiting for transfers between devices  14.3 us (10%)
  local copies, waits for them, and re-layouts  8.9 us (6%)
    psum x1, blocking collectives, group_stats(): table = lax.psum(table, name)  33 us
    all_gather x1, blocking collectives, body(): lax.all_gather(spatial_weight, 'tm', axis=2, tiled=True)  29.3 us
    pallas_call x1, Pallas kernels, spatial_call(): pl.pallas_call(spatial_kernel, out_shape=jax.ShapeDtypeStruct(residual.sh...  16.9 us
    pallas_call x1, Pallas kernels, temporal_call(): pl.pallas_call(temporal_kernel, out_shape=jax.ShapeDtypeStruct(residual.s...  10.6 us
    select_n x1, other arithmetic, body(): jnp.where(inside[:, None, None, None], act_two, jnp.zeros_like(act_two))  7.66 us
    ppermute x3, waiting for transfers between devices, swap_chan(): return lax.ppermute(block, 'chan', [(0, 1), (1, 0)])  7.34 us
    ppermute x3, starting transfers between devices, gather_tm(): pieces.append(lax.ppermute(piece, 'tm', pairs))  6.13 us
    ppermute x1, starting transfers between devices, body(): before = lax.ppermute(hidden[-1:], 'tm', forward)  4.22 us
  transfers between devices with their start and end apart: 11, of which 5 were waited for; matrix products, arithmetic and copies ran while one was open for 12% of the time, Pallas kernels for 0%

profile of v25, /device:TPU:0, one launch (start us, length us, event | category | flops | bytes accessed | tf_op | source)
XLA Modules:
  0.0 148.9 jit_solution(17201441063078835916)
XLA Ops:
  0.0 5.1 %collective-permute-start.4 = (bf16[3,80,160]{2,1,0:T(8,128)(2,1)}, bf16[3,80,160]{2,1,0:T(8,128)(2,1)S(1)}, u32[]{:S(2)}, u32[]{:S(2)}) collective-permute-start(bf16[3,80,160]{2,1,0:T(8,128)(2,1)} %param.16), channel_id=1, source_target_pairs={{0,12},{4,0},{8,4},{12,8},{1,13},{5,1},{9,5},{13,9},{2,14},{6,2},{... | collective-permute-start | bytes 230408 | tf_op jit(solution)/shard_map/ppermute | solution.py:42
  5.1 0.0 collective-permute-start.6
  5.1 1.0 collective-permute-start.5
  6.1 2.3 %convert_reduce_fusion = f32[2,160]{1,0:T(2,128)S(1)} fusion(bf16[2,36,160,128]{3,2,1,0:T(8,128)(2,1)} %res_ref.1), kind=kLoop, calls=%fused_computation.3 | loop fusion | flops 2948800 | bytes 2950400 | tf_op jit(solution)/shard_map/reduce_sum | solution.py:51
  8.4 0.1 reduce_sum.101
  8.5 0.1 reduce_sum.120
  8.6 0.1 sub.75
  8.7 0.1 sub.76
  8.8 2.7 %fusion.3 = f32[2,160]{1,0:T(2,128)S(1)} fusion(bf16[2,36,160,128]{3,2,1,0:T(8,128)(2,1)} %res_ref.1, f32[2,160]{1,0:T(2,128)S(1)} %sub.76), kind=kLoop, calls=%fused_computation.9 | loop fusion | flops 5897920 | bytes 2951680 | tf_op jit(solution)/shard_map/reduce_sum | solution.py:53
  11.5 0.1 reduce_sum.122
  11.6 0.1 reduce_sum.123
  11.7 1.6 %collective-permute-start = (f32[2,2,2,16]{3,2,1,0:T(2,128)S(1)}, f32[2,2,2,16]{3,2,1,0:T(2,128)S(1)}, u32[]{:S(2)}, u32[]{:S(2)}) collective-permute-start(f32[2,2,2,16]{3,2,1,0:T(2,128)S(1)} %constant_dynamic-update-slice_fusion.3), channel_id=1, source_target_pairs={{0,2},{2,0},{1,3},{3,1},{4,6},{6,4},{5,7},{7,5},{8,10},{10,8},{9,1... | collective-permute-start | bytes 1544 | tf_op jit(solution)/shard_map/ppermute | solution.py:65
  13.3 0.1 copy.17.b_ref
  13.4 2.0 %collective-permute-done = f32[2,2,2,16]{3,2,1,0:T(2,128)S(1)} collective-permute-done((f32[2,2,2,16]{3,2,1,0:T(2,128)S(1)}, f32[2,2,2,16]{3,2,1,0:T(2,128)S(1)}, u32[]{:S(2)}, u32[]{:S(2)}) %collective-permute-start) | collective-permute-done | bytes 544 | tf_op jit(solution)/shard_map/ppermute | solution.py:65
  15.5 0.1 mul.90
  15.6 0.1 mul.91
  15.7 0.1 sub.79
  15.7 0.1 sub.80
  15.8 0.0 copy-start.3
  15.9 0.0 copy-start.2
  15.9 3.4 %fusion.12.xo_ref = bf16[2,36,160,128]{3,2,1,0:T(8,128)(2,1)} fusion(bf16[2,36,160,128]{3,2,1,0:T(8,128)(2,1)S(1)} %copy-done, f32[160]{0:T(256)S(1)} %copy-done.4, f32[160]{0:T(256)S(1)} %copy-done.5, f32[2,160]{1,0:T(2,128)S(1)} %mul.91, f32[2,160]{1,0:T(2,128)S(1)} %sub.80), kind=kLoop, calls=%fused_computation.18 | loop fusion | flops 14745600 | bytes 5902080 | tf_op jit(solution)/shard_map/convert_element_type | solution.py:84
  19.3 0.0 collective-permute-start.2
  19.3 29.3 %all_gather.3 = bf16[3,3,320,160]{3,2,1,0:T(8,128)(2,1)S(1)} all-gather(bf16[3,3,80,160]{3,2,1,0:T(8,128)(2,1)S(1)} %copy-done.3), channel_id=1, replica_groups=mesh['groups'=2,'tm'=4,'height'=2,'chan'=2] {'tm'}, dimensions={2}, use_global_device_ids=true | all-gather | bytes 1152000 | tf_op jit(solution)/shard_map/all_gather | solution.py:262
  48.6 0.9 copy.16
  49.5 0.7 constant_dynamic-slice_fusion.2
  50.2 0.9 slice_select_fusion
  51.2 1.6 %collective-permute-start.1 = (bf16[2,1,160,128]{3,2,1,0:T(8,128)(2,1)S(1)}, bf16[2,1,160,128]{3,2,1,0:T(8,128)(2,1)S(1)}, u32[]{:S(2)}, u32[]{:S(2)}) collective-permute-start(bf16[2,1,160,128]{3,2,1,0:T(8,128)(2,1)S(1)} %slice_select_fusion), channel_id=1, source_target_pairs={{0,2},{2,0},{1,3},{3,1},{4,6},{6,4},{5,7},{7,5},{8,10},{10,8},{9,1... | collective-permute-start | bytes 245768 | tf_op jit(solution)/shard_map/ppermute | solution.py:24
  52.7 0.0 collective-permute-done.4
  52.8 0.0 collective-permute-done.5
  52.8 0.0 collective-permute-done.6
  52.9 2.8 %collective-permute-done.1 = bf16[2,1,160,128]{3,2,1,0:T(8,128)(2,1)S(1)} collective-permute-done((bf16[2,1,160,128]{3,2,1,0:T(8,128)(2,1)S(1)}, bf16[2,1,160,128]{3,2,1,0:T(8,128)(2,1)S(1)}, u32[]{:S(2)}, u32[]{:S(2)}) %collective-permute-start.1) | collective-permute-done | bytes 81952 | tf_op jit(solution)/shard_map/ppermute | solution.py:24
  55.7 0.1 collective-permute-start.3
  55.9 1.3 collective-permute-done.3.et_ref
  57.2 0.0 collective-permute-done.2.xt_ref
  57.2 16.9 %shard_map.91.refs_8_ = bf16[2,36,160,128]{3,2,1,0:T(8,128)(2,1)S(1)} custom-call(bf16[2,36,160,128]{3,2,1,0:T(8,128)(2,1)} %fusion.12.xo_ref, bf16[2,2,160,128]{3,2,1,0:T(8,128)(2,1)S(1)} %pad_maximum_fusion.eo_ref, bf16[2,36,160,128]{3,2,1,0:T(8,128)(2,1)} %collective-permute-done.2.xt_ref, bf16[2,2,160,128]{3,2,1,0:T(8,128)(2,1)S(1)} %collective-permute-done.3.et_ref, ...), custom_call_target="tpu_custom_call" | custom-call | flops 8493465600 | bytes 12718080 | tf_op jit(solution)/shard_map/pallas_call | solution.py:147
  74.1 0.0 copy-start.6
  74.1 0.0 copy-start.7
  74.1 0.5 convert_reduce_fusion.1
  74.7 1.8 %fusion.20 = (bf16[1,36,160,128]{3,2,1,0:T(8,128)(2,1)}, bf16[1,36,160,128]{3,2,1,0:T(8,128)(2,1)}) fusion(bf16[2,36,160,128]{3,2,1,0:T(8,128)(2,1)S(1)} %shard_map.91.refs_8_), kind=kLoop, calls=%fused_computation.64 | loop fusion | bytes 5898240 | tf_op jit(solution)/shard_map/slice | solution.py:290
  76.5 0.1 reduce_sum.128
  76.5 0.1 reduce_sum.129
  76.7 4.2 %collective-permute-start.7 = (bf16[1,36,160,128]{3,2,1,0:T(8,128)(2,1)}, bf16[1,36,160,128]{3,2,1,0:T(8,128)(2,1)}, u32[]{:S(2)}, u32[]{:S(2)}) collective-permute-start(bf16[1,36,160,128]{3,2,1,0:T(8,128)(2,1)} %get-tuple-element.9), channel_id=1, source_target_pairs={{0,4},{4,8},{8,12},{1,5},{5,9},{9,13},{2,6},{6,10},{10,14},{3,7},{... | collective-permute-start | bytes 4423688 | tf_op jit(solution)/shard_map/ppermute | solution.py:290
  80.9 1.3 collective-permute-start.8
  82.2 0.1 sub.87
  82.3 0.1 sub.88
  82.4 0.9 fusion.1
  83.3 0.1 reduce_sum.131
  83.4 0.1 reduce_sum.132
  83.5 1.6 %collective-permute-start.9 = (f32[8,2,16]{2,1,0:T(2,128)S(1)}, f32[8,2,16]{2,1,0:T(2,128)S(1)}, u32[]{:S(2)}, u32[]{:S(2)}) collective-permute-start(f32[8,2,16]{2,1,0:T(2,128)S(1)} %constant_dynamic-update-slice_fusion.1), channel_id=1, source_target_pairs={{0,2},{2,0},{1,3},{3,1},{4,6},{6,4},{5,7},{7,5},{8,10},{10,8},{9,1... | collective-permute-start | bytes 3080 | tf_op jit(solution)/shard_map/ppermute | solution.py:65
  85.1 2.1 %collective-permute-done.9 = f32[8,2,16]{2,1,0:T(2,128)S(1)} collective-permute-done((f32[8,2,16]{2,1,0:T(2,128)S(1)}, f32[8,2,16]{2,1,0:T(2,128)S(1)}, u32[]{:S(2)}, u32[]{:S(2)}) %collective-permute-start.9) | collective-permute-done | bytes 1056 | tf_op jit(solution)/shard_map/ppermute | solution.py:65
  87.3 33.0 %psum.7 = f32[8,2,16]{2,1,0:T(2,128)S(1)} all-reduce(f32[8,2,16]{2,1,0:T(2,128)S(1)} %constant_dynamic-update-slice_fusion), channel_id=1, replica_groups=mesh['groups'=2,'tm'=4,'height'=2,'chan'=2] {'tm'}, use_global_device_ids=true, to_apply=%region_11.12 | all-reduce | flops 256 | bytes 2048 | tf_op jit(solution)/shard_map/psum | solution.py:67
  120.3 0.1 mul.103
  120.4 0.1 mul.104
  120.5 0.1 sub.91
  120.5 0.1 sub.92
  120.6 0.0 copy-start.9
  120.7 7.7 %fusion.13.refs_0_.refs_1_.refs_2_ = bf16[4,36,160,128]{3,2,1,0:T(8,128)(2,1)} fusion(bf16[1,36,160,128]{3,2,1,0:T(8,128)(2,1)} %collective-permute-done.8, bf16[2,36,160,128]{3,2,1,0:T(8,128)(2,1)S(1)} %shard_map.91.refs_8_, bf16[1,36,160,128]{3,2,1,0:T(8,128)(2,1)} %collective-permute-done.7, f32[160]{0:T(256)S(1)} %copy-done.6, f32[160]{0:T(256)S(1)} %copy-done.7, ...), kind=kLoop, calls=%fused_computation.19 | loop fusion | flops 38338560 | bytes 11799044 | tf_op jit(solution)/shard_map/jit(_where)/select_n | solution.py:302
  128.4 0.1 copy.19.refs_9_
  128.5 1.1 fusion.21
  129.6 1.1 copy.18
  130.6 1.4 reshape.107
  132.0 0.2 dynamic-slice_bitcast_fusion
  132.3 6.0 %collective-permute-done.10.refs_3_.refs_4_.refs_5_ = bf16[4,36,160,128]{3,2,1,0:T(8,128)(2,1)} collective-permute-done((bf16[4,36,160,128]{3,2,1,0:T(8,128)(2,1)}, bf16[4,36,160,128]{3,2,1,0:T(8,128)(2,1)}, u32[]{:S(2)}, u32[]{:S(2)}) %collective-permute-start.10) | collective-permute-done | bytes 5898272 | tf_op jit(solution)/shard_map/ppermute | solution.py:16
  138.3 10.6 %shard_map.92 = bf16[2,36,160,128]{3,2,1,0:T(8,128)(2,1)} custom-call(bf16[4,36,160,128]{3,2,1,0:T(8,128)(2,1)} %fusion.13.refs_0_.refs_1_.refs_2_, bf16[4,36,160,128]{3,2,1,0:T(8,128)(2,1)} %fusion.13.refs_0_.refs_1_.refs_2_, bf16[4,36,160,128]{3,2,1,0:T(8,128)(2,1)} %fusion.13.refs_0_.refs_1_.refs_2_, ...), custom_call_target="tpu_custom_call" | custom-call | flops 2831155200 | bytes 23900160 | tf_op jit(solution)/shard_map/pallas_call | solution.py:203
  (46 shorter events, 0.4 us)
Async XLA Ops:
  0.0 15.8 %copy-start = (bf16[2,36,160,128]{3,2,1,0:T(8,128)(2,1)S(1)}, bf16[2,36,160,128]{3,2,1,0:T(8,128)(2,1)}, u32[]{:S(2)}) copy-start(bf16[2,36,160,128]{3,2,1,0:T(8,128)(2,1)} %res_ref.1) | copy-start | bytes 8847364
  0.0 13.3 %copy-start.8 = (f32[160]{0:T(256)S(1)}, f32[160]{0:T(256)}, u32[]{:S(2)}) copy-start(f32[160]{0:T(256)} %param.13) | copy-start | bytes 1924
  0.0 15.8 %copy-start.4 = (f32[160]{0:T(256)S(1)}, f32[160]{0:T(256)}, u32[]{:S(2)}) copy-start(f32[160]{0:T(256)} %param.11) | copy-start | bytes 1924
  0.0 15.8 %copy-start.5 = (f32[160]{0:T(256)S(1)}, f32[160]{0:T(256)}, u32[]{:S(2)}) copy-start(f32[160]{0:T(256)} %param.10) | copy-start | bytes 1924
  0.0 52.7 %collective-permute-start.4 = (bf16[3,80,160]{2,1,0:T(8,128)(2,1)}, bf16[3,80,160]{2,1,0:T(8,128)(2,1)S(1)}, u32[]{:S(2)}, u32[]{:S(2)}) collective-permute-start(bf16[3,80,160]{2,1,0:T(8,128)(2,1)} %param.16), channel_id=1, source_target_pairs={{0,12},{4,0},{8,4},{12,8},{1,13},{5,1},{9,5},{13,9},{2,14},{6,2},{... | collective-permute-start | bytes 230408 | tf_op jit(solution)/shard_map/ppermute | solution.py:42
  5.1 47.7 %collective-permute-start.6 = (bf16[3,80,160]{2,1,0:T(8,128)(2,1)}, bf16[3,80,160]{2,1,0:T(8,128)(2,1)S(1)}, u32[]{:S(2)}, u32[]{:S(2)}) collective-permute-start(bf16[3,80,160]{2,1,0:T(8,128)(2,1)} %param.16), channel_id=1, source_target_pairs={{0,4},{4,8},{8,12},{12,0},{1,5},{5,9},{9,13},{13,1},{2,6},{6,10},{... | collective-permute-start | bytes 230408 | tf_op jit(solution)/shard_map/ppermute | solution.py:42
  5.1 47.6 %collective-permute-start.5 = (bf16[3,80,160]{2,1,0:T(8,128)(2,1)}, bf16[3,80,160]{2,1,0:T(8,128)(2,1)S(1)}, u32[]{:S(2)}, u32[]{:S(2)}) collective-permute-start(bf16[3,80,160]{2,1,0:T(8,128)(2,1)} %param.16), channel_id=1, source_target_pairs={{0,8},{4,12},{8,0},{12,4},{1,9},{5,13},{9,1},{13,5},{2,10},{6,14},... | collective-permute-start | bytes 230408 | tf_op jit(solution)/shard_map/ppermute | solution.py:42
  11.7 3.7 %collective-permute-start = (f32[2,2,2,16]{3,2,1,0:T(2,128)S(1)}, f32[2,2,2,16]{3,2,1,0:T(2,128)S(1)}, u32[]{:S(2)}, u32[]{:S(2)}) collective-permute-start(f32[2,2,2,16]{3,2,1,0:T(2,128)S(1)} %constant_dynamic-update-slice_fusion.3), channel_id=1, source_target_pairs={{0,2},{2,0},{1,3},{3,1},{4,6},{6,4},{5,7},{7,5},{8,10},{10,8},{9,1... | collective-permute-start | bytes 1544 | tf_op jit(solution)/shard_map/ppermute | solution.py:65
  15.8 3.4 %copy-start.3 = (bf16[3,3,80,160]{3,2,1,0:T(8,128)(2,1)S(1)}, bf16[3,3,80,160]{3,2,1,0:T(8,128)(2,1)}, u32[]{:S(2)}) copy-start(bf16[3,3,80,160]{3,2,1,0:T(8,128)(2,1)} %param.12) | copy-start | bytes 691204
  15.9 34.3 %copy-start.2 = (bf16[3,80,160]{2,1,0:T(8,128)(2,1)S(1)}, bf16[3,80,160]{2,1,0:T(8,128)(2,1)}, u32[]{:S(2)}) copy-start(bf16[3,80,160]{2,1,0:T(8,128)(2,1)} %param.16) | copy-start | bytes 230404
  19.3 37.9 %collective-permute-start.2 = (bf16[2,36,160,128]{3,2,1,0:T(8,128)(2,1)}, bf16[2,36,160,128]{3,2,1,0:T(8,128)(2,1)}, u32[]{:S(2)}, u32[]{:S(2)}) collective-permute-start(bf16[2,36,160,128]{3,2,1,0:T(8,128)(2,1)} %fusion.12.xo_ref), channel_id=1, source_target_pairs={{0,1},{1,0},{2,3},{3,2},{4,5},{5,4},{6,7},{7,6},{8,9},{9,8},{10,11... | collective-permute-start | bytes 8847368 | tf_op jit(solution)/shard_map/ppermute | solution.py:16
  51.2 4.5 %collective-permute-start.1 = (bf16[2,1,160,128]{3,2,1,0:T(8,128)(2,1)S(1)}, bf16[2,1,160,128]{3,2,1,0:T(8,128)(2,1)S(1)}, u32[]{:S(2)}, u32[]{:S(2)}) collective-permute-start(bf16[2,1,160,128]{3,2,1,0:T(8,128)(2,1)S(1)} %slice_select_fusion), channel_id=1, source_target_pairs={{0,2},{2,0},{1,3},{3,1},{4,6},{6,4},{5,7},{7,5},{8,10},{10,8},{9,1... | collective-permute-start | bytes 245768 | tf_op jit(solution)/shard_map/ppermute | solution.py:24
  55.7 1.5 collective-permute-start.3
  55.8 18.3 %copy-start.1 = (bf16[8,3,80,160]{3,2,1,0:T(8,128)(2,1)}, bf16[8,3,80,160]{3,2,1,0:T(8,128)(2,1)S(1)}, u32[]{:S(2)}) copy-start(bf16[8,3,80,160]{3,2,1,0:T(8,128)(2,1)S(1)} %bitcast_dynamic-update-slice_fusion.1) | copy-start | bytes 1843204
  74.1 46.6 %copy-start.6 = (f32[160]{0:T(256)S(1)}, f32[160]{0:T(256)}, u32[]{:S(2)}) copy-start(f32[160]{0:T(256)} %param.15) | copy-start | bytes 1924
  74.1 46.5 %copy-start.7 = (f32[160]{0:T(256)S(1)}, f32[160]{0:T(256)}, u32[]{:S(2)}) copy-start(f32[160]{0:T(256)} %param.14) | copy-start | bytes 1924
  76.7 44.0 %collective-permute-start.7 = (bf16[1,36,160,128]{3,2,1,0:T(8,128)(2,1)}, bf16[1,36,160,128]{3,2,1,0:T(8,128)(2,1)}, u32[]{:S(2)}, u32[]{:S(2)}) collective-permute-start(bf16[1,36,160,128]{3,2,1,0:T(8,128)(2,1)} %get-tuple-element.9), channel_id=1, source_target_pairs={{0,4},{4,8},{8,12},{1,5},{5,9},{9,13},{2,6},{6,10},{10,14},{3,7},{... | collective-permute-start | bytes 4423688 | tf_op jit(solution)/shard_map/ppermute | solution.py:290
  80.9 39.8 %collective-permute-start.8 = (bf16[1,36,160,128]{3,2,1,0:T(8,128)(2,1)}, bf16[1,36,160,128]{3,2,1,0:T(8,128)(2,1)}, u32[]{:S(2)}, u32[]{:S(2)}) collective-permute-start(bf16[1,36,160,128]{3,2,1,0:T(8,128)(2,1)} %get-tuple-element.10), channel_id=1, source_target_pairs={{4,0},{8,4},{12,8},{5,1},{9,5},{13,9},{6,2},{10,6},{14,10},{7,3},{... | collective-permute-start | bytes 4423688 | tf_op jit(solution)/shard_map/ppermute | solution.py:291
  83.5 3.7 %collective-permute-start.9 = (f32[8,2,16]{2,1,0:T(2,128)S(1)}, f32[8,2,16]{2,1,0:T(2,128)S(1)}, u32[]{:S(2)}, u32[]{:S(2)}) collective-permute-start(f32[8,2,16]{2,1,0:T(2,128)S(1)} %constant_dynamic-update-slice_fusion.1), channel_id=1, source_target_pairs={{0,2},{2,0},{1,3},{3,1},{4,6},{6,4},{5,7},{7,5},{8,10},{10,8},{9,1... | collective-permute-start | bytes 3080 | tf_op jit(solution)/shard_map/ppermute | solution.py:65
  120.6 7.7 %copy-start.9 = (f32[160]{0:T(256)S(1)}, f32[160]{0:T(256)}, u32[]{:S(2)}) copy-start(f32[160]{0:T(256)} %param.17) | copy-start | bytes 1924
  128.4 9.9 %collective-permute-start.10 = (bf16[4,36,160,128]{3,2,1,0:T(8,128)(2,1)}, bf16[4,36,160,128]{3,2,1,0:T(8,128)(2,1)}, u32[]{:S(2)}, u32[]{:S(2)}) collective-permute-start(bf16[4,36,160,128]{3,2,1,0:T(8,128)(2,1)} %fusion.13.refs_0_.refs_1_.refs_2_), channel_id=1, source_target_pairs={{0,1},{1,0},{2,3},{3,2},{4,5},{5,4},{6,7},{7,6},{8,9},{9,8},{10,11... | collective-permute-start | bytes 17694728 | tf_op jit(solution)/shard_map/ppermute | solution.py:16
